TPU v7x, 32 devices: a whole 2x2x4 slice. The times are simulated.
32 devices in a mesh: groups: 2 (over y), region: 4 (over z), seg: 2 (over x), tb: 2 (over core).
Axes of the slice: x: 2, y: 2, z: 4, core: 2. Of those that a mesh axis runs over, the one named last changes fastest.
Arguments:
- records: bfloat16 [16, 3, 1024], P(('groups', 'region'), None, 'seg'), parts along dimension 0, may hold values from -6 to 6
- templates: bfloat16 [4, 64, 16, 3, 512], P(('groups', 'tb'), None, 'region'), parts along dimension 0, may hold values from -6 to 6
- channel_mask: int32 [4, 64, 16, 3], P(('groups', 'tb'), None, 'region'), parts along dimension 0, may hold values 0 or 1
- station_region: int32 [16], P(('groups', 'region')), parts along dimension 0, may hold values from 0 to 3, as said below
Outputs:
- detect: float32 [4, 64, 1024], P(('groups', 'tb'), None, 'seg'), parts along dimension 0
There are 2 independent parts, one for each index of `groups`. A program takes and returns all parts, laid end to end along the dimension named above; each array names one. Nothing has to cross between parts.
Inputs may be any that keep to these rules, and one draw needn't show every extreme that they name: `station_region`: the 2 stations of one device (aligned blocks of 2 station numbers) name distinct regions. No region is named by more than 4 stations, and one region by exactly 4.
All inputs are finite; a program needn't handle non-finite values. No bound on the sum of `channel_mask` on one device may be relied on, other than what follows from the above.
Results may differ from a plain program's by a relative error of at most 0.0041.
Values may be sent and summed in bfloat16 or wider, within the bound.
No kernel may reach another device: no remote copies, remote signals or barrier semaphores. Data moves between devices by JAX's collectives and lax.ppermute only.
A program may use at most 64 MiB of HBM per device.

v0:
```python
import jax
import jax.numpy as jnp
from jax import lax
from jax.sharding import PartitionSpec as P


def shifted_2(shard, axis, by):
    peers = lax.axis_size(axis)
    pairs = [(i, i + by) for i in range(peers) if 0 <= i + by < peers]
    return lax.ppermute(shard, axis, pairs)


def window_rows(stretch, columns, filter_taps):
    channels, window_span = stretch.shape
    repeated = jnp.broadcast_to(stretch[:, None, :], (channels, columns + 1, window_span))
    repeated = repeated.reshape(channels, (columns + 1) * window_span)
    shifted = repeated[:, : columns * (window_span + 1)].reshape(channels, columns, window_span + 1)
    return shifted[:, :, :filter_taps]


def scaled_windows(stretch, columns, filter_taps):
    widened = window_rows(stretch, columns, filter_taps).astype(jnp.float32)
    energy = jnp.sum(widened * widened, axis=2)
    return (widened / jnp.sqrt(jnp.maximum(energy, 1.0))[:, :, None]).astype(jnp.bfloat16)


def correlate(normed, flat_owned, seg_len):
    stacked_rows, channels, filter_taps = normed.shape
    columns = 128

    def one_block(block_index, stacked):
        offset = block_index * columns
        stretch = lax.dynamic_slice_in_dim(flat_owned, offset, columns + filter_taps - 1, 1)
        scaled = scaled_windows(stretch, columns, filter_taps)
        block_sum = lax.dot_general(
            normed, scaled, (((1, 2), (0, 2)), ((), ())), preferred_element_type=jnp.float32
        )
        return lax.dynamic_update_slice_in_dim(stacked, block_sum, offset, 1)

    return lax.fori_loop(
        0, seg_len // columns, one_block, jnp.zeros((stacked_rows, seg_len), jnp.float32)
    )


def gather_owned(rows_in, station_region, capacity):
    regions = lax.axis_size("region")
    local_count = rows_in.shape[0]
    station_ids = lax.axis_index("region") * local_count + jnp.arange(local_count, dtype=jnp.int32)
    targets = jnp.arange(regions, dtype=jnp.int32)
    select = station_region[None, :] == targets[:, None]
    outgoing = jnp.dot(
        select.astype(jnp.bfloat16),
        rows_in.reshape(local_count, -1),
        preferred_element_type=jnp.float32,
    ).astype(jnp.bfloat16)
    outgoing = outgoing.reshape((regions,) + rows_in.shape[1:])
    sent_ids = jnp.sum(jnp.where(select, station_ids[None, :] + 1, 0), axis=1) - 1
    arrived, arrived_ids = (
        lax.all_to_all(outgoing, "region", split_axis=0, concat_axis=0, tiled=True),
        lax.all_to_all(sent_ids, "region", split_axis=0, concat_axis=0, tiled=True),
    )
    present = arrived_ids >= 0
    before = present[None, :] & (arrived_ids[None, :] < arrived_ids[:, None])
    slot_ranks = jnp.sum(before.astype(jnp.int32), axis=1)
    slot_index = jnp.arange(capacity, dtype=jnp.int32)
    placing = present[None, :] & (slot_ranks[None, :] == slot_index[:, None])
    owned_rows = jnp.dot(
        placing.astype(jnp.bfloat16),
        arrived.reshape(regions, -1),
        preferred_element_type=jnp.float32,
    ).astype(jnp.bfloat16)
    owned_rows = owned_rows.reshape((capacity,) + arrived.shape[1:])
    filled = jnp.sum(placing.astype(jnp.float32), axis=1)
    return (owned_rows, filled)


def per_device(records, templates, channel_mask, station_region):
    local_batches, kept, capacity, components, filter_taps = templates.shape
    seg_len = records.shape[2]
    owned_rows, filled = gather_owned(records, station_region, capacity)
    following = shifted_2(owned_rows, "seg", -1)
    owned_rows = jnp.concatenate([owned_rows, following], axis=2)
    flat_owned = owned_rows.reshape(capacity * components, seg_len + filter_taps)
    weight = channel_mask.astype(jnp.float32) * filled[None, None, :, None]
    widened_templates = templates.astype(jnp.float32)
    template_norm = jnp.sqrt(
        jnp.sum(widened_templates * widened_templates, axis=4, keepdims=True) + 1e-06
    )
    normed = (widened_templates * weight[..., None] / template_norm).astype(jnp.bfloat16)
    normed = normed.reshape(local_batches * kept, capacity * components, filter_taps)
    total_len = seg_len * lax.axis_size("seg")
    stacked = lax.psum(correlate(normed, flat_owned, seg_len), "region")
    power_sum = lax.psum(jnp.sum(stacked * stacked, axis=1), "seg")
    detect = stacked / jnp.sqrt(power_sum / total_len + 1e-06)[:, None]
    return detect.reshape(local_batches, kept, seg_len)


def solution(mesh):
    placed = (
        P(("groups", "region"), None, "seg"),
        P(("groups", "tb"), None, "region", None, None),
        P(("groups", "tb"), None, "region", None),
        P(("groups", "region")),
    )
    return jax.shard_map(
        per_device,
        mesh=mesh,
        in_specs=placed,
        out_specs=P(("groups", "tb"), None, "seg"),
        check_vma=False,
    )
```

profile of v0, /device:TPU:0, one launch (start us, length us, event | category | flops | bytes accessed | tf_op | source)
XLA Modules:
  0.0 112.3 jit_solution(9152218978814384433)
XLA Ops:
  8.0 6.3 %all-to-all-start = ((s32[4,1,1]{2,1,0:T(1,128)}), s32[4,1,1]{2,1,0:T(1,128)S(1)}, u32[]{:S(2)}, u32[]{:S(2)}) async-start(s32[4,1,1]{2,1,0:T(1,128)} %copy.20), calls=%async_computation | async-start | bytes 4096 | tf_op jit(solution)/shard_map/all_to_all | solution.py:60
  15.9 1.6 %fusion.13 = f32[64,4,3]{1,2,0:T(4,128)S(1)} fusion(bf16[1,64,4,3,512]{4,2,3,1,0:T(4,128)(2,1)} %param.7), kind=kLoop, calls=%fused_computation.16 | loop fusion | flops 1178880 | bytes 789504 | tf_op jit(solution)/shard_map/reduce_sum | solution.py:87
  17.6 2.1 %all-to-all-done = s32[4,1,1]{2,1,0:T(1,128)S(1)} async-done(((s32[4,1,1]{2,1,0:T(1,128)}), s32[4,1,1]{2,1,0:T(1,128)S(1)}, u32[]{:S(2)}, u32[]{:S(2)}) %all-to-all-start) | async-done | bytes 48 | tf_op jit(solution)/shard_map/all_to_all | solution.py:60
  19.8 3.3 %all-to-all-start.1 = ((bf16[4,3,512]{2,1,0:T(4,128)(2,1)}), bf16[4,3,512]{2,1,0:T(4,128)(2,1)S(1)}, u32[]{:S(2)}, u32[]{:S(2)}) async-start(bf16[4,3,512]{2,1,0:T(4,128)(2,1)} %copy.21), calls=%async_computation.1 | async-start | bytes 32768 | tf_op jit(solution)/shard_map/all_to_all | solution.py:59
  24.5 4.1 %all-to-all-done.1 = bf16[4,3,512]{2,1,0:T(4,128)(2,1)S(1)} async-done(((bf16[4,3,512]{2,1,0:T(4,128)(2,1)}), bf16[4,3,512]{2,1,0:T(4,128)(2,1)S(1)}, u32[]{:S(2)}, u32[]{:S(2)}) %all-to-all-start.1) | async-done | bytes 12320 | tf_op jit(solution)/shard_map/all_to_all | solution.py:59
  28.7 1.3 %collective-permute-start = (bf16[4,3,512]{2,0,1:T(4,128)(2,1)S(1)}, bf16[4,3,512]{2,0,1:T(4,128)(2,1)S(1)}, u32[]{:S(2)}, u32[]{:S(2)}) collective-permute-start(bf16[4,3,512]{2,0,1:T(4,128)(2,1)S(1)} %bitcast.37), channel_id=1, source_target_pairs={{2,0},{3,1},{6,4},{7,5},{10,8},{11,9},{14,12},{15,13},{18,16},{19,... | collective-permute-start | bytes 36872 | tf_op jit(solution)/shard_map/ppermute | solution.py:10
  30.7 3.6 %collective-permute-done = bf16[4,3,512]{2,0,1:T(4,128)(2,1)S(1)} collective-permute-done((bf16[4,3,512]{2,0,1:T(4,128)(2,1)S(1)}, bf16[4,3,512]{2,0,1:T(4,128)(2,1)S(1)}, u32[]{:S(2)}, u32[]{:S(2)}) %collective-permute-start) | collective-permute-done | bytes 12320 | tf_op jit(solution)/shard_map/ppermute | solution.py:10
  35.0 30.8 %while.13 = (s32[]{:T(128)}, f32[64,512]{1,0:T(8,128)}, bf16[12,1024]{1,0:T(8,128)(2,1)S(1)}, bf16[64,12,512]{2,0,1:T(8,128)(2,1)S(1)}, s32[]{:T(128)}, /*index=5*/s32[]{:T(128)}, s32[]{:T(128)}, s32[]{:T(128)}, s32[]{:T(128)}) while((s32[]{:T(128)}, f32[64,512]{1,0:T(8,128)}, bf16[12,1024]{1,0:T(8,128)(2,1)S(1)}, ...), condition=%wide.region_6.7_spmd, body=%wide.region_4.6_spmd.sunk | while | flops 105381896 | bytes 23079964 | solution.py:40
  35.0 1.5 %broadcast_in_dim.53 = bf16[12,129,639]{2,1,0:T(8,128)(2,1)} broadcast(bf16[12,639]{1,0:T(8,128)(2,1)S(1)} %constant_dynamic-slice_fusion.2), dimensions={0,2} | broadcast | bytes 1993680 | tf_op jit(solution)/shard_map/while/body/eval_jaxpr/broadcast_in_dim | solution.py:15
  36.6 3.6 %reshape.98 = bf16[12,82431]{1,0:T(8,128)(2,1)S(1)} reshape(bf16[12,129,639]{2,1,0:T(8,128)(2,1)} %broadcast_in_dim.53) | data formatting | bytes 3956688 | tf_op jit(solution)/shard_map/while/body/eval_jaxpr/reshape | solution.py:16
  41.3 1.4 %fusion.29 = f32[64,512]{1,0:T(8,128)} fusion(f32[64,512]{1,0:T(8,128)} %get-tuple-element.128, s32[]{:T(128)S(6)} %select_n.22, bf16[64,12,512]{2,0,1:T(8,128)(2,1)S(1)} %get-tuple-element.139, f32[12,128]{1,0:T(8,128)S(1)} %maximum_sqrt_fusion.2, bf16[12,128,640]{2,1,0:T(8,128)(2,1)S(1)} %slice.33), kind=kOutput, calls=%fused_computation.7.clone.1 | convolution fusion | flops 103022592 | bytes 2400260 | tf_op jit(solution)/shard_map/while/body/eval_jaxpr/dot_general | solution.py:35
  42.7 1.5 %broadcast_in_dim.53 = bf16[12,129,639]{2,1,0:T(8,128)(2,1)} broadcast(bf16[12,639]{1,0:T(8,128)(2,1)S(1)} %constant_dynamic-slice_fusion.2), dimensions={0,2} | broadcast | bytes 1993680 | tf_op jit(solution)/shard_map/while/body/eval_jaxpr/broadcast_in_dim | solution.py:15
  44.3 3.6 %reshape.98 = bf16[12,82431]{1,0:T(8,128)(2,1)S(1)} reshape(bf16[12,129,639]{2,1,0:T(8,128)(2,1)} %broadcast_in_dim.53) | data formatting | bytes 3956688 | tf_op jit(solution)/shard_map/while/body/eval_jaxpr/reshape | solution.py:16
  49.0 1.4 %fusion.29 = f32[64,512]{1,0:T(8,128)} fusion(f32[64,512]{1,0:T(8,128)} %get-tuple-element.128, s32[]{:T(128)S(6)} %select_n.22, bf16[64,12,512]{2,0,1:T(8,128)(2,1)S(1)} %get-tuple-element.139, f32[12,128]{1,0:T(8,128)S(1)} %maximum_sqrt_fusion.2, bf16[12,128,640]{2,1,0:T(8,128)(2,1)S(1)} %slice.33), kind=kOutput, calls=%fused_computation.7.clone.1 | convolution fusion | flops 103022592 | bytes 2400260 | tf_op jit(solution)/shard_map/while/body/eval_jaxpr/dot_general | solution.py:35
  50.4 1.5 %broadcast_in_dim.53 = bf16[12,129,639]{2,1,0:T(8,128)(2,1)} broadcast(bf16[12,639]{1,0:T(8,128)(2,1)S(1)} %constant_dynamic-slice_fusion.2), dimensions={0,2} | broadcast | bytes 1993680 | tf_op jit(solution)/shard_map/while/body/eval_jaxpr/broadcast_in_dim | solution.py:15
  52.0 3.6 %reshape.98 = bf16[12,82431]{1,0:T(8,128)(2,1)S(1)} reshape(bf16[12,129,639]{2,1,0:T(8,128)(2,1)} %broadcast_in_dim.53) | data formatting | bytes 3956688 | tf_op jit(solution)/shard_map/while/body/eval_jaxpr/reshape | solution.py:16
  56.7 1.4 %fusion.29 = f32[64,512]{1,0:T(8,128)} fusion(f32[64,512]{1,0:T(8,128)} %get-tuple-element.128, s32[]{:T(128)S(6)} %select_n.22, bf16[64,12,512]{2,0,1:T(8,128)(2,1)S(1)} %get-tuple-element.139, f32[12,128]{1,0:T(8,128)S(1)} %maximum_sqrt_fusion.2, bf16[12,128,640]{2,1,0:T(8,128)(2,1)S(1)} %slice.33), kind=kOutput, calls=%fused_computation.7.clone.1 | convolution fusion | flops 103022592 | bytes 2400260 | tf_op jit(solution)/shard_map/while/body/eval_jaxpr/dot_general | solution.py:35
  58.1 1.5 %broadcast_in_dim.53 = bf16[12,129,639]{2,1,0:T(8,128)(2,1)} broadcast(bf16[12,639]{1,0:T(8,128)(2,1)S(1)} %constant_dynamic-slice_fusion.2), dimensions={0,2} | broadcast | bytes 1993680 | tf_op jit(solution)/shard_map/while/body/eval_jaxpr/broadcast_in_dim | solution.py:15
  59.7 3.6 %reshape.98 = bf16[12,82431]{1,0:T(8,128)(2,1)S(1)} reshape(bf16[12,129,639]{2,1,0:T(8,128)(2,1)} %broadcast_in_dim.53) | data formatting | bytes 3956688 | tf_op jit(solution)/shard_map/while/body/eval_jaxpr/reshape | solution.py:16
  64.4 1.4 %fusion.29 = f32[64,512]{1,0:T(8,128)} fusion(f32[64,512]{1,0:T(8,128)} %get-tuple-element.128, s32[]{:T(128)S(6)} %select_n.22, bf16[64,12,512]{2,0,1:T(8,128)(2,1)S(1)} %get-tuple-element.139, f32[12,128]{1,0:T(8,128)S(1)} %maximum_sqrt_fusion.2, bf16[12,128,640]{2,1,0:T(8,128)(2,1)S(1)} %slice.33), kind=kOutput, calls=%fused_computation.7.clone.1 | convolution fusion | flops 103022592 | bytes 2400260 | tf_op jit(solution)/shard_map/while/body/eval_jaxpr/dot_general | solution.py:35
  65.9 32.0 %all-reduce.2.cloned.1.call-done = f32[64,512]{1,0:T(8,128)} async-done(((f32[64,512]{1,0:T(8,128)}), f32[64,512]{1,0:T(8,128)}) %all-reduce.2.cloned.1.call-update) | async-done | bytes 131088 | tf_op jit(solution)/shard_map/psum | solution.py:92
  97.8 1.0 multiply_reduce_fusion
  98.8 4.9 %psum.15 = f32[64]{0:T(128)S(1)} all-reduce(f32[64]{0:T(128)S(1)} %multiply_reduce_fusion), channel_id=1, replica_groups=mesh['groups'=2,'region'=4,'seg'=2,'tb'=2] {'seg'}, use_global_device_ids=true, to_apply=%region_9.10 | all-reduce | flops 64 | bytes 512 | tf_op jit(solution)/shard_map/psum | solution.py:93
  103.8 1.6 %divide_bitcast_fusion = f32[1,64,512]{2,1,0:T(8,128)} fusion(f32[64,512]{1,0:T(8,128)} %all-reduce.2.cloned.1.call-done, f32[64]{0:T(128)S(1)} %add_sqrt_fusion.1), kind=kLoop, calls=%fused_computation.17 | loop fusion | flops 32768 | bytes 262400 | tf_op jit(solution)/shard_map/reshape | solution.py:95
  (53 shorter events, 10.7 us)
Async XLA Ops:
  6.5 7.8 %copy-start = (bf16[2,3,512]{2,0,1:T(2,128)(2,1)S(1)}, bf16[2,3,512]{2,0,1:T(2,128)(2,1)}, u32[]{:S(2)}) copy-start(bf16[2,3,512]{2,0,1:T(2,128)(2,1)} %param.6) | copy-start | bytes 18436
  6.5 23.5 %copy-start.1 = (bf16[1,64,4,3,512]{4,2,3,1,0:T(4,128)(2,1)S(1)}, bf16[1,64,4,3,512]{4,2,3,1,0:T(4,128)(2,1)}, u32[]{:S(2)}) copy-start(bf16[1,64,4,3,512]{4,2,3,1,0:T(4,128)(2,1)} %param.7) | copy-start | bytes 2359300
  8.0 11.7 %all-to-all-start = ((s32[4,1,1]{2,1,0:T(1,128)}), s32[4,1,1]{2,1,0:T(1,128)S(1)}, u32[]{:S(2)}, u32[]{:S(2)}) async-start(s32[4,1,1]{2,1,0:T(1,128)} %copy.20), calls=%async_computation | async-start | bytes 4096 | tf_op jit(solution)/shard_map/all_to_all | solution.py:60
  19.8 8.8 %all-to-all-start.1 = ((bf16[4,3,512]{2,1,0:T(4,128)(2,1)}), bf16[4,3,512]{2,1,0:T(4,128)(2,1)S(1)}, u32[]{:S(2)}, u32[]{:S(2)}) async-start(bf16[4,3,512]{2,1,0:T(4,128)(2,1)} %copy.21), calls=%async_computation.1 | async-start | bytes 32768 | tf_op jit(solution)/shard_map/all_to_all | solution.py:59
  23.0 74.8 %all-reduce.2.cloned.1.call-start = ((), (), s32[]{:S(2)}) async-start(), calls=%async_computation.2 | async-start | bytes 262144 | tf_op jit(solution)/shard_map/psum | solution.py:92
  28.7 5.6 %collective-permute-start = (bf16[4,3,512]{2,0,1:T(4,128)(2,1)S(1)}, bf16[4,3,512]{2,0,1:T(4,128)(2,1)S(1)}, u32[]{:S(2)}, u32[]{:S(2)}) collective-permute-start(bf16[4,3,512]{2,0,1:T(4,128)(2,1)S(1)} %bitcast.37), channel_id=1, source_target_pairs={{2,0},{3,1},{6,4},{7,5},{10,8},{11,9},{14,12},{15,13},{18,16},{19,... | collective-permute-start | bytes 36872 | tf_op jit(solution)/shard_map/ppermute | solution.py:10
Sparse Core Ops, SparseCore 0:
  66.0 31.8 all-reduce.1
where the time goes:
time: 113 us; the launch traced here: 112 us
  waiting for transfers between devices  41.8 us (37%)
  local copies, waits for them, and re-layouts  25.8 us (23%)
  between operations  13.5 us (12%)
  starting transfers between devices  10.9 us (10%)
  other arithmetic  8.53 us (8%)
  matrix products  6.61 us (6%)
  blocking collectives  4.94 us (4%)
    psum x1, waiting for transfers between devices, per_device(): stacked = lax.psum(correlate(normed, flat_owned, seg_len), 'region')  32 us
    reshape x4, local copies, waits for them, and re-layouts, window_rows(): repeated = repeated.reshape(channels, (columns + 1) * window_span)  14.4 us
    all_to_all x1, starting transfers between devices, gather_owned(): lax.all_to_all(sent_ids, 'region', split_axis=0, concat_axis=0, tiled=True)  6.32 us
    broadcast_in_dim x4, local copies, waits for them, and re-layouts, window_rows(): jnp.broadcast_to(stretch[:, None, :], (channels, columns + 1, window_span))  6.07 us
    dot_general x4, matrix products, one_block(): lax.dot_general(normed, scaled, (((1, 2), (0, 2)), ((), ())), preferred_e...  5.57 us
    psum x1, blocking collectives, per_device(): power_sum = lax.psum(jnp.sum(stacked * stacked, axis=1), 'seg')  4.94 us
    all_to_all x1, waiting for transfers between devices, gather_owned(): lax.all_to_all(outgoing, 'region', split_axis=0, concat_axis=0, tiled=True)  4.14 us
    ppermute x1, waiting for transfers between devices, shifted_2(): return lax.ppermute(shard, axis, pairs)  3.57 us
  transfers between devices with their start and end apart: 4, of which 4 were waited for; matrix products, arithmetic and copies ran while one was open for 5% of the time, Pallas kernels for 0%

commit v1 on v0

v1 whole, which is shorter than its diff:
```python
import jax
import jax.numpy as jnp
from jax import lax
from jax.sharding import PartitionSpec as P


def window_rows(stretch, columns, filter_taps):
    channels, window_span = stretch.shape
    repeated = jnp.broadcast_to(stretch[:, None, :], (channels, columns + 1, window_span))
    repeated = repeated.reshape(channels, (columns + 1) * window_span)
    shifted = repeated[:, : columns * (window_span + 1)].reshape(channels, columns, window_span + 1)
    return shifted[:, :, :filter_taps]


def scaled_windows(stretch, columns, filter_taps):
    widened = window_rows(stretch, columns, filter_taps).astype(jnp.float32)
    energy = jnp.sum(widened * widened, axis=2)
    return (widened / jnp.sqrt(jnp.maximum(energy, 1.0))[:, :, None]).astype(jnp.bfloat16)


def correlate(normed, flat_owned, seg_len):
    stacked_rows, channels, filter_taps = normed.shape
    columns = 128

    def one_block(block_index, stacked):
        offset = block_index * columns
        stretch = lax.dynamic_slice_in_dim(flat_owned, offset, columns + filter_taps - 1, 1)
        scaled = scaled_windows(stretch, columns, filter_taps)
        block_sum = lax.dot_general(
            normed, scaled, (((1, 2), (0, 2)), ((), ())), preferred_element_type=jnp.float32
        )
        return lax.dynamic_update_slice_in_dim(stacked, block_sum, offset, 1)

    return lax.fori_loop(
        0, seg_len // columns, one_block, jnp.zeros((stacked_rows, seg_len), jnp.float32)
    )


def ordered_sum(part, axis):
    size = lax.axis_size(axis)
    if size == 1:
        return part
    me = lax.axis_index(axis)
    received = [part] + [
        lax.ppermute(part, axis, [(i, (i + k) % size) for i in range(size)]) for k in range(1, size)
    ]
    stack = jnp.stack(received)
    order = (me - jnp.arange(size, dtype=jnp.int32)) % size
    return jnp.sum(jnp.take(stack, order, axis=0), axis=0)


def gather_owned(records, station_region, capacity, filter_taps):
    local_count, components, seg_len = records.shape
    regions = lax.axis_size("region")
    segs = lax.axis_size("seg")
    tag = jnp.broadcast_to(station_region.astype(jnp.bfloat16)[:, None, None], (local_count, 1, seg_len))
    payload = jnp.concatenate([records, tag], axis=1)
    axes = ("region", "seg")
    same_seg = [payload]
    for k in range(1, regions):
        pairs = [
            (r * segs + s, ((r + k) % regions) * segs + s) for r in range(regions) for s in range(segs)
        ]
        same_seg.append(lax.ppermute(payload, axes, pairs))
    next_seg = []
    for k in range(regions):
        pairs = [
            (r * segs + s + 1, ((r + k) % regions) * segs + s)
            for r in range(regions)
            for s in range(segs - 1)
        ]
        next_seg.append(lax.ppermute(records[:, :, :filter_taps], axes, pairs))
    me = lax.axis_index("region")
    order = (me - jnp.arange(regions, dtype=jnp.int32)) % regions
    here = jnp.take(jnp.stack(same_seg), order, axis=0)
    ahead = jnp.take(jnp.stack(next_seg), order, axis=0)
    stations = regions * local_count
    here = here.reshape(stations, components + 1, seg_len)
    ahead = ahead.reshape(stations, components, filter_taps)
    region_of = here[:, components, 0].astype(jnp.int32)
    rows = jnp.concatenate([here[:, :components, :], ahead], axis=2)
    station_ids = jnp.arange(stations, dtype=jnp.int32)
    earlier = (region_of[None, :] == region_of[:, None]) & (station_ids[None, :] < station_ids[:, None])
    ranks = jnp.sum(earlier.astype(jnp.int32), axis=1)
    slot_index = jnp.arange(capacity, dtype=jnp.int32)
    placing = (region_of[None, :] == me) & (ranks[None, :] == slot_index[:, None])
    owned_rows = jnp.dot(
        placing.astype(jnp.bfloat16), rows.reshape(stations, -1), preferred_element_type=jnp.float32
    ).astype(jnp.bfloat16)
    owned_rows = owned_rows.reshape(capacity, components, seg_len + filter_taps)
    filled = jnp.sum(placing.astype(jnp.float32), axis=1)
    return owned_rows, filled


def per_device(records, templates, channel_mask, station_region):
    local_batches, kept, capacity, components, filter_taps = templates.shape
    seg_len = records.shape[2]
    owned_rows, filled = gather_owned(records, station_region, capacity, filter_taps)
    flat_owned = owned_rows.reshape(capacity * components, seg_len + filter_taps)
    weight = channel_mask.astype(jnp.float32) * filled[None, None, :, None]
    widened_templates = templates.astype(jnp.float32)
    template_norm = jnp.sqrt(
        jnp.sum(widened_templates * widened_templates, axis=4, keepdims=True) + 1e-06
    )
    normed = (widened_templates * weight[..., None] / template_norm).astype(jnp.bfloat16)
    normed = normed.reshape(local_batches * kept, capacity * components, filter_taps)
    total_len = seg_len * lax.axis_size("seg")
    stacked = ordered_sum(correlate(normed, flat_owned, seg_len), "region")
    power_sum = ordered_sum(jnp.sum(stacked * stacked, axis=1), "seg")
    detect = stacked / jnp.sqrt(power_sum / total_len + 1e-06)[:, None]
    return detect.reshape(local_batches, kept, seg_len)


def solution(mesh):
    placed = (
        P(("groups", "region"), None, "seg"),
        P(("groups", "tb"), None, "region", None, None),
        P(("groups", "tb"), None, "region", None),
        P(("groups", "region")),
    )
    return jax.shard_map(
        per_device,
        mesh=mesh,
        in_specs=placed,
        out_specs=P(("groups", "tb"), None, "seg"),
        check_vma=False,
    )
```

time: 113 us -> 75 us (0.66)
  waiting for transfers between devices: 41.8 us -> 14.6 us
  between operations: 13.5 us -> 0.23 us
  starting transfers between devices: 10.9 us -> 17.8 us
  blocking collectives: 4.94 us -> 0 us
  local copies, waits for them, and re-layouts: 25.8 us -> 27.1 us
    psum x1 -> x0, waiting for transfers between devices: 32 us -> none  [per_device(): stacked = lax.psum(correlate(normed, flat_owned, seg_len), 'region')]
    ppermute x1 -> x11, starting transfers between devices: 1.28 us -> 17.8 us  [the longest x4 6.39 us: ordered_sum(): lax.ppermute(part, axis, [(i, (i + k) % size) for i in range(size)])]
    ppermute x1 -> x11, waiting for transfers between devices: 3.57 us -> 14.6 us  [the longest x4 10.8 us: ordered_sum(): lax.ppermute(part, axis, [(i, (i + k) % size) for i in range(size)])]
    all_to_all x2 -> x0, starting transfers between devices: 9.57 us -> none  [the longest x1 6.32 us: gather_owned(): lax.all_to_all(sent_ids, 'region', split_axis=0, concat_axis=0, tiled=True)]
    all_to_all x2 -> x0, waiting for transfers between devices: 6.26 us -> none  [the longest x1 4.14 us: gather_owned(): lax.all_to_all(outgoing, 'region', split_axis=0, concat_axis=0, tiled=True)]
    psum x1 -> x0, blocking collectives: 4.94 us -> none  [per_device(): power_sum = lax.psum(jnp.sum(stacked * stacked, axis=1), 'seg')]
    gather x0 -> x6, local copies, waits for them, and re-layouts: none -> 2.4 us  [the longest x2 1.14 us: ordered_sum(): return jnp.sum(jnp.take(stack, order, axis=0), axis=0)]
    another operation x0 -> x5, other arithmetic: none -> 1.75 us  [the longest x2 0.95 us: ordered_sum(): stack = jnp.stack(received)]
  transfers between devices with their start and end apart: 4 -> 11, of which waited for: 4 -> 5; matrix products, arithmetic and copies ran while one was open for 5% -> 7% of each run, Pallas kernels for 0% -> 0%
where the time goes in v1:
time: 75 us; the launch traced here: 74.6 us
  local copies, waits for them, and re-layouts  27.1 us (36%)
  starting transfers between devices  17.8 us (24%)
  waiting for transfers between devices  14.6 us (19%)
  other arithmetic  8.86 us (12%)
  matrix products  5.77 us (8%)
    reshape x4, local copies, waits for them, and re-layouts, window_rows(): repeated = repeated.reshape(channels, (columns + 1) * window_span)  14.4 us
    ppermute x4, waiting for transfers between devices, ordered_sum(): lax.ppermute(part, axis, [(i, (i + k) % size) for i in range(size)])  10.8 us
    ppermute x4, starting transfers between devices, ordered_sum(): lax.ppermute(part, axis, [(i, (i + k) % size) for i in range(size)])  6.39 us
    ppermute x3, starting transfers between devices, gather_owned(): same_seg.append(lax.ppermute(payload, axes, pairs))  6.11 us
    broadcast_in_dim x4, local copies, waits for them, and re-layouts, window_rows(): jnp.broadcast_to(stretch[:, None, :], (channels, columns + 1, window_span))  6.07 us
    dot_general x4, matrix products, one_block(): lax.dot_general(normed, scaled, (((1, 2), (0, 2)), ((), ())), preferred_e...  5.63 us
    ppermute x4, starting transfers between devices, gather_owned(): next_seg.append(lax.ppermute(records[:, :, :filter_taps], axes, pairs))  5.29 us
    ppermute x3, waiting for transfers between devices, gather_owned(): same_seg.append(lax.ppermute(payload, axes, pairs))  3.72 us
  transfers between devices with their start and end apart: 11, of which 5 were waited for; matrix products, arithmetic and copies ran while one was open for 7% of the time, Pallas kernels for 0%

profile of v1, /device:TPU:0, one launch (start us, length us, event | category | flops | bytes accessed | tf_op | source)
XLA Modules:
  0.0 74.6 jit_solution(119158243789793440)
XLA Ops:
  0.0 1.4 %collective-permute-start.6 = (bf16[2,3,512]{2,0,1:T(2,128)(2,1)}, bf16[2,3,512]{2,0,1:T(2,128)(2,1)S(1)}, u32[]{:S(2)}, u32[]{:S(2)}) collective-permute-start(bf16[2,3,512]{2,0,1:T(2,128)(2,1)} %param.6), channel_id=1, source_target_pairs={{2,12},{6,0},{10,4},{14,8},{3,13},{7,1},{11,5},{15,9},{18,28},{22,... | collective-permute-start | bytes 18440 | tf_op jit(solution)/shard_map/ppermute | solution.py:72
  1.4 1.3 %collective-permute-start.5 = (bf16[2,3,512]{2,0,1:T(2,128)(2,1)}, bf16[2,3,512]{2,0,1:T(2,128)(2,1)S(1)}, u32[]{:S(2)}, u32[]{:S(2)}) collective-permute-start(bf16[2,3,512]{2,0,1:T(2,128)(2,1)} %param.6), channel_id=1, source_target_pairs={{2,8},{6,12},{10,0},{14,4},{3,9},{7,13},{11,1},{15,5},{18,24},{22,... | collective-permute-start | bytes 18440 | tf_op jit(solution)/shard_map/ppermute | solution.py:72
  2.7 1.3 %collective-permute-start.4 = (bf16[2,3,512]{2,0,1:T(2,128)(2,1)}, bf16[2,3,512]{2,0,1:T(2,128)(2,1)S(1)}, u32[]{:S(2)}, u32[]{:S(2)}) collective-permute-start(bf16[2,3,512]{2,0,1:T(2,128)(2,1)} %param.6), channel_id=1, source_target_pairs={{2,4},{6,8},{10,12},{14,0},{3,5},{7,9},{11,13},{15,1},{18,20},{22,... | collective-permute-start | bytes 18440 | tf_op jit(solution)/shard_map/ppermute | solution.py:72
  6.8 5.1 %collective-permute-start.2 = (bf16[2,4,512]{2,0,1:T(2,128)(2,1)S(1)}, bf16[2,4,512]{2,0,1:T(2,128)(2,1)S(1)}, u32[]{:S(2)}, u32[]{:S(2)}) collective-permute-start(bf16[2,4,512]{2,0,1:T(2,128)(2,1)S(1)} %pad_maximum_fusion.3), channel_id=1, source_target_pairs={{0,12},{2,14},{4,0},{6,2},{8,4},{10,6},{12,8},{14,10},{1,13},{3,15... | collective-permute-start | bytes 24584 | tf_op jit(solution)/shard_map/ppermute | solution.py:64
  12.6 1.6 %fusion.13 = f32[64,4,3]{1,2,0:T(4,128)S(1)} fusion(bf16[1,64,4,3,512]{4,2,3,1,0:T(4,128)(2,1)} %param.7), kind=kLoop, calls=%fused_computation.19 | loop fusion | flops 1178880 | bytes 789504 | tf_op jit(solution)/shard_map/reduce_sum | solution.py:103
  16.4 2.7 %collective-permute-done.1 = bf16[2,4,512]{2,0,1:T(2,128)(2,1)S(1)} collective-permute-done((bf16[2,4,512]{2,0,1:T(2,128)(2,1)S(1)}, bf16[2,4,512]{2,0,1:T(2,128)(2,1)S(1)}, u32[]{:S(2)}, u32[]{:S(2)}) %collective-permute-start.1) | collective-permute-done | bytes 8224 | tf_op jit(solution)/shard_map/ppermute | solution.py:64
  23.2 30.9 %while.13 = (s32[]{:T(128)}, f32[64,512]{1,0:T(8,128)}, bf16[12,1024]{1,0:T(8,128)(2,1)S(1)}, bf16[64,12,512]{2,0,1:T(8,128)(2,1)S(1)}, s32[]{:T(128)}, /*index=5*/s32[]{:T(128)}, s32[]{:T(128)}, s32[]{:T(128)}, s32[]{:T(128)}) while((s32[]{:T(128)}, f32[64,512]{1,0:T(8,128)}, bf16[12,1024]{1,0:T(8,128)(2,1)S(1)}, ...), condition=%wide.region_5.6_spmd, body=%wide.region_3.5_spmd.sunk | while | flops 105381896 | bytes 23079972 | solution.py:34
  23.2 1.5 %broadcast_in_dim.104 = bf16[12,129,639]{2,1,0:T(8,128)(2,1)} broadcast(bf16[12,639]{1,0:T(8,128)(2,1)S(1)} %constant_dynamic-slice_fusion.2), dimensions={0,2} | broadcast | bytes 1993680 | tf_op jit(solution)/shard_map/while/body/eval_jaxpr/broadcast_in_dim | solution.py:9
  24.8 3.6 %reshape.249 = bf16[12,82431]{1,0:T(8,128)(2,1)S(1)} reshape(bf16[12,129,639]{2,1,0:T(8,128)(2,1)} %broadcast_in_dim.104) | data formatting | bytes 3956688 | tf_op jit(solution)/shard_map/while/body/eval_jaxpr/reshape | solution.py:10
  29.6 1.4 %fusion.36 = f32[64,512]{1,0:T(8,128)} fusion(f32[64,512]{1,0:T(8,128)} %get-tuple-element.128, s32[]{:T(128)S(6)} %select_n.155, bf16[64,12,512]{2,0,1:T(8,128)(2,1)S(1)} %get-tuple-element.139, f32[12,128]{1,0:T(8,128)S(1)} %maximum_sqrt_fusion.2, bf16[12,128,640]{2,1,0:T(8,128)(2,1)S(1)} %slice.54), kind=kOutput, calls=%fused_computation.11.clone.1 | convolution fusion | flops 103022592 | bytes 2400260 | tf_op jit(solution)/shard_map/while/body/eval_jaxpr/dot_general | solution.py:29
  31.0 1.5 %broadcast_in_dim.104 = bf16[12,129,639]{2,1,0:T(8,128)(2,1)} broadcast(bf16[12,639]{1,0:T(8,128)(2,1)S(1)} %constant_dynamic-slice_fusion.2), dimensions={0,2} | broadcast | bytes 1993680 | tf_op jit(solution)/shard_map/while/body/eval_jaxpr/broadcast_in_dim | solution.py:9
  32.5 3.6 %reshape.249 = bf16[12,82431]{1,0:T(8,128)(2,1)S(1)} reshape(bf16[12,129,639]{2,1,0:T(8,128)(2,1)} %broadcast_in_dim.104) | data formatting | bytes 3956688 | tf_op jit(solution)/shard_map/while/body/eval_jaxpr/reshape | solution.py:10
  37.3 1.4 %fusion.36 = f32[64,512]{1,0:T(8,128)} fusion(f32[64,512]{1,0:T(8,128)} %get-tuple-element.128, s32[]{:T(128)S(6)} %select_n.155, bf16[64,12,512]{2,0,1:T(8,128)(2,1)S(1)} %get-tuple-element.139, f32[12,128]{1,0:T(8,128)S(1)} %maximum_sqrt_fusion.2, bf16[12,128,640]{2,1,0:T(8,128)(2,1)S(1)} %slice.54), kind=kOutput, calls=%fused_computation.11.clone.1 | convolution fusion | flops 103022592 | bytes 2400260 | tf_op jit(solution)/shard_map/while/body/eval_jaxpr/dot_general | solution.py:29
  38.7 1.5 %broadcast_in_dim.104 = bf16[12,129,639]{2,1,0:T(8,128)(2,1)} broadcast(bf16[12,639]{1,0:T(8,128)(2,1)S(1)} %constant_dynamic-slice_fusion.2), dimensions={0,2} | broadcast | bytes 1993680 | tf_op jit(solution)/shard_map/while/body/eval_jaxpr/broadcast_in_dim | solution.py:9
  40.2 3.6 %reshape.249 = bf16[12,82431]{1,0:T(8,128)(2,1)S(1)} reshape(bf16[12,129,639]{2,1,0:T(8,128)(2,1)} %broadcast_in_dim.104) | data formatting | bytes 3956688 | tf_op jit(solution)/shard_map/while/body/eval_jaxpr/reshape | solution.py:10
  45.0 1.4 %fusion.36 = f32[64,512]{1,0:T(8,128)} fusion(f32[64,512]{1,0:T(8,128)} %get-tuple-element.128, s32[]{:T(128)S(6)} %select_n.155, bf16[64,12,512]{2,0,1:T(8,128)(2,1)S(1)} %get-tuple-element.139, f32[12,128]{1,0:T(8,128)S(1)} %maximum_sqrt_fusion.2, bf16[12,128,640]{2,1,0:T(8,128)(2,1)S(1)} %slice.54), kind=kOutput, calls=%fused_computation.11.clone.1 | convolution fusion | flops 103022592 | bytes 2400260 | tf_op jit(solution)/shard_map/while/body/eval_jaxpr/dot_general | solution.py:29
  46.4 1.5 %broadcast_in_dim.104 = bf16[12,129,639]{2,1,0:T(8,128)(2,1)} broadcast(bf16[12,639]{1,0:T(8,128)(2,1)S(1)} %constant_dynamic-slice_fusion.2), dimensions={0,2} | broadcast | bytes 1993680 | tf_op jit(solution)/shard_map/while/body/eval_jaxpr/broadcast_in_dim | solution.py:9
  47.9 3.6 %reshape.249 = bf16[12,82431]{1,0:T(8,128)(2,1)S(1)} reshape(bf16[12,129,639]{2,1,0:T(8,128)(2,1)} %broadcast_in_dim.104) | data formatting | bytes 3956688 | tf_op jit(solution)/shard_map/while/body/eval_jaxpr/reshape | solution.py:10
  52.7 1.4 %fusion.36 = f32[64,512]{1,0:T(8,128)} fusion(f32[64,512]{1,0:T(8,128)} %get-tuple-element.128, s32[]{:T(128)S(6)} %select_n.155, bf16[64,12,512]{2,0,1:T(8,128)(2,1)S(1)} %get-tuple-element.139, f32[12,128]{1,0:T(8,128)S(1)} %maximum_sqrt_fusion.2, bf16[12,128,640]{2,1,0:T(8,128)(2,1)S(1)} %slice.54), kind=kOutput, calls=%fused_computation.11.clone.1 | convolution fusion | flops 103022592 | bytes 2400260 | tf_op jit(solution)/shard_map/while/body/eval_jaxpr/dot_general | solution.py:29
  55.2 2.0 %collective-permute-start.7 = (f32[64,512]{1,0:T(8,128)}, f32[64,512]{1,0:T(8,128)S(1)}, u32[]{:S(2)}, u32[]{:S(2)}) collective-permute-start(f32[64,512]{1,0:T(8,128)} %get-tuple-element.84), channel_id=1, source_target_pairs={{0,4},{4,8},{8,12},{12,0},{1,5},{5,9},{9,13},{13,1},{2,6},{6,10},{... | collective-permute-start | bytes 393224 | tf_op jit(solution)/shard_map/ppermute | solution.py:45
  57.2 2.8 %collective-permute-done.9 = f32[64,512]{1,0:T(8,128)S(1)} collective-permute-done((f32[64,512]{1,0:T(8,128)}, f32[64,512]{1,0:T(8,128)S(1)}, u32[]{:S(2)}, u32[]{:S(2)}) %collective-permute-start.9) | collective-permute-done | bytes 131104 | tf_op jit(solution)/shard_map/ppermute | solution.py:45
  60.0 6.5 %collective-permute-done.8 = f32[64,512]{1,0:T(8,128)S(1)} collective-permute-done((f32[64,512]{1,0:T(8,128)}, f32[64,512]{1,0:T(8,128)S(1)}, u32[]{:S(2)}, u32[]{:S(2)}) %collective-permute-start.8) | collective-permute-done | bytes 131104 | tf_op jit(solution)/shard_map/ppermute | solution.py:45
  68.3 3.3 %collective-permute-start.10 = (f32[64]{0:T(128)S(1)}, f32[64]{0:T(128)S(1)}, u32[]{:S(2)}, u32[]{:S(2)}) collective-permute-start(f32[64]{0:T(128)S(1)} %multiply_reduce_fusion), channel_id=1, source_target_pairs={{0,2},{2,0},{1,3},{3,1},{4,6},{6,4},{5,7},{7,5},{8,10},{10,8},{9,1... | collective-permute-start | bytes 776 | tf_op jit(solution)/shard_map/ppermute | solution.py:45
  71.6 1.5 %collective-permute-done.10 = f32[64]{0:T(128)S(1)} collective-permute-done((f32[64]{0:T(128)S(1)}, f32[64]{0:T(128)S(1)}, u32[]{:S(2)}, u32[]{:S(2)}) %collective-permute-start.10) | collective-permute-done | bytes 288 | tf_op jit(solution)/shard_map/ppermute | solution.py:45
  (83 shorter events, 18.4 us)
Async XLA Ops:
  0.0 21.9 %copy-start = (bf16[1,64,4,3,512]{4,2,3,1,0:T(4,128)(2,1)S(1)}, bf16[1,64,4,3,512]{4,2,3,1,0:T(4,128)(2,1)}, u32[]{:S(2)}) copy-start(bf16[1,64,4,3,512]{4,2,3,1,0:T(4,128)(2,1)} %param.7) | copy-start | bytes 2359300
  0.0 21.7 %copy-start.1 = (s32[1,64,4,3]{1,2,3,0:T(4,128)S(1)}, s32[1,64,4,3]{1,2,3,0:T(4,128)}, u32[]{:S(2)}) copy-start(s32[1,64,4,3]{1,2,3,0:T(4,128)} %param.8) | copy-start | bytes 9220
  0.0 14.5 %collective-permute-start.6 = (bf16[2,3,512]{2,0,1:T(2,128)(2,1)}, bf16[2,3,512]{2,0,1:T(2,128)(2,1)S(1)}, u32[]{:S(2)}, u32[]{:S(2)}) collective-permute-start(bf16[2,3,512]{2,0,1:T(2,128)(2,1)} %param.6), channel_id=1, source_target_pairs={{2,12},{6,0},{10,4},{14,8},{3,13},{7,1},{11,5},{15,9},{18,28},{22,... | collective-permute-start | bytes 18440 | tf_op jit(solution)/shard_map/ppermute | solution.py:72
  1.4 13.1 %collective-permute-start.5 = (bf16[2,3,512]{2,0,1:T(2,128)(2,1)}, bf16[2,3,512]{2,0,1:T(2,128)(2,1)S(1)}, u32[]{:S(2)}, u32[]{:S(2)}) collective-permute-start(bf16[2,3,512]{2,0,1:T(2,128)(2,1)} %param.6), channel_id=1, source_target_pairs={{2,8},{6,12},{10,0},{14,4},{3,9},{7,13},{11,1},{15,5},{18,24},{22,... | collective-permute-start | bytes 18440 | tf_op jit(solution)/shard_map/ppermute | solution.py:72
  2.7 12.8 %collective-permute-start.4 = (bf16[2,3,512]{2,0,1:T(2,128)(2,1)}, bf16[2,3,512]{2,0,1:T(2,128)(2,1)S(1)}, u32[]{:S(2)}, u32[]{:S(2)}) collective-permute-start(bf16[2,3,512]{2,0,1:T(2,128)(2,1)} %param.6), channel_id=1, source_target_pairs={{2,4},{6,8},{10,12},{14,0},{3,5},{7,9},{11,13},{15,1},{18,20},{22,... | collective-permute-start | bytes 18440 | tf_op jit(solution)/shard_map/ppermute | solution.py:72
  4.0 11.5 %collective-permute-start.3 = (bf16[2,3,512]{2,0,1:T(2,128)(2,1)}, bf16[2,3,512]{2,0,1:T(2,128)(2,1)S(1)}, u32[]{:S(2)}, u32[]{:S(2)}) collective-permute-start(bf16[2,3,512]{2,0,1:T(2,128)(2,1)} %param.6), channel_id=1, source_target_pairs={{2,0},{6,4},{10,8},{14,12},{3,1},{7,5},{11,9},{15,13},{18,16},{22,... | collective-permute-start | bytes 18440 | tf_op jit(solution)/shard_map/ppermute | solution.py:72
  6.8 9.6 %collective-permute-start.2 = (bf16[2,4,512]{2,0,1:T(2,128)(2,1)S(1)}, bf16[2,4,512]{2,0,1:T(2,128)(2,1)S(1)}, u32[]{:S(2)}, u32[]{:S(2)}) collective-permute-start(bf16[2,4,512]{2,0,1:T(2,128)(2,1)S(1)} %pad_maximum_fusion.3), channel_id=1, source_target_pairs={{0,12},{2,14},{4,0},{6,2},{8,4},{10,6},{12,8},{14,10},{1,13},{3,15... | collective-permute-start | bytes 24584 | tf_op jit(solution)/shard_map/ppermute | solution.py:64
  14.5 4.6 %collective-permute-start.1 = (bf16[2,4,512]{2,0,1:T(2,128)(2,1)S(1)}, bf16[2,4,512]{2,0,1:T(2,128)(2,1)S(1)}, u32[]{:S(2)}, u32[]{:S(2)}) collective-permute-start(bf16[2,4,512]{2,0,1:T(2,128)(2,1)S(1)} %pad_maximum_fusion.3), channel_id=1, source_target_pairs={{0,8},{2,10},{4,12},{6,14},{8,0},{10,2},{12,4},{14,6},{1,9},{3,11}... | collective-permute-start | bytes 24584 | tf_op jit(solution)/shard_map/ppermute | solution.py:64
  14.6 5.5 %collective-permute-start = (bf16[2,4,512]{2,0,1:T(2,128)(2,1)S(1)}, bf16[2,4,512]{2,0,1:T(2,128)(2,1)S(1)}, u32[]{:S(2)}, u32[]{:S(2)}) collective-permute-start(bf16[2,4,512]{2,0,1:T(2,128)(2,1)S(1)} %pad_maximum_fusion.3), channel_id=1, source_target_pairs={{0,4},{2,6},{4,8},{6,10},{8,12},{10,14},{12,0},{14,2},{1,5},{3,7},... | collective-permute-start | bytes 24584 | tf_op jit(solution)/shard_map/ppermute | solution.py:64
  54.1 5.9 %collective-permute-start.9 = (f32[64,512]{1,0:T(8,128)}, f32[64,512]{1,0:T(8,128)S(1)}, u32[]{:S(2)}, u32[]{:S(2)}) collective-permute-start(f32[64,512]{1,0:T(8,128)} %get-tuple-element.84), channel_id=1, source_target_pairs={{0,12},{4,0},{8,4},{12,8},{1,13},{5,1},{9,5},{13,9},{2,14},{6,2},{... | collective-permute-start | bytes 393224 | tf_op jit(solution)/shard_map/ppermute | solution.py:45
  54.6 12.0 %collective-permute-start.8 = (f32[64,512]{1,0:T(8,128)}, f32[64,512]{1,0:T(8,128)S(1)}, u32[]{:S(2)}, u32[]{:S(2)}) collective-permute-start(f32[64,512]{1,0:T(8,128)} %get-tuple-element.84), channel_id=1, source_target_pairs={{0,8},{4,12},{8,0},{12,4},{1,9},{5,13},{9,1},{13,5},{2,10},{6,14},... | collective-permute-start | bytes 393224 | tf_op jit(solution)/shard_map/ppermute | solution.py:45
  55.2 11.4 %collective-permute-start.7 = (f32[64,512]{1,0:T(8,128)}, f32[64,512]{1,0:T(8,128)S(1)}, u32[]{:S(2)}, u32[]{:S(2)}) collective-permute-start(f32[64,512]{1,0:T(8,128)} %get-tuple-element.84), channel_id=1, source_target_pairs={{0,4},{4,8},{8,12},{12,0},{1,5},{5,9},{9,13},{13,1},{2,6},{6,10},{... | collective-permute-start | bytes 393224 | tf_op jit(solution)/shard_map/ppermute | solution.py:45
  68.3 4.8 %collective-permute-start.10 = (f32[64]{0:T(128)S(1)}, f32[64]{0:T(128)S(1)}, u32[]{:S(2)}, u32[]{:S(2)}) collective-permute-start(f32[64]{0:T(128)S(1)} %multiply_reduce_fusion), channel_id=1, source_target_pairs={{0,2},{2,0},{1,3},{3,1},{4,6},{6,4},{5,7},{7,5},{8,10},{10,8},{9,1... | collective-permute-start | bytes 776 | tf_op jit(solution)/shard_map/ppermute | solution.py:45

commit v2 on v1

--- a/solution.py
+++ b/solution.py
@@ -2,38 +2,52 @@
 import jax.numpy as jnp
 from jax import lax
 from jax.sharding import PartitionSpec as P
+from jax.experimental import pallas as pl
+from jax.experimental.pallas import tpu as pltpu
 
 
-def window_rows(stretch, columns, filter_taps):
-    channels, window_span = stretch.shape
-    repeated = jnp.broadcast_to(stretch[:, None, :], (channels, columns + 1, window_span))
-    repeated = repeated.reshape(channels, (columns + 1) * window_span)
-    shifted = repeated[:, : columns * (window_span + 1)].reshape(channels, columns, window_span + 1)
-    return shifted[:, :, :filter_taps]
+def hankel_kernel(x_ref, n_ref, o_ref, h_ref):
+    channels, rows, width = n_ref.shape
+    taps_blocks = width // 128
+    out_blocks = o_ref.shape[1] // 128
+    blocks = taps_blocks + out_blocks
+    row = lax.broadcasted_iota(jnp.int32, (128, 128), 0)
+    lane = lax.broadcasted_iota(jnp.int32, (128, 128), 1)
+    low = lane <= row
 
+    def one_channel(c, acc):
+        rolled = [
+            pltpu.roll(x_ref[pl.ds(c * blocks + m, 128, stride=0), :], 1, 1, stride=1, stride_axis=0)
+            for m in range(blocks)
+        ]
+        squares = []
+        for m in range(blocks - 1):
+            window = jnp.where(low, rolled[m], rolled[m + 1])
+            squares.append(jnp.sum(window * window, axis=0, keepdims=True))
+            window = window.astype(jnp.bfloat16)
+            for p in range(taps_blocks):
+                a = m - p
+                if 0 <= a < out_blocks:
+                    h_ref[p * 128 : (p + 1) * 128, a * 128 : (a + 1) * 128] = window
+        energy = jnp.concatenate(
+            [sum(squares[a + p] for p in range(taps_blocks)) for a in range(out_blocks)], axis=1
+        )
+        part = jnp.dot(n_ref[c], h_ref[...], preferred_element_type=jnp.float32)
+        return acc + part * (1.0 / jnp.sqrt(jnp.maximum(energy, 1.0)))
 
-def scaled_windows(stretch, columns, filter_taps):
-    widened = window_rows(stretch, columns, filter_taps).astype(jnp.float32)
-    energy = jnp.sum(widened * widened, axis=2)
-    return (widened / jnp.sqrt(jnp.maximum(energy, 1.0))[:, :, None]).astype(jnp.bfloat16)
+    o_ref[...] = lax.fori_loop(0, channels, one_channel, jnp.zeros(o_ref.shape, jnp.float32))
 
 
 def correlate(normed, flat_owned, seg_len):
-    stacked_rows, channels, filter_taps = normed.shape
-    columns = 128
-
-    def one_block(block_index, stacked):
-        offset = block_index * columns
-        stretch = lax.dynamic_slice_in_dim(flat_owned, offset, columns + filter_taps - 1, 1)
-        scaled = scaled_windows(stretch, columns, filter_taps)
-        block_sum = lax.dot_general(
-            normed, scaled, (((1, 2), (0, 2)), ((), ())), preferred_element_type=jnp.float32
-        )
-        return lax.dynamic_update_slice_in_dim(stacked, block_sum, offset, 1)
-
-    return lax.fori_loop(
-        0, seg_len // columns, one_block, jnp.zeros((stacked_rows, seg_len), jnp.float32)
-    )
+    rows, channels, filter_taps = normed.shape
+    flipped = normed.reshape(rows, channels, filter_taps // 128, 128)[..., ::-1]
+    flipped = jnp.transpose(flipped.reshape(rows, channels, filter_taps), (1, 0, 2))
+    blocks = flat_owned.astype(jnp.float32).reshape(channels * (flat_owned.shape[1] // 128), 128)
+    return pl.pallas_call(
+        hankel_kernel,
+        out_shape=jax.ShapeDtypeStruct((rows, seg_len), jnp.float32),
+        scratch_shapes=[pltpu.VMEM((filter_taps, seg_len), jnp.bfloat16)],
+    )(blocks, flipped)
 
 
 def ordered_sum(part, axis):

time: 75 us -> 53.6 us (0.71)
  local copies, waits for them, and re-layouts: 27.1 us -> 7.77 us
  Pallas kernels: 0 us -> 6.68 us
  matrix products: 5.77 us -> 0.13 us
  waiting for transfers between devices: 14.6 us -> 10.8 us
  starting transfers between devices: 17.8 us -> 20.2 us
  other arithmetic: 8.86 us -> 7.32 us
    reshape x8 -> x1, local copies, waits for them, and re-layouts: 15.1 us -> 1.17 us  [correlate(): flipped.reshape(rows, channels, filter_taps)]
    broadcast_in_dim x5 -> x0, local copies, waits for them, and re-layouts: 6.74 us -> none  [the longest x4 6.07 us: window_rows(): jnp.broadcast_to(stretch[:, None, :], (channels, columns + 1, window_span))]
    pallas_call x0 -> x1, Pallas kernels: none -> 6.68 us  [correlate(): pl.pallas_call(hankel_kernel, out_shape=jax.ShapeDtypeStruct((rows, seg_l...]
    dot_general x4 -> x0, matrix products: 5.63 us -> none  [one_block(): lax.dot_general(normed, scaled, (((1, 2), (0, 2)), ((), ())), preferred_e...]
    rev x0 -> x1, local copies, waits for them, and re-layouts: none -> 2.81 us  [correlate(): flipped = normed.reshape(rows, channels, filter_taps // 128, 128)[..., ::-1]]
    ppermute x3, waiting for transfers between devices: 3.72 us -> 1.51 us  [gather_owned(): same_seg.append(lax.ppermute(payload, axes, pairs))]
    while x4 -> x0, local copies, waits for them, and re-layouts: 1.65 us -> none
    ppermute x4, starting transfers between devices: 6.39 us -> 8.01 us  [ordered_sum(): lax.ppermute(part, axis, [(i, (i + k) % size) for i in range(size)])]
  transfers between devices with their start and end apart: 11 -> 11, of which waited for: 5 -> 4; matrix products, arithmetic and copies ran while one was open for 7% -> 9% of each run, Pallas kernels for 0% -> 0%
where the time goes in v2:
time: 53.6 us; the launch traced here: 53.1 us
  starting transfers between devices  20.2 us (38%)
  waiting for transfers between devices  10.8 us (20%)
  local copies, waits for them, and re-layouts  7.77 us (14%)
  other arithmetic  7.32 us (14%)
  Pallas kernels  6.68 us (12%)
    ppermute x4, waiting for transfers between devices, ordered_sum(): lax.ppermute(part, axis, [(i, (i + k) % size) for i in range(size)])  9.26 us
    ppermute x4, starting transfers between devices, ordered_sum(): lax.ppermute(part, axis, [(i, (i + k) % size) for i in range(size)])  8.01 us
    ppermute x3, starting transfers between devices, gather_owned(): same_seg.append(lax.ppermute(payload, axes, pairs))  7.03 us
    pallas_call x1, Pallas kernels, correlate(): pl.pallas_call(hankel_kernel, out_shape=jax.ShapeDtypeStruct((rows, seg_l...  6.68 us
    ppermute x4, starting transfers between devices, gather_owned(): next_seg.append(lax.ppermute(records[:, :, :filter_taps], axes, pairs))  5.16 us
    rev x1, local copies, waits for them, and re-layouts, correlate(): flipped = normed.reshape(rows, channels, filter_taps // 128, 128)[..., ::-1]  2.81 us
    reduce_sum x1, other arithmetic, per_device(): jnp.sum(widened_templates * widened_templates, axis=4, keepdims=True)  1.65 us
    ppermute x3, waiting for transfers between devices, gather_owned(): same_seg.append(lax.ppermute(payload, axes, pairs))  1.51 us
  transfers between devices with their start and end apart: 11, of which 4 were waited for; matrix products, arithmetic and copies ran while one was open for 9% of the time, Pallas kernels for 0%

profile of v2, /device:TPU:0, one launch (start us, length us, event | category | flops | bytes accessed | tf_op | source)
XLA Modules:
  0.0 53.1 jit_solution(4850773203342425564)
XLA Ops:
  0.0 1.3 %collective-permute-start.3 = (bf16[2,3,512]{2,0,1:T(2,128)(2,1)}, bf16[2,3,512]{2,0,1:T(2,128)(2,1)S(1)}, u32[]{:S(2)}, u32[]{:S(2)}) collective-permute-start(bf16[2,3,512]{2,0,1:T(2,128)(2,1)} %param.4), channel_id=1, source_target_pairs={{2,0},{6,4},{10,8},{14,12},{3,1},{7,5},{11,9},{15,13},{18,16},{22,... | collective-permute-start | bytes 18440 | tf_op jit(solution)/shard_map/ppermute | solution.py:86
  1.3 1.3 %collective-permute-start.4 = (bf16[2,3,512]{2,0,1:T(2,128)(2,1)}, bf16[2,3,512]{2,0,1:T(2,128)(2,1)S(1)}, u32[]{:S(2)}, u32[]{:S(2)}) collective-permute-start(bf16[2,3,512]{2,0,1:T(2,128)(2,1)} %param.4), channel_id=1, source_target_pairs={{2,4},{6,8},{10,12},{14,0},{3,5},{7,9},{11,13},{15,1},{18,20},{22,... | collective-permute-start | bytes 18440 | tf_op jit(solution)/shard_map/ppermute | solution.py:86
  2.6 1.3 %collective-permute-start.5 = (bf16[2,3,512]{2,0,1:T(2,128)(2,1)}, bf16[2,3,512]{2,0,1:T(2,128)(2,1)S(1)}, u32[]{:S(2)}, u32[]{:S(2)}) collective-permute-start(bf16[2,3,512]{2,0,1:T(2,128)(2,1)} %param.4), channel_id=1, source_target_pairs={{2,8},{6,12},{10,0},{14,4},{3,9},{7,13},{11,1},{15,5},{18,24},{22,... | collective-permute-start | bytes 18440 | tf_op jit(solution)/shard_map/ppermute | solution.py:86
  3.9 1.3 %collective-permute-start.6 = (bf16[2,3,512]{2,0,1:T(2,128)(2,1)}, bf16[2,3,512]{2,0,1:T(2,128)(2,1)S(1)}, u32[]{:S(2)}, u32[]{:S(2)}) collective-permute-start(bf16[2,3,512]{2,0,1:T(2,128)(2,1)} %param.4), channel_id=1, source_target_pairs={{2,12},{6,0},{10,4},{14,8},{3,13},{7,1},{11,5},{15,9},{18,28},{22,... | collective-permute-start | bytes 18440 | tf_op jit(solution)/shard_map/ppermute | solution.py:86
  5.2 0.7 %convert_element_type.46 = bf16[2]{0:T(256)(128)(2,1)S(1)} convert(s32[2]{0:T(128)} %param.7) | non-fusion elementwise | flops 2 | bytes 12 | tf_op jit(solution)/shard_map/convert_element_type | solution.py:70
  5.9 0.7 %pad_maximum_fusion.3 = bf16[2,4,512]{2,0,1:T(2,128)(2,1)S(1)} fusion(bf16[2,1,512]{2,0,1:T(2,128)(2,1)S(1)} %broadcast_in_dim.65, bf16[2,3,512]{2,0,1:T(2,128)(2,1)} %param.4), kind=kLoop, calls=%fused_computation.21 | loop fusion | flops 4096 | bytes 16384 | tf_op jit(solution)/shard_map/concatenate | solution.py:71
  6.6 3.1 %collective-permute-start = (bf16[2,4,512]{2,0,1:T(2,128)(2,1)S(1)}, bf16[2,4,512]{2,0,1:T(2,128)(2,1)S(1)}, u32[]{:S(2)}, u32[]{:S(2)}) collective-permute-start(bf16[2,4,512]{2,0,1:T(2,128)(2,1)S(1)} %pad_maximum_fusion.3), channel_id=1, source_target_pairs={{0,4},{2,6},{4,8},{6,10},{8,12},{10,14},{12,0},{14,2},{1,5},{3,7},... | collective-permute-start | bytes 24584 | tf_op jit(solution)/shard_map/ppermute | solution.py:78
  9.7 0.7 %fusion.17 = bf16[1,2,4,512]{3,1,2,0:T(2,128)(2,1)S(1)} fusion(bf16[2,1,512]{2,0,1:T(2,128)(2,1)S(1)} %broadcast_in_dim.65, bf16[2,3,512]{2,0,1:T(2,128)(2,1)} %param.4), kind=kLoop, calls=%fused_computation.63 | loop fusion | flops 4096 | bytes 16384 | tf_op jit(solution)/shard_map/stack | solution.py:89
  10.5 1.6 %fusion.3 = f32[64,4,3]{1,2,0:T(4,128)S(1)} fusion(bf16[1,64,4,3,512]{4,2,3,1,0:T(4,128)(2,1)} %param.5), kind=kLoop, calls=%fused_computation.10 | loop fusion | flops 1178880 | bytes 789504 | tf_op jit(solution)/shard_map/reduce_sum | solution.py:117
  12.4 2.6 %collective-permute-start.1 = (bf16[2,4,512]{2,0,1:T(2,128)(2,1)S(1)}, bf16[2,4,512]{2,0,1:T(2,128)(2,1)S(1)}, u32[]{:S(2)}, u32[]{:S(2)}) collective-permute-start(bf16[2,4,512]{2,0,1:T(2,128)(2,1)S(1)} %pad_maximum_fusion.3), channel_id=1, source_target_pairs={{0,8},{2,10},{4,12},{6,14},{8,0},{10,2},{12,4},{14,6},{1,9},{3,11}... | collective-permute-start | bytes 24584 | tf_op jit(solution)/shard_map/ppermute | solution.py:78
  15.0 1.3 %collective-permute-start.2 = (bf16[2,4,512]{2,0,1:T(2,128)(2,1)S(1)}, bf16[2,4,512]{2,0,1:T(2,128)(2,1)S(1)}, u32[]{:S(2)}, u32[]{:S(2)}) collective-permute-start(bf16[2,4,512]{2,0,1:T(2,128)(2,1)S(1)} %pad_maximum_fusion.3), channel_id=1, source_target_pairs={{0,12},{2,14},{4,0},{6,2},{8,4},{10,6},{12,8},{14,10},{1,13},{3,15... | collective-permute-start | bytes 24584 | tf_op jit(solution)/shard_map/ppermute | solution.py:78
  17.2 1.5 %collective-permute-done.2 = bf16[2,4,512]{2,0,1:T(2,128)(2,1)S(1)} collective-permute-done((bf16[2,4,512]{2,0,1:T(2,128)(2,1)S(1)}, bf16[2,4,512]{2,0,1:T(2,128)(2,1)S(1)}, u32[]{:S(2)}, u32[]{:S(2)}) %collective-permute-start.2) | collective-permute-done | bytes 8224 | tf_op jit(solution)/shard_map/ppermute | solution.py:78
  18.7 0.6 %gather_fusion = bf16[4,2,4,512]{3,1,2,0:T(2,128)(2,1)S(1)} fusion(bf16[4,2,4,512]{3,1,2,0:T(2,128)(2,1)S(1)} %pad_maximum_fusion.1, s32[1024]{0:T(1024)S(1)} %pad_clamp_fusion.1), kind=kCustom, calls=%fused_computation | custom fusion | bytes 65552 | tf_op jit(solution)/shard_map/jit(_take)/gather | solution.py:89
  20.2 0.6 %reshape.197.x_ref = f32[96,128]{1,0:T(8,128)} reshape(f32[4,3072]{1,0:T(4,128)S(1)} %fusion) | data formatting | bytes 98304 | tf_op jit(solution)/shard_map/convert_element_type | solution.py:45
  21.9 2.8 %rev.3 = bf16[64,12,4,128]{3,2,0,1:T(4,128)(2,1)S(1)} reverse(bf16[64,12,4,128]{3,2,0,1:T(4,128)(2,1)S(1)} %reshape_reshape.4), dimensions={3} | reverse | bytes 1572864 | tf_op jit(solution)/shard_map/rev | solution.py:43
  24.8 1.2 %reshape.195 = bf16[64,12,512]{2,0,1:T(8,128)(2,1)} reshape(bf16[64,12,4,128]{3,2,0,1:T(4,128)(2,1)S(1)} %rev.3) | data formatting | bytes 1572864 | tf_op jit(solution)/shard_map/reshape | solution.py:44
  25.9 6.7 %shard_map.46 = f32[64,512]{1,0:T(8,128)} custom-call(f32[96,128]{1,0:T(8,128)} %reshape.197.x_ref, bf16[12,64,512]{2,1,0:T(8,128)(2,1)} %bitcast.39), custom_call_target="tpu_custom_call" | custom-call | tf_op jit(solution)/shard_map/pallas_call | solution.py:46
  32.6 3.7 %collective-permute-start.8 = (f32[64,512]{1,0:T(8,128)}, f32[64,512]{1,0:T(8,128)S(1)}, u32[]{:S(2)}, u32[]{:S(2)}) collective-permute-start(f32[64,512]{1,0:T(8,128)} %shard_map.46), channel_id=1, source_target_pairs={{0,8},{4,12},{8,0},{12,4},{1,9},{5,13},{9,1},{13,5},{2,10},{6,14},... | collective-permute-start | bytes 393224 | tf_op jit(solution)/shard_map/ppermute | solution.py:59
  36.5 4.7 %collective-permute-done.7 = f32[64,512]{1,0:T(8,128)S(1)} collective-permute-done((f32[64,512]{1,0:T(8,128)}, f32[64,512]{1,0:T(8,128)S(1)}, u32[]{:S(2)}, u32[]{:S(2)}) %collective-permute-start.7) | collective-permute-done | bytes 131104 | tf_op jit(solution)/shard_map/ppermute | solution.py:59
  41.2 3.1 %collective-permute-done.8 = f32[64,512]{1,0:T(8,128)S(1)} collective-permute-done((f32[64,512]{1,0:T(8,128)}, f32[64,512]{1,0:T(8,128)S(1)}, u32[]{:S(2)}, u32[]{:S(2)}) %collective-permute-start.8) | collective-permute-done | bytes 131104 | tf_op jit(solution)/shard_map/ppermute | solution.py:59
  44.2 0.9 %pad_maximum_fusion = f32[4,64,512]{2,1,0:T(8,128)S(1)} fusion(f32[1,64,512]{2,1,0:T(8,128)S(1)} %bitcast.45, f32[1,64,512]{2,1,0:T(8,128)S(1)} %bitcast.44, f32[1,64,512]{2,1,0:T(8,128)S(1)} %bitcast.43, f32[1,64,512]{2,1,0:T(8,128)} %bitcast.40), kind=kLoop, calls=%fused_computation.11 | loop fusion | flops 393216 | bytes 1048576 | tf_op jit(solution)/shard_map/stack | solution.py:61
  46.0 4.2 %collective-permute-start.10 = (f32[64]{0:T(128)S(1)}, f32[64]{0:T(128)S(1)}, u32[]{:S(2)}, u32[]{:S(2)}) collective-permute-start(f32[64]{0:T(128)S(1)} %multiply_reduce_fusion), channel_id=1, source_target_pairs={{0,2},{2,0},{1,3},{3,1},{4,6},{6,4},{5,7},{7,5},{8,10},{10,8},{9,1... | collective-permute-start | bytes 776 | tf_op jit(solution)/shard_map/ppermute | solution.py:59
  50.2 1.5 %collective-permute-done.10 = f32[64]{0:T(128)S(1)} collective-permute-done((f32[64]{0:T(128)S(1)}, f32[64]{0:T(128)S(1)}, u32[]{:S(2)}, u32[]{:S(2)}) %collective-permute-start.10) | collective-permute-done | bytes 288 | tf_op jit(solution)/shard_map/ppermute | solution.py:59
  52.4 0.7 %bitcast_divide_fusion = f32[1,64,512]{2,1,0:T(8,128)} fusion(f32[64,512]{1,0:T(8,128)S(1)} %select_reduce_fusion, f32[64]{0:T(128)S(1)} %add_sqrt_fusion.1), kind=kLoop, calls=%fused_computation.13 | loop fusion | flops 32768 | bytes 262400 | tf_op jit(solution)/shard_map/div | solution.py:124
  (49 shorter events, 4.7 us)
Async XLA Ops:
  0.0 12.4 %collective-permute-start.3 = (bf16[2,3,512]{2,0,1:T(2,128)(2,1)}, bf16[2,3,512]{2,0,1:T(2,128)(2,1)S(1)}, u32[]{:S(2)}, u32[]{:S(2)}) collective-permute-start(bf16[2,3,512]{2,0,1:T(2,128)(2,1)} %param.4), channel_id=1, source_target_pairs={{2,0},{6,4},{10,8},{14,12},{3,1},{7,5},{11,9},{15,13},{18,16},{22,... | collective-permute-start | bytes 18440 | tf_op jit(solution)/shard_map/ppermute | solution.py:86
  1.3 13.7 %collective-permute-start.4 = (bf16[2,3,512]{2,0,1:T(2,128)(2,1)}, bf16[2,3,512]{2,0,1:T(2,128)(2,1)S(1)}, u32[]{:S(2)}, u32[]{:S(2)}) collective-permute-start(bf16[2,3,512]{2,0,1:T(2,128)(2,1)} %param.4), channel_id=1, source_target_pairs={{2,4},{6,8},{10,12},{14,0},{3,5},{7,9},{11,13},{15,1},{18,20},{22,... | collective-permute-start | bytes 18440 | tf_op jit(solution)/shard_map/ppermute | solution.py:86
  2.6 13.8 %collective-permute-start.5 = (bf16[2,3,512]{2,0,1:T(2,128)(2,1)}, bf16[2,3,512]{2,0,1:T(2,128)(2,1)S(1)}, u32[]{:S(2)}, u32[]{:S(2)}) collective-permute-start(bf16[2,3,512]{2,0,1:T(2,128)(2,1)} %param.4), channel_id=1, source_target_pairs={{2,8},{6,12},{10,0},{14,4},{3,9},{7,13},{11,1},{15,5},{18,24},{22,... | collective-permute-start | bytes 18440 | tf_op jit(solution)/shard_map/ppermute | solution.py:86
  3.9 12.5 %collective-permute-start.6 = (bf16[2,3,512]{2,0,1:T(2,128)(2,1)}, bf16[2,3,512]{2,0,1:T(2,128)(2,1)S(1)}, u32[]{:S(2)}, u32[]{:S(2)}) collective-permute-start(bf16[2,3,512]{2,0,1:T(2,128)(2,1)} %param.4), channel_id=1, source_target_pairs={{2,12},{6,0},{10,4},{14,8},{3,13},{7,1},{11,5},{15,9},{18,28},{22,... | collective-permute-start | bytes 18440 | tf_op jit(solution)/shard_map/ppermute | solution.py:86
  6.6 10.5 %collective-permute-start = (bf16[2,4,512]{2,0,1:T(2,128)(2,1)S(1)}, bf16[2,4,512]{2,0,1:T(2,128)(2,1)S(1)}, u32[]{:S(2)}, u32[]{:S(2)}) collective-permute-start(bf16[2,4,512]{2,0,1:T(2,128)(2,1)S(1)} %pad_maximum_fusion.3), channel_id=1, source_target_pairs={{0,4},{2,6},{4,8},{6,10},{8,12},{10,14},{12,0},{14,2},{1,5},{3,7},... | collective-permute-start | bytes 24584 | tf_op jit(solution)/shard_map/ppermute | solution.py:78
  12.1 8.7 %copy-start.1 = (s32[1,64,4,3]{1,2,3,0:T(4,128)S(1)}, s32[1,64,4,3]{1,2,3,0:T(4,128)}, u32[]{:S(2)}) copy-start(s32[1,64,4,3]{1,2,3,0:T(4,128)} %param.6) | copy-start | bytes 9220
  12.1 8.9 %copy-start = (bf16[1,64,4,3,512]{4,2,3,1,0:T(4,128)(2,1)S(1)}, bf16[1,64,4,3,512]{4,2,3,1,0:T(4,128)(2,1)}, u32[]{:S(2)}) copy-start(bf16[1,64,4,3,512]{4,2,3,1,0:T(4,128)(2,1)} %param.5) | copy-start | bytes 2359300
  12.4 4.7 %collective-permute-start.1 = (bf16[2,4,512]{2,0,1:T(2,128)(2,1)S(1)}, bf16[2,4,512]{2,0,1:T(2,128)(2,1)S(1)}, u32[]{:S(2)}, u32[]{:S(2)}) collective-permute-start(bf16[2,4,512]{2,0,1:T(2,128)(2,1)S(1)} %pad_maximum_fusion.3), channel_id=1, source_target_pairs={{0,8},{2,10},{4,12},{6,14},{8,0},{10,2},{12,4},{14,6},{1,9},{3,11}... | collective-permute-start | bytes 24584 | tf_op jit(solution)/shard_map/ppermute | solution.py:78
  15.0 3.7 %collective-permute-start.2 = (bf16[2,4,512]{2,0,1:T(2,128)(2,1)S(1)}, bf16[2,4,512]{2,0,1:T(2,128)(2,1)S(1)}, u32[]{:S(2)}, u32[]{:S(2)}) collective-permute-start(bf16[2,4,512]{2,0,1:T(2,128)(2,1)S(1)} %pad_maximum_fusion.3), channel_id=1, source_target_pairs={{0,12},{2,14},{4,0},{6,2},{8,4},{10,6},{12,8},{14,10},{1,13},{3,15... | collective-permute-start | bytes 24584 | tf_op jit(solution)/shard_map/ppermute | solution.py:78
  32.6 8.5 %collective-permute-start.7 = (f32[64,512]{1,0:T(8,128)}, f32[64,512]{1,0:T(8,128)S(1)}, u32[]{:S(2)}, u32[]{:S(2)}) collective-permute-start(f32[64,512]{1,0:T(8,128)} %shard_map.46), channel_id=1, source_target_pairs={{0,4},{4,8},{8,12},{12,0},{1,5},{5,9},{9,13},{13,1},{2,6},{6,10},{... | collective-permute-start | bytes 393224 | tf_op jit(solution)/shard_map/ppermute | solution.py:59
  32.6 11.6 %collective-permute-start.8 = (f32[64,512]{1,0:T(8,128)}, f32[64,512]{1,0:T(8,128)S(1)}, u32[]{:S(2)}, u32[]{:S(2)}) collective-permute-start(f32[64,512]{1,0:T(8,128)} %shard_map.46), channel_id=1, source_target_pairs={{0,8},{4,12},{8,0},{12,4},{1,9},{5,13},{9,1},{13,5},{2,10},{6,14},... | collective-permute-start | bytes 393224 | tf_op jit(solution)/shard_map/ppermute | solution.py:59
  36.3 7.9 %collective-permute-start.9 = (f32[64,512]{1,0:T(8,128)}, f32[64,512]{1,0:T(8,128)S(1)}, u32[]{:S(2)}, u32[]{:S(2)}) collective-permute-start(f32[64,512]{1,0:T(8,128)} %shard_map.46), channel_id=1, source_target_pairs={{0,12},{4,0},{8,4},{12,8},{1,13},{5,1},{9,5},{13,9},{2,14},{6,2},{... | collective-permute-start | bytes 393224 | tf_op jit(solution)/shard_map/ppermute | solution.py:59
  46.0 5.7 %collective-permute-start.10 = (f32[64]{0:T(128)S(1)}, f32[64]{0:T(128)S(1)}, u32[]{:S(2)}, u32[]{:S(2)}) collective-permute-start(f32[64]{0:T(128)S(1)} %multiply_reduce_fusion), channel_id=1, source_target_pairs={{0,2},{2,0},{1,3},{3,1},{4,6},{6,4},{5,7},{7,5},{8,10},{10,8},{9,1... | collective-permute-start | bytes 776 | tf_op jit(solution)/shard_map/ppermute | solution.py:59

commit v3 on v2

--- a/solution.py
+++ b/solution.py
@@ -7,17 +7,18 @@
 
 
 def hankel_kernel(x_ref, n_ref, o_ref, h_ref):
-    channels, rows, width = n_ref.shape
+    width = h_ref.shape[0]
+    channels = n_ref.shape[1] // width
     taps_blocks = width // 128
     out_blocks = o_ref.shape[1] // 128
     blocks = taps_blocks + out_blocks
     row = lax.broadcasted_iota(jnp.int32, (128, 128), 0)
     lane = lax.broadcasted_iota(jnp.int32, (128, 128), 1)
-    low = lane <= row
+    low = lane >= row
 
     def one_channel(c, acc):
         rolled = [
-            pltpu.roll(x_ref[pl.ds(c * blocks + m, 128, stride=0), :], 1, 1, stride=1, stride_axis=0)
+            pltpu.roll(x_ref[pl.ds(c * blocks + m, 128, stride=0), :], 0, 1, stride=1, stride_axis=0)
             for m in range(blocks)
         ]
         squares = []
@@ -32,22 +33,26 @@
         energy = jnp.concatenate(
             [sum(squares[a + p] for p in range(taps_blocks)) for a in range(out_blocks)], axis=1
         )
-        part = jnp.dot(n_ref[c], h_ref[...], preferred_element_type=jnp.float32)
+        start = pl.multiple_of(c * width, 128)
+        part = jnp.dot(n_ref[:, pl.ds(start, width)], h_ref[...], preferred_element_type=jnp.float32)
         return acc + part * (1.0 / jnp.sqrt(jnp.maximum(energy, 1.0)))
 
     o_ref[...] = lax.fori_loop(0, channels, one_channel, jnp.zeros(o_ref.shape, jnp.float32))
 
 
+def unflip(stacked):
+    rows, seg_len = stacked.shape
+    return stacked.reshape(rows, seg_len // 128, 128)[..., ::-1].reshape(rows, seg_len)
+
+
 def correlate(normed, flat_owned, seg_len):
     rows, channels, filter_taps = normed.shape
-    flipped = normed.reshape(rows, channels, filter_taps // 128, 128)[..., ::-1]
-    flipped = jnp.transpose(flipped.reshape(rows, channels, filter_taps), (1, 0, 2))
-    blocks = flat_owned.astype(jnp.float32).reshape(channels * (flat_owned.shape[1] // 128), 128)
+    blocks = flat_owned.reshape(channels * (flat_owned.shape[1] // 128), 128)[:, ::-1]
     return pl.pallas_call(
         hankel_kernel,
         out_shape=jax.ShapeDtypeStruct((rows, seg_len), jnp.float32),
         scratch_shapes=[pltpu.VMEM((filter_taps, seg_len), jnp.bfloat16)],
-    )(blocks, flipped)
+    )(blocks.astype(jnp.float32), normed.reshape(rows, channels * filter_taps))
 
 
 def ordered_sum(part, axis):
@@ -121,7 +126,7 @@
     total_len = seg_len * lax.axis_size("seg")
     stacked = ordered_sum(correlate(normed, flat_owned, seg_len), "region")
     power_sum = ordered_sum(jnp.sum(stacked * stacked, axis=1), "seg")
-    detect = stacked / jnp.sqrt(power_sum / total_len + 1e-06)[:, None]
+    detect = unflip(stacked) / jnp.sqrt(power_sum / total_len + 1e-06)[:, None]
     return detect.reshape(local_batches, kept, seg_len)
 
 

time: 53.6 us -> 51.8 us (0.966)
  local copies, waits for them, and re-layouts: 7.77 us -> 5.58 us
  other arithmetic: 7.32 us -> 8.02 us
    rev x1 -> x2, local copies, waits for them, and re-layouts: 2.81 us -> 0.27 us  [the longest x1 0.18 us: unflip(): stacked.reshape(rows, seg_len // 128, 128)[..., ::-1].reshape(rows, seg_len)]
    another operation x1 -> x2, local copies, waits for them, and re-layouts: 0.18 us -> 1.85 us  [the longest x1 1.84 us: correlate(): normed.reshape(rows, channels * filter_taps)]
    reshape x1 -> x2, local copies, waits for them, and re-layouts: 1.17 us -> 0.1 us  [unflip(): stacked.reshape(rows, seg_len // 128, 128)[..., ::-1].reshape(rows, seg_len)]
    convert_element_type x1 -> x0, local copies, waits for them, and re-layouts: 0.64 us -> none  [correlate(): flat_owned.astype(jnp.float32)]
    convert_element_type x0 -> x1, other arithmetic: none -> 0.63 us  [correlate(): blocks.astype(jnp.float32)]
  transfers between devices with their start and end apart: 11 -> 11, of which waited for: 4 -> 4; matrix products, arithmetic and copies ran while one was open for 9% -> 10% of each run, Pallas kernels for 0% -> 0%
where the time goes in v3:
time: 51.8 us; the launch traced here: 51.3 us
  starting transfers between devices  20.2 us (39%)
  waiting for transfers between devices  10.5 us (20%)
  other arithmetic  8.02 us (15%)
  Pallas kernels  6.68 us (13%)
  local copies, waits for them, and re-layouts  5.58 us (11%)
    ppermute x4, waiting for transfers between devices, ordered_sum(): lax.ppermute(part, axis, [(i, (i + k) % size) for i in range(size)])  8.96 us
    ppermute x4, starting transfers between devices, ordered_sum(): lax.ppermute(part, axis, [(i, (i + k) % size) for i in range(size)])  8 us
    ppermute x3, starting transfers between devices, gather_owned(): same_seg.append(lax.ppermute(payload, axes, pairs))  7.03 us
    pallas_call x1, Pallas kernels, correlate(): pl.pallas_call(hankel_kernel, out_shape=jax.ShapeDtypeStruct((rows, seg_l...  6.68 us
    ppermute x4, starting transfers between devices, gather_owned(): next_seg.append(lax.ppermute(records[:, :, :filter_taps], axes, pairs))  5.16 us
    another operation x1, local copies, waits for them, and re-layouts, correlate(): normed.reshape(rows, channels * filter_taps)  1.84 us
    reduce_sum x1, other arithmetic, per_device(): jnp.sum(widened_templates * widened_templates, axis=4, keepdims=True)  1.72 us
    ppermute x3, waiting for transfers between devices, gather_owned(): same_seg.append(lax.ppermute(payload, axes, pairs))  1.51 us
  transfers between devices with their start and end apart: 11, of which 4 were waited for; matrix products, arithmetic and copies ran while one was open for 10% of the time, Pallas kernels for 0%

profile of v3, /device:TPU:0, one launch (start us, length us, event | category | flops | bytes accessed | tf_op | source)
XLA Modules:
  0.0 51.3 jit_solution(9108806695120888945)
XLA Ops:
  0.0 1.3 %collective-permute-start.3 = (bf16[2,3,512]{2,0,1:T(2,128)(2,1)}, bf16[2,3,512]{2,0,1:T(2,128)(2,1)S(1)}, u32[]{:S(2)}, u32[]{:S(2)}) collective-permute-start(bf16[2,3,512]{2,0,1:T(2,128)(2,1)} %param.4), channel_id=1, source_target_pairs={{2,0},{6,4},{10,8},{14,12},{3,1},{7,5},{11,9},{15,13},{18,16},{22,... | collective-permute-start | bytes 18440 | tf_op jit(solution)/shard_map/ppermute | solution.py:91
  1.3 1.3 %collective-permute-start.4 = (bf16[2,3,512]{2,0,1:T(2,128)(2,1)}, bf16[2,3,512]{2,0,1:T(2,128)(2,1)S(1)}, u32[]{:S(2)}, u32[]{:S(2)}) collective-permute-start(bf16[2,3,512]{2,0,1:T(2,128)(2,1)} %param.4), channel_id=1, source_target_pairs={{2,4},{6,8},{10,12},{14,0},{3,5},{7,9},{11,13},{15,1},{18,20},{22,... | collective-permute-start | bytes 18440 | tf_op jit(solution)/shard_map/ppermute | solution.py:91
  2.6 1.3 %collective-permute-start.5 = (bf16[2,3,512]{2,0,1:T(2,128)(2,1)}, bf16[2,3,512]{2,0,1:T(2,128)(2,1)S(1)}, u32[]{:S(2)}, u32[]{:S(2)}) collective-permute-start(bf16[2,3,512]{2,0,1:T(2,128)(2,1)} %param.4), channel_id=1, source_target_pairs={{2,8},{6,12},{10,0},{14,4},{3,9},{7,13},{11,1},{15,5},{18,24},{22,... | collective-permute-start | bytes 18440 | tf_op jit(solution)/shard_map/ppermute | solution.py:91
  3.9 1.3 %collective-permute-start.6 = (bf16[2,3,512]{2,0,1:T(2,128)(2,1)}, bf16[2,3,512]{2,0,1:T(2,128)(2,1)S(1)}, u32[]{:S(2)}, u32[]{:S(2)}) collective-permute-start(bf16[2,3,512]{2,0,1:T(2,128)(2,1)} %param.4), channel_id=1, source_target_pairs={{2,12},{6,0},{10,4},{14,8},{3,13},{7,1},{11,5},{15,9},{18,28},{22,... | collective-permute-start | bytes 18440 | tf_op jit(solution)/shard_map/ppermute | solution.py:91
  5.2 0.7 %convert_element_type.42 = bf16[2]{0:T(256)(128)(2,1)S(1)} convert(s32[2]{0:T(128)} %param.7) | non-fusion elementwise | flops 2 | bytes 12 | tf_op jit(solution)/shard_map/convert_element_type | solution.py:75
  5.9 0.7 %pad_maximum_fusion.3 = bf16[2,4,512]{2,0,1:T(2,128)(2,1)S(1)} fusion(bf16[2,1,512]{2,0,1:T(2,128)(2,1)S(1)} %broadcast_in_dim.65, bf16[2,3,512]{2,0,1:T(2,128)(2,1)} %param.4), kind=kLoop, calls=%fused_computation.20 | loop fusion | flops 4096 | bytes 16384 | tf_op jit(solution)/shard_map/concatenate | solution.py:76
  6.6 3.1 %collective-permute-start = (bf16[2,4,512]{2,0,1:T(2,128)(2,1)S(1)}, bf16[2,4,512]{2,0,1:T(2,128)(2,1)S(1)}, u32[]{:S(2)}, u32[]{:S(2)}) collective-permute-start(bf16[2,4,512]{2,0,1:T(2,128)(2,1)S(1)} %pad_maximum_fusion.3), channel_id=1, source_target_pairs={{0,4},{2,6},{4,8},{6,10},{8,12},{10,14},{12,0},{14,2},{1,5},{3,7},... | collective-permute-start | bytes 24584 | tf_op jit(solution)/shard_map/ppermute | solution.py:83
  9.7 0.7 %fusion.16 = bf16[1,2,4,512]{3,1,2,0:T(2,128)(2,1)S(1)} fusion(bf16[2,1,512]{2,0,1:T(2,128)(2,1)S(1)} %broadcast_in_dim.65, bf16[2,3,512]{2,0,1:T(2,128)(2,1)} %param.4), kind=kLoop, calls=%fused_computation.62 | loop fusion | flops 4096 | bytes 16384 | tf_op jit(solution)/shard_map/stack | solution.py:94
  10.5 1.7 %fusion.2 = f32[64,4,3]{1,2,0:T(4,128)S(1)} fusion(bf16[1,64,4,3,512]{4,2,3,1,0:T(4,128)(2,1)} %param.5), kind=kLoop, calls=%fused_computation.9 | loop fusion | flops 1178880 | bytes 789504 | tf_op jit(solution)/shard_map/reduce_sum | solution.py:122
  12.5 2.6 %collective-permute-start.1 = (bf16[2,4,512]{2,0,1:T(2,128)(2,1)S(1)}, bf16[2,4,512]{2,0,1:T(2,128)(2,1)S(1)}, u32[]{:S(2)}, u32[]{:S(2)}) collective-permute-start(bf16[2,4,512]{2,0,1:T(2,128)(2,1)S(1)} %pad_maximum_fusion.3), channel_id=1, source_target_pairs={{0,8},{2,10},{4,12},{6,14},{8,0},{10,2},{12,4},{14,6},{1,9},{3,11}... | collective-permute-start | bytes 24584 | tf_op jit(solution)/shard_map/ppermute | solution.py:83
  15.1 1.3 %collective-permute-start.2 = (bf16[2,4,512]{2,0,1:T(2,128)(2,1)S(1)}, bf16[2,4,512]{2,0,1:T(2,128)(2,1)S(1)}, u32[]{:S(2)}, u32[]{:S(2)}) collective-permute-start(bf16[2,4,512]{2,0,1:T(2,128)(2,1)S(1)} %pad_maximum_fusion.3), channel_id=1, source_target_pairs={{0,12},{2,14},{4,0},{6,2},{8,4},{10,6},{12,8},{14,10},{1,13},{3,15... | collective-permute-start | bytes 24584 | tf_op jit(solution)/shard_map/ppermute | solution.py:83
  16.5 0.6 %gather_fusion.1 = bf16[4,2,3,512]{3,1,2,0:T(2,128)(2,1)S(1)} fusion(bf16[4,2,3,512]{3,1,2,0:T(2,128)(2,1)S(1)} %pad_maximum_fusion.2, s32[1024]{0:T(1024)S(1)} %pad_clamp_fusion.1), kind=kCustom, calls=%fused_computation.1 | custom fusion | bytes 49168 | tf_op jit(solution)/shard_map/jit(_take)/gather | solution.py:95
  17.2 1.5 %collective-permute-done.2 = bf16[2,4,512]{2,0,1:T(2,128)(2,1)S(1)} collective-permute-done((bf16[2,4,512]{2,0,1:T(2,128)(2,1)S(1)}, bf16[2,4,512]{2,0,1:T(2,128)(2,1)S(1)}, u32[]{:S(2)}, u32[]{:S(2)}) %collective-permute-start.2) | collective-permute-done | bytes 8224 | tf_op jit(solution)/shard_map/ppermute | solution.py:83
  18.8 0.6 %gather_fusion = bf16[4,2,4,512]{3,1,2,0:T(2,128)(2,1)S(1)} fusion(bf16[4,2,4,512]{3,1,2,0:T(2,128)(2,1)S(1)} %pad_maximum_fusion.1, s32[1024]{0:T(1024)S(1)} %pad_clamp_fusion.1), kind=kCustom, calls=%fused_computation | custom fusion | bytes 65552 | tf_op jit(solution)/shard_map/jit(_take)/gather | solution.py:94
  20.4 0.6 %convert_element_type.47.x_ref = f32[96,128]{1,0:T(8,128)} convert(bf16[96,128]{1,0:T(8,128)(2,1)S(1)} %rev.6) | non-fusion elementwise | flops 12288 | bytes 73728 | tf_op jit(solution)/shard_map/convert_element_type | solution.py:55
  22.3 1.8 %reshape_reshape.3.n_ref = bf16[64,6144]{1,0:T(8,128)(2,1)} reshape(bf16[1,64,4,3,512]{4,3,2,1,0:T(4,128)(2,1)S(1)} %copy.21) | data formatting | bytes 1572864 | tf_op jit(solution)/shard_map/reshape;reshape | solution.py:55
  24.2 6.7 %shard_map.46 = f32[64,512]{1,0:T(8,128)} custom-call(f32[96,128]{1,0:T(8,128)} %convert_element_type.47.x_ref, bf16[64,6144]{1,0:T(8,128)(2,1)} %reshape_reshape.3.n_ref), custom_call_target="tpu_custom_call" | custom-call | tf_op jit(solution)/shard_map/pallas_call | solution.py:51
  30.9 3.7 %collective-permute-start.8 = (f32[64,512]{1,0:T(8,128)}, f32[64,512]{1,0:T(8,128)S(1)}, u32[]{:S(2)}, u32[]{:S(2)}) collective-permute-start(f32[64,512]{1,0:T(8,128)} %shard_map.46), channel_id=1, source_target_pairs={{0,8},{4,12},{8,0},{12,4},{1,9},{5,13},{9,1},{13,5},{2,10},{6,14},... | collective-permute-start | bytes 393224 | tf_op jit(solution)/shard_map/ppermute | solution.py:64
  34.7 4.7 %collective-permute-done.7 = f32[64,512]{1,0:T(8,128)S(1)} collective-permute-done((f32[64,512]{1,0:T(8,128)}, f32[64,512]{1,0:T(8,128)S(1)}, u32[]{:S(2)}, u32[]{:S(2)}) %collective-permute-start.7) | collective-permute-done | bytes 131104 | tf_op jit(solution)/shard_map/ppermute | solution.py:64
  39.4 3.1 %collective-permute-done.8 = f32[64,512]{1,0:T(8,128)S(1)} collective-permute-done((f32[64,512]{1,0:T(8,128)}, f32[64,512]{1,0:T(8,128)S(1)}, u32[]{:S(2)}, u32[]{:S(2)}) %collective-permute-start.8) | collective-permute-done | bytes 131104 | tf_op jit(solution)/shard_map/ppermute | solution.py:64
  42.5 0.9 %pad_maximum_fusion = f32[4,64,512]{2,1,0:T(8,128)S(1)} fusion(f32[1,64,512]{2,1,0:T(8,128)S(1)} %bitcast.35, f32[1,64,512]{2,1,0:T(8,128)S(1)} %bitcast.34, f32[1,64,512]{2,1,0:T(8,128)S(1)} %bitcast.33, f32[1,64,512]{2,1,0:T(8,128)} %bitcast.30), kind=kLoop, calls=%fused_computation.10 | loop fusion | flops 393216 | bytes 1048576 | tf_op jit(solution)/shard_map/stack | solution.py:66
  44.2 4.2 %collective-permute-start.10 = (f32[64]{0:T(128)S(1)}, f32[64]{0:T(128)S(1)}, u32[]{:S(2)}, u32[]{:S(2)}) collective-permute-start(f32[64]{0:T(128)S(1)} %multiply_reduce_fusion), channel_id=1, source_target_pairs={{0,2},{2,0},{1,3},{3,1},{4,6},{6,4},{5,7},{7,5},{8,10},{10,8},{9,1... | collective-permute-start | bytes 776 | tf_op jit(solution)/shard_map/ppermute | solution.py:64
  48.7 1.2 %collective-permute-done.10 = f32[64]{0:T(128)S(1)} collective-permute-done((f32[64]{0:T(128)S(1)}, f32[64]{0:T(128)S(1)}, u32[]{:S(2)}, u32[]{:S(2)}) %collective-permute-start.10) | collective-permute-done | bytes 288 | tf_op jit(solution)/shard_map/ppermute | solution.py:64
  50.6 0.7 %broadcast_divide_fusion = f32[1,64,512]{2,1,0:T(8,128)} fusion(f32[1,64,512]{2,1,0:T(8,128)S(1)} %reshape.198, f32[64]{0:T(128)S(1)} %add_sqrt_fusion.1), kind=kLoop, calls=%fused_computation.15 | loop fusion | flops 32768 | bytes 262400 | tf_op jit(solution)/shard_map/div | solution.py:129
  (52 shorter events, 4.7 us)
Async XLA Ops:
  0.0 12.5 %collective-permute-start.3 = (bf16[2,3,512]{2,0,1:T(2,128)(2,1)}, bf16[2,3,512]{2,0,1:T(2,128)(2,1)S(1)}, u32[]{:S(2)}, u32[]{:S(2)}) collective-permute-start(bf16[2,3,512]{2,0,1:T(2,128)(2,1)} %param.4), channel_id=1, source_target_pairs={{2,0},{6,4},{10,8},{14,12},{3,1},{7,5},{11,9},{15,13},{18,16},{22,... | collective-permute-start | bytes 18440 | tf_op jit(solution)/shard_map/ppermute | solution.py:91
  1.3 13.8 %collective-permute-start.4 = (bf16[2,3,512]{2,0,1:T(2,128)(2,1)}, bf16[2,3,512]{2,0,1:T(2,128)(2,1)S(1)}, u32[]{:S(2)}, u32[]{:S(2)}) collective-permute-start(bf16[2,3,512]{2,0,1:T(2,128)(2,1)} %param.4), channel_id=1, source_target_pairs={{2,4},{6,8},{10,12},{14,0},{3,5},{7,9},{11,13},{15,1},{18,20},{22,... | collective-permute-start | bytes 18440 | tf_op jit(solution)/shard_map/ppermute | solution.py:91
  2.6 13.8 %collective-permute-start.5 = (bf16[2,3,512]{2,0,1:T(2,128)(2,1)}, bf16[2,3,512]{2,0,1:T(2,128)(2,1)S(1)}, u32[]{:S(2)}, u32[]{:S(2)}) collective-permute-start(bf16[2,3,512]{2,0,1:T(2,128)(2,1)} %param.4), channel_id=1, source_target_pairs={{2,8},{6,12},{10,0},{14,4},{3,9},{7,13},{11,1},{15,5},{18,24},{22,... | collective-permute-start | bytes 18440 | tf_op jit(solution)/shard_map/ppermute | solution.py:91
  3.9 12.5 %collective-permute-start.6 = (bf16[2,3,512]{2,0,1:T(2,128)(2,1)}, bf16[2,3,512]{2,0,1:T(2,128)(2,1)S(1)}, u32[]{:S(2)}, u32[]{:S(2)}) collective-permute-start(bf16[2,3,512]{2,0,1:T(2,128)(2,1)} %param.4), channel_id=1, source_target_pairs={{2,12},{6,0},{10,4},{14,8},{3,13},{7,1},{11,5},{15,9},{18,28},{22,... | collective-permute-start | bytes 18440 | tf_op jit(solution)/shard_map/ppermute | solution.py:91
  6.6 10.6 %collective-permute-start = (bf16[2,4,512]{2,0,1:T(2,128)(2,1)S(1)}, bf16[2,4,512]{2,0,1:T(2,128)(2,1)S(1)}, u32[]{:S(2)}, u32[]{:S(2)}) collective-permute-start(bf16[2,4,512]{2,0,1:T(2,128)(2,1)S(1)} %pad_maximum_fusion.3), channel_id=1, source_target_pairs={{0,4},{2,6},{4,8},{6,10},{8,12},{10,14},{12,0},{14,2},{1,5},{3,7},... | collective-permute-start | bytes 24584 | tf_op jit(solution)/shard_map/ppermute | solution.py:83
  10.5 10.6 %copy-start.1 = (s32[1,64,4,3]{1,2,3,0:T(4,128)S(1)}, s32[1,64,4,3]{1,2,3,0:T(4,128)}, u32[]{:S(2)}) copy-start(s32[1,64,4,3]{1,2,3,0:T(4,128)} %param.6) | copy-start | bytes 9220
  10.5 10.8 %copy-start = (bf16[1,64,4,3,512]{4,2,3,1,0:T(4,128)(2,1)S(1)}, bf16[1,64,4,3,512]{4,2,3,1,0:T(4,128)(2,1)}, u32[]{:S(2)}) copy-start(bf16[1,64,4,3,512]{4,2,3,1,0:T(4,128)(2,1)} %param.5) | copy-start | bytes 2359300
  12.5 4.7 %collective-permute-start.1 = (bf16[2,4,512]{2,0,1:T(2,128)(2,1)S(1)}, bf16[2,4,512]{2,0,1:T(2,128)(2,1)S(1)}, u32[]{:S(2)}, u32[]{:S(2)}) collective-permute-start(bf16[2,4,512]{2,0,1:T(2,128)(2,1)S(1)} %pad_maximum_fusion.3), channel_id=1, source_target_pairs={{0,8},{2,10},{4,12},{6,14},{8,0},{10,2},{12,4},{14,6},{1,9},{3,11}... | collective-permute-start | bytes 24584 | tf_op jit(solution)/shard_map/ppermute | solution.py:83
  15.1 3.7 %collective-permute-start.2 = (bf16[2,4,512]{2,0,1:T(2,128)(2,1)S(1)}, bf16[2,4,512]{2,0,1:T(2,128)(2,1)S(1)}, u32[]{:S(2)}, u32[]{:S(2)}) collective-permute-start(bf16[2,4,512]{2,0,1:T(2,128)(2,1)S(1)} %pad_maximum_fusion.3), channel_id=1, source_target_pairs={{0,12},{2,14},{4,0},{6,2},{8,4},{10,6},{12,8},{14,10},{1,13},{3,15... | collective-permute-start | bytes 24584 | tf_op jit(solution)/shard_map/ppermute | solution.py:83
  30.8 8.5 %collective-permute-start.7 = (f32[64,512]{1,0:T(8,128)}, f32[64,512]{1,0:T(8,128)S(1)}, u32[]{:S(2)}, u32[]{:S(2)}) collective-permute-start(f32[64,512]{1,0:T(8,128)} %shard_map.46), channel_id=1, source_target_pairs={{0,4},{4,8},{8,12},{12,0},{1,5},{5,9},{9,13},{13,1},{2,6},{6,10},{... | collective-permute-start | bytes 393224 | tf_op jit(solution)/shard_map/ppermute | solution.py:64
  30.9 11.6 %collective-permute-start.8 = (f32[64,512]{1,0:T(8,128)}, f32[64,512]{1,0:T(8,128)S(1)}, u32[]{:S(2)}, u32[]{:S(2)}) collective-permute-start(f32[64,512]{1,0:T(8,128)} %shard_map.46), channel_id=1, source_target_pairs={{0,8},{4,12},{8,0},{12,4},{1,9},{5,13},{9,1},{13,5},{2,10},{6,14},... | collective-permute-start | bytes 393224 | tf_op jit(solution)/shard_map/ppermute | solution.py:64
  34.6 7.9 %collective-permute-start.9 = (f32[64,512]{1,0:T(8,128)}, f32[64,512]{1,0:T(8,128)S(1)}, u32[]{:S(2)}, u32[]{:S(2)}) collective-permute-start(f32[64,512]{1,0:T(8,128)} %shard_map.46), channel_id=1, source_target_pairs={{0,12},{4,0},{8,4},{12,8},{1,13},{5,1},{9,5},{13,9},{2,14},{6,2},{... | collective-permute-start | bytes 393224 | tf_op jit(solution)/shard_map/ppermute | solution.py:64
  44.2 5.7 %collective-permute-start.10 = (f32[64]{0:T(128)S(1)}, f32[64]{0:T(128)S(1)}, u32[]{:S(2)}, u32[]{:S(2)}) collective-permute-start(f32[64]{0:T(128)S(1)} %multiply_reduce_fusion), channel_id=1, source_target_pairs={{0,2},{2,0},{1,3},{3,1},{4,6},{6,4},{5,7},{7,5},{8,10},{10,8},{9,1... | collective-permute-start | bytes 776 | tf_op jit(solution)/shard_map/ppermute | solution.py:64

commit v4 on v3

--- a/solution.py
+++ b/solution.py
@@ -57,15 +57,17 @@
 
 def ordered_sum(part, axis):
     size = lax.axis_size(axis)
-    if size == 1:
-        return part
-    me = lax.axis_index(axis)
     received = [part] + [
         lax.ppermute(part, axis, [(i, (i + k) % size) for i in range(size)]) for k in range(1, size)
     ]
-    stack = jnp.stack(received)
+    if size & (size - 1) == 0:
+        while len(received) > 1:
+            half = len(received) // 2
+            received = [received[k] + received[k + half] for k in range(half)]
+        return received[0]
+    me = lax.axis_index(axis)
     order = (me - jnp.arange(size, dtype=jnp.int32)) % size
-    return jnp.sum(jnp.take(stack, order, axis=0), axis=0)
+    return jnp.sum(jnp.take(jnp.stack(received), order, axis=0), axis=0)
 
 
 def gather_owned(records, station_region, capacity, filter_taps):
@@ -90,15 +92,14 @@
         ]
         next_seg.append(lax.ppermute(records[:, :, :filter_taps], axes, pairs))
     me = lax.axis_index("region")
-    order = (me - jnp.arange(regions, dtype=jnp.int32)) % regions
-    here = jnp.take(jnp.stack(same_seg), order, axis=0)
-    ahead = jnp.take(jnp.stack(next_seg), order, axis=0)
     stations = regions * local_count
-    here = here.reshape(stations, components + 1, seg_len)
-    ahead = ahead.reshape(stations, components, filter_taps)
+    shift = jnp.arange(regions, dtype=jnp.int32)[:, None]
+    local = jnp.arange(local_count, dtype=jnp.int32)[None, :]
+    station_ids = (((me - shift) % regions) * local_count + local).reshape(stations)
+    here = jnp.concatenate(same_seg, axis=0)
+    ahead = jnp.concatenate(next_seg, axis=0)
     region_of = here[:, components, 0].astype(jnp.int32)
     rows = jnp.concatenate([here[:, :components, :], ahead], axis=2)
-    station_ids = jnp.arange(stations, dtype=jnp.int32)
     earlier = (region_of[None, :] == region_of[:, None]) & (station_ids[None, :] < station_ids[:, None])
     ranks = jnp.sum(earlier.astype(jnp.int32), axis=1)
     slot_index = jnp.arange(capacity, dtype=jnp.int32)

time: 51.8 us -> 51.5 us (level)
  waiting for transfers between devices: 10.5 us -> 19.2 us
  starting transfers between devices: 20.2 us -> 15.3 us
  local copies, waits for them, and re-layouts: 5.58 us -> 3.09 us
  other arithmetic: 8.02 us -> 6.66 us
    ppermute x4, waiting for transfers between devices: 0.01 us -> 6.26 us  [gather_owned(): next_seg.append(lax.ppermute(records[:, :, :filter_taps], axes, pairs))]
    ppermute x4, starting transfers between devices: 8 us -> 3.9 us  [ordered_sum(): lax.ppermute(part, axis, [(i, (i + k) % size) for i in range(size)])]
    ppermute x4, waiting for transfers between devices: 8.96 us -> 12.6 us  [ordered_sum(): lax.ppermute(part, axis, [(i, (i + k) % size) for i in range(size)])]
    gather x6 -> x0, local copies, waits for them, and re-layouts: 2.4 us -> none  [the longest x2 1.14 us: ordered_sum(): return jnp.sum(jnp.take(stack, order, axis=0), axis=0)]
    another operation x5 -> x0, other arithmetic: 1.75 us -> none  [the longest x2 0.95 us: ordered_sum(): stack = jnp.stack(received)]
    ppermute x3, waiting for transfers between devices: 1.51 us -> 0.34 us  [gather_owned(): same_seg.append(lax.ppermute(payload, axes, pairs))]
    reduce_sum x1, other arithmetic: 0.11 us -> 1.04 us  [per_device(): power_sum = ordered_sum(jnp.sum(stacked * stacked, axis=1), 'seg')]
    ppermute x3, starting transfers between devices: 7.03 us -> 6.13 us  [gather_owned(): same_seg.append(lax.ppermute(payload, axes, pairs))]
  transfers between devices with their start and end apart: 11 -> 11, of which waited for: 4 -> 7; matrix products, arithmetic and copies ran while one was open for 10% -> 8% of each run, Pallas kernels for 0% -> 0%
where the time goes in v4:
time: 51.5 us; the launch traced here: 51.2 us
  waiting for transfers between devices  19.2 us (37%)
  starting transfers between devices  15.3 us (30%)
  Pallas kernels  6.67 us (13%)
  other arithmetic  6.66 us (13%)
  local copies, waits for them, and re-layouts  3.09 us (6%)
    ppermute x4, waiting for transfers between devices, ordered_sum(): lax.ppermute(part, axis, [(i, (i + k) % size) for i in range(size)])  12.6 us
    pallas_call x1, Pallas kernels, correlate(): pl.pallas_call(hankel_kernel, out_shape=jax.ShapeDtypeStruct((rows, seg_l...  6.67 us
    ppermute x4, waiting for transfers between devices, gather_owned(): next_seg.append(lax.ppermute(records[:, :, :filter_taps], axes, pairs))  6.26 us
    ppermute x3, starting transfers between devices, gather_owned(): same_seg.append(lax.ppermute(payload, axes, pairs))  6.13 us
    ppermute x4, starting transfers between devices, gather_owned(): next_seg.append(lax.ppermute(records[:, :, :filter_taps], axes, pairs))  5.27 us
    ppermute x4, starting transfers between devices, ordered_sum(): lax.ppermute(part, axis, [(i, (i + k) % size) for i in range(size)])  3.9 us
    another operation x1, local copies, waits for them, and re-layouts, correlate(): normed.reshape(rows, channels * filter_taps)  1.84 us
    reduce_sum x1, other arithmetic, per_device(): jnp.sum(widened_templates * widened_templates, axis=4, keepdims=True)  1.65 us
  transfers between devices with their start and end apart: 11, of which 7 were waited for; matrix products, arithmetic and copies ran while one was open for 8% of the time, Pallas kernels for 0%

profile of v4, /device:TPU:0, one launch (start us, length us, event | category | flops | bytes accessed | tf_op | source)
XLA Modules:
  0.0 51.2 jit_solution(5535165722867878436)
XLA Ops:
  0.0 1.4 %collective-permute-start.4 = (bf16[2,3,512]{2,0,1:T(2,128)(2,1)}, bf16[2,3,512]{2,0,1:T(2,128)(2,1)S(1)}, u32[]{:S(2)}, u32[]{:S(2)}) collective-permute-start(bf16[2,3,512]{2,0,1:T(2,128)(2,1)} %param.4), channel_id=1, source_target_pairs={{2,4},{6,8},{10,12},{14,0},{3,5},{7,9},{11,13},{15,1},{18,20},{22,... | collective-permute-start | bytes 18440 | tf_op jit(solution)/shard_map/ppermute | solution.py:93
  1.4 1.3 %collective-permute-start.3 = (bf16[2,3,512]{2,0,1:T(2,128)(2,1)}, bf16[2,3,512]{2,0,1:T(2,128)(2,1)S(1)}, u32[]{:S(2)}, u32[]{:S(2)}) collective-permute-start(bf16[2,3,512]{2,0,1:T(2,128)(2,1)} %param.4), channel_id=1, source_target_pairs={{2,0},{6,4},{10,8},{14,12},{3,1},{7,5},{11,9},{15,13},{18,16},{22,... | collective-permute-start | bytes 18440 | tf_op jit(solution)/shard_map/ppermute | solution.py:93
  2.7 0.7 %convert_element_type.42 = bf16[2]{0:T(256)(128)(2,1)S(1)} convert(s32[2]{0:T(128)} %param.7) | non-fusion elementwise | flops 2 | bytes 12 | tf_op jit(solution)/shard_map/convert_element_type | solution.py:77
  3.5 0.7 %pad_maximum_fusion.4 = bf16[2,4,512]{2,0,1:T(2,128)(2,1)S(1)} fusion(bf16[2,1,512]{2,0,1:T(2,128)(2,1)S(1)} %broadcast_in_dim.2, bf16[2,3,512]{2,0,1:T(2,128)(2,1)} %param.4), kind=kLoop, calls=%fused_computation.15 | loop fusion | flops 4096 | bytes 16384 | tf_op jit(solution)/shard_map/concatenate | solution.py:78
  4.2 5.1 %collective-permute-start.2 = (bf16[2,4,512]{2,0,1:T(2,128)(2,1)S(1)}, bf16[2,4,512]{2,0,1:T(2,128)(2,1)S(1)}, u32[]{:S(2)}, u32[]{:S(2)}) collective-permute-start(bf16[2,4,512]{2,0,1:T(2,128)(2,1)S(1)} %pad_maximum_fusion.4), channel_id=1, source_target_pairs={{0,12},{2,14},{4,0},{6,2},{8,4},{10,6},{12,8},{14,10},{1,13},{3,15... | collective-permute-start | bytes 24584 | tf_op jit(solution)/shard_map/ppermute | solution.py:85
  9.3 1.0 %collective-permute-start = (bf16[2,4,512]{2,0,1:T(2,128)(2,1)S(1)}, bf16[2,4,512]{2,0,1:T(2,128)(2,1)S(1)}, u32[]{:S(2)}, u32[]{:S(2)}) collective-permute-start(bf16[2,4,512]{2,0,1:T(2,128)(2,1)S(1)} %pad_maximum_fusion.4), channel_id=1, source_target_pairs={{0,4},{2,6},{4,8},{6,10},{8,12},{10,14},{12,0},{14,2},{1,5},{3,7},... | collective-permute-start | bytes 24584 | tf_op jit(solution)/shard_map/ppermute | solution.py:85
  10.3 1.6 %fusion.2 = f32[64,4,3]{1,2,0:T(4,128)S(1)} fusion(bf16[1,64,4,3,512]{4,2,3,1,0:T(4,128)(2,1)} %param.5), kind=kLoop, calls=%fused_computation.5 | loop fusion | flops 1178880 | bytes 789504 | tf_op jit(solution)/shard_map/reduce_sum | solution.py:123
  12.2 1.3 %collective-permute-start.6 = (bf16[2,3,512]{2,0,1:T(2,128)(2,1)S(1)}, bf16[2,3,512]{2,0,1:T(2,128)(2,1)S(1)}, u32[]{:S(2)}, u32[]{:S(2)}) collective-permute-start(bf16[2,3,512]{2,0,1:T(2,128)(2,1)S(1)} %copy-done.1), channel_id=1, source_target_pairs={{2,12},{6,0},{10,4},{14,8},{3,13},{7,1},{11,5},{15,9},{18,28},{22,... | collective-permute-start | bytes 18440 | tf_op jit(solution)/shard_map/ppermute | solution.py:93
  13.8 1.3 %collective-permute-start.5 = (bf16[2,3,512]{2,0,1:T(2,128)(2,1)S(1)}, bf16[2,3,512]{2,0,1:T(2,128)(2,1)S(1)}, u32[]{:S(2)}, u32[]{:S(2)}) collective-permute-start(bf16[2,3,512]{2,0,1:T(2,128)(2,1)S(1)} %copy-done.1), channel_id=1, source_target_pairs={{2,8},{6,12},{10,0},{14,4},{3,9},{7,13},{11,1},{15,5},{18,24},{22,... | collective-permute-start | bytes 18440 | tf_op jit(solution)/shard_map/ppermute | solution.py:93
  15.6 4.0 %collective-permute-done.6 = bf16[2,3,512]{2,0,1:T(2,128)(2,1)S(1)} collective-permute-done((bf16[2,3,512]{2,0,1:T(2,128)(2,1)S(1)}, bf16[2,3,512]{2,0,1:T(2,128)(2,1)S(1)}, u32[]{:S(2)}, u32[]{:S(2)}) %collective-permute-start.6) | collective-permute-done | bytes 6176 | tf_op jit(solution)/shard_map/ppermute | solution.py:93
  19.6 2.2 %collective-permute-done.5 = bf16[2,3,512]{2,0,1:T(2,128)(2,1)S(1)} collective-permute-done((bf16[2,3,512]{2,0,1:T(2,128)(2,1)S(1)}, bf16[2,3,512]{2,0,1:T(2,128)(2,1)S(1)}, u32[]{:S(2)}, u32[]{:S(2)}) %collective-permute-start.5) | collective-permute-done | bytes 6176 | tf_op jit(solution)/shard_map/ppermute | solution.py:93
  22.2 0.6 %convert_element_type.47.x_ref = f32[96,128]{1,0:T(8,128)} convert(bf16[96,128]{1,0:T(8,128)(2,1)S(1)} %rev.6) | non-fusion elementwise | flops 12288 | bytes 73728 | tf_op jit(solution)/shard_map/convert_element_type | solution.py:55
  23.0 0.5 fusion.1
  23.5 0.6 %copy.10 = bf16[1,64,4,3,512]{4,3,2,1,0:T(4,128)(2,1)S(1)} copy(bf16[1,64,4,3,512]{4,2,3,1,0:T(4,128)(2,1)S(1)} %fusion.1) | data formatting | bytes 1572864 | tf_op jit(solution)/shard_map/convert_element_type | solution.py:125
  24.1 1.8 %reshape_reshape.3.n_ref = bf16[64,6144]{1,0:T(8,128)(2,1)} reshape(bf16[1,64,4,3,512]{4,3,2,1,0:T(4,128)(2,1)S(1)} %copy.10) | data formatting | bytes 1572864 | tf_op jit(solution)/shard_map/reshape;reshape | solution.py:55
  25.9 6.7 %shard_map.46 = f32[64,512]{1,0:T(8,128)} custom-call(f32[96,128]{1,0:T(8,128)} %convert_element_type.47.x_ref, bf16[64,6144]{1,0:T(8,128)(2,1)} %reshape_reshape.3.n_ref), custom_call_target="tpu_custom_call" | custom-call | tf_op jit(solution)/shard_map/pallas_call | solution.py:51
  32.6 1.8 %collective-permute-start.9 = (f32[64,512]{1,0:T(8,128)}, f32[64,512]{1,0:T(8,128)S(1)}, u32[]{:S(2)}, u32[]{:S(2)}) collective-permute-start(f32[64,512]{1,0:T(8,128)} %shard_map.46), channel_id=1, source_target_pairs={{0,12},{4,0},{8,4},{12,8},{1,13},{5,1},{9,5},{13,9},{2,14},{6,2},{... | collective-permute-start | bytes 393224 | tf_op jit(solution)/shard_map/ppermute | solution.py:61
  34.6 1.8 %collective-permute-start.7 = (f32[64,512]{1,0:T(8,128)}, f32[64,512]{1,0:T(8,128)S(1)}, u32[]{:S(2)}, u32[]{:S(2)}) collective-permute-start(f32[64,512]{1,0:T(8,128)} %shard_map.46), channel_id=1, source_target_pairs={{0,8},{4,12},{8,0},{12,4},{1,9},{5,13},{9,1},{13,5},{2,10},{6,14},... | collective-permute-start | bytes 393224 | tf_op jit(solution)/shard_map/ppermute | solution.py:61
  36.4 3.7 %collective-permute-done.9 = f32[64,512]{1,0:T(8,128)S(1)} collective-permute-done((f32[64,512]{1,0:T(8,128)}, f32[64,512]{1,0:T(8,128)S(1)}, u32[]{:S(2)}, u32[]{:S(2)}) %collective-permute-start.9) | collective-permute-done | bytes 131104 | tf_op jit(solution)/shard_map/ppermute | solution.py:61
  40.2 2.4 %collective-permute-done.8 = f32[64,512]{1,0:T(8,128)S(1)} collective-permute-done((f32[64,512]{1,0:T(8,128)}, f32[64,512]{1,0:T(8,128)S(1)}, u32[]{:S(2)}, u32[]{:S(2)}) %collective-permute-start.8) | collective-permute-done | bytes 131104 | tf_op jit(solution)/shard_map/ppermute | solution.py:61
  42.5 3.3 %collective-permute-done.7 = f32[64,512]{1,0:T(8,128)S(1)} collective-permute-done((f32[64,512]{1,0:T(8,128)}, f32[64,512]{1,0:T(8,128)S(1)}, u32[]{:S(2)}, u32[]{:S(2)}) %collective-permute-start.7) | collective-permute-done | bytes 131104 | tf_op jit(solution)/shard_map/ppermute | solution.py:61
  45.8 1.0 %multiply_reduce_fusion = (f32[64]{0:T(128)S(1)}, f32[64,512]{1,0:T(8,128)S(1)}) fusion(f32[64,512]{1,0:T(8,128)S(1)} %collective-permute-done.8, f32[64,512]{1,0:T(8,128)S(1)} %collective-permute-done.9, f32[64,512]{1,0:T(8,128)} %shard_map.46, f32[64,512]{1,0:T(8,128)S(1)} %collective-permute-done.7), kind=kLoop, calls=%fused_computation.6 | loop fusion | flops 163776 | bytes 655616 | tf_op jit(solution)/shard_map/reduce_sum | solution.py:129
  47.2 3.2 %collective-permute-done.10 = f32[64]{0:T(128)S(1)} collective-permute-done((f32[64]{0:T(128)S(1)}, f32[64]{0:T(128)S(1)}, u32[]{:S(2)}, u32[]{:S(2)}) %collective-permute-start.10) | collective-permute-done | bytes 288 | tf_op jit(solution)/shard_map/ppermute | solution.py:61
  50.4 0.7 %broadcast_divide_fusion = f32[1,64,512]{2,1,0:T(8,128)} fusion(f32[1,64,512]{2,1,0:T(8,128)S(1)} %reshape.129, f32[64]{0:T(128)S(1)} %add_sqrt_fusion.1), kind=kLoop, calls=%fused_computation.9 | loop fusion | flops 32768 | bytes 262400 | tf_op jit(solution)/shard_map/div | solution.py:130
  (33 shorter events, 2.2 us)
Async XLA Ops:
  0.0 12.2 %copy-start.1 = (bf16[2,3,512]{2,0,1:T(2,128)(2,1)S(1)}, bf16[2,3,512]{2,0,1:T(2,128)(2,1)}, u32[]{:S(2)}) copy-start(bf16[2,3,512]{2,0,1:T(2,128)(2,1)} %param.4) | copy-start | bytes 18436
  0.0 23.0 %copy-start = (bf16[1,64,4,3,512]{4,2,3,1,0:T(4,128)(2,1)S(1)}, bf16[1,64,4,3,512]{4,2,3,1,0:T(4,128)(2,1)}, u32[]{:S(2)}) copy-start(bf16[1,64,4,3,512]{4,2,3,1,0:T(4,128)(2,1)} %param.5) | copy-start | bytes 2359300
  0.0 22.8 %copy-start.2 = (s32[1,64,4,3]{1,2,3,0:T(4,128)S(1)}, s32[1,64,4,3]{1,2,3,0:T(4,128)}, u32[]{:S(2)}) copy-start(s32[1,64,4,3]{1,2,3,0:T(4,128)} %param.6) | copy-start | bytes 9220
  0.0 15.6 %collective-permute-start.4 = (bf16[2,3,512]{2,0,1:T(2,128)(2,1)}, bf16[2,3,512]{2,0,1:T(2,128)(2,1)S(1)}, u32[]{:S(2)}, u32[]{:S(2)}) collective-permute-start(bf16[2,3,512]{2,0,1:T(2,128)(2,1)} %param.4), channel_id=1, source_target_pairs={{2,4},{6,8},{10,12},{14,0},{3,5},{7,9},{11,13},{15,1},{18,20},{22,... | collective-permute-start | bytes 18440 | tf_op jit(solution)/shard_map/ppermute | solution.py:93
  1.4 14.2 %collective-permute-start.3 = (bf16[2,3,512]{2,0,1:T(2,128)(2,1)}, bf16[2,3,512]{2,0,1:T(2,128)(2,1)S(1)}, u32[]{:S(2)}, u32[]{:S(2)}) collective-permute-start(bf16[2,3,512]{2,0,1:T(2,128)(2,1)} %param.4), channel_id=1, source_target_pairs={{2,0},{6,4},{10,8},{14,12},{3,1},{7,5},{11,9},{15,13},{18,16},{22,... | collective-permute-start | bytes 18440 | tf_op jit(solution)/shard_map/ppermute | solution.py:93
  4.2 8.0 %collective-permute-start.2 = (bf16[2,4,512]{2,0,1:T(2,128)(2,1)S(1)}, bf16[2,4,512]{2,0,1:T(2,128)(2,1)S(1)}, u32[]{:S(2)}, u32[]{:S(2)}) collective-permute-start(bf16[2,4,512]{2,0,1:T(2,128)(2,1)S(1)} %pad_maximum_fusion.4), channel_id=1, source_target_pairs={{0,12},{2,14},{4,0},{6,2},{8,4},{10,6},{12,8},{14,10},{1,13},{3,15... | collective-permute-start | bytes 24584 | tf_op jit(solution)/shard_map/ppermute | solution.py:85
  9.3 4.5 %collective-permute-start.1 = (bf16[2,4,512]{2,0,1:T(2,128)(2,1)S(1)}, bf16[2,4,512]{2,0,1:T(2,128)(2,1)S(1)}, u32[]{:S(2)}, u32[]{:S(2)}) collective-permute-start(bf16[2,4,512]{2,0,1:T(2,128)(2,1)S(1)} %pad_maximum_fusion.4), channel_id=1, source_target_pairs={{0,8},{2,10},{4,12},{6,14},{8,0},{10,2},{12,4},{14,6},{1,9},{3,11}... | collective-permute-start | bytes 24584 | tf_op jit(solution)/shard_map/ppermute | solution.py:85
  9.3 5.8 %collective-permute-start = (bf16[2,4,512]{2,0,1:T(2,128)(2,1)S(1)}, bf16[2,4,512]{2,0,1:T(2,128)(2,1)S(1)}, u32[]{:S(2)}, u32[]{:S(2)}) collective-permute-start(bf16[2,4,512]{2,0,1:T(2,128)(2,1)S(1)} %pad_maximum_fusion.4), channel_id=1, source_target_pairs={{0,4},{2,6},{4,8},{6,10},{8,12},{10,14},{12,0},{14,2},{1,5},{3,7},... | collective-permute-start | bytes 24584 | tf_op jit(solution)/shard_map/ppermute | solution.py:85
  12.2 7.4 %collective-permute-start.6 = (bf16[2,3,512]{2,0,1:T(2,128)(2,1)S(1)}, bf16[2,3,512]{2,0,1:T(2,128)(2,1)S(1)}, u32[]{:S(2)}, u32[]{:S(2)}) collective-permute-start(bf16[2,3,512]{2,0,1:T(2,128)(2,1)S(1)} %copy-done.1), channel_id=1, source_target_pairs={{2,12},{6,0},{10,4},{14,8},{3,13},{7,1},{11,5},{15,9},{18,28},{22,... | collective-permute-start | bytes 18440 | tf_op jit(solution)/shard_map/ppermute | solution.py:93
  13.8 8.0 %collective-permute-start.5 = (bf16[2,3,512]{2,0,1:T(2,128)(2,1)S(1)}, bf16[2,3,512]{2,0,1:T(2,128)(2,1)S(1)}, u32[]{:S(2)}, u32[]{:S(2)}) collective-permute-start(bf16[2,3,512]{2,0,1:T(2,128)(2,1)S(1)} %copy-done.1), channel_id=1, source_target_pairs={{2,8},{6,12},{10,0},{14,4},{3,9},{7,13},{11,1},{15,5},{18,24},{22,... | collective-permute-start | bytes 18440 | tf_op jit(solution)/shard_map/ppermute | solution.py:93
  32.6 7.6 %collective-permute-start.9 = (f32[64,512]{1,0:T(8,128)}, f32[64,512]{1,0:T(8,128)S(1)}, u32[]{:S(2)}, u32[]{:S(2)}) collective-permute-start(f32[64,512]{1,0:T(8,128)} %shard_map.46), channel_id=1, source_target_pairs={{0,12},{4,0},{8,4},{12,8},{1,13},{5,1},{9,5},{13,9},{2,14},{6,2},{... | collective-permute-start | bytes 393224 | tf_op jit(solution)/shard_map/ppermute | solution.py:61
  34.4 8.1 %collective-permute-start.8 = (f32[64,512]{1,0:T(8,128)}, f32[64,512]{1,0:T(8,128)S(1)}, u32[]{:S(2)}, u32[]{:S(2)}) collective-permute-start(f32[64,512]{1,0:T(8,128)} %shard_map.46), channel_id=1, source_target_pairs={{0,4},{4,8},{8,12},{12,0},{1,5},{5,9},{9,13},{13,1},{2,6},{6,10},{... | collective-permute-start | bytes 393224 | tf_op jit(solution)/shard_map/ppermute | solution.py:61
  34.6 11.2 %collective-permute-start.7 = (f32[64,512]{1,0:T(8,128)}, f32[64,512]{1,0:T(8,128)S(1)}, u32[]{:S(2)}, u32[]{:S(2)}) collective-permute-start(f32[64,512]{1,0:T(8,128)} %shard_map.46), channel_id=1, source_target_pairs={{0,8},{4,12},{8,0},{12,4},{1,9},{5,13},{9,1},{13,5},{2,10},{6,14},... | collective-permute-start | bytes 393224 | tf_op jit(solution)/shard_map/ppermute | solution.py:61
  46.8 3.6 %collective-permute-start.10 = (f32[64]{0:T(128)S(1)}, f32[64]{0:T(128)S(1)}, u32[]{:S(2)}, u32[]{:S(2)}) collective-permute-start(f32[64]{0:T(128)S(1)} %get-tuple-element.5), channel_id=1, source_target_pairs={{0,2},{2,0},{1,3},{3,1},{4,6},{6,4},{5,7},{7,5},{8,10},{10,8},{9,1... | collective-permute-start | bytes 776 | tf_op jit(solution)/shard_map/ppermute | solution.py:61

commit v5 on v4

--- a/solution.py
+++ b/solution.py
@@ -6,7 +6,7 @@
 from jax.experimental.pallas import tpu as pltpu
 
 
-def hankel_kernel(x_ref, n_ref, o_ref, h_ref):
+def hankel_kernel(x_ref, n_ref, fill_ref, o_ref, h_ref):
     width = h_ref.shape[0]
     channels = n_ref.shape[1] // width
     taps_blocks = width // 128
@@ -35,7 +35,7 @@
         )
         start = pl.multiple_of(c * width, 128)
         part = jnp.dot(n_ref[:, pl.ds(start, width)], h_ref[...], preferred_element_type=jnp.float32)
-        return acc + part * (1.0 / jnp.sqrt(jnp.maximum(energy, 1.0)))
+        return acc + part * (fill_ref[c] / jnp.sqrt(jnp.maximum(energy, 1.0)))
 
     o_ref[...] = lax.fori_loop(0, channels, one_channel, jnp.zeros(o_ref.shape, jnp.float32))
 
@@ -45,14 +45,19 @@
     return stacked.reshape(rows, seg_len // 128, 128)[..., ::-1].reshape(rows, seg_len)
 
 
-def correlate(normed, flat_owned, seg_len):
+def correlate(normed, flat_owned, filled, seg_len):
     rows, channels, filter_taps = normed.shape
     blocks = flat_owned.reshape(channels * (flat_owned.shape[1] // 128), 128)[:, ::-1]
     return pl.pallas_call(
         hankel_kernel,
         out_shape=jax.ShapeDtypeStruct((rows, seg_len), jnp.float32),
+        in_specs=[
+            pl.BlockSpec(memory_space=pltpu.VMEM),
+            pl.BlockSpec(memory_space=pltpu.VMEM),
+            pl.BlockSpec(memory_space=pltpu.SMEM),
+        ],
         scratch_shapes=[pltpu.VMEM((filter_taps, seg_len), jnp.bfloat16)],
-    )(blocks.astype(jnp.float32), normed.reshape(rows, channels * filter_taps))
+    )(blocks.astype(jnp.float32), normed.reshape(rows, channels * filter_taps), filled)
 
 
 def ordered_sum(part, axis):
@@ -117,7 +122,7 @@
     seg_len = records.shape[2]
     owned_rows, filled = gather_owned(records, station_region, capacity, filter_taps)
     flat_owned = owned_rows.reshape(capacity * components, seg_len + filter_taps)
-    weight = channel_mask.astype(jnp.float32) * filled[None, None, :, None]
+    weight = channel_mask.astype(jnp.float32)
     widened_templates = templates.astype(jnp.float32)
     template_norm = jnp.sqrt(
         jnp.sum(widened_templates * widened_templates, axis=4, keepdims=True) + 1e-06
@@ -125,7 +130,8 @@
     normed = (widened_templates * weight[..., None] / template_norm).astype(jnp.bfloat16)
     normed = normed.reshape(local_batches * kept, capacity * components, filter_taps)
     total_len = seg_len * lax.axis_size("seg")
-    stacked = ordered_sum(correlate(normed, flat_owned, seg_len), "region")
+    filled_channels = jnp.repeat(filled, components)
+    stacked = ordered_sum(correlate(normed, flat_owned, filled_channels, seg_len), "region")
     power_sum = ordered_sum(jnp.sum(stacked * stacked, axis=1), "seg")
     detect = unflip(stacked) / jnp.sqrt(power_sum / total_len + 1e-06)[:, None]
     return detect.reshape(local_batches, kept, seg_len)

time: 51.5 us -> 52.9 us (1.027)
  local copies, waits for them, and re-layouts: 3.09 us -> 3.81 us
  other arithmetic: 6.66 us -> 7.31 us
    reshape x0 -> x1, local copies, waits for them, and re-layouts: none -> 0.66 us  [per_device(): filled_channels = jnp.repeat(filled, components)]
    mul x1, other arithmetic: 0.07 us -> 0.69 us  [per_device(): widened_templates * weight[..., None] / template_norm]
  transfers between devices with their start and end apart: 11 -> 11, of which waited for: 7 -> 6; matrix products, arithmetic and copies ran while one was open for 8% -> 15% of each run, Pallas kernels for 0% -> 0%
where the time goes in v5:
time: 52.9 us; the launch traced here: 52.6 us
  waiting for transfers between devices  19.2 us (36%)
  starting transfers between devices  15.3 us (29%)
  other arithmetic  7.31 us (14%)
  Pallas kernels  6.7 us (13%)
  local copies, waits for them, and re-layouts  3.81 us (7%)
    ppermute x4, waiting for transfers between devices, ordered_sum(): lax.ppermute(part, axis, [(i, (i + k) % size) for i in range(size)])  12.6 us
    pallas_call x1, Pallas kernels, correlate(): pl.pallas_call(hankel_kernel, out_shape=jax.ShapeDtypeStruct((rows, seg_l...  6.7 us
    ppermute x4, waiting for transfers between devices, gather_owned(): next_seg.append(lax.ppermute(records[:, :, :filter_taps], axes, pairs))  6.57 us
    ppermute x3, starting transfers between devices, gather_owned(): same_seg.append(lax.ppermute(payload, axes, pairs))  6.11 us
    ppermute x4, starting transfers between devices, gather_owned(): next_seg.append(lax.ppermute(records[:, :, :filter_taps], axes, pairs))  5.28 us
    ppermute x4, starting transfers between devices, ordered_sum(): lax.ppermute(part, axis, [(i, (i + k) % size) for i in range(size)])  3.9 us
    another operation x1, local copies, waits for them, and re-layouts, correlate(): normed.reshape(rows, channels * filter_taps)  1.84 us
    reduce_sum x1, other arithmetic, per_device(): jnp.sum(widened_templates * widened_templates, axis=4, keepdims=True)  1.65 us
  transfers between devices with their start and end apart: 11, of which 6 were waited for; matrix products, arithmetic and copies ran while one was open for 15% of the time, Pallas kernels for 0%

profile of v5, /device:TPU:0, one launch (start us, length us, event | category | flops | bytes accessed | tf_op | source)
XLA Modules:
  0.0 52.6 jit_solution(17476800861295381565)
XLA Ops:
  0.0 1.4 %collective-permute-start.4 = (bf16[2,3,512]{2,0,1:T(2,128)(2,1)}, bf16[2,3,512]{2,0,1:T(2,128)(2,1)S(1)}, u32[]{:S(2)}, u32[]{:S(2)}) collective-permute-start(bf16[2,3,512]{2,0,1:T(2,128)(2,1)} %param.4), channel_id=1, source_target_pairs={{2,4},{6,8},{10,12},{14,0},{3,5},{7,9},{11,13},{15,1},{18,20},{22,... | collective-permute-start | bytes 18440 | tf_op jit(solution)/shard_map/ppermute | solution.py:98
  1.4 1.3 %collective-permute-start.3 = (bf16[2,3,512]{2,0,1:T(2,128)(2,1)}, bf16[2,3,512]{2,0,1:T(2,128)(2,1)S(1)}, u32[]{:S(2)}, u32[]{:S(2)}) collective-permute-start(bf16[2,3,512]{2,0,1:T(2,128)(2,1)} %param.4), channel_id=1, source_target_pairs={{2,0},{6,4},{10,8},{14,12},{3,1},{7,5},{11,9},{15,13},{18,16},{22,... | collective-permute-start | bytes 18440 | tf_op jit(solution)/shard_map/ppermute | solution.py:98
  2.7 0.7 %convert_element_type.42 = bf16[2]{0:T(256)(128)(2,1)S(1)} convert(s32[2]{0:T(128)} %param.7) | non-fusion elementwise | flops 2 | bytes 12 | tf_op jit(solution)/shard_map/convert_element_type | solution.py:82
  3.5 0.7 %pad_maximum_fusion.4 = bf16[2,4,512]{2,0,1:T(2,128)(2,1)S(1)} fusion(bf16[2,1,512]{2,0,1:T(2,128)(2,1)S(1)} %broadcast_in_dim.4, bf16[2,3,512]{2,0,1:T(2,128)(2,1)} %param.4), kind=kLoop, calls=%fused_computation.15 | loop fusion | flops 4096 | bytes 16384 | tf_op jit(solution)/shard_map/concatenate | solution.py:83
  4.2 5.1 %collective-permute-start.2 = (bf16[2,4,512]{2,0,1:T(2,128)(2,1)S(1)}, bf16[2,4,512]{2,0,1:T(2,128)(2,1)S(1)}, u32[]{:S(2)}, u32[]{:S(2)}) collective-permute-start(bf16[2,4,512]{2,0,1:T(2,128)(2,1)S(1)} %pad_maximum_fusion.4), channel_id=1, source_target_pairs={{0,12},{2,14},{4,0},{6,2},{8,4},{10,6},{12,8},{14,10},{1,13},{3,15... | collective-permute-start | bytes 24584 | tf_op jit(solution)/shard_map/ppermute | solution.py:90
  9.3 1.0 %collective-permute-start = (bf16[2,4,512]{2,0,1:T(2,128)(2,1)S(1)}, bf16[2,4,512]{2,0,1:T(2,128)(2,1)S(1)}, u32[]{:S(2)}, u32[]{:S(2)}) collective-permute-start(bf16[2,4,512]{2,0,1:T(2,128)(2,1)S(1)} %pad_maximum_fusion.4), channel_id=1, source_target_pairs={{0,4},{2,6},{4,8},{6,10},{8,12},{10,14},{12,0},{14,2},{1,5},{3,7},... | collective-permute-start | bytes 24584 | tf_op jit(solution)/shard_map/ppermute | solution.py:90
  10.3 0.7 %convert_bitcast_fusion = f32[64,4,3]{0,1,2:T(4,128)S(1)} fusion(s32[1,64,4,3]{1,2,3,0:T(4,128)} %param.6), kind=kLoop, calls=%fused_computation.16 | loop fusion | flops 768 | bytes 6144 | tf_op jit(solution)/shard_map/mul | solution.py:130
  11.1 1.7 %fusion.2 = f32[64,4,3]{1,2,0:T(4,128)S(1)} fusion(bf16[1,64,4,3,512]{4,2,3,1,0:T(4,128)(2,1)} %param.5), kind=kLoop, calls=%fused_computation.5 | loop fusion | flops 1178880 | bytes 789504 | tf_op jit(solution)/shard_map/reduce_sum | solution.py:128
  14.1 1.8 %reshape_reshape.3.n_ref = bf16[64,6144]{1,0:T(8,128)(2,1)} reshape(bf16[1,64,4,3,512]{4,3,2,1,0:T(4,128)(2,1)S(1)} %copy.10) | data formatting | bytes 1572864 | tf_op jit(solution)/shard_map/reshape;reshape | solution.py:60
  16.0 1.3 %collective-permute-start.6 = (bf16[2,3,512]{2,0,1:T(2,128)(2,1)S(1)}, bf16[2,3,512]{2,0,1:T(2,128)(2,1)S(1)}, u32[]{:S(2)}, u32[]{:S(2)}) collective-permute-start(bf16[2,3,512]{2,0,1:T(2,128)(2,1)S(1)} %copy-done.1), channel_id=1, source_target_pairs={{2,12},{6,0},{10,4},{14,8},{3,13},{7,1},{11,5},{15,9},{18,28},{22,... | collective-permute-start | bytes 18440 | tf_op jit(solution)/shard_map/ppermute | solution.py:98
  17.3 1.3 %collective-permute-start.5 = (bf16[2,3,512]{2,0,1:T(2,128)(2,1)S(1)}, bf16[2,3,512]{2,0,1:T(2,128)(2,1)S(1)}, u32[]{:S(2)}, u32[]{:S(2)}) collective-permute-start(bf16[2,3,512]{2,0,1:T(2,128)(2,1)S(1)} %copy-done.1), channel_id=1, source_target_pairs={{2,8},{6,12},{10,0},{14,4},{3,9},{7,13},{11,1},{15,5},{18,24},{22,... | collective-permute-start | bytes 18440 | tf_op jit(solution)/shard_map/ppermute | solution.py:98
  19.0 4.4 %collective-permute-done.6 = bf16[2,3,512]{2,0,1:T(2,128)(2,1)S(1)} collective-permute-done((bf16[2,3,512]{2,0,1:T(2,128)(2,1)S(1)}, bf16[2,3,512]{2,0,1:T(2,128)(2,1)S(1)}, u32[]{:S(2)}, u32[]{:S(2)}) %collective-permute-start.6) | collective-permute-done | bytes 6176 | tf_op jit(solution)/shard_map/ppermute | solution.py:98
  23.4 2.2 %collective-permute-done.5 = bf16[2,3,512]{2,0,1:T(2,128)(2,1)S(1)} collective-permute-done((bf16[2,3,512]{2,0,1:T(2,128)(2,1)S(1)}, bf16[2,3,512]{2,0,1:T(2,128)(2,1)S(1)}, u32[]{:S(2)}, u32[]{:S(2)}) %collective-permute-start.5) | collective-permute-done | bytes 6176 | tf_op jit(solution)/shard_map/ppermute | solution.py:98
  26.0 0.7 %reshape.128.fill_ref = f32[12]{0:T(128)} reshape(f32[4,3]{1,0:T(4,128)S(1)} %broadcast_in_dim.5) | data formatting | bytes 96 | tf_op jit(solution)/shard_map/reshape | solution.py:133
  26.7 0.6 %convert_element_type.47.x_ref = f32[96,128]{1,0:T(8,128)} convert(bf16[96,128]{1,0:T(8,128)(2,1)S(1)} %rev.6) | non-fusion elementwise | flops 12288 | bytes 73728 | tf_op jit(solution)/shard_map/convert_element_type | solution.py:60
  27.3 6.7 %shard_map.46 = f32[64,512]{1,0:T(8,128)} custom-call(f32[96,128]{1,0:T(8,128)} %convert_element_type.47.x_ref, bf16[64,6144]{1,0:T(8,128)(2,1)} %reshape_reshape.3.n_ref, f32[12]{0:T(128)} %reshape.128.fill_ref), custom_call_target="tpu_custom_call" | custom-call | tf_op jit(solution)/shard_map/pallas_call | solution.py:51
  34.0 1.8 %collective-permute-start.9 = (f32[64,512]{1,0:T(8,128)}, f32[64,512]{1,0:T(8,128)S(1)}, u32[]{:S(2)}, u32[]{:S(2)}) collective-permute-start(f32[64,512]{1,0:T(8,128)} %shard_map.46), channel_id=1, source_target_pairs={{0,12},{4,0},{8,4},{12,8},{1,13},{5,1},{9,5},{13,9},{2,14},{6,2},{... | collective-permute-start | bytes 393224 | tf_op jit(solution)/shard_map/ppermute | solution.py:66
  36.0 1.8 %collective-permute-start.7 = (f32[64,512]{1,0:T(8,128)}, f32[64,512]{1,0:T(8,128)S(1)}, u32[]{:S(2)}, u32[]{:S(2)}) collective-permute-start(f32[64,512]{1,0:T(8,128)} %shard_map.46), channel_id=1, source_target_pairs={{0,8},{4,12},{8,0},{12,4},{1,9},{5,13},{9,1},{13,5},{2,10},{6,14},... | collective-permute-start | bytes 393224 | tf_op jit(solution)/shard_map/ppermute | solution.py:66
  37.8 3.7 %collective-permute-done.9 = f32[64,512]{1,0:T(8,128)S(1)} collective-permute-done((f32[64,512]{1,0:T(8,128)}, f32[64,512]{1,0:T(8,128)S(1)}, u32[]{:S(2)}, u32[]{:S(2)}) %collective-permute-start.9) | collective-permute-done | bytes 131104 | tf_op jit(solution)/shard_map/ppermute | solution.py:66
  41.6 2.4 %collective-permute-done.8 = f32[64,512]{1,0:T(8,128)S(1)} collective-permute-done((f32[64,512]{1,0:T(8,128)}, f32[64,512]{1,0:T(8,128)S(1)}, u32[]{:S(2)}, u32[]{:S(2)}) %collective-permute-start.8) | collective-permute-done | bytes 131104 | tf_op jit(solution)/shard_map/ppermute | solution.py:66
  43.9 3.3 %collective-permute-done.7 = f32[64,512]{1,0:T(8,128)S(1)} collective-permute-done((f32[64,512]{1,0:T(8,128)}, f32[64,512]{1,0:T(8,128)S(1)}, u32[]{:S(2)}, u32[]{:S(2)}) %collective-permute-start.7) | collective-permute-done | bytes 131104 | tf_op jit(solution)/shard_map/ppermute | solution.py:66
  47.2 1.0 %multiply_reduce_fusion = (f32[64]{0:T(128)S(1)}, f32[64,512]{1,0:T(8,128)S(1)}) fusion(f32[64,512]{1,0:T(8,128)S(1)} %collective-permute-done.8, f32[64,512]{1,0:T(8,128)S(1)} %collective-permute-done.9, f32[64,512]{1,0:T(8,128)} %shard_map.46, f32[64,512]{1,0:T(8,128)S(1)} %collective-permute-done.7), kind=kLoop, calls=%fused_computation.6 | loop fusion | flops 163776 | bytes 655616 | tf_op jit(solution)/shard_map/reduce_sum | solution.py:135
  48.6 3.2 %collective-permute-done.10 = f32[64]{0:T(128)S(1)} collective-permute-done((f32[64]{0:T(128)S(1)}, f32[64]{0:T(128)S(1)}, u32[]{:S(2)}, u32[]{:S(2)}) %collective-permute-start.10) | collective-permute-done | bytes 288 | tf_op jit(solution)/shard_map/ppermute | solution.py:66
  51.8 0.7 %broadcast_divide_fusion = f32[1,64,512]{2,1,0:T(8,128)} fusion(f32[1,64,512]{2,1,0:T(8,128)S(1)} %reshape.130, f32[64]{0:T(128)S(1)} %add_sqrt_fusion.1), kind=kLoop, calls=%fused_computation.9 | loop fusion | flops 32768 | bytes 262400 | tf_op jit(solution)/shard_map/div | solution.py:136
  (33 shorter events, 2.9 us)
Async XLA Ops:
  0.0 12.9 %copy-start = (bf16[1,64,4,3,512]{4,2,3,1,0:T(4,128)(2,1)S(1)}, bf16[1,64,4,3,512]{4,2,3,1,0:T(4,128)(2,1)}, u32[]{:S(2)}) copy-start(bf16[1,64,4,3,512]{4,2,3,1,0:T(4,128)(2,1)} %param.5) | copy-start | bytes 2359300
  0.0 19.0 %collective-permute-start.4 = (bf16[2,3,512]{2,0,1:T(2,128)(2,1)}, bf16[2,3,512]{2,0,1:T(2,128)(2,1)S(1)}, u32[]{:S(2)}, u32[]{:S(2)}) collective-permute-start(bf16[2,3,512]{2,0,1:T(2,128)(2,1)} %param.4), channel_id=1, source_target_pairs={{2,4},{6,8},{10,12},{14,0},{3,5},{7,9},{11,13},{15,1},{18,20},{22,... | collective-permute-start | bytes 18440 | tf_op jit(solution)/shard_map/ppermute | solution.py:98
  1.4 17.6 %collective-permute-start.3 = (bf16[2,3,512]{2,0,1:T(2,128)(2,1)}, bf16[2,3,512]{2,0,1:T(2,128)(2,1)S(1)}, u32[]{:S(2)}, u32[]{:S(2)}) collective-permute-start(bf16[2,3,512]{2,0,1:T(2,128)(2,1)} %param.4), channel_id=1, source_target_pairs={{2,0},{6,4},{10,8},{14,12},{3,1},{7,5},{11,9},{15,13},{18,16},{22,... | collective-permute-start | bytes 18440 | tf_op jit(solution)/shard_map/ppermute | solution.py:98
  4.2 11.8 %collective-permute-start.2 = (bf16[2,4,512]{2,0,1:T(2,128)(2,1)S(1)}, bf16[2,4,512]{2,0,1:T(2,128)(2,1)S(1)}, u32[]{:S(2)}, u32[]{:S(2)}) collective-permute-start(bf16[2,4,512]{2,0,1:T(2,128)(2,1)S(1)} %pad_maximum_fusion.4), channel_id=1, source_target_pairs={{0,12},{2,14},{4,0},{6,2},{8,4},{10,6},{12,8},{14,10},{1,13},{3,15... | collective-permute-start | bytes 24584 | tf_op jit(solution)/shard_map/ppermute | solution.py:90
  9.3 8.0 %collective-permute-start.1 = (bf16[2,4,512]{2,0,1:T(2,128)(2,1)S(1)}, bf16[2,4,512]{2,0,1:T(2,128)(2,1)S(1)}, u32[]{:S(2)}, u32[]{:S(2)}) collective-permute-start(bf16[2,4,512]{2,0,1:T(2,128)(2,1)S(1)} %pad_maximum_fusion.4), channel_id=1, source_target_pairs={{0,8},{2,10},{4,12},{6,14},{8,0},{10,2},{12,4},{14,6},{1,9},{3,11}... | collective-permute-start | bytes 24584 | tf_op jit(solution)/shard_map/ppermute | solution.py:90
  9.3 9.3 %collective-permute-start = (bf16[2,4,512]{2,0,1:T(2,128)(2,1)S(1)}, bf16[2,4,512]{2,0,1:T(2,128)(2,1)S(1)}, u32[]{:S(2)}, u32[]{:S(2)}) collective-permute-start(bf16[2,4,512]{2,0,1:T(2,128)(2,1)S(1)} %pad_maximum_fusion.4), channel_id=1, source_target_pairs={{0,4},{2,6},{4,8},{6,10},{8,12},{10,14},{12,0},{14,2},{1,5},{3,7},... | collective-permute-start | bytes 24584 | tf_op jit(solution)/shard_map/ppermute | solution.py:90
  14.1 1.9 %copy-start.1 = (bf16[2,3,512]{2,0,1:T(2,128)(2,1)S(1)}, bf16[2,3,512]{2,0,1:T(2,128)(2,1)}, u32[]{:S(2)}) copy-start(bf16[2,3,512]{2,0,1:T(2,128)(2,1)} %param.4) | copy-start | bytes 18436
  16.0 7.4 %collective-permute-start.6 = (bf16[2,3,512]{2,0,1:T(2,128)(2,1)S(1)}, bf16[2,3,512]{2,0,1:T(2,128)(2,1)S(1)}, u32[]{:S(2)}, u32[]{:S(2)}) collective-permute-start(bf16[2,3,512]{2,0,1:T(2,128)(2,1)S(1)} %copy-done.1), channel_id=1, source_target_pairs={{2,12},{6,0},{10,4},{14,8},{3,13},{7,1},{11,5},{15,9},{18,28},{22,... | collective-permute-start | bytes 18440 | tf_op jit(solution)/shard_map/ppermute | solution.py:98
  17.3 8.3 %collective-permute-start.5 = (bf16[2,3,512]{2,0,1:T(2,128)(2,1)S(1)}, bf16[2,3,512]{2,0,1:T(2,128)(2,1)S(1)}, u32[]{:S(2)}, u32[]{:S(2)}) collective-permute-start(bf16[2,3,512]{2,0,1:T(2,128)(2,1)S(1)} %copy-done.1), channel_id=1, source_target_pairs={{2,8},{6,12},{10,0},{14,4},{3,9},{7,13},{11,1},{15,5},{18,24},{22,... | collective-permute-start | bytes 18440 | tf_op jit(solution)/shard_map/ppermute | solution.py:98
  34.0 7.6 %collective-permute-start.9 = (f32[64,512]{1,0:T(8,128)}, f32[64,512]{1,0:T(8,128)S(1)}, u32[]{:S(2)}, u32[]{:S(2)}) collective-permute-start(f32[64,512]{1,0:T(8,128)} %shard_map.46), channel_id=1, source_target_pairs={{0,12},{4,0},{8,4},{12,8},{1,13},{5,1},{9,5},{13,9},{2,14},{6,2},{... | collective-permute-start | bytes 393224 | tf_op jit(solution)/shard_map/ppermute | solution.py:66
  35.8 8.1 %collective-permute-start.8 = (f32[64,512]{1,0:T(8,128)}, f32[64,512]{1,0:T(8,128)S(1)}, u32[]{:S(2)}, u32[]{:S(2)}) collective-permute-start(f32[64,512]{1,0:T(8,128)} %shard_map.46), channel_id=1, source_target_pairs={{0,4},{4,8},{8,12},{12,0},{1,5},{5,9},{9,13},{13,1},{2,6},{6,10},{... | collective-permute-start | bytes 393224 | tf_op jit(solution)/shard_map/ppermute | solution.py:66
  36.0 11.2 %collective-permute-start.7 = (f32[64,512]{1,0:T(8,128)}, f32[64,512]{1,0:T(8,128)S(1)}, u32[]{:S(2)}, u32[]{:S(2)}) collective-permute-start(f32[64,512]{1,0:T(8,128)} %shard_map.46), channel_id=1, source_target_pairs={{0,8},{4,12},{8,0},{12,4},{1,9},{5,13},{9,1},{13,5},{2,10},{6,14},... | collective-permute-start | bytes 393224 | tf_op jit(solution)/shard_map/ppermute | solution.py:66
  48.2 3.6 %collective-permute-start.10 = (f32[64]{0:T(128)S(1)}, f32[64]{0:T(128)S(1)}, u32[]{:S(2)}, u32[]{:S(2)}) collective-permute-start(f32[64]{0:T(128)S(1)} %get-tuple-element.5), channel_id=1, source_target_pairs={{0,2},{2,0},{1,3},{3,1},{4,6},{6,4},{5,7},{7,5},{8,10},{10,8},{9,1... | collective-permute-start | bytes 776 | tf_op jit(solution)/shard_map/ppermute | solution.py:66

commit v6 on v5

--- a/solution.py
+++ b/solution.py
@@ -79,32 +79,25 @@
     local_count, components, seg_len = records.shape
     regions = lax.axis_size("region")
     segs = lax.axis_size("seg")
-    tag = jnp.broadcast_to(station_region.astype(jnp.bfloat16)[:, None, None], (local_count, 1, seg_len))
-    payload = jnp.concatenate([records, tag], axis=1)
-    axes = ("region", "seg")
-    same_seg = [payload]
-    for k in range(1, regions):
-        pairs = [
-            (r * segs + s, ((r + k) % regions) * segs + s) for r in range(regions) for s in range(segs)
-        ]
-        same_seg.append(lax.ppermute(payload, axes, pairs))
-    next_seg = []
-    for k in range(regions):
-        pairs = [
-            (r * segs + s + 1, ((r + k) % regions) * segs + s)
-            for r in range(regions)
-            for s in range(segs - 1)
-        ]
-        next_seg.append(lax.ppermute(records[:, :, :filter_taps], axes, pairs))
+    ahead = lax.ppermute(
+        records[:, :, :filter_taps], "seg", [(s + 1, s) for s in range(segs - 1)]
+    )
+    tag = jnp.broadcast_to(station_region.astype(jnp.bfloat16)[:, None, None], (local_count, 1, seg_len + filter_taps))
+    payload = jnp.concatenate(
+        [jnp.concatenate([records, ahead], axis=2), tag], axis=1
+    )
+    gathered = [payload] + [
+        lax.ppermute(payload, "region", [(r, (r + k) % regions) for r in range(regions)])
+        for k in range(1, regions)
+    ]
     me = lax.axis_index("region")
     stations = regions * local_count
     shift = jnp.arange(regions, dtype=jnp.int32)[:, None]
     local = jnp.arange(local_count, dtype=jnp.int32)[None, :]
     station_ids = (((me - shift) % regions) * local_count + local).reshape(stations)
-    here = jnp.concatenate(same_seg, axis=0)
-    ahead = jnp.concatenate(next_seg, axis=0)
+    here = jnp.concatenate(gathered, axis=0)
     region_of = here[:, components, 0].astype(jnp.int32)
-    rows = jnp.concatenate([here[:, :components, :], ahead], axis=2)
+    rows = here[:, :components, :]
     earlier = (region_of[None, :] == region_of[:, None]) & (station_ids[None, :] < station_ids[:, None])
     ranks = jnp.sum(earlier.astype(jnp.int32), axis=1)
     slot_index = jnp.arange(capacity, dtype=jnp.int32)

time: 52.9 us -> 43.6 us (0.82)
  waiting for transfers between devices: 19.2 us -> 13.8 us
  starting transfers between devices: 15.3 us -> 12.7 us
  other arithmetic: 7.31 us -> 5.97 us
    ppermute x7 -> x4, starting transfers between devices: 11.4 us -> 7.23 us  [the longest x3 5.82 us: gather_owned(): lax.ppermute(payload, 'region', [(r, (r + k) % regions) for r in range(re...]
    ppermute x7 -> x4, waiting for transfers between devices: 6.58 us -> 3.52 us  [the longest x3 1.97 us: gather_owned(): lax.ppermute(payload, 'region', [(r, (r + k) % regions) for r in range(re...]
    ppermute x4, waiting for transfers between devices: 12.6 us -> 10.3 us  [ordered_sum(): lax.ppermute(part, axis, [(i, (i + k) % size) for i in range(size)])]
    ppermute x4, starting transfers between devices: 3.9 us -> 5.48 us  [ordered_sum(): lax.ppermute(part, axis, [(i, (i + k) % size) for i in range(size)])]
    concatenate x2, other arithmetic: 0.77 us -> 0.08 us  [the longest x1 0.06 us: gather_owned(): here = jnp.concatenate(gathered, axis=0)]
    convert_element_type x1, other arithmetic: 0.66 us -> 0.01 us  [gather_owned(): station_region.astype(jnp.bfloat16)[:, None, None]]
  transfers between devices with their start and end apart: 11 -> 8, of which waited for: 6 -> 7; matrix products, arithmetic and copies ran while one was open for 15% -> 14% of each run, Pallas kernels for 0% -> 0%
where the time goes in v6:
time: 43.6 us; the launch traced here: 43.3 us
  waiting for transfers between devices  13.8 us (32%)
  starting transfers between devices  12.7 us (29%)
  Pallas kernels  6.7 us (15%)
  other arithmetic  5.97 us (14%)
  local copies, waits for them, and re-layouts  3.82 us (9%)
    ppermute x4, waiting for transfers between devices, ordered_sum(): lax.ppermute(part, axis, [(i, (i + k) % size) for i in range(size)])  10.3 us
    pallas_call x1, Pallas kernels, correlate(): pl.pallas_call(hankel_kernel, out_shape=jax.ShapeDtypeStruct((rows, seg_l...  6.7 us
    ppermute x3, starting transfers between devices, gather_owned(): lax.ppermute(payload, 'region', [(r, (r + k) % regions) for r in range(re...  5.82 us
    ppermute x4, starting transfers between devices, ordered_sum(): lax.ppermute(part, axis, [(i, (i + k) % size) for i in range(size)])  5.48 us
    ppermute x3, waiting for transfers between devices, gather_owned(): lax.ppermute(payload, 'region', [(r, (r + k) % regions) for r in range(re...  1.97 us
    another operation x1, local copies, waits for them, and re-layouts, correlate(): normed.reshape(rows, channels * filter_taps)  1.84 us
    reduce_sum x1, other arithmetic, per_device(): jnp.sum(widened_templates * widened_templates, axis=4, keepdims=True)  1.65 us
    ppermute x1, waiting for transfers between devices, gather_owned(): lax.ppermute(records[:, :, :filter_taps], 'seg', [(s + 1, s) for s in ran...  1.55 us
  transfers between devices with their start and end apart: 8, of which 7 were waited for; matrix products, arithmetic and copies ran while one was open for 14% of the time, Pallas kernels for 0%

profile of v6, /device:TPU:0, one launch (start us, length us, event | category | flops | bytes accessed | tf_op | source)
XLA Modules:
  0.0 43.3 jit_solution(1571956823692523295)
XLA Ops:
  0.0 1.4 %collective-permute-start = (bf16[2,3,512]{2,0,1:T(2,128)(2,1)}, bf16[2,3,512]{2,0,1:T(2,128)(2,1)S(1)}, u32[]{:S(2)}, u32[]{:S(2)}) collective-permute-start(bf16[2,3,512]{2,0,1:T(2,128)(2,1)} %param.4), channel_id=1, source_target_pairs={{2,0},{3,1},{6,4},{7,5},{10,8},{11,9},{14,12},{15,13},{18,16},{19,... | collective-permute-start | bytes 18440 | tf_op jit(solution)/shard_map/ppermute | solution.py:82
  1.4 0.7 %convert_bitcast_fusion = f32[64,4,3]{0,1,2:T(4,128)S(1)} fusion(s32[1,64,4,3]{1,2,3,0:T(4,128)} %param.6), kind=kLoop, calls=%fused_computation.16 | loop fusion | flops 768 | bytes 6144 | tf_op jit(solution)/shard_map/mul | solution.py:123
  2.3 1.7 %fusion.2 = f32[64,4,3]{1,2,0:T(4,128)S(1)} fusion(bf16[1,64,4,3,512]{4,2,3,1,0:T(4,128)(2,1)} %param.5), kind=kLoop, calls=%fused_computation.5 | loop fusion | flops 1178880 | bytes 789504 | tf_op jit(solution)/shard_map/reduce_sum | solution.py:121
  4.0 0.5 %fusion.1 = bf16[1,64,4,3,512]{4,2,3,1,0:T(4,128)(2,1)S(1)} fusion(bf16[1,64,4,3,512]{4,2,3,1,0:T(4,128)(2,1)S(1)} %copy-done, f32[64,4,3]{1,2,0:T(4,128)S(1)} %add_sqrt_fusion, f32[64,4,3]{1,2,0:T(4,128)S(1)} %copy.9), kind=kLoop, calls=%fused_computation.4 | loop fusion | flops 1572864 | bytes 1579008 | tf_op jit(solution)/shard_map/convert_element_type | solution.py:123
  4.6 1.6 %collective-permute-done = bf16[2,3,512]{2,0,1:T(2,128)(2,1)S(1)} collective-permute-done((bf16[2,3,512]{2,0,1:T(2,128)(2,1)}, bf16[2,3,512]{2,0,1:T(2,128)(2,1)S(1)}, u32[]{:S(2)}, u32[]{:S(2)}) %collective-permute-start) | collective-permute-done | bytes 6176 | tf_op jit(solution)/shard_map/ppermute | solution.py:82
  6.3 4.8 %collective-permute-start.3 = (bf16[2,4,1024]{2,0,1:T(2,128)(2,1)S(1)}, bf16[2,4,1024]{2,0,1:T(2,128)(2,1)S(1)}, u32[]{:S(2)}, u32[]{:S(2)}) collective-permute-start(bf16[2,4,1024]{2,0,1:T(2,128)(2,1)S(1)} %pad_maximum_fusion.5), channel_id=1, source_target_pairs={{0,12},{4,0},{8,4},{12,8},{1,13},{5,1},{9,5},{13,9},{2,14},{6,2},{... | collective-permute-start | bytes 49160 | tf_op jit(solution)/shard_map/ppermute | solution.py:90
  11.1 1.0 %collective-permute-start.1 = (bf16[2,4,1024]{2,0,1:T(2,128)(2,1)S(1)}, bf16[2,4,1024]{2,0,1:T(2,128)(2,1)S(1)}, u32[]{:S(2)}, u32[]{:S(2)}) collective-permute-start(bf16[2,4,1024]{2,0,1:T(2,128)(2,1)S(1)} %pad_maximum_fusion.5), channel_id=1, source_target_pairs={{0,4},{4,8},{8,12},{12,0},{1,5},{5,9},{9,13},{13,1},{2,6},{6,10},{... | collective-permute-start | bytes 49160 | tf_op jit(solution)/shard_map/ppermute | solution.py:90
  12.2 0.6 %copy.10 = bf16[1,64,4,3,512]{4,3,2,1,0:T(4,128)(2,1)S(1)} copy(bf16[1,64,4,3,512]{4,2,3,1,0:T(4,128)(2,1)S(1)} %fusion.1) | data formatting | bytes 1572864 | tf_op jit(solution)/shard_map/convert_element_type | solution.py:123
  12.8 1.8 %reshape_reshape.3.n_ref = bf16[64,6144]{1,0:T(8,128)(2,1)} reshape(bf16[1,64,4,3,512]{4,3,2,1,0:T(4,128)(2,1)S(1)} %copy.10) | data formatting | bytes 1572864 | tf_op jit(solution)/shard_map/reshape;reshape | solution.py:60
  14.6 1.1 %collective-permute-done.2 = bf16[2,4,1024]{2,0,1:T(2,128)(2,1)S(1)} collective-permute-done((bf16[2,4,1024]{2,0,1:T(2,128)(2,1)S(1)}, bf16[2,4,1024]{2,0,1:T(2,128)(2,1)S(1)}, u32[]{:S(2)}, u32[]{:S(2)}) %collective-permute-start.2) | collective-permute-done | bytes 16416 | tf_op jit(solution)/shard_map/ppermute | solution.py:90
  15.7 0.9 %collective-permute-done.1 = bf16[2,4,1024]{2,0,1:T(2,128)(2,1)S(1)} collective-permute-done((bf16[2,4,1024]{2,0,1:T(2,128)(2,1)S(1)}, bf16[2,4,1024]{2,0,1:T(2,128)(2,1)S(1)}, u32[]{:S(2)}, u32[]{:S(2)}) %collective-permute-start.1) | collective-permute-done | bytes 16416 | tf_op jit(solution)/shard_map/ppermute | solution.py:90
  17.4 0.7 %reshape.128.fill_ref = f32[12]{0:T(128)} reshape(f32[4,3]{1,0:T(4,128)S(1)} %broadcast_in_dim.5) | data formatting | bytes 96 | tf_op jit(solution)/shard_map/reshape | solution.py:126
  18.1 0.6 %convert_element_type.47.x_ref = f32[96,128]{1,0:T(8,128)} convert(bf16[96,128]{1,0:T(8,128)(2,1)S(1)} %rev.6) | non-fusion elementwise | flops 12288 | bytes 73728 | tf_op jit(solution)/shard_map/convert_element_type | solution.py:60
  18.7 6.7 %shard_map.46 = f32[64,512]{1,0:T(8,128)} custom-call(f32[96,128]{1,0:T(8,128)} %convert_element_type.47.x_ref, bf16[64,6144]{1,0:T(8,128)(2,1)} %reshape_reshape.3.n_ref, f32[12]{0:T(128)} %reshape.128.fill_ref), custom_call_target="tpu_custom_call" | custom-call | tf_op jit(solution)/shard_map/pallas_call | solution.py:51
  25.4 0.9 %collective-permute-start.6 = (f32[64,512]{1,0:T(8,128)}, f32[64,512]{1,0:T(8,128)S(1)}, u32[]{:S(2)}, u32[]{:S(2)}) collective-permute-start(f32[64,512]{1,0:T(8,128)} %shard_map.46), channel_id=1, source_target_pairs={{0,12},{4,0},{8,4},{12,8},{1,13},{5,1},{9,5},{13,9},{2,14},{6,2},{... | collective-permute-start | bytes 393224 | tf_op jit(solution)/shard_map/ppermute | solution.py:66
  26.3 1.2 %collective-permute-start.5 = (f32[64,512]{1,0:T(8,128)}, f32[64,512]{1,0:T(8,128)S(1)}, u32[]{:S(2)}, u32[]{:S(2)}) collective-permute-start(f32[64,512]{1,0:T(8,128)} %shard_map.46), channel_id=1, source_target_pairs={{0,4},{4,8},{8,12},{12,0},{1,5},{5,9},{9,13},{13,1},{2,6},{6,10},{... | collective-permute-start | bytes 393224 | tf_op jit(solution)/shard_map/ppermute | solution.py:66
  27.4 1.1 %collective-permute-start.4 = (f32[64,512]{1,0:T(8,128)}, f32[64,512]{1,0:T(8,128)S(1)}, u32[]{:S(2)}, u32[]{:S(2)}) collective-permute-start(f32[64,512]{1,0:T(8,128)} %shard_map.46), channel_id=1, source_target_pairs={{0,8},{4,12},{8,0},{12,4},{1,9},{5,13},{9,1},{13,5},{2,10},{6,14},... | collective-permute-start | bytes 393224 | tf_op jit(solution)/shard_map/ppermute | solution.py:66
  28.6 3.5 %collective-permute-done.6 = f32[64,512]{1,0:T(8,128)S(1)} collective-permute-done((f32[64,512]{1,0:T(8,128)}, f32[64,512]{1,0:T(8,128)S(1)}, u32[]{:S(2)}, u32[]{:S(2)}) %collective-permute-start.6) | collective-permute-done | bytes 131104 | tf_op jit(solution)/shard_map/ppermute | solution.py:66
  32.1 2.4 %collective-permute-done.5 = f32[64,512]{1,0:T(8,128)S(1)} collective-permute-done((f32[64,512]{1,0:T(8,128)}, f32[64,512]{1,0:T(8,128)S(1)}, u32[]{:S(2)}, u32[]{:S(2)}) %collective-permute-start.5) | collective-permute-done | bytes 131104 | tf_op jit(solution)/shard_map/ppermute | solution.py:66
  34.4 3.2 %collective-permute-done.4 = f32[64,512]{1,0:T(8,128)S(1)} collective-permute-done((f32[64,512]{1,0:T(8,128)}, f32[64,512]{1,0:T(8,128)S(1)}, u32[]{:S(2)}, u32[]{:S(2)}) %collective-permute-start.4) | collective-permute-done | bytes 131104 | tf_op jit(solution)/shard_map/ppermute | solution.py:66
  37.7 1.0 %multiply_reduce_fusion = (f32[64]{0:T(128)S(1)}, f32[64,512]{1,0:T(8,128)S(1)}) fusion(f32[64,512]{1,0:T(8,128)S(1)} %collective-permute-done.5, f32[64,512]{1,0:T(8,128)S(1)} %collective-permute-done.6, f32[64,512]{1,0:T(8,128)} %shard_map.46, f32[64,512]{1,0:T(8,128)S(1)} %collective-permute-done.4), kind=kLoop, calls=%fused_computation.6 | loop fusion | flops 163776 | bytes 655616 | tf_op jit(solution)/shard_map/reduce_sum | solution.py:128
  38.7 2.3 %collective-permute-start.7 = (f32[64]{0:T(128)S(1)}, f32[64]{0:T(128)S(1)}, u32[]{:S(2)}, u32[]{:S(2)}) collective-permute-start(f32[64]{0:T(128)S(1)} %get-tuple-element.5), channel_id=1, source_target_pairs={{0,2},{2,0},{1,3},{3,1},{4,6},{6,4},{5,7},{7,5},{8,10},{10,8},{9,1... | collective-permute-start | bytes 776 | tf_op jit(solution)/shard_map/ppermute | solution.py:66
  41.4 1.2 %collective-permute-done.7 = f32[64]{0:T(128)S(1)} collective-permute-done((f32[64]{0:T(128)S(1)}, f32[64]{0:T(128)S(1)}, u32[]{:S(2)}, u32[]{:S(2)}) %collective-permute-start.7) | collective-permute-done | bytes 288 | tf_op jit(solution)/shard_map/ppermute | solution.py:66
  42.6 0.7 %broadcast_divide_fusion = f32[1,64,512]{2,1,0:T(8,128)} fusion(f32[1,64,512]{2,1,0:T(8,128)S(1)} %reshape.130, f32[64]{0:T(128)S(1)} %add_sqrt_fusion.1), kind=kLoop, calls=%fused_computation.9 | loop fusion | flops 32768 | bytes 262400 | tf_op jit(solution)/shard_map/div | solution.py:129
  (29 shorter events, 1.6 us)
Async XLA Ops:
  0.0 4.0 %copy-start = (bf16[1,64,4,3,512]{4,2,3,1,0:T(4,128)(2,1)S(1)}, bf16[1,64,4,3,512]{4,2,3,1,0:T(4,128)(2,1)}, u32[]{:S(2)}) copy-start(bf16[1,64,4,3,512]{4,2,3,1,0:T(4,128)(2,1)} %param.5) | copy-start | bytes 2359300
  0.0 6.2 %collective-permute-start = (bf16[2,3,512]{2,0,1:T(2,128)(2,1)}, bf16[2,3,512]{2,0,1:T(2,128)(2,1)S(1)}, u32[]{:S(2)}, u32[]{:S(2)}) collective-permute-start(bf16[2,3,512]{2,0,1:T(2,128)(2,1)} %param.4), channel_id=1, source_target_pairs={{2,0},{3,1},{6,4},{7,5},{10,8},{11,9},{14,12},{15,13},{18,16},{19,... | collective-permute-start | bytes 18440 | tf_op jit(solution)/shard_map/ppermute | solution.py:82
  3.9 0.7 %copy-start.2 = (s32[2]{0:T(128)S(1)}, s32[2]{0:T(128)}, u32[]{:S(2)}) copy-start(s32[2]{0:T(128)} %param.7) | copy-start | bytes 28
  3.9 2.3 %copy-start.1 = (bf16[2,3,512]{2,0,1:T(2,128)(2,1)S(1)}, bf16[2,3,512]{2,0,1:T(2,128)(2,1)}, u32[]{:S(2)}) copy-start(bf16[2,3,512]{2,0,1:T(2,128)(2,1)} %param.4) | copy-start | bytes 18436
  6.3 8.4 %collective-permute-start.3 = (bf16[2,4,1024]{2,0,1:T(2,128)(2,1)S(1)}, bf16[2,4,1024]{2,0,1:T(2,128)(2,1)S(1)}, u32[]{:S(2)}, u32[]{:S(2)}) collective-permute-start(bf16[2,4,1024]{2,0,1:T(2,128)(2,1)S(1)} %pad_maximum_fusion.5), channel_id=1, source_target_pairs={{0,12},{4,0},{8,4},{12,8},{1,13},{5,1},{9,5},{13,9},{2,14},{6,2},{... | collective-permute-start | bytes 49160 | tf_op jit(solution)/shard_map/ppermute | solution.py:90
  11.1 4.6 %collective-permute-start.2 = (bf16[2,4,1024]{2,0,1:T(2,128)(2,1)S(1)}, bf16[2,4,1024]{2,0,1:T(2,128)(2,1)S(1)}, u32[]{:S(2)}, u32[]{:S(2)}) collective-permute-start(bf16[2,4,1024]{2,0,1:T(2,128)(2,1)S(1)} %pad_maximum_fusion.5), channel_id=1, source_target_pairs={{0,8},{4,12},{8,0},{12,4},{1,9},{5,13},{9,1},{13,5},{2,10},{6,14},... | collective-permute-start | bytes 49160 | tf_op jit(solution)/shard_map/ppermute | solution.py:90
  11.1 5.5 %collective-permute-start.1 = (bf16[2,4,1024]{2,0,1:T(2,128)(2,1)S(1)}, bf16[2,4,1024]{2,0,1:T(2,128)(2,1)S(1)}, u32[]{:S(2)}, u32[]{:S(2)}) collective-permute-start(bf16[2,4,1024]{2,0,1:T(2,128)(2,1)S(1)} %pad_maximum_fusion.5), channel_id=1, source_target_pairs={{0,4},{4,8},{8,12},{12,0},{1,5},{5,9},{9,13},{13,1},{2,6},{6,10},{... | collective-permute-start | bytes 49160 | tf_op jit(solution)/shard_map/ppermute | solution.py:90
  25.4 6.6 %collective-permute-start.6 = (f32[64,512]{1,0:T(8,128)}, f32[64,512]{1,0:T(8,128)S(1)}, u32[]{:S(2)}, u32[]{:S(2)}) collective-permute-start(f32[64,512]{1,0:T(8,128)} %shard_map.46), channel_id=1, source_target_pairs={{0,12},{4,0},{8,4},{12,8},{1,13},{5,1},{9,5},{13,9},{2,14},{6,2},{... | collective-permute-start | bytes 393224 | tf_op jit(solution)/shard_map/ppermute | solution.py:66
  26.3 8.2 %collective-permute-start.5 = (f32[64,512]{1,0:T(8,128)}, f32[64,512]{1,0:T(8,128)S(1)}, u32[]{:S(2)}, u32[]{:S(2)}) collective-permute-start(f32[64,512]{1,0:T(8,128)} %shard_map.46), channel_id=1, source_target_pairs={{0,4},{4,8},{8,12},{12,0},{1,5},{5,9},{9,13},{13,1},{2,6},{6,10},{... | collective-permute-start | bytes 393224 | tf_op jit(solution)/shard_map/ppermute | solution.py:66
  27.4 10.2 %collective-permute-start.4 = (f32[64,512]{1,0:T(8,128)}, f32[64,512]{1,0:T(8,128)S(1)}, u32[]{:S(2)}, u32[]{:S(2)}) collective-permute-start(f32[64,512]{1,0:T(8,128)} %shard_map.46), channel_id=1, source_target_pairs={{0,8},{4,12},{8,0},{12,4},{1,9},{5,13},{9,1},{13,5},{2,10},{6,14},... | collective-permute-start | bytes 393224 | tf_op jit(solution)/shard_map/ppermute | solution.py:66
  38.7 3.8 %collective-permute-start.7 = (f32[64]{0:T(128)S(1)}, f32[64]{0:T(128)S(1)}, u32[]{:S(2)}, u32[]{:S(2)}) collective-permute-start(f32[64]{0:T(128)S(1)} %get-tuple-element.5), channel_id=1, source_target_pairs={{0,2},{2,0},{1,3},{3,1},{4,6},{6,4},{5,7},{7,5},{8,10},{10,8},{9,1... | collective-permute-start | bytes 776 | tf_op jit(solution)/shard_map/ppermute | solution.py:66

commit v7 on v6

--- a/solution.py
+++ b/solution.py
@@ -6,7 +6,7 @@
 from jax.experimental.pallas import tpu as pltpu
 
 
-def hankel_kernel(x_ref, n_ref, fill_ref, o_ref, h_ref):
+def hankel_kernel(x_ref, n_ref, o_ref, h_ref):
     width = h_ref.shape[0]
     channels = n_ref.shape[1] // width
     taps_blocks = width // 128
@@ -35,7 +35,7 @@
         )
         start = pl.multiple_of(c * width, 128)
         part = jnp.dot(n_ref[:, pl.ds(start, width)], h_ref[...], preferred_element_type=jnp.float32)
-        return acc + part * (fill_ref[c] / jnp.sqrt(jnp.maximum(energy, 1.0)))
+        return acc + part * (1.0 / jnp.sqrt(jnp.maximum(energy, 1.0)))
 
     o_ref[...] = lax.fori_loop(0, channels, one_channel, jnp.zeros(o_ref.shape, jnp.float32))
 
@@ -45,19 +45,14 @@
     return stacked.reshape(rows, seg_len // 128, 128)[..., ::-1].reshape(rows, seg_len)
 
 
-def correlate(normed, flat_owned, filled, seg_len):
+def correlate(normed, flat_owned, seg_len):
     rows, channels, filter_taps = normed.shape
     blocks = flat_owned.reshape(channels * (flat_owned.shape[1] // 128), 128)[:, ::-1]
     return pl.pallas_call(
         hankel_kernel,
         out_shape=jax.ShapeDtypeStruct((rows, seg_len), jnp.float32),
-        in_specs=[
-            pl.BlockSpec(memory_space=pltpu.VMEM),
-            pl.BlockSpec(memory_space=pltpu.VMEM),
-            pl.BlockSpec(memory_space=pltpu.SMEM),
-        ],
         scratch_shapes=[pltpu.VMEM((filter_taps, seg_len), jnp.bfloat16)],
-    )(blocks.astype(jnp.float32), normed.reshape(rows, channels * filter_taps), filled)
+    )(blocks, normed.reshape(rows, channels * filter_taps))
 
 
 def ordered_sum(part, axis):
@@ -114,6 +109,7 @@
     local_batches, kept, capacity, components, filter_taps = templates.shape
     seg_len = records.shape[2]
     owned_rows, filled = gather_owned(records, station_region, capacity, filter_taps)
+    owned_rows = owned_rows.astype(jnp.float32) * filled[:, None, None]
     flat_owned = owned_rows.reshape(capacity * components, seg_len + filter_taps)
     weight = channel_mask.astype(jnp.float32)
     widened_templates = templates.astype(jnp.float32)
@@ -123,11 +119,38 @@
     normed = (widened_templates * weight[..., None] / template_norm).astype(jnp.bfloat16)
     normed = normed.reshape(local_batches * kept, capacity * components, filter_taps)
     total_len = seg_len * lax.axis_size("seg")
-    filled_channels = jnp.repeat(filled, components)
-    stacked = ordered_sum(correlate(normed, flat_owned, filled_channels, seg_len), "region")
-    power_sum = ordered_sum(jnp.sum(stacked * stacked, axis=1), "seg")
+    stacked, power_sum = region_sum(correlate(normed, flat_owned, seg_len))
+    power_sum = ordered_sum(power_sum, "seg")
     detect = unflip(stacked) / jnp.sqrt(power_sum / total_len + 1e-06)[:, None]
     return detect.reshape(local_batches, kept, seg_len)
+
+
+def region_sum(part):
+    regions = lax.axis_size("region")
+    rows, width = part.shape
+    chunk = width // regions
+    me = lax.axis_index("region")
+    chunks = part.reshape(rows, regions, chunk)
+
+    def shifted(value, k):
+        return lax.ppermute(value, "region", [(r, (r + k) % regions) for r in range(regions)])
+
+    own = jnp.take(chunks, me, axis=1)
+    for k in range(1, regions):
+        own = own + shifted(jnp.take(chunks, (me + k) % regions, axis=1), k)
+    power = jnp.sum(own * own, axis=1)
+    power_rows = -(-rows // chunk)
+    packed = jnp.pad(power, (0, power_rows * chunk - rows)).reshape(power_rows, chunk)
+    bundle = jnp.concatenate([own, packed], axis=0)
+    received = [bundle] + [shifted(bundle, k) for k in range(1, regions)]
+    powers = [b[rows:].reshape(-1)[:rows] for b in received]
+    while len(powers) > 1:
+        half = len(powers) // 2
+        powers = [powers[k] + powers[k + half] for k in range(half)]
+    order = (me - jnp.arange(regions, dtype=jnp.int32)) % regions
+    pieces = jnp.stack([b[:rows] for b in received], axis=1)
+    full = jnp.take(pieces, order, axis=1).reshape(rows, width)
+    return full, powers[0]
 
 
 def solution(mesh):

time: 43.6 us -> 44.4 us (1.018)
  starting transfers between devices: 12.7 us -> 16.3 us
  waiting for transfers between devices: 13.8 us -> 11.5 us
  other arithmetic: 5.97 us -> 3.87 us
  local copies, waits for them, and re-layouts: 3.82 us -> 5.39 us
    ppermute x4 -> x1, waiting for transfers between devices: 10.3 us -> 2.27 us  [ordered_sum(): lax.ppermute(part, axis, [(i, (i + k) % size) for i in range(size)])]
    ppermute x0 -> x6, starting transfers between devices: none -> 7.83 us  [shifted(): lax.ppermute(value, 'region', [(r, (r + k) % regions) for r in range(regi...]
    ppermute x0 -> x6, waiting for transfers between devices: none -> 7.03 us  [shifted(): lax.ppermute(value, 'region', [(r, (r + k) % regions) for r in range(regi...]
    ppermute x4 -> x1, starting transfers between devices: 5.48 us -> 0.33 us  [ordered_sum(): lax.ppermute(part, axis, [(i, (i + k) % size) for i in range(size)])]
    ppermute x3, waiting for transfers between devices: 1.97 us -> 0.01 us  [gather_owned(): lax.ppermute(payload, 'region', [(r, (r + k) % regions) for r in range(re...]
    reduce_sum x1, other arithmetic: 1.05 us -> 0.11 us  [region_sum(): power = jnp.sum(own * own, axis=1)]
    ppermute x3, starting transfers between devices: 5.82 us -> 6.72 us  [gather_owned(): lax.ppermute(payload, 'region', [(r, (r + k) % regions) for r in range(re...]
    mul x1, other arithmetic: 0.7 us -> 0.01 us  [per_device(): widened_templates * weight[..., None] / template_norm]
  transfers between devices with their start and end apart: 8 -> 11, of which waited for: 7 -> 8; matrix products, arithmetic and copies ran while one was open for 14% -> 13% of each run, Pallas kernels for 0% -> 0%
where the time goes in v7:
time: 44.4 us; the launch traced here: 44.1 us
  starting transfers between devices  16.3 us (37%)
  waiting for transfers between devices  11.5 us (26%)
  Pallas kernels  6.67 us (15%)
  local copies, waits for them, and re-layouts  5.39 us (12%)
  other arithmetic  3.87 us (9%)
    ppermute x6, starting transfers between devices, shifted(): lax.ppermute(value, 'region', [(r, (r + k) % regions) for r in range(regi...  7.83 us
    ppermute x6, waiting for transfers between devices, shifted(): lax.ppermute(value, 'region', [(r, (r + k) % regions) for r in range(regi...  7.03 us
    ppermute x3, starting transfers between devices, gather_owned(): lax.ppermute(payload, 'region', [(r, (r + k) % regions) for r in range(re...  6.72 us
    pallas_call x1, Pallas kernels, correlate(): pl.pallas_call(hankel_kernel, out_shape=jax.ShapeDtypeStruct((rows, seg_l...  6.67 us
    ppermute x1, waiting for transfers between devices, ordered_sum(): lax.ppermute(part, axis, [(i, (i + k) % size) for i in range(size)])  2.27 us
    ppermute x1, waiting for transfers between devices, gather_owned(): lax.ppermute(records[:, :, :filter_taps], 'seg', [(s + 1, s) for s in ran...  2.19 us
    another operation x1, local copies, waits for them, and re-layouts, correlate(): normed.reshape(rows, channels * filter_taps)  1.84 us
    reduce_sum x1, other arithmetic, per_device(): jnp.sum(widened_templates * widened_templates, axis=4, keepdims=True)  1.65 us
  transfers between devices with their start and end apart: 11, of which 8 were waited for; matrix products, arithmetic and copies ran while one was open for 13% of the time, Pallas kernels for 0%

profile of v7, /device:TPU:0, one launch (start us, length us, event | category | flops | bytes accessed | tf_op | source)
XLA Modules:
  0.0 44.1 jit_solution(15581149503680898105)
XLA Ops:
  0.0 1.4 %collective-permute-start = (bf16[2,3,512]{2,0,1:T(2,128)(2,1)}, bf16[2,3,512]{2,0,1:T(2,128)(2,1)S(1)}, u32[]{:S(2)}, u32[]{:S(2)}) collective-permute-start(bf16[2,3,512]{2,0,1:T(2,128)(2,1)} %param.6), channel_id=1, source_target_pairs={{2,0},{3,1},{6,4},{7,5},{10,8},{11,9},{14,12},{15,13},{18,16},{19,... | collective-permute-start | bytes 18440 | tf_op jit(solution)/shard_map/ppermute | solution.py:77
  1.4 1.6 %fusion.3 = f32[64,4,3]{1,2,0:T(4,128)S(1)} fusion(bf16[1,64,4,3,512]{4,2,3,1,0:T(4,128)(2,1)} %param.7), kind=kLoop, calls=%fused_computation.7 | loop fusion | flops 1178880 | bytes 789504 | tf_op jit(solution)/shard_map/reduce_sum | solution.py:117
  3.4 0.5 %fusion.2 = bf16[1,64,4,3,512]{4,2,3,1,0:T(4,128)(2,1)S(1)} fusion(bf16[1,64,4,3,512]{4,2,3,1,0:T(4,128)(2,1)S(1)} %copy-done, f32[64,4,3]{1,2,0:T(4,128)S(1)} %add_sqrt_fusion, f32[64,4,3]{1,2,0:T(4,128)S(1)} %copy.19), kind=kLoop, calls=%fused_computation.6 | loop fusion | flops 1572864 | bytes 1579008 | tf_op jit(solution)/shard_map/convert_element_type | solution.py:119
  4.0 2.2 %collective-permute-done = bf16[2,3,512]{2,0,1:T(2,128)(2,1)S(1)} collective-permute-done((bf16[2,3,512]{2,0,1:T(2,128)(2,1)}, bf16[2,3,512]{2,0,1:T(2,128)(2,1)S(1)}, u32[]{:S(2)}, u32[]{:S(2)}) %collective-permute-start) | collective-permute-done | bytes 6176 | tf_op jit(solution)/shard_map/ppermute | solution.py:77
  6.3 2.8 %collective-permute-start.1 = (bf16[2,4,1024]{2,0,1:T(2,128)(2,1)S(1)}, bf16[2,4,1024]{2,0,1:T(2,128)(2,1)S(1)}, u32[]{:S(2)}, u32[]{:S(2)}) collective-permute-start(bf16[2,4,1024]{2,0,1:T(2,128)(2,1)S(1)} %pad_maximum_fusion.7), channel_id=1, source_target_pairs={{0,4},{4,8},{8,12},{12,0},{1,5},{5,9},{9,13},{13,1},{2,6},{6,10},{... | collective-permute-start | bytes 49160 | tf_op jit(solution)/shard_map/ppermute | solution.py:85
  9.0 2.6 %collective-permute-start.2 = (bf16[2,4,1024]{2,0,1:T(2,128)(2,1)S(1)}, bf16[2,4,1024]{2,0,1:T(2,128)(2,1)S(1)}, u32[]{:S(2)}, u32[]{:S(2)}) collective-permute-start(bf16[2,4,1024]{2,0,1:T(2,128)(2,1)S(1)} %pad_maximum_fusion.7), channel_id=1, source_target_pairs={{0,8},{4,12},{8,0},{12,4},{1,9},{5,13},{9,1},{13,5},{2,10},{6,14},... | collective-permute-start | bytes 49160 | tf_op jit(solution)/shard_map/ppermute | solution.py:85
  11.6 1.3 %collective-permute-start.3 = (bf16[2,4,1024]{2,0,1:T(2,128)(2,1)S(1)}, bf16[2,4,1024]{2,0,1:T(2,128)(2,1)S(1)}, u32[]{:S(2)}, u32[]{:S(2)}) collective-permute-start(bf16[2,4,1024]{2,0,1:T(2,128)(2,1)S(1)} %pad_maximum_fusion.7), channel_id=1, source_target_pairs={{0,12},{4,0},{8,4},{12,8},{1,13},{5,1},{9,5},{13,9},{2,14},{6,2},{... | collective-permute-start | bytes 49160 | tf_op jit(solution)/shard_map/ppermute | solution.py:85
  13.1 0.6 %copy.20 = bf16[1,64,4,3,512]{4,3,2,1,0:T(4,128)(2,1)S(1)} copy(bf16[1,64,4,3,512]{4,2,3,1,0:T(4,128)(2,1)S(1)} %fusion.2) | data formatting | bytes 1572864 | tf_op jit(solution)/shard_map/convert_element_type | solution.py:119
  13.7 1.8 %reshape_reshape.4.n_ref = bf16[64,6144]{1,0:T(8,128)(2,1)} reshape(bf16[1,64,4,3,512]{4,3,2,1,0:T(4,128)(2,1)S(1)} %copy.20) | data formatting | bytes 1572864 | tf_op jit(solution)/shard_map/reshape;reshape | solution.py:55
  16.3 0.7 %rev.6.x_ref = f32[96,128]{1,0:T(8,128)} reverse(f32[96,128]{1,0:T(8,128)S(1)} %mul.38), dimensions={1} | reverse | bytes 98304 | tf_op jit(solution)/shard_map/rev | solution.py:50
  17.0 6.7 %shard_map.46 = f32[64,512]{1,0:T(8,128)} custom-call(f32[96,128]{1,0:T(8,128)} %rev.6.x_ref, bf16[64,6144]{1,0:T(8,128)(2,1)} %reshape_reshape.4.n_ref), custom_call_target="tpu_custom_call" | custom-call | tf_op jit(solution)/shard_map/pallas_call | solution.py:51
  23.7 0.9 %reshape.183 = f32[64,4,128]{2,1,0:T(4,128)S(1)} reshape(f32[64,512]{1,0:T(8,128)} %shard_map.46) | data formatting | bytes 262144 | tf_op jit(solution)/shard_map/reshape | solution.py:133
  24.8 0.7 %collective-permute-start.4 = (f32[64,128]{1,0:T(8,128)S(1)}, f32[64,128]{1,0:T(8,128)S(1)}, u32[]{:S(2)}, u32[]{:S(2)}) collective-permute-start(f32[64,128]{1,0:T(8,128)S(1)} %select_bitcast_fusion.3), channel_id=1, source_target_pairs={{0,4},{4,8},{8,12},{12,0},{1,5},{5,9},{9,13},{13,1},{2,6},{6,10},{... | collective-permute-start | bytes 98312 | tf_op jit(solution)/shard_map/ppermute | solution.py:136
  25.5 2.9 %collective-permute-start.5 = (f32[64,128]{1,0:T(8,128)S(1)}, f32[64,128]{1,0:T(8,128)S(1)}, u32[]{:S(2)}, u32[]{:S(2)}) collective-permute-start(f32[64,128]{1,0:T(8,128)S(1)} %select_bitcast_fusion.2), channel_id=1, source_target_pairs={{0,8},{4,12},{8,0},{12,4},{1,9},{5,13},{9,1},{13,5},{2,10},{6,14},... | collective-permute-start | bytes 98312 | tf_op jit(solution)/shard_map/ppermute | solution.py:136
  28.8 1.9 %collective-permute-done.4 = f32[64,128]{1,0:T(8,128)S(1)} collective-permute-done((f32[64,128]{1,0:T(8,128)S(1)}, f32[64,128]{1,0:T(8,128)S(1)}, u32[]{:S(2)}, u32[]{:S(2)}) %collective-permute-start.4) | collective-permute-done | bytes 32800 | tf_op jit(solution)/shard_map/ppermute | solution.py:136
  31.1 1.7 %collective-permute-done.6 = f32[64,128]{1,0:T(8,128)S(1)} collective-permute-done((f32[64,128]{1,0:T(8,128)S(1)}, f32[64,128]{1,0:T(8,128)S(1)}, u32[]{:S(2)}, u32[]{:S(2)}) %collective-permute-start.6) | collective-permute-done | bytes 32800 | tf_op jit(solution)/shard_map/ppermute | solution.py:136
  32.8 1.4 %collective-permute-start.7 = (f32[65,128]{1,0:T(8,128)S(1)}, f32[65,128]{1,0:T(8,128)S(1)}, u32[]{:S(2)}, u32[]{:S(2)}) collective-permute-start(f32[65,128]{1,0:T(8,128)S(1)} %pad_maximum_fusion.6), channel_id=1, source_target_pairs={{0,4},{4,8},{8,12},{12,0},{1,5},{5,9},{9,13},{13,1},{2,6},{6,10},{... | collective-permute-start | bytes 99848 | tf_op jit(solution)/shard_map/ppermute | solution.py:136
  34.2 1.3 %collective-permute-start.8 = (f32[65,128]{1,0:T(8,128)S(1)}, f32[65,128]{1,0:T(8,128)S(1)}, u32[]{:S(2)}, u32[]{:S(2)}) collective-permute-start(f32[65,128]{1,0:T(8,128)S(1)} %pad_maximum_fusion.6), channel_id=1, source_target_pairs={{0,8},{4,12},{8,0},{12,4},{1,9},{5,13},{9,1},{13,5},{2,10},{6,14},... | collective-permute-start | bytes 99848 | tf_op jit(solution)/shard_map/ppermute | solution.py:136
  35.5 1.2 %collective-permute-start.9 = (f32[65,128]{1,0:T(8,128)S(1)}, f32[65,128]{1,0:T(8,128)S(1)}, u32[]{:S(2)}, u32[]{:S(2)}) collective-permute-start(f32[65,128]{1,0:T(8,128)S(1)} %pad_maximum_fusion.6), channel_id=1, source_target_pairs={{0,12},{4,0},{8,4},{12,8},{1,13},{5,1},{9,5},{13,9},{2,14},{6,2},{... | collective-permute-start | bytes 99848 | tf_op jit(solution)/shard_map/ppermute | solution.py:136
  36.7 1.9 %collective-permute-done.7 = f32[65,128]{1,0:T(8,128)S(1)} collective-permute-done((f32[65,128]{1,0:T(8,128)S(1)}, f32[65,128]{1,0:T(8,128)S(1)}, u32[]{:S(2)}, u32[]{:S(2)}) %collective-permute-start.7) | collective-permute-done | bytes 33312 | tf_op jit(solution)/shard_map/ppermute | solution.py:136
  38.7 0.9 %collective-permute-done.8 = f32[65,128]{1,0:T(8,128)S(1)} collective-permute-done((f32[65,128]{1,0:T(8,128)S(1)}, f32[65,128]{1,0:T(8,128)S(1)}, u32[]{:S(2)}, u32[]{:S(2)}) %collective-permute-start.8) | collective-permute-done | bytes 33312 | tf_op jit(solution)/shard_map/ppermute | solution.py:136
  40.2 0.6 %gather_fusion = f32[4,64,128]{2,1,0:T(8,128)S(1)} fusion(f32[64,4,128]{2,0,1:T(8,128)S(1)} %pad_maximum_fusion, s32[1024]{0:T(1024)S(1)} %pad_clamp_fusion), kind=kCustom, calls=%fused_computation | custom fusion | bytes 262160 | tf_op jit(solution)/shard_map/jit(_take)/gather | solution.py:152
  41.1 2.3 %collective-permute-done.10 = f32[64]{0:T(128)S(1)} collective-permute-done((f32[64]{0:T(128)S(1)}, f32[64]{0:T(128)S(1)}, u32[]{:S(2)}, u32[]{:S(2)}) %collective-permute-start.10) | collective-permute-done | bytes 288 | tf_op jit(solution)/shard_map/ppermute | solution.py:61
  43.4 0.7 %broadcast_divide_fusion = f32[1,64,512]{2,1,0:T(8,128)} fusion(f32[1,64,512]{2,1,0:T(8,128)S(1)} %reshape.185, f32[64]{0:T(128)S(1)} %add_sqrt_fusion.1), kind=kLoop, calls=%fused_computation.11 | loop fusion | flops 32768 | bytes 262400 | tf_op jit(solution)/shard_map/div | solution.py:124
  (54 shorter events, 3.3 us)
Async XLA Ops:
  0.0 3.4 %copy-start = (bf16[1,64,4,3,512]{4,2,3,1,0:T(4,128)(2,1)S(1)}, bf16[1,64,4,3,512]{4,2,3,1,0:T(4,128)(2,1)}, u32[]{:S(2)}) copy-start(bf16[1,64,4,3,512]{4,2,3,1,0:T(4,128)(2,1)} %param.7) | copy-start | bytes 2359300
  0.0 3.2 %copy-start.2 = (s32[1,64,4,3]{1,2,3,0:T(4,128)S(1)}, s32[1,64,4,3]{1,2,3,0:T(4,128)}, u32[]{:S(2)}) copy-start(s32[1,64,4,3]{1,2,3,0:T(4,128)} %param.8) | copy-start | bytes 9220
  0.0 6.2 %collective-permute-start = (bf16[2,3,512]{2,0,1:T(2,128)(2,1)}, bf16[2,3,512]{2,0,1:T(2,128)(2,1)S(1)}, u32[]{:S(2)}, u32[]{:S(2)}) collective-permute-start(bf16[2,3,512]{2,0,1:T(2,128)(2,1)} %param.6), channel_id=1, source_target_pairs={{2,0},{3,1},{6,4},{7,5},{10,8},{11,9},{14,12},{15,13},{18,16},{19,... | collective-permute-start | bytes 18440 | tf_op jit(solution)/shard_map/ppermute | solution.py:77
  3.2 0.8 %copy-start.3 = (s32[2]{0:T(128)S(1)}, s32[2]{0:T(128)}, u32[]{:S(2)}) copy-start(s32[2]{0:T(128)} %param.9) | copy-start | bytes 28
  3.2 3.0 %copy-start.1 = (bf16[2,3,512]{2,0,1:T(2,128)(2,1)S(1)}, bf16[2,3,512]{2,0,1:T(2,128)(2,1)}, u32[]{:S(2)}) copy-start(bf16[2,3,512]{2,0,1:T(2,128)(2,1)} %param.6) | copy-start | bytes 18436
  6.3 9.3 %collective-permute-start.1 = (bf16[2,4,1024]{2,0,1:T(2,128)(2,1)S(1)}, bf16[2,4,1024]{2,0,1:T(2,128)(2,1)S(1)}, u32[]{:S(2)}, u32[]{:S(2)}) collective-permute-start(bf16[2,4,1024]{2,0,1:T(2,128)(2,1)S(1)} %pad_maximum_fusion.7), channel_id=1, source_target_pairs={{0,4},{4,8},{8,12},{12,0},{1,5},{5,9},{9,13},{13,1},{2,6},{6,10},{... | collective-permute-start | bytes 49160 | tf_op jit(solution)/shard_map/ppermute | solution.py:85
  9.0 6.5 %collective-permute-start.2 = (bf16[2,4,1024]{2,0,1:T(2,128)(2,1)S(1)}, bf16[2,4,1024]{2,0,1:T(2,128)(2,1)S(1)}, u32[]{:S(2)}, u32[]{:S(2)}) collective-permute-start(bf16[2,4,1024]{2,0,1:T(2,128)(2,1)S(1)} %pad_maximum_fusion.7), channel_id=1, source_target_pairs={{0,8},{4,12},{8,0},{12,4},{1,9},{5,13},{9,1},{13,5},{2,10},{6,14},... | collective-permute-start | bytes 49160 | tf_op jit(solution)/shard_map/ppermute | solution.py:85
  11.6 3.9 %collective-permute-start.3 = (bf16[2,4,1024]{2,0,1:T(2,128)(2,1)S(1)}, bf16[2,4,1024]{2,0,1:T(2,128)(2,1)S(1)}, u32[]{:S(2)}, u32[]{:S(2)}) collective-permute-start(bf16[2,4,1024]{2,0,1:T(2,128)(2,1)S(1)} %pad_maximum_fusion.7), channel_id=1, source_target_pairs={{0,12},{4,0},{8,4},{12,8},{1,13},{5,1},{9,5},{13,9},{2,14},{6,2},{... | collective-permute-start | bytes 49160 | tf_op jit(solution)/shard_map/ppermute | solution.py:85
  24.8 5.9 %collective-permute-start.4 = (f32[64,128]{1,0:T(8,128)S(1)}, f32[64,128]{1,0:T(8,128)S(1)}, u32[]{:S(2)}, u32[]{:S(2)}) collective-permute-start(f32[64,128]{1,0:T(8,128)S(1)} %select_bitcast_fusion.3), channel_id=1, source_target_pairs={{0,4},{4,8},{8,12},{12,0},{1,5},{5,9},{9,13},{13,1},{2,6},{6,10},{... | collective-permute-start | bytes 98312 | tf_op jit(solution)/shard_map/ppermute | solution.py:136
  25.5 5.5 %collective-permute-start.5 = (f32[64,128]{1,0:T(8,128)S(1)}, f32[64,128]{1,0:T(8,128)S(1)}, u32[]{:S(2)}, u32[]{:S(2)}) collective-permute-start(f32[64,128]{1,0:T(8,128)S(1)} %select_bitcast_fusion.2), channel_id=1, source_target_pairs={{0,8},{4,12},{8,0},{12,4},{1,9},{5,13},{9,1},{13,5},{2,10},{6,14},... | collective-permute-start | bytes 98312 | tf_op jit(solution)/shard_map/ppermute | solution.py:136
  28.4 4.3 %collective-permute-start.6 = (f32[64,128]{1,0:T(8,128)S(1)}, f32[64,128]{1,0:T(8,128)S(1)}, u32[]{:S(2)}, u32[]{:S(2)}) collective-permute-start(f32[64,128]{1,0:T(8,128)S(1)} %select_bitcast_fusion.1), channel_id=1, source_target_pairs={{0,12},{4,0},{8,4},{12,8},{1,13},{5,1},{9,5},{13,9},{2,14},{6,2},{... | collective-permute-start | bytes 98312 | tf_op jit(solution)/shard_map/ppermute | solution.py:136
  32.8 5.8 %collective-permute-start.7 = (f32[65,128]{1,0:T(8,128)S(1)}, f32[65,128]{1,0:T(8,128)S(1)}, u32[]{:S(2)}, u32[]{:S(2)}) collective-permute-start(f32[65,128]{1,0:T(8,128)S(1)} %pad_maximum_fusion.6), channel_id=1, source_target_pairs={{0,4},{4,8},{8,12},{12,0},{1,5},{5,9},{9,13},{13,1},{2,6},{6,10},{... | collective-permute-start | bytes 99848 | tf_op jit(solution)/shard_map/ppermute | solution.py:136
  34.2 5.3 %collective-permute-start.8 = (f32[65,128]{1,0:T(8,128)S(1)}, f32[65,128]{1,0:T(8,128)S(1)}, u32[]{:S(2)}, u32[]{:S(2)}) collective-permute-start(f32[65,128]{1,0:T(8,128)S(1)} %pad_maximum_fusion.6), channel_id=1, source_target_pairs={{0,8},{4,12},{8,0},{12,4},{1,9},{5,13},{9,1},{13,5},{2,10},{6,14},... | collective-permute-start | bytes 99848 | tf_op jit(solution)/shard_map/ppermute | solution.py:136
  35.5 4.3 %collective-permute-start.9 = (f32[65,128]{1,0:T(8,128)S(1)}, f32[65,128]{1,0:T(8,128)S(1)}, u32[]{:S(2)}, u32[]{:S(2)}) collective-permute-start(f32[65,128]{1,0:T(8,128)S(1)} %pad_maximum_fusion.6), channel_id=1, source_target_pairs={{0,12},{4,0},{8,4},{12,8},{1,13},{5,1},{9,5},{13,9},{2,14},{6,2},{... | collective-permute-start | bytes 99848 | tf_op jit(solution)/shard_map/ppermute | solution.py:136
  39.8 3.5 %collective-permute-start.10 = (f32[64]{0:T(128)S(1)}, f32[64]{0:T(128)S(1)}, u32[]{:S(2)}, u32[]{:S(2)}) collective-permute-start(f32[64]{0:T(128)S(1)} %fusion.14), channel_id=1, source_target_pairs={{0,2},{2,0},{1,3},{3,1},{4,6},{6,4},{5,7},{7,5},{8,10},{10,8},{9,1... | collective-permute-start | bytes 776 | tf_op jit(solution)/shard_map/ppermute | solution.py:61

commit v8 on v6

--- a/solution.py
+++ b/solution.py
@@ -6,7 +6,7 @@
 from jax.experimental.pallas import tpu as pltpu
 
 
-def hankel_kernel(x_ref, n_ref, fill_ref, o_ref, h_ref):
+def hankel_kernel(x_ref, n_ref, o_ref, h_ref):
     width = h_ref.shape[0]
     channels = n_ref.shape[1] // width
     taps_blocks = width // 128
@@ -35,7 +35,7 @@
         )
         start = pl.multiple_of(c * width, 128)
         part = jnp.dot(n_ref[:, pl.ds(start, width)], h_ref[...], preferred_element_type=jnp.float32)
-        return acc + part * (fill_ref[c] / jnp.sqrt(jnp.maximum(energy, 1.0)))
+        return acc + part * (1.0 / jnp.sqrt(jnp.maximum(energy, 1.0)))
 
     o_ref[...] = lax.fori_loop(0, channels, one_channel, jnp.zeros(o_ref.shape, jnp.float32))
 
@@ -45,32 +45,28 @@
     return stacked.reshape(rows, seg_len // 128, 128)[..., ::-1].reshape(rows, seg_len)
 
 
-def correlate(normed, flat_owned, filled, seg_len):
+def correlate(normed, flat_owned, seg_len):
     rows, channels, filter_taps = normed.shape
     blocks = flat_owned.reshape(channels * (flat_owned.shape[1] // 128), 128)[:, ::-1]
     return pl.pallas_call(
         hankel_kernel,
         out_shape=jax.ShapeDtypeStruct((rows, seg_len), jnp.float32),
-        in_specs=[
-            pl.BlockSpec(memory_space=pltpu.VMEM),
-            pl.BlockSpec(memory_space=pltpu.VMEM),
-            pl.BlockSpec(memory_space=pltpu.SMEM),
-        ],
         scratch_shapes=[pltpu.VMEM((filter_taps, seg_len), jnp.bfloat16)],
-    )(blocks.astype(jnp.float32), normed.reshape(rows, channels * filter_taps), filled)
+    )(blocks, normed.reshape(rows, channels * filter_taps))
 
 
 def ordered_sum(part, axis):
     size = lax.axis_size(axis)
+    if size & (size - 1) == 0:
+        step = 1
+        while step < size:
+            part = part + lax.ppermute(part, axis, [(i, i ^ step) for i in range(size)])
+            step *= 2
+        return part
+    me = lax.axis_index(axis)
     received = [part] + [
         lax.ppermute(part, axis, [(i, (i + k) % size) for i in range(size)]) for k in range(1, size)
     ]
-    if size & (size - 1) == 0:
-        while len(received) > 1:
-            half = len(received) // 2
-            received = [received[k] + received[k + half] for k in range(half)]
-        return received[0]
-    me = lax.axis_index(axis)
     order = (me - jnp.arange(size, dtype=jnp.int32)) % size
     return jnp.sum(jnp.take(jnp.stack(received), order, axis=0), axis=0)
 
@@ -114,6 +110,7 @@
     local_batches, kept, capacity, components, filter_taps = templates.shape
     seg_len = records.shape[2]
     owned_rows, filled = gather_owned(records, station_region, capacity, filter_taps)
+    owned_rows = owned_rows.astype(jnp.float32) * filled[:, None, None]
     flat_owned = owned_rows.reshape(capacity * components, seg_len + filter_taps)
     weight = channel_mask.astype(jnp.float32)
     widened_templates = templates.astype(jnp.float32)
@@ -123,8 +120,7 @@
     normed = (widened_templates * weight[..., None] / template_norm).astype(jnp.bfloat16)
     normed = normed.reshape(local_batches * kept, capacity * components, filter_taps)
     total_len = seg_len * lax.axis_size("seg")
-    filled_channels = jnp.repeat(filled, components)
-    stacked = ordered_sum(correlate(normed, flat_owned, filled_channels, seg_len), "region")
+    stacked = ordered_sum(correlate(normed, flat_owned, seg_len), "region")
     power_sum = ordered_sum(jnp.sum(stacked * stacked, axis=1), "seg")
     detect = unflip(stacked) / jnp.sqrt(power_sum / total_len + 1e-06)[:, None]
     return detect.reshape(local_batches, kept, seg_len)

time: 43.6 us -> 42.9 us (0.984)
  waiting for transfers between devices: 13.8 us -> 16.1 us
  starting transfers between devices: 12.7 us -> 10.4 us
  other arithmetic: 5.97 us -> 5.35 us
    ppermute x4 -> x3, starting transfers between devices: 5.48 us -> 3.17 us  [ordered_sum(): part = part + lax.ppermute(part, axis, [(i, i ^ step) for i in range(size)])]
    ppermute x4 -> x3, waiting for transfers between devices: 10.3 us -> 12.6 us  [ordered_sum(): part = part + lax.ppermute(part, axis, [(i, i ^ step) for i in range(size)])]
    reduce_sum x1, other arithmetic: 1.05 us -> 0.11 us  [per_device(): power_sum = ordered_sum(jnp.sum(stacked * stacked, axis=1), 'seg')]
    add x0 -> x1, other arithmetic: none -> 0.93 us  [ordered_sum(): part = part + lax.ppermute(part, axis, [(i, i ^ step) for i in range(size)])]
    reshape x1 -> x0, local copies, waits for them, and re-layouts: 0.66 us -> none  [per_device(): filled_channels = jnp.repeat(filled, components)]
    convert_element_type x1 -> x0, other arithmetic: 0.62 us -> none  [correlate(): blocks.astype(jnp.float32)]
    rev x1, local copies, waits for them, and re-layouts: 0.09 us -> 0.7 us  [correlate(): flat_owned.reshape(channels * (flat_owned.shape[1] // 128), 128)[:, ::-1]]
  transfers between devices with their start and end apart: 8 -> 7, of which waited for: 7 -> 6; matrix products, arithmetic and copies ran while one was open for 14% -> 14% of each run, Pallas kernels for 0% -> 0%
where the time goes in v8:
time: 42.9 us; the launch traced here: 42.6 us
  waiting for transfers between devices  16.1 us (38%)
  starting transfers between devices  10.4 us (24%)
  Pallas kernels  6.67 us (16%)
  other arithmetic  5.35 us (12%)
  local copies, waits for them, and re-layouts  3.8 us (9%)
    ppermute x3, waiting for transfers between devices, ordered_sum(): part = part + lax.ppermute(part, axis, [(i, i ^ step) for i in range(size)])  12.6 us
    pallas_call x1, Pallas kernels, correlate(): pl.pallas_call(hankel_kernel, out_shape=jax.ShapeDtypeStruct((rows, seg_l...  6.67 us
    ppermute x3, starting transfers between devices, gather_owned(): lax.ppermute(payload, 'region', [(r, (r + k) % regions) for r in range(re...  5.82 us
    ppermute x3, starting transfers between devices, ordered_sum(): part = part + lax.ppermute(part, axis, [(i, i ^ step) for i in range(size)])  3.17 us
    ppermute x3, waiting for transfers between devices, gather_owned(): lax.ppermute(payload, 'region', [(r, (r + k) % regions) for r in range(re...  1.97 us
    another operation x1, local copies, waits for them, and re-layouts, correlate(): normed.reshape(rows, channels * filter_taps)  1.84 us
    reduce_sum x1, other arithmetic, per_device(): jnp.sum(widened_templates * widened_templates, axis=4, keepdims=True)  1.65 us
    ppermute x1, waiting for transfers between devices, gather_owned(): lax.ppermute(records[:, :, :filter_taps], 'seg', [(s + 1, s) for s in ran...  1.55 us
  transfers between devices with their start and end apart: 7, of which 6 were waited for; matrix products, arithmetic and copies ran while one was open for 14% of the time, Pallas kernels for 0%

profile of v8, /device:TPU:0, one launch (start us, length us, event | category | flops | bytes accessed | tf_op | source)
XLA Modules:
  0.0 42.6 jit_solution(1674175071255867480)
XLA Ops:
  0.0 1.4 %collective-permute-start = (bf16[2,3,512]{2,0,1:T(2,128)(2,1)}, bf16[2,3,512]{2,0,1:T(2,128)(2,1)S(1)}, u32[]{:S(2)}, u32[]{:S(2)}) collective-permute-start(bf16[2,3,512]{2,0,1:T(2,128)(2,1)} %param.4), channel_id=1, source_target_pairs={{2,0},{3,1},{6,4},{7,5},{10,8},{11,9},{14,12},{15,13},{18,16},{19,... | collective-permute-start | bytes 18440 | tf_op jit(solution)/shard_map/ppermute | solution.py:78
  1.4 0.7 %convert_bitcast_fusion = f32[64,4,3]{0,1,2:T(4,128)S(1)} fusion(s32[1,64,4,3]{1,2,3,0:T(4,128)} %param.6), kind=kLoop, calls=%fused_computation.16 | loop fusion | flops 768 | bytes 6144 | tf_op jit(solution)/shard_map/mul | solution.py:120
  2.3 1.7 %fusion.3 = f32[64,4,3]{1,2,0:T(4,128)S(1)} fusion(bf16[1,64,4,3,512]{4,2,3,1,0:T(4,128)(2,1)} %param.5), kind=kLoop, calls=%fused_computation.6 | loop fusion | flops 1178880 | bytes 789504 | tf_op jit(solution)/shard_map/reduce_sum | solution.py:118
  4.0 0.5 %fusion.2 = bf16[1,64,4,3,512]{4,2,3,1,0:T(4,128)(2,1)S(1)} fusion(bf16[1,64,4,3,512]{4,2,3,1,0:T(4,128)(2,1)S(1)} %copy-done, f32[64,4,3]{1,2,0:T(4,128)S(1)} %add_sqrt_fusion, f32[64,4,3]{1,2,0:T(4,128)S(1)} %copy.9), kind=kLoop, calls=%fused_computation.5 | loop fusion | flops 1572864 | bytes 1579008 | tf_op jit(solution)/shard_map/convert_element_type | solution.py:120
  4.6 1.6 %collective-permute-done = bf16[2,3,512]{2,0,1:T(2,128)(2,1)S(1)} collective-permute-done((bf16[2,3,512]{2,0,1:T(2,128)(2,1)}, bf16[2,3,512]{2,0,1:T(2,128)(2,1)S(1)}, u32[]{:S(2)}, u32[]{:S(2)}) %collective-permute-start) | collective-permute-done | bytes 6176 | tf_op jit(solution)/shard_map/ppermute | solution.py:78
  6.3 4.8 %collective-permute-start.3 = (bf16[2,4,1024]{2,0,1:T(2,128)(2,1)S(1)}, bf16[2,4,1024]{2,0,1:T(2,128)(2,1)S(1)}, u32[]{:S(2)}, u32[]{:S(2)}) collective-permute-start(bf16[2,4,1024]{2,0,1:T(2,128)(2,1)S(1)} %pad_maximum_fusion.5), channel_id=1, source_target_pairs={{0,12},{4,0},{8,4},{12,8},{1,13},{5,1},{9,5},{13,9},{2,14},{6,2},{... | collective-permute-start | bytes 49160 | tf_op jit(solution)/shard_map/ppermute | solution.py:86
  11.1 1.0 %collective-permute-start.1 = (bf16[2,4,1024]{2,0,1:T(2,128)(2,1)S(1)}, bf16[2,4,1024]{2,0,1:T(2,128)(2,1)S(1)}, u32[]{:S(2)}, u32[]{:S(2)}) collective-permute-start(bf16[2,4,1024]{2,0,1:T(2,128)(2,1)S(1)} %pad_maximum_fusion.5), channel_id=1, source_target_pairs={{0,4},{4,8},{8,12},{12,0},{1,5},{5,9},{9,13},{13,1},{2,6},{6,10},{... | collective-permute-start | bytes 49160 | tf_op jit(solution)/shard_map/ppermute | solution.py:86
  12.2 0.6 %copy.10 = bf16[1,64,4,3,512]{4,3,2,1,0:T(4,128)(2,1)S(1)} copy(bf16[1,64,4,3,512]{4,2,3,1,0:T(4,128)(2,1)S(1)} %fusion.2) | data formatting | bytes 1572864 | tf_op jit(solution)/shard_map/convert_element_type | solution.py:120
  12.8 1.8 %reshape_reshape.4.n_ref = bf16[64,6144]{1,0:T(8,128)(2,1)} reshape(bf16[1,64,4,3,512]{4,3,2,1,0:T(4,128)(2,1)S(1)} %copy.10) | data formatting | bytes 1572864 | tf_op jit(solution)/shard_map/reshape;reshape | solution.py:55
  14.6 1.1 %collective-permute-done.2 = bf16[2,4,1024]{2,0,1:T(2,128)(2,1)S(1)} collective-permute-done((bf16[2,4,1024]{2,0,1:T(2,128)(2,1)S(1)}, bf16[2,4,1024]{2,0,1:T(2,128)(2,1)S(1)}, u32[]{:S(2)}, u32[]{:S(2)}) %collective-permute-start.2) | collective-permute-done | bytes 16416 | tf_op jit(solution)/shard_map/ppermute | solution.py:86
  15.7 0.9 %collective-permute-done.1 = bf16[2,4,1024]{2,0,1:T(2,128)(2,1)S(1)} collective-permute-done((bf16[2,4,1024]{2,0,1:T(2,128)(2,1)S(1)}, bf16[2,4,1024]{2,0,1:T(2,128)(2,1)S(1)}, u32[]{:S(2)}, u32[]{:S(2)}) %collective-permute-start.1) | collective-permute-done | bytes 16416 | tf_op jit(solution)/shard_map/ppermute | solution.py:86
  16.7 0.2 convert_reduce_fusion.1
  17.1 0.1 fusion
  17.4 0.7 %rev.6.x_ref = f32[96,128]{1,0:T(8,128)} reverse(f32[96,128]{1,0:T(8,128)S(1)} %mul.38), dimensions={1} | reverse | bytes 98304 | tf_op jit(solution)/shard_map/rev | solution.py:50
  18.1 6.7 %shard_map.46 = f32[64,512]{1,0:T(8,128)} custom-call(f32[96,128]{1,0:T(8,128)} %rev.6.x_ref, bf16[64,6144]{1,0:T(8,128)(2,1)} %reshape_reshape.4.n_ref), custom_call_target="tpu_custom_call" | custom-call | tf_op jit(solution)/shard_map/pallas_call | solution.py:51
  24.8 0.5 %collective-permute-start.4 = (f32[64,512]{1,0:T(8,128)}, f32[64,512]{1,0:T(8,128)S(1)}, u32[]{:S(2)}, u32[]{:S(2)}) collective-permute-start(f32[64,512]{1,0:T(8,128)} %shard_map.46), channel_id=1, source_target_pairs={{0,4},{4,0},{8,12},{12,8},{1,5},{5,1},{9,13},{13,9},{2,6},{6,2},{1... | collective-permute-start | bytes 393224 | tf_op jit(solution)/shard_map/ppermute | solution.py:63
  25.3 4.7 %collective-permute-done.4 = f32[64,512]{1,0:T(8,128)S(1)} collective-permute-done((f32[64,512]{1,0:T(8,128)}, f32[64,512]{1,0:T(8,128)S(1)}, u32[]{:S(2)}, u32[]{:S(2)}) %collective-permute-start.4) | collective-permute-done | bytes 131104 | tf_op jit(solution)/shard_map/ppermute | solution.py:63
  29.9 0.9 %add.68 = f32[64,512]{1,0:T(8,128)S(1)} add(f32[64,512]{1,0:T(8,128)} %shard_map.46, f32[64,512]{1,0:T(8,128)S(1)} %collective-permute-done.4) | non-fusion elementwise | flops 32768 | bytes 393216 | tf_op jit(solution)/shard_map/add | solution.py:63
  30.9 1.2 %collective-permute-start.5 = (f32[64,512]{1,0:T(8,128)S(1)}, f32[64,512]{1,0:T(8,128)S(1)}, u32[]{:S(2)}, u32[]{:S(2)}) collective-permute-start(f32[64,512]{1,0:T(8,128)S(1)} %add.68), channel_id=1, source_target_pairs={{0,8},{4,12},{8,0},{12,4},{1,9},{5,13},{9,1},{13,5},{2,10},{6,14},... | collective-permute-start | bytes 393224 | tf_op jit(solution)/shard_map/ppermute | solution.py:63
  32.1 6.1 %collective-permute-done.5 = f32[64,512]{1,0:T(8,128)S(1)} collective-permute-done((f32[64,512]{1,0:T(8,128)S(1)}, f32[64,512]{1,0:T(8,128)S(1)}, u32[]{:S(2)}, u32[]{:S(2)}) %collective-permute-start.5) | collective-permute-done | bytes 131104 | tf_op jit(solution)/shard_map/ppermute | solution.py:63
  38.3 1.5 %collective-permute-start.6 = (f32[64]{0:T(128)S(1)}, f32[64]{0:T(128)S(1)}, u32[]{:S(2)}, u32[]{:S(2)}) collective-permute-start(f32[64]{0:T(128)S(1)} %get-tuple-element.5), channel_id=1, source_target_pairs={{0,2},{2,0},{1,3},{3,1},{4,6},{6,4},{5,7},{7,5},{8,10},{10,8},{9,1... | collective-permute-start | bytes 776 | tf_op jit(solution)/shard_map/ppermute | solution.py:63
  39.8 0.2 rev.7
  40.0 1.9 %collective-permute-done.6 = f32[64]{0:T(128)S(1)} collective-permute-done((f32[64]{0:T(128)S(1)}, f32[64]{0:T(128)S(1)}, u32[]{:S(2)}, u32[]{:S(2)}) %collective-permute-start.6) | collective-permute-done | bytes 288 | tf_op jit(solution)/shard_map/ppermute | solution.py:63
  41.9 0.7 %broadcast_divide_fusion = f32[1,64,512]{2,1,0:T(8,128)} fusion(f32[1,64,512]{2,1,0:T(8,128)S(1)} %reshape.132, f32[64]{0:T(128)S(1)} %add_sqrt_fusion.1), kind=kLoop, calls=%fused_computation.9 | loop fusion | flops 32768 | bytes 262400 | tf_op jit(solution)/shard_map/div | solution.py:125
  (28 shorter events, 1.2 us)
Async XLA Ops:
  0.0 4.0 %copy-start = (bf16[1,64,4,3,512]{4,2,3,1,0:T(4,128)(2,1)S(1)}, bf16[1,64,4,3,512]{4,2,3,1,0:T(4,128)(2,1)}, u32[]{:S(2)}) copy-start(bf16[1,64,4,3,512]{4,2,3,1,0:T(4,128)(2,1)} %param.5) | copy-start | bytes 2359300
  0.0 6.2 %collective-permute-start = (bf16[2,3,512]{2,0,1:T(2,128)(2,1)}, bf16[2,3,512]{2,0,1:T(2,128)(2,1)S(1)}, u32[]{:S(2)}, u32[]{:S(2)}) collective-permute-start(bf16[2,3,512]{2,0,1:T(2,128)(2,1)} %param.4), channel_id=1, source_target_pairs={{2,0},{3,1},{6,4},{7,5},{10,8},{11,9},{14,12},{15,13},{18,16},{19,... | collective-permute-start | bytes 18440 | tf_op jit(solution)/shard_map/ppermute | solution.py:78
  3.9 0.7 %copy-start.2 = (s32[2]{0:T(128)S(1)}, s32[2]{0:T(128)}, u32[]{:S(2)}) copy-start(s32[2]{0:T(128)} %param.7) | copy-start | bytes 28
  3.9 2.3 %copy-start.1 = (bf16[2,3,512]{2,0,1:T(2,128)(2,1)S(1)}, bf16[2,3,512]{2,0,1:T(2,128)(2,1)}, u32[]{:S(2)}) copy-start(bf16[2,3,512]{2,0,1:T(2,128)(2,1)} %param.4) | copy-start | bytes 18436
  6.3 8.4 %collective-permute-start.3 = (bf16[2,4,1024]{2,0,1:T(2,128)(2,1)S(1)}, bf16[2,4,1024]{2,0,1:T(2,128)(2,1)S(1)}, u32[]{:S(2)}, u32[]{:S(2)}) collective-permute-start(bf16[2,4,1024]{2,0,1:T(2,128)(2,1)S(1)} %pad_maximum_fusion.5), channel_id=1, source_target_pairs={{0,12},{4,0},{8,4},{12,8},{1,13},{5,1},{9,5},{13,9},{2,14},{6,2},{... | collective-permute-start | bytes 49160 | tf_op jit(solution)/shard_map/ppermute | solution.py:86
  11.1 4.6 %collective-permute-start.2 = (bf16[2,4,1024]{2,0,1:T(2,128)(2,1)S(1)}, bf16[2,4,1024]{2,0,1:T(2,128)(2,1)S(1)}, u32[]{:S(2)}, u32[]{:S(2)}) collective-permute-start(bf16[2,4,1024]{2,0,1:T(2,128)(2,1)S(1)} %pad_maximum_fusion.5), channel_id=1, source_target_pairs={{0,8},{4,12},{8,0},{12,4},{1,9},{5,13},{9,1},{13,5},{2,10},{6,14},... | collective-permute-start | bytes 49160 | tf_op jit(solution)/shard_map/ppermute | solution.py:86
  11.1 5.5 %collective-permute-start.1 = (bf16[2,4,1024]{2,0,1:T(2,128)(2,1)S(1)}, bf16[2,4,1024]{2,0,1:T(2,128)(2,1)S(1)}, u32[]{:S(2)}, u32[]{:S(2)}) collective-permute-start(bf16[2,4,1024]{2,0,1:T(2,128)(2,1)S(1)} %pad_maximum_fusion.5), channel_id=1, source_target_pairs={{0,4},{4,8},{8,12},{12,0},{1,5},{5,9},{9,13},{13,1},{2,6},{6,10},{... | collective-permute-start | bytes 49160 | tf_op jit(solution)/shard_map/ppermute | solution.py:86
  24.8 5.2 %collective-permute-start.4 = (f32[64,512]{1,0:T(8,128)}, f32[64,512]{1,0:T(8,128)S(1)}, u32[]{:S(2)}, u32[]{:S(2)}) collective-permute-start(f32[64,512]{1,0:T(8,128)} %shard_map.46), channel_id=1, source_target_pairs={{0,4},{4,0},{8,12},{12,8},{1,5},{5,1},{9,13},{13,9},{2,6},{6,2},{1... | collective-permute-start | bytes 393224 | tf_op jit(solution)/shard_map/ppermute | solution.py:63
  30.9 7.3 %collective-permute-start.5 = (f32[64,512]{1,0:T(8,128)S(1)}, f32[64,512]{1,0:T(8,128)S(1)}, u32[]{:S(2)}, u32[]{:S(2)}) collective-permute-start(f32[64,512]{1,0:T(8,128)S(1)} %add.68), channel_id=1, source_target_pairs={{0,8},{4,12},{8,0},{12,4},{1,9},{5,13},{9,1},{13,5},{2,10},{6,14},... | collective-permute-start | bytes 393224 | tf_op jit(solution)/shard_map/ppermute | solution.py:63
  38.3 3.6 %collective-permute-start.6 = (f32[64]{0:T(128)S(1)}, f32[64]{0:T(128)S(1)}, u32[]{:S(2)}, u32[]{:S(2)}) collective-permute-start(f32[64]{0:T(128)S(1)} %get-tuple-element.5), channel_id=1, source_target_pairs={{0,2},{2,0},{1,3},{3,1},{4,6},{6,4},{5,7},{7,5},{8,10},{10,8},{9,1... | collective-permute-start | bytes 776 | tf_op jit(solution)/shard_map/ppermute | solution.py:63

commit v9 on v8

--- a/solution.py
+++ b/solution.py
@@ -82,16 +82,25 @@
     payload = jnp.concatenate(
         [jnp.concatenate([records, ahead], axis=2), tag], axis=1
     )
-    gathered = [payload] + [
-        lax.ppermute(payload, "region", [(r, (r + k) % regions) for r in range(regions)])
-        for k in range(1, regions)
-    ]
     me = lax.axis_index("region")
     stations = regions * local_count
-    shift = jnp.arange(regions, dtype=jnp.int32)[:, None]
+    if regions & (regions - 1) == 0:
+        here = payload
+        step = 1
+        while step < regions:
+            theirs = lax.ppermute(here, "region", [(r, r ^ step) for r in range(regions)])
+            here = jnp.concatenate([here, theirs], axis=0)
+            step *= 2
+        source = me ^ jnp.arange(regions, dtype=jnp.int32)[:, None]
+    else:
+        gathered = [payload] + [
+            lax.ppermute(payload, "region", [(r, (r + k) % regions) for r in range(regions)])
+            for k in range(1, regions)
+        ]
+        here = jnp.concatenate(gathered, axis=0)
+        source = (me - jnp.arange(regions, dtype=jnp.int32)[:, None]) % regions
     local = jnp.arange(local_count, dtype=jnp.int32)[None, :]
-    station_ids = (((me - shift) % regions) * local_count + local).reshape(stations)
-    here = jnp.concatenate(gathered, axis=0)
+    station_ids = (source * local_count + local).reshape(stations)
     region_of = here[:, components, 0].astype(jnp.int32)
     rows = here[:, :components, :]
     earlier = (region_of[None, :] == region_of[:, None]) & (station_ids[None, :] < station_ids[:, None])

time: 42.9 us -> 42.2 us (0.984)
  waiting for transfers between devices: 16.1 us -> 11.6 us
  starting transfers between devices: 10.4 us -> 14.1 us
    ppermute x3, waiting for transfers between devices: 12.6 us -> 8.35 us  [ordered_sum(): part = part + lax.ppermute(part, axis, [(i, i ^ step) for i in range(size)])]
    ppermute x3, starting transfers between devices: 3.17 us -> 6.81 us  [ordered_sum(): part = part + lax.ppermute(part, axis, [(i, i ^ step) for i in range(size)])]
    ppermute x3 -> x2, waiting for transfers between devices: 1.97 us -> 1.72 us  [gather_owned(): lax.ppermute(here, 'region', [(r, r ^ step) for r in range(regions)])]
    ppermute x3 -> x2, starting transfers between devices: 5.82 us -> 5.89 us  [gather_owned(): lax.ppermute(here, 'region', [(r, r ^ step) for r in range(regions)])]
  transfers between devices with their start and end apart: 7 -> 6, of which waited for: 6 -> 5; matrix products, arithmetic and copies ran while one was open for 14% -> 14% of each run, Pallas kernels for 0% -> 0%
where the time goes in v9:
time: 42.2 us; the launch traced here: 41.9 us
  starting transfers between devices  14.1 us (33%)
  waiting for transfers between devices  11.6 us (27%)
  Pallas kernels  6.68 us (16%)
  other arithmetic  5.37 us (13%)
  local copies, waits for them, and re-layouts  3.81 us (9%)
    ppermute x3, waiting for transfers between devices, ordered_sum(): part = part + lax.ppermute(part, axis, [(i, i ^ step) for i in range(size)])  8.35 us
    ppermute x3, starting transfers between devices, ordered_sum(): part = part + lax.ppermute(part, axis, [(i, i ^ step) for i in range(size)])  6.81 us
    pallas_call x1, Pallas kernels, correlate(): pl.pallas_call(hankel_kernel, out_shape=jax.ShapeDtypeStruct((rows, seg_l...  6.68 us
    ppermute x2, starting transfers between devices, gather_owned(): lax.ppermute(here, 'region', [(r, r ^ step) for r in range(regions)])  5.89 us
    another operation x1, local copies, waits for them, and re-layouts, correlate(): normed.reshape(rows, channels * filter_taps)  1.84 us
    ppermute x2, waiting for transfers between devices, gather_owned(): lax.ppermute(here, 'region', [(r, r ^ step) for r in range(regions)])  1.72 us
    reduce_sum x1, other arithmetic, per_device(): jnp.sum(widened_templates * widened_templates, axis=4, keepdims=True)  1.65 us
    ppermute x1, waiting for transfers between devices, gather_owned(): lax.ppermute(records[:, :, :filter_taps], 'seg', [(s + 1, s) for s in ran...  1.57 us
  transfers between devices with their start and end apart: 6, of which 5 were waited for; matrix products, arithmetic and copies ran while one was open for 14% of the time, Pallas kernels for 0%

profile of v9, /device:TPU:0, one launch (start us, length us, event | category | flops | bytes accessed | tf_op | source)
XLA Modules:
  0.0 41.9 jit_solution(16318043293682208198)
XLA Ops:
  0.0 1.4 %collective-permute-start = (bf16[2,3,512]{2,0,1:T(2,128)(2,1)}, bf16[2,3,512]{2,0,1:T(2,128)(2,1)S(1)}, u32[]{:S(2)}, u32[]{:S(2)}) collective-permute-start(bf16[2,3,512]{2,0,1:T(2,128)(2,1)} %param.4), channel_id=1, source_target_pairs={{2,0},{3,1},{6,4},{7,5},{10,8},{11,9},{14,12},{15,13},{18,16},{19,... | collective-permute-start | bytes 18440 | tf_op jit(solution)/shard_map/ppermute | solution.py:78
  1.4 0.7 %convert_bitcast_fusion = f32[64,4,3]{0,1,2:T(4,128)S(1)} fusion(s32[1,64,4,3]{1,2,3,0:T(4,128)} %param.6), kind=kLoop, calls=%fused_computation.16 | loop fusion | flops 768 | bytes 6144 | tf_op jit(solution)/shard_map/mul | solution.py:129
  2.1 0.1 copy.9
  2.3 1.7 %fusion.3 = f32[64,4,3]{1,2,0:T(4,128)S(1)} fusion(bf16[1,64,4,3,512]{4,2,3,1,0:T(4,128)(2,1)} %param.5), kind=kLoop, calls=%fused_computation.6 | loop fusion | flops 1178880 | bytes 789504 | tf_op jit(solution)/shard_map/reduce_sum | solution.py:127
  4.0 0.5 %fusion.2 = bf16[1,64,4,3,512]{4,2,3,1,0:T(4,128)(2,1)S(1)} fusion(bf16[1,64,4,3,512]{4,2,3,1,0:T(4,128)(2,1)S(1)} %copy-done, f32[64,4,3]{1,2,0:T(4,128)S(1)} %add_sqrt_fusion, f32[64,4,3]{1,2,0:T(4,128)S(1)} %copy.9), kind=kLoop, calls=%fused_computation.5 | loop fusion | flops 1572864 | bytes 1579008 | tf_op jit(solution)/shard_map/convert_element_type | solution.py:129
  4.6 1.6 %collective-permute-done = bf16[2,3,512]{2,0,1:T(2,128)(2,1)S(1)} collective-permute-done((bf16[2,3,512]{2,0,1:T(2,128)(2,1)}, bf16[2,3,512]{2,0,1:T(2,128)(2,1)S(1)}, u32[]{:S(2)}, u32[]{:S(2)}) %collective-permute-start) | collective-permute-done | bytes 6176 | tf_op jit(solution)/shard_map/ppermute | solution.py:78
  6.3 2.8 %collective-permute-start.1 = (bf16[2,4,1024]{2,0,1:T(2,128)(2,1)S(1)}, bf16[2,4,1024]{2,0,1:T(2,128)(2,1)S(1)}, u32[]{:S(2)}, u32[]{:S(2)}) collective-permute-start(bf16[2,4,1024]{2,0,1:T(2,128)(2,1)S(1)} %pad_maximum_fusion.5), channel_id=1, source_target_pairs={{0,4},{4,0},{8,12},{12,8},{1,5},{5,1},{9,13},{13,9},{2,6},{6,2},{1... | collective-permute-start | bytes 49160 | tf_op jit(solution)/shard_map/ppermute | solution.py:91
  9.1 1.7 %collective-permute-done.1 = bf16[2,4,1024]{2,0,1:T(2,128)(2,1)S(1)} collective-permute-done((bf16[2,4,1024]{2,0,1:T(2,128)(2,1)S(1)}, bf16[2,4,1024]{2,0,1:T(2,128)(2,1)S(1)}, u32[]{:S(2)}, u32[]{:S(2)}) %collective-permute-start.1) | collective-permute-done | bytes 16416 | tf_op jit(solution)/shard_map/ppermute | solution.py:91
  10.8 3.1 %collective-permute-start.2 = (bf16[4,4,1024]{2,0,1:T(4,128)(2,1)S(1)}, bf16[4,4,1024]{2,0,1:T(4,128)(2,1)S(1)}, u32[]{:S(2)}, u32[]{:S(2)}) collective-permute-start(bf16[4,4,1024]{2,0,1:T(4,128)(2,1)S(1)} %pad_maximum_fusion.4), channel_id=1, source_target_pairs={{0,8},{4,12},{8,0},{12,4},{1,9},{5,13},{9,1},{13,5},{2,10},{6,14},... | collective-permute-start | bytes 98312 | tf_op jit(solution)/shard_map/ppermute | solution.py:91
  14.1 0.6 %copy.10 = bf16[1,64,4,3,512]{4,3,2,1,0:T(4,128)(2,1)S(1)} copy(bf16[1,64,4,3,512]{4,2,3,1,0:T(4,128)(2,1)S(1)} %fusion.2) | data formatting | bytes 1572864 | tf_op jit(solution)/shard_map/convert_element_type | solution.py:129
  14.6 1.8 %reshape_reshape.4.n_ref = bf16[64,6144]{1,0:T(8,128)(2,1)} reshape(bf16[1,64,4,3,512]{4,3,2,1,0:T(4,128)(2,1)S(1)} %copy.10) | data formatting | bytes 1572864 | tf_op jit(solution)/shard_map/reshape;reshape | solution.py:55
  16.6 0.2 convert_reduce_fusion.1
  17.0 0.1 fusion
  17.2 0.7 %rev.6.x_ref = f32[96,128]{1,0:T(8,128)} reverse(f32[96,128]{1,0:T(8,128)S(1)} %mul.38), dimensions={1} | reverse | bytes 98304 | tf_op jit(solution)/shard_map/rev | solution.py:50
  17.9 6.7 %shard_map.46 = f32[64,512]{1,0:T(8,128)} custom-call(f32[96,128]{1,0:T(8,128)} %rev.6.x_ref, bf16[64,6144]{1,0:T(8,128)(2,1)} %reshape_reshape.4.n_ref), custom_call_target="tpu_custom_call" | custom-call | tf_op jit(solution)/shard_map/pallas_call | solution.py:51
  24.6 1.6 %collective-permute-start.3 = (f32[64,512]{1,0:T(8,128)}, f32[64,512]{1,0:T(8,128)S(1)}, u32[]{:S(2)}, u32[]{:S(2)}) collective-permute-start(f32[64,512]{1,0:T(8,128)} %shard_map.46), channel_id=1, source_target_pairs={{0,4},{4,0},{8,12},{12,8},{1,5},{5,1},{9,13},{13,9},{2,6},{6,2},{1... | collective-permute-start | bytes 393224 | tf_op jit(solution)/shard_map/ppermute | solution.py:63
  26.2 3.6 %collective-permute-done.3 = f32[64,512]{1,0:T(8,128)S(1)} collective-permute-done((f32[64,512]{1,0:T(8,128)}, f32[64,512]{1,0:T(8,128)S(1)}, u32[]{:S(2)}, u32[]{:S(2)}) %collective-permute-start.3) | collective-permute-done | bytes 131104 | tf_op jit(solution)/shard_map/ppermute | solution.py:63
  29.8 0.9 %add.56 = f32[64,512]{1,0:T(8,128)S(1)} add(f32[64,512]{1,0:T(8,128)} %shard_map.46, f32[64,512]{1,0:T(8,128)S(1)} %collective-permute-done.3) | non-fusion elementwise | flops 32768 | bytes 393216 | tf_op jit(solution)/shard_map/add | solution.py:63
  30.7 2.4 %collective-permute-start.4 = (f32[64,512]{1,0:T(8,128)S(1)}, f32[64,512]{1,0:T(8,128)S(1)}, u32[]{:S(2)}, u32[]{:S(2)}) collective-permute-start(f32[64,512]{1,0:T(8,128)S(1)} %add.56), channel_id=1, source_target_pairs={{0,8},{4,12},{8,0},{12,4},{1,9},{5,13},{9,1},{13,5},{2,10},{6,14},... | collective-permute-start | bytes 393224 | tf_op jit(solution)/shard_map/ppermute | solution.py:63
  33.1 3.5 %collective-permute-done.4 = f32[64,512]{1,0:T(8,128)S(1)} collective-permute-done((f32[64,512]{1,0:T(8,128)S(1)}, f32[64,512]{1,0:T(8,128)S(1)}, u32[]{:S(2)}, u32[]{:S(2)}) %collective-permute-start.4) | collective-permute-done | bytes 131104 | tf_op jit(solution)/shard_map/ppermute | solution.py:63
  36.8 2.8 %collective-permute-start.5 = (f32[64]{0:T(128)S(1)}, f32[64]{0:T(128)S(1)}, u32[]{:S(2)}, u32[]{:S(2)}) collective-permute-start(f32[64]{0:T(128)S(1)} %get-tuple-element.5), channel_id=1, source_target_pairs={{0,2},{2,0},{1,3},{3,1},{4,6},{6,4},{5,7},{7,5},{8,10},{10,8},{9,1... | collective-permute-start | bytes 776 | tf_op jit(solution)/shard_map/ppermute | solution.py:63
  39.7 0.2 rev.7
  39.9 1.2 %collective-permute-done.5 = f32[64]{0:T(128)S(1)} collective-permute-done((f32[64]{0:T(128)S(1)}, f32[64]{0:T(128)S(1)}, u32[]{:S(2)}, u32[]{:S(2)}) %collective-permute-start.5) | collective-permute-done | bytes 288 | tf_op jit(solution)/shard_map/ppermute | solution.py:63
  41.1 0.7 %broadcast_divide_fusion = f32[1,64,512]{2,1,0:T(8,128)} fusion(f32[1,64,512]{2,1,0:T(8,128)S(1)} %reshape.115, f32[64]{0:T(128)S(1)} %add_sqrt_fusion.1), kind=kLoop, calls=%fused_computation.9 | loop fusion | flops 32768 | bytes 262400 | tf_op jit(solution)/shard_map/div | solution.py:134
  (27 shorter events, 1.1 us)
Async XLA Ops:
  0.0 4.0 %copy-start = (bf16[1,64,4,3,512]{4,2,3,1,0:T(4,128)(2,1)S(1)}, bf16[1,64,4,3,512]{4,2,3,1,0:T(4,128)(2,1)}, u32[]{:S(2)}) copy-start(bf16[1,64,4,3,512]{4,2,3,1,0:T(4,128)(2,1)} %param.5) | copy-start | bytes 2359300
  0.0 6.2 %collective-permute-start = (bf16[2,3,512]{2,0,1:T(2,128)(2,1)}, bf16[2,3,512]{2,0,1:T(2,128)(2,1)S(1)}, u32[]{:S(2)}, u32[]{:S(2)}) collective-permute-start(bf16[2,3,512]{2,0,1:T(2,128)(2,1)} %param.4), channel_id=1, source_target_pairs={{2,0},{3,1},{6,4},{7,5},{10,8},{11,9},{14,12},{15,13},{18,16},{19,... | collective-permute-start | bytes 18440 | tf_op jit(solution)/shard_map/ppermute | solution.py:78
  3.9 0.7 %copy-start.2 = (s32[2]{0:T(128)S(1)}, s32[2]{0:T(128)}, u32[]{:S(2)}) copy-start(s32[2]{0:T(128)} %param.7) | copy-start | bytes 28
  3.9 2.3 %copy-start.1 = (bf16[2,3,512]{2,0,1:T(2,128)(2,1)S(1)}, bf16[2,3,512]{2,0,1:T(2,128)(2,1)}, u32[]{:S(2)}) copy-start(bf16[2,3,512]{2,0,1:T(2,128)(2,1)} %param.4) | copy-start | bytes 18436
  6.3 4.5 %collective-permute-start.1 = (bf16[2,4,1024]{2,0,1:T(2,128)(2,1)S(1)}, bf16[2,4,1024]{2,0,1:T(2,128)(2,1)S(1)}, u32[]{:S(2)}, u32[]{:S(2)}) collective-permute-start(bf16[2,4,1024]{2,0,1:T(2,128)(2,1)S(1)} %pad_maximum_fusion.5), channel_id=1, source_target_pairs={{0,4},{4,0},{8,12},{12,8},{1,5},{5,1},{9,13},{13,9},{2,6},{6,2},{1... | collective-permute-start | bytes 49160 | tf_op jit(solution)/shard_map/ppermute | solution.py:91
  10.8 5.7 %collective-permute-start.2 = (bf16[4,4,1024]{2,0,1:T(4,128)(2,1)S(1)}, bf16[4,4,1024]{2,0,1:T(4,128)(2,1)S(1)}, u32[]{:S(2)}, u32[]{:S(2)}) collective-permute-start(bf16[4,4,1024]{2,0,1:T(4,128)(2,1)S(1)} %pad_maximum_fusion.4), channel_id=1, source_target_pairs={{0,8},{4,12},{8,0},{12,4},{1,9},{5,13},{9,1},{13,5},{2,10},{6,14},... | collective-permute-start | bytes 98312 | tf_op jit(solution)/shard_map/ppermute | solution.py:91
  24.6 5.2 %collective-permute-start.3 = (f32[64,512]{1,0:T(8,128)}, f32[64,512]{1,0:T(8,128)S(1)}, u32[]{:S(2)}, u32[]{:S(2)}) collective-permute-start(f32[64,512]{1,0:T(8,128)} %shard_map.46), channel_id=1, source_target_pairs={{0,4},{4,0},{8,12},{12,8},{1,5},{5,1},{9,13},{13,9},{2,6},{6,2},{1... | collective-permute-start | bytes 393224 | tf_op jit(solution)/shard_map/ppermute | solution.py:63
  30.7 5.9 %collective-permute-start.4 = (f32[64,512]{1,0:T(8,128)S(1)}, f32[64,512]{1,0:T(8,128)S(1)}, u32[]{:S(2)}, u32[]{:S(2)}) collective-permute-start(f32[64,512]{1,0:T(8,128)S(1)} %add.56), channel_id=1, source_target_pairs={{0,8},{4,12},{8,0},{12,4},{1,9},{5,13},{9,1},{13,5},{2,10},{6,14},... | collective-permute-start | bytes 393224 | tf_op jit(solution)/shard_map/ppermute | solution.py:63
  36.8 4.4 %collective-permute-start.5 = (f32[64]{0:T(128)S(1)}, f32[64]{0:T(128)S(1)}, u32[]{:S(2)}, u32[]{:S(2)}) collective-permute-start(f32[64]{0:T(128)S(1)} %get-tuple-element.5), channel_id=1, source_target_pairs={{0,2},{2,0},{1,3},{3,1},{4,6},{6,4},{5,7},{7,5},{8,10},{10,8},{9,1... | collective-permute-start | bytes 776 | tf_op jit(solution)/shard_map/ppermute | solution.py:63

commit v10 on v9

--- a/solution.py
+++ b/solution.py
@@ -6,9 +6,9 @@
 from jax.experimental.pallas import tpu as pltpu
 
 
-def hankel_kernel(x_ref, n_ref, o_ref, h_ref):
+def hankel_kernel(x_ref, t_ref, m_ref, o_ref, h_ref):
     width = h_ref.shape[0]
-    channels = n_ref.shape[1] // width
+    channels = t_ref.shape[1] // width
     taps_blocks = width // 128
     out_blocks = o_ref.shape[1] // 128
     blocks = taps_blocks + out_blocks
@@ -17,6 +17,10 @@
     low = lane >= row
 
     def one_channel(c, acc):
+        start = pl.multiple_of(c * width, 128)
+        widened = t_ref[:, pl.ds(start, width)].astype(jnp.float32)
+        norm = jnp.sqrt(jnp.sum(widened * widened, axis=1, keepdims=True) + 1e-06)
+        normed = (widened * m_ref[c] / norm).astype(jnp.bfloat16)
         rolled = [
             pltpu.roll(x_ref[pl.ds(c * blocks + m, 128, stride=0), :], 0, 1, stride=1, stride_axis=0)
             for m in range(blocks)
@@ -33,8 +37,7 @@
         energy = jnp.concatenate(
             [sum(squares[a + p] for p in range(taps_blocks)) for a in range(out_blocks)], axis=1
         )
-        start = pl.multiple_of(c * width, 128)
-        part = jnp.dot(n_ref[:, pl.ds(start, width)], h_ref[...], preferred_element_type=jnp.float32)
+        part = jnp.dot(normed, h_ref[...], preferred_element_type=jnp.float32)
         return acc + part * (1.0 / jnp.sqrt(jnp.maximum(energy, 1.0)))
 
     o_ref[...] = lax.fori_loop(0, channels, one_channel, jnp.zeros(o_ref.shape, jnp.float32))
@@ -45,14 +48,14 @@
     return stacked.reshape(rows, seg_len // 128, 128)[..., ::-1].reshape(rows, seg_len)
 
 
-def correlate(normed, flat_owned, seg_len):
-    rows, channels, filter_taps = normed.shape
+def correlate(templates, mask, flat_owned, seg_len):
+    rows, channels, filter_taps = templates.shape
     blocks = flat_owned.reshape(channels * (flat_owned.shape[1] // 128), 128)[:, ::-1]
     return pl.pallas_call(
         hankel_kernel,
         out_shape=jax.ShapeDtypeStruct((rows, seg_len), jnp.float32),
         scratch_shapes=[pltpu.VMEM((filter_taps, seg_len), jnp.bfloat16)],
-    )(blocks, normed.reshape(rows, channels * filter_taps))
+    )(blocks, templates.reshape(rows, channels * filter_taps), jnp.transpose(mask)[:, :, None])
 
 
 def ordered_sum(part, axis):
@@ -121,15 +124,11 @@
     owned_rows, filled = gather_owned(records, station_region, capacity, filter_taps)
     owned_rows = owned_rows.astype(jnp.float32) * filled[:, None, None]
     flat_owned = owned_rows.reshape(capacity * components, seg_len + filter_taps)
-    weight = channel_mask.astype(jnp.float32)
-    widened_templates = templates.astype(jnp.float32)
-    template_norm = jnp.sqrt(
-        jnp.sum(widened_templates * widened_templates, axis=4, keepdims=True) + 1e-06
-    )
-    normed = (widened_templates * weight[..., None] / template_norm).astype(jnp.bfloat16)
-    normed = normed.reshape(local_batches * kept, capacity * components, filter_taps)
+    rows = local_batches * kept
+    raw = templates.reshape(rows, capacity * components, filter_taps)
+    mask = channel_mask.astype(jnp.float32).reshape(rows, capacity * components)
     total_len = seg_len * lax.axis_size("seg")
-    stacked = ordered_sum(correlate(normed, flat_owned, seg_len), "region")
+    stacked = ordered_sum(correlate(raw, mask, flat_owned, seg_len), "region")
     power_sum = ordered_sum(jnp.sum(stacked * stacked, axis=1), "seg")
     detect = unflip(stacked) / jnp.sqrt(power_sum / total_len + 1e-06)[:, None]
     return detect.reshape(local_batches, kept, seg_len)

time: 42.2 us -> 45.2 us (1.071)
  waiting for transfers between devices: 11.6 us -> 19.5 us
  starting transfers between devices: 14.1 us -> 9.01 us
  other arithmetic: 5.37 us -> 2.42 us
  local copies, waits for them, and re-layouts: 3.81 us -> 5.79 us
  Pallas kernels: 6.68 us -> 7.95 us
    ppermute x3, starting transfers between devices: 6.81 us -> 1.71 us  [ordered_sum(): part = part + lax.ppermute(part, axis, [(i, i ^ step) for i in range(size)])]
    ppermute x3, waiting for transfers between devices: 8.35 us -> 13.1 us  [ordered_sum(): part = part + lax.ppermute(part, axis, [(i, i ^ step) for i in range(size)])]
    ppermute x1, waiting for transfers between devices: 1.57 us -> 4.69 us  [gather_owned(): lax.ppermute(records[:, :, :filter_taps], 'seg', [(s + 1, s) for s in ran...]
    unnamed x6 -> x7, local copies, waits for them, and re-layouts: 0.02 us -> 1.7 us
    reduce_sum x1 -> x0, other arithmetic: 1.65 us -> none  [per_device(): jnp.sum(widened_templates * widened_templates, axis=4, keepdims=True)]
    pallas_call x1, Pallas kernels: 6.68 us -> 7.95 us  [correlate(): pl.pallas_call(hankel_kernel, out_shape=jax.ShapeDtypeStruct((rows, seg_l...]
    broadcast_in_dim x0 -> x1, local copies, waits for them, and re-layouts: none -> 0.96 us  [correlate(): jnp.transpose(mask)[:, :, None]]
    mul x1 -> x0, other arithmetic: 0.7 us -> none  [per_device(): widened_templates * weight[..., None] / template_norm]
  transfers between devices with their start and end apart: 6 -> 6, of which waited for: 5 -> 5; matrix products, arithmetic and copies ran while one was open for 14% -> 11% of each run, Pallas kernels for 0% -> 0%
where the time goes in v10:
time: 45.2 us; the launch traced here: 45 us
  waiting for transfers between devices  19.5 us (43%)
  starting transfers between devices  9.01 us (20%)
  Pallas kernels  7.95 us (18%)
  local copies, waits for them, and re-layouts  5.79 us (13%)
  other arithmetic  2.42 us (5%)
    ppermute x3, waiting for transfers between devices, ordered_sum(): part = part + lax.ppermute(part, axis, [(i, i ^ step) for i in range(size)])  13.1 us
    pallas_call x1, Pallas kernels, correlate(): pl.pallas_call(hankel_kernel, out_shape=jax.ShapeDtypeStruct((rows, seg_l...  7.95 us
    ppermute x2, starting transfers between devices, gather_owned(): lax.ppermute(here, 'region', [(r, r ^ step) for r in range(regions)])  5.89 us
    ppermute x1, waiting for transfers between devices, gather_owned(): lax.ppermute(records[:, :, :filter_taps], 'seg', [(s + 1, s) for s in ran...  4.69 us
    another operation x1, local copies, waits for them, and re-layouts, correlate(): templates.reshape(rows, channels * filter_taps)  1.84 us
    ppermute x2, waiting for transfers between devices, gather_owned(): lax.ppermute(here, 'region', [(r, r ^ step) for r in range(regions)])  1.72 us
    ppermute x3, starting transfers between devices, ordered_sum(): part = part + lax.ppermute(part, axis, [(i, i ^ step) for i in range(size)])  1.71 us
    unnamed x7, local copies, waits for them, and re-layouts  1.7 us
  transfers between devices with their start and end apart: 6, of which 5 were waited for; matrix products, arithmetic and copies ran while one was open for 11% of the time, Pallas kernels for 0%

profile of v10, /device:TPU:0, one launch (start us, length us, event | category | flops | bytes accessed | tf_op | source)
XLA Modules:
  0.0 45.0 jit_solution(10392028995183263463)
XLA Ops:
  0.0 1.4 %collective-permute-start = (bf16[2,3,512]{2,0,1:T(2,128)(2,1)}, bf16[2,3,512]{2,0,1:T(2,128)(2,1)S(1)}, u32[]{:S(2)}, u32[]{:S(2)}) collective-permute-start(bf16[2,3,512]{2,0,1:T(2,128)(2,1)} %param.4), channel_id=1, source_target_pairs={{2,0},{3,1},{6,4},{7,5},{10,8},{11,9},{14,12},{15,13},{18,16},{19,... | collective-permute-start | bytes 18440 | tf_op jit(solution)/shard_map/ppermute | solution.py:81
  1.5 4.7 %collective-permute-done = bf16[2,3,512]{2,0,1:T(2,128)(2,1)S(1)} collective-permute-done((bf16[2,3,512]{2,0,1:T(2,128)(2,1)}, bf16[2,3,512]{2,0,1:T(2,128)(2,1)S(1)}, u32[]{:S(2)}, u32[]{:S(2)}) %collective-permute-start) | collective-permute-done | bytes 6176 | tf_op jit(solution)/shard_map/ppermute | solution.py:81
  6.3 2.8 %collective-permute-start.1 = (bf16[2,4,1024]{2,0,1:T(2,128)(2,1)S(1)}, bf16[2,4,1024]{2,0,1:T(2,128)(2,1)S(1)}, u32[]{:S(2)}, u32[]{:S(2)}) collective-permute-start(bf16[2,4,1024]{2,0,1:T(2,128)(2,1)S(1)} %pad_maximum_fusion.5), channel_id=1, source_target_pairs={{0,4},{4,0},{8,12},{12,8},{1,5},{5,1},{9,13},{13,9},{2,6},{6,2},{1... | collective-permute-start | bytes 49160 | tf_op jit(solution)/shard_map/ppermute | solution.py:94
  9.0 1.7 %collective-permute-done.1 = bf16[2,4,1024]{2,0,1:T(2,128)(2,1)S(1)} collective-permute-done((bf16[2,4,1024]{2,0,1:T(2,128)(2,1)S(1)}, bf16[2,4,1024]{2,0,1:T(2,128)(2,1)S(1)}, u32[]{:S(2)}, u32[]{:S(2)}) %collective-permute-start.1) | collective-permute-done | bytes 16416 | tf_op jit(solution)/shard_map/ppermute | solution.py:94
  10.8 3.1 %collective-permute-start.2 = (bf16[4,4,1024]{2,0,1:T(4,128)(2,1)S(1)}, bf16[4,4,1024]{2,0,1:T(4,128)(2,1)S(1)}, u32[]{:S(2)}, u32[]{:S(2)}) collective-permute-start(bf16[4,4,1024]{2,0,1:T(4,128)(2,1)S(1)} %pad_maximum_fusion.4), channel_id=1, source_target_pairs={{0,8},{4,12},{8,0},{12,4},{1,9},{5,13},{9,1},{13,5},{2,10},{6,14},... | collective-permute-start | bytes 98312 | tf_op jit(solution)/shard_map/ppermute | solution.py:94
  14.0 0.1 add.42
  14.1 1.7 %copy.10 = bf16[1,64,4,3,512]{4,3,2,1,0:T(4,128)(2,1)S(1)} copy(bf16[1,64,4,3,512]{4,2,3,1,0:T(4,128)(2,1)} %param.5) | data formatting | bytes 1572864 | tf_op args[1]
  15.8 1.8 %reshape_reshape.4.t_ref = bf16[64,6144]{1,0:T(8,128)(2,1)} reshape(bf16[1,64,4,3,512]{4,3,2,1,0:T(4,128)(2,1)S(1)} %copy.10) | data formatting | bytes 1572864 | tf_op jit(solution)/shard_map/reshape;reshape | solution.py:58
  17.6 1.0 %copy.12.m_ref = f32[12,64,1]{2,1,0:T(8,128)} copy(f32[12,64,1]{1,0,2:T(8,128)S(1)} %bitcast.8) | data formatting | bytes 6144 | tf_op jit(solution)/shard_map/broadcast_in_dim | solution.py:58
  18.6 0.1 convert_reduce_fusion
  18.7 0.2 convert_reduce_fusion.1
  18.9 0.1 convert_reduce_fusion.2
  19.0 0.1 mul.23
  19.2 0.1 fusion
  19.4 0.7 %rev.6.x_ref = f32[96,128]{1,0:T(8,128)} reverse(f32[96,128]{1,0:T(8,128)S(1)} %mul.25), dimensions={1} | reverse | bytes 98304 | tf_op jit(solution)/shard_map/rev | solution.py:53
  20.1 8.0 %shard_map.46 = f32[64,512]{1,0:T(8,128)} custom-call(f32[96,128]{1,0:T(8,128)} %rev.6.x_ref, bf16[64,6144]{1,0:T(8,128)(2,1)} %reshape_reshape.4.t_ref, f32[12,64,1]{2,1,0:T(8,128)} %copy.12.m_ref), custom_call_target="tpu_custom_call" | custom-call | tf_op jit(solution)/shard_map/pallas_call | solution.py:54
  28.0 1.6 %collective-permute-start.3 = (f32[64,512]{1,0:T(8,128)}, f32[64,512]{1,0:T(8,128)S(1)}, u32[]{:S(2)}, u32[]{:S(2)}) collective-permute-start(f32[64,512]{1,0:T(8,128)} %shard_map.46), channel_id=1, source_target_pairs={{0,4},{4,0},{8,12},{12,8},{1,5},{5,1},{9,13},{13,9},{2,6},{6,2},{1... | collective-permute-start | bytes 393224 | tf_op jit(solution)/shard_map/ppermute | solution.py:66
  29.6 4.0 %collective-permute-done.3 = f32[64,512]{1,0:T(8,128)S(1)} collective-permute-done((f32[64,512]{1,0:T(8,128)}, f32[64,512]{1,0:T(8,128)S(1)}, u32[]{:S(2)}, u32[]{:S(2)}) %collective-permute-start.3) | collective-permute-done | bytes 131104 | tf_op jit(solution)/shard_map/ppermute | solution.py:66
  33.6 0.9 %add.43 = f32[64,512]{1,0:T(8,128)S(1)} add(f32[64,512]{1,0:T(8,128)} %shard_map.46, f32[64,512]{1,0:T(8,128)S(1)} %collective-permute-done.3) | non-fusion elementwise | flops 32768 | bytes 393216 | tf_op jit(solution)/shard_map/add | solution.py:66
  34.6 5.9 %collective-permute-done.4 = f32[64,512]{1,0:T(8,128)S(1)} collective-permute-done((f32[64,512]{1,0:T(8,128)S(1)}, f32[64,512]{1,0:T(8,128)S(1)}, u32[]{:S(2)}, u32[]{:S(2)}) %collective-permute-start.4) | collective-permute-done | bytes 131104 | tf_op jit(solution)/shard_map/ppermute | solution.py:66
  40.5 0.1 multiply_reduce_fusion
  40.7 0.2 rev.7
  41.0 3.2 %collective-permute-done.5 = f32[64]{0:T(128)S(1)} collective-permute-done((f32[64]{0:T(128)S(1)}, f32[64]{0:T(128)S(1)}, u32[]{:S(2)}, u32[]{:S(2)}) %collective-permute-start.5) | collective-permute-done | bytes 288 | tf_op jit(solution)/shard_map/ppermute | solution.py:66
  44.2 0.7 %broadcast_divide_fusion = f32[1,64,512]{2,1,0:T(8,128)} fusion(f32[1,64,512]{2,1,0:T(8,128)S(1)} %reshape.105, f32[64]{0:T(128)S(1)} %add_sqrt_fusion), kind=kLoop, calls=%fused_computation.3 | loop fusion | flops 32768 | bytes 262400 | tf_op jit(solution)/shard_map/div | solution.py:133
  (26 shorter events, 0.6 us)
Async XLA Ops:
  0.0 1.4 %copy-start.2 = (s32[2]{0:T(128)S(1)}, s32[2]{0:T(128)}, u32[]{:S(2)}) copy-start(s32[2]{0:T(128)} %param.7) | copy-start | bytes 28
  0.0 6.2 %collective-permute-start = (bf16[2,3,512]{2,0,1:T(2,128)(2,1)}, bf16[2,3,512]{2,0,1:T(2,128)(2,1)S(1)}, u32[]{:S(2)}, u32[]{:S(2)}) collective-permute-start(bf16[2,3,512]{2,0,1:T(2,128)(2,1)} %param.4), channel_id=1, source_target_pairs={{2,0},{3,1},{6,4},{7,5},{10,8},{11,9},{14,12},{15,13},{18,16},{19,... | collective-permute-start | bytes 18440 | tf_op jit(solution)/shard_map/ppermute | solution.py:81
  1.4 4.8 %copy-start = (bf16[2,3,512]{2,0,1:T(2,128)(2,1)S(1)}, bf16[2,3,512]{2,0,1:T(2,128)(2,1)}, u32[]{:S(2)}) copy-start(bf16[2,3,512]{2,0,1:T(2,128)(2,1)} %param.4) | copy-start | bytes 18436
  6.3 4.5 %collective-permute-start.1 = (bf16[2,4,1024]{2,0,1:T(2,128)(2,1)S(1)}, bf16[2,4,1024]{2,0,1:T(2,128)(2,1)S(1)}, u32[]{:S(2)}, u32[]{:S(2)}) collective-permute-start(bf16[2,4,1024]{2,0,1:T(2,128)(2,1)S(1)} %pad_maximum_fusion.5), channel_id=1, source_target_pairs={{0,4},{4,0},{8,12},{12,8},{1,5},{5,1},{9,13},{13,9},{2,6},{6,2},{1... | collective-permute-start | bytes 49160 | tf_op jit(solution)/shard_map/ppermute | solution.py:94
  10.8 7.8 %collective-permute-start.2 = (bf16[4,4,1024]{2,0,1:T(4,128)(2,1)S(1)}, bf16[4,4,1024]{2,0,1:T(4,128)(2,1)S(1)}, u32[]{:S(2)}, u32[]{:S(2)}) collective-permute-start(bf16[4,4,1024]{2,0,1:T(4,128)(2,1)S(1)} %pad_maximum_fusion.4), channel_id=1, source_target_pairs={{0,8},{4,12},{8,0},{12,4},{1,9},{5,13},{9,1},{13,5},{2,10},{6,14},... | collective-permute-start | bytes 98312 | tf_op jit(solution)/shard_map/ppermute | solution.py:94
  15.8 1.9 %copy-start.1 = (s32[1,64,4,3]{1,2,3,0:T(4,128)S(1)}, s32[1,64,4,3]{1,2,3,0:T(4,128)}, u32[]{:S(2)}) copy-start(s32[1,64,4,3]{1,2,3,0:T(4,128)} %param.6) | copy-start | bytes 9220
  28.0 5.6 %collective-permute-start.3 = (f32[64,512]{1,0:T(8,128)}, f32[64,512]{1,0:T(8,128)S(1)}, u32[]{:S(2)}, u32[]{:S(2)}) collective-permute-start(f32[64,512]{1,0:T(8,128)} %shard_map.46), channel_id=1, source_target_pairs={{0,4},{4,0},{8,12},{12,8},{1,5},{5,1},{9,13},{13,9},{2,6},{6,2},{1... | collective-permute-start | bytes 393224 | tf_op jit(solution)/shard_map/ppermute | solution.py:66
  34.6 5.9 %collective-permute-start.4 = (f32[64,512]{1,0:T(8,128)S(1)}, f32[64,512]{1,0:T(8,128)S(1)}, u32[]{:S(2)}, u32[]{:S(2)}) collective-permute-start(f32[64,512]{1,0:T(8,128)S(1)} %add.43), channel_id=1, source_target_pairs={{0,8},{4,12},{8,0},{12,4},{1,9},{5,13},{9,1},{13,5},{2,10},{6,14},... | collective-permute-start | bytes 393224 | tf_op jit(solution)/shard_map/ppermute | solution.py:66
  40.6 3.6 %collective-permute-start.5 = (f32[64]{0:T(128)S(1)}, f32[64]{0:T(128)S(1)}, u32[]{:S(2)}, u32[]{:S(2)}) collective-permute-start(f32[64]{0:T(128)S(1)} %get-tuple-element.5), channel_id=1, source_target_pairs={{0,2},{2,0},{1,3},{3,1},{4,6},{6,4},{5,7},{7,5},{8,10},{10,8},{9,1... | collective-permute-start | bytes 776 | tf_op jit(solution)/shard_map/ppermute | solution.py:66

commit v11 on v9

--- a/solution.py
+++ b/solution.py
@@ -46,13 +46,15 @@
 
 
 def correlate(normed, flat_owned, seg_len):
-    rows, channels, filter_taps = normed.shape
-    blocks = flat_owned.reshape(channels * (flat_owned.shape[1] // 128), 128)[:, ::-1]
+    channels = flat_owned.shape[0]
+    rows = normed.shape[0]
+    filter_taps = normed.shape[1] // channels
+    blocks = flat_owned.reshape(channels * (flat_owned.shape[1] // 128), 128)
     return pl.pallas_call(
         hankel_kernel,
         out_shape=jax.ShapeDtypeStruct((rows, seg_len), jnp.float32),
         scratch_shapes=[pltpu.VMEM((filter_taps, seg_len), jnp.bfloat16)],
-    )(blocks, normed.reshape(rows, channels * filter_taps))
+    )(blocks, normed)
 
 
 def ordered_sum(part, axis):
@@ -71,13 +73,16 @@
     return jnp.sum(jnp.take(jnp.stack(received), order, axis=0), axis=0)
 
 
-def gather_owned(records, station_region, capacity, filter_taps):
+def gather_owned(records, station_region, capacity, filter_taps, prepared):
     local_count, components, seg_len = records.shape
     regions = lax.axis_size("region")
     segs = lax.axis_size("seg")
+    records = records.reshape(local_count, components, seg_len // 128, 128)[..., ::-1]
+    records = records.reshape(local_count, components, seg_len)
     ahead = lax.ppermute(
         records[:, :, :filter_taps], "seg", [(s + 1, s) for s in range(segs - 1)]
     )
+    ahead, prepared = lax.optimization_barrier((ahead, prepared))
     tag = jnp.broadcast_to(station_region.astype(jnp.bfloat16)[:, None, None], (local_count, 1, seg_len + filter_taps))
     payload = jnp.concatenate(
         [jnp.concatenate([records, ahead], axis=2), tag], axis=1
@@ -112,22 +117,22 @@
     ).astype(jnp.bfloat16)
     owned_rows = owned_rows.reshape(capacity, components, seg_len + filter_taps)
     filled = jnp.sum(placing.astype(jnp.float32), axis=1)
-    return owned_rows, filled
+    return owned_rows, filled, prepared
 
 
 def per_device(records, templates, channel_mask, station_region):
     local_batches, kept, capacity, components, filter_taps = templates.shape
     seg_len = records.shape[2]
-    owned_rows, filled = gather_owned(records, station_region, capacity, filter_taps)
-    owned_rows = owned_rows.astype(jnp.float32) * filled[:, None, None]
-    flat_owned = owned_rows.reshape(capacity * components, seg_len + filter_taps)
     weight = channel_mask.astype(jnp.float32)
     widened_templates = templates.astype(jnp.float32)
     template_norm = jnp.sqrt(
         jnp.sum(widened_templates * widened_templates, axis=4, keepdims=True) + 1e-06
     )
     normed = (widened_templates * weight[..., None] / template_norm).astype(jnp.bfloat16)
-    normed = normed.reshape(local_batches * kept, capacity * components, filter_taps)
+    normed = normed.reshape(local_batches * kept, capacity * components * filter_taps)
+    owned_rows, filled, normed = gather_owned(records, station_region, capacity, filter_taps, normed)
+    owned_rows = owned_rows.astype(jnp.float32) * filled[:, None, None]
+    flat_owned = owned_rows.reshape(capacity * components, seg_len + filter_taps)
     total_len = seg_len * lax.axis_size("seg")
     stacked = ordered_sum(correlate(normed, flat_owned, seg_len), "region")
     power_sum = ordered_sum(jnp.sum(stacked * stacked, axis=1), "seg")

time: 42.2 us -> 44.1 us (1.045)
  starting transfers between devices: 14.1 us -> 16.7 us
  waiting for transfers between devices: 11.6 us -> 10.9 us
    reshape x0 -> x3, local copies, waits for them, and re-layouts: none -> 2.64 us  [the longest x1 1.84 us: per_device(): normed.reshape(local_batches * kept, capacity * components * filter_taps)]
    ppermute x3, starting transfers between devices: 6.81 us -> 9.24 us  [ordered_sum(): part = part + lax.ppermute(part, axis, [(i, i ^ step) for i in range(size)])]
    another operation x1 -> x0, local copies, waits for them, and re-layouts: 1.84 us -> none  [correlate(): normed.reshape(rows, channels * filter_taps)]
    ppermute x2, waiting for transfers between devices: 1.72 us -> 3.41 us  [gather_owned(): lax.ppermute(here, 'region', [(r, r ^ step) for r in range(regions)])]
    ppermute x1, waiting for transfers between devices: 1.57 us -> 0.01 us  [gather_owned(): lax.ppermute(records[:, :, :filter_taps], 'seg', [(s + 1, s) for s in ran...]
    ppermute x3, waiting for transfers between devices: 8.35 us -> 7.45 us  [ordered_sum(): part = part + lax.ppermute(part, axis, [(i, i ^ step) for i in range(size)])]
    mul x1, other arithmetic: 0.7 us -> 0.01 us  [per_device(): widened_templates * weight[..., None] / template_norm]
    mul x1, other arithmetic: 0.01 us -> 0.62 us  [per_device(): owned_rows = owned_rows.astype(jnp.float32) * filled[:, None, None]]
  transfers between devices with their start and end apart: 6 -> 6, of which waited for: 5 -> 5; matrix products, arithmetic and copies ran while one was open for 14% -> 12% of each run, Pallas kernels for 0% -> 0%
where the time goes in v11:
time: 44.1 us; the launch traced here: 43.9 us
  starting transfers between devices  16.7 us (38%)
  waiting for transfers between devices  10.9 us (25%)
  Pallas kernels  6.68 us (15%)
  other arithmetic  5.28 us (12%)
  local copies, waits for them, and re-layouts  4.06 us (9%)
    ppermute x3, starting transfers between devices, ordered_sum(): part = part + lax.ppermute(part, axis, [(i, i ^ step) for i in range(size)])  9.24 us
    ppermute x3, waiting for transfers between devices, ordered_sum(): part = part + lax.ppermute(part, axis, [(i, i ^ step) for i in range(size)])  7.45 us
    pallas_call x1, Pallas kernels, correlate(): pl.pallas_call(hankel_kernel, out_shape=jax.ShapeDtypeStruct((rows, seg_l...  6.68 us
    ppermute x2, starting transfers between devices, gather_owned(): lax.ppermute(here, 'region', [(r, r ^ step) for r in range(regions)])  6.19 us
    ppermute x2, waiting for transfers between devices, gather_owned(): lax.ppermute(here, 'region', [(r, r ^ step) for r in range(regions)])  3.41 us
    reshape x1, local copies, waits for them, and re-layouts, per_device(): normed.reshape(local_batches * kept, capacity * components * filter_taps)  1.84 us
    reduce_sum x1, other arithmetic, per_device(): jnp.sum(widened_templates * widened_templates, axis=4, keepdims=True)  1.65 us
    ppermute x1, starting transfers between devices, gather_owned(): lax.ppermute(records[:, :, :filter_taps], 'seg', [(s + 1, s) for s in ran...  1.29 us
  transfers between devices with their start and end apart: 6, of which 5 were waited for; matrix products, arithmetic and copies ran while one was open for 12% of the time, Pallas kernels for 0%

profile of v11, /device:TPU:0, one launch (start us, length us, event | category | flops | bytes accessed | tf_op | source)
XLA Modules:
  0.0 43.9 jit_solution(15219121119306584444)
XLA Ops:
  0.0 0.8 %reshape.122 = bf16[2,3,4,128]{3,2,0,1:T(4,128)(2,1)S(1)} reshape(bf16[2,3,512]{2,0,1:T(2,128)(2,1)} %param.4) | data formatting | bytes 12288 | tf_op jit(solution)/shard_map/reshape | solution.py:80
  0.9 1.3 %collective-permute-start = (bf16[2,3,512]{2,0,1:T(2,128)(2,1)S(1)}, bf16[2,3,512]{2,0,1:T(2,128)(2,1)S(1)}, u32[]{:S(2)}, u32[]{:S(2)}) collective-permute-start(bf16[2,3,512]{2,0,1:T(2,128)(2,1)S(1)} %reshape.123), channel_id=1, source_target_pairs={{2,0},{3,1},{6,4},{7,5},{10,8},{11,9},{14,12},{15,13},{18,16},{19,... | collective-permute-start | bytes 18440 | tf_op jit(solution)/shard_map/ppermute | solution.py:82
  2.2 1.6 %fusion.3 = f32[64,4,3]{1,2,0:T(4,128)S(1)} fusion(bf16[1,64,4,3,512]{4,2,3,1,0:T(4,128)(2,1)} %param.5), kind=kLoop, calls=%fused_computation.6 | loop fusion | flops 1178880 | bytes 789504 | tf_op jit(solution)/shard_map/reduce_sum | solution.py:129
  4.0 0.1 copy.23
  4.1 0.5 %fusion.2 = bf16[1,64,4,3,512]{4,2,3,1,0:T(4,128)(2,1)S(1)} fusion(bf16[1,64,4,3,512]{4,2,3,1,0:T(4,128)(2,1)S(1)} %copy-done, f32[64,4,3]{1,2,0:T(4,128)S(1)} %add_sqrt_fusion, f32[64,4,3]{1,2,0:T(4,128)S(1)} %copy.23), kind=kLoop, calls=%fused_computation.5 | loop fusion | flops 1572864 | bytes 1579008 | tf_op jit(solution)/shard_map/convert_element_type | solution.py:131
  4.6 0.6 %copy.24 = bf16[1,64,4,3,512]{4,3,2,1,0:T(4,128)(2,1)S(1)} copy(bf16[1,64,4,3,512]{4,2,3,1,0:T(4,128)(2,1)S(1)} %fusion.2) | data formatting | bytes 1572864 | tf_op jit(solution)/shard_map/convert_element_type | solution.py:131
  5.2 1.8 %reshape.124.n_ref = bf16[64,6144]{1,0:T(8,128)(2,1)} reshape(bf16[1,64,4,3,512]{4,3,2,1,0:T(4,128)(2,1)S(1)} %copy.24) | data formatting | bytes 1572864 | tf_op jit(solution)/shard_map/reshape | solution.py:132
  7.2 3.1 %collective-permute-start.1 = (bf16[2,4,1024]{2,1,0:T(4,128)(2,1)S(1)}, bf16[2,4,1024]{2,1,0:T(4,128)(2,1)S(1)}, u32[]{:S(2)}, u32[]{:S(2)}) collective-permute-start(bf16[2,4,1024]{2,1,0:T(4,128)(2,1)S(1)} %pad_maximum_fusion.3), channel_id=1, source_target_pairs={{0,4},{4,0},{8,12},{12,8},{1,5},{5,1},{9,13},{13,9},{2,6},{6,2},{1... | collective-permute-start | bytes 49160 | tf_op jit(solution)/shard_map/ppermute | solution.py:96
  10.3 1.7 %collective-permute-done.1 = bf16[2,4,1024]{2,1,0:T(4,128)(2,1)S(1)} collective-permute-done((bf16[2,4,1024]{2,1,0:T(4,128)(2,1)S(1)}, bf16[2,4,1024]{2,1,0:T(4,128)(2,1)S(1)}, u32[]{:S(2)}, u32[]{:S(2)}) %collective-permute-start.1) | collective-permute-done | bytes 16416 | tf_op jit(solution)/shard_map/ppermute | solution.py:96
  12.0 3.1 %collective-permute-start.2 = (bf16[4,4,1024]{2,1,0:T(4,128)(2,1)S(1)}, bf16[4,4,1024]{2,1,0:T(4,128)(2,1)S(1)}, u32[]{:S(2)}, u32[]{:S(2)}) collective-permute-start(bf16[4,4,1024]{2,1,0:T(4,128)(2,1)S(1)} %pad_maximum_fusion.2), channel_id=1, source_target_pairs={{0,8},{4,12},{8,0},{12,4},{1,9},{5,13},{9,1},{13,5},{2,10},{6,14},... | collective-permute-start | bytes 98312 | tf_op jit(solution)/shard_map/ppermute | solution.py:96
  15.3 1.7 %collective-permute-done.2 = bf16[4,4,1024]{2,1,0:T(4,128)(2,1)S(1)} collective-permute-done((bf16[4,4,1024]{2,1,0:T(4,128)(2,1)S(1)}, bf16[4,4,1024]{2,1,0:T(4,128)(2,1)S(1)}, u32[]{:S(2)}, u32[]{:S(2)}) %collective-permute-start.2) | collective-permute-done | bytes 32800 | tf_op jit(solution)/shard_map/ppermute | solution.py:96
  17.2 0.2 convert_reduce_fusion.1
  17.5 0.1 fusion
  17.8 0.6 %mul.42.x_ref = f32[96,128]{1,0:T(8,128)} multiply(f32[96,128]{1,0:T(8,128)S(1)} %reshape.129, f32[96,128]{1,0:T(8,128)S(1)} %mul.41) | non-fusion elementwise | flops 12288 | bytes 147456 | tf_op jit(solution)/shard_map/mul | solution.py:134
  18.4 6.7 %shard_map.46 = f32[64,512]{1,0:T(8,128)} custom-call(f32[96,128]{1,0:T(8,128)} %mul.42.x_ref, bf16[64,6144]{1,0:T(8,128)(2,1)} %reshape.124.n_ref), custom_call_target="tpu_custom_call" | custom-call | tf_op jit(solution)/shard_map/pallas_call | solution.py:53
  25.1 1.9 %collective-permute-start.3 = (f32[64,512]{1,0:T(8,128)}, f32[64,512]{1,0:T(8,128)S(1)}, u32[]{:S(2)}, u32[]{:S(2)}) collective-permute-start(f32[64,512]{1,0:T(8,128)} %shard_map.46), channel_id=1, source_target_pairs={{0,4},{4,0},{8,12},{12,8},{1,5},{5,1},{9,13},{13,9},{2,6},{6,2},{1... | collective-permute-start | bytes 393224 | tf_op jit(solution)/shard_map/ppermute | solution.py:65
  27.0 3.3 %collective-permute-done.3 = f32[64,512]{1,0:T(8,128)S(1)} collective-permute-done((f32[64,512]{1,0:T(8,128)}, f32[64,512]{1,0:T(8,128)S(1)}, u32[]{:S(2)}, u32[]{:S(2)}) %collective-permute-start.3) | collective-permute-done | bytes 131104 | tf_op jit(solution)/shard_map/ppermute | solution.py:65
  30.3 0.9 %add.56 = f32[64,512]{1,0:T(8,128)S(1)} add(f32[64,512]{1,0:T(8,128)} %shard_map.46, f32[64,512]{1,0:T(8,128)S(1)} %collective-permute-done.3) | non-fusion elementwise | flops 32768 | bytes 393216 | tf_op jit(solution)/shard_map/add | solution.py:65
  31.2 3.0 %collective-permute-start.4 = (f32[64,512]{1,0:T(8,128)S(1)}, f32[64,512]{1,0:T(8,128)S(1)}, u32[]{:S(2)}, u32[]{:S(2)}) collective-permute-start(f32[64,512]{1,0:T(8,128)S(1)} %add.56), channel_id=1, source_target_pairs={{0,8},{4,12},{8,0},{12,4},{1,9},{5,13},{9,1},{13,5},{2,10},{6,14},... | collective-permute-start | bytes 393224 | tf_op jit(solution)/shard_map/ppermute | solution.py:65
  34.2 3.0 %collective-permute-done.4 = f32[64,512]{1,0:T(8,128)S(1)} collective-permute-done((f32[64,512]{1,0:T(8,128)S(1)}, f32[64,512]{1,0:T(8,128)S(1)}, u32[]{:S(2)}, u32[]{:S(2)}) %collective-permute-start.4) | collective-permute-done | bytes 131104 | tf_op jit(solution)/shard_map/ppermute | solution.py:65
  37.3 4.3 %collective-permute-start.5 = (f32[64]{0:T(128)S(1)}, f32[64]{0:T(128)S(1)}, u32[]{:S(2)}, u32[]{:S(2)}) collective-permute-start(f32[64]{0:T(128)S(1)} %get-tuple-element.9), channel_id=1, source_target_pairs={{0,2},{2,0},{1,3},{3,1},{4,6},{6,4},{5,7},{7,5},{8,10},{10,8},{9,1... | collective-permute-start | bytes 776 | tf_op jit(solution)/shard_map/ppermute | solution.py:65
  41.7 0.2 rev.7
  41.9 1.2 %collective-permute-done.5 = f32[64]{0:T(128)S(1)} collective-permute-done((f32[64]{0:T(128)S(1)}, f32[64]{0:T(128)S(1)}, u32[]{:S(2)}, u32[]{:S(2)}) %collective-permute-start.5) | collective-permute-done | bytes 288 | tf_op jit(solution)/shard_map/ppermute | solution.py:65
  43.2 0.7 %broadcast_divide_fusion = f32[1,64,512]{2,1,0:T(8,128)} fusion(f32[1,64,512]{2,1,0:T(8,128)S(1)} %reshape.127, f32[64]{0:T(128)S(1)} %add_sqrt_fusion.1), kind=kLoop, calls=%fused_computation.9 | loop fusion | flops 32768 | bytes 262400 | tf_op jit(solution)/shard_map/div | solution.py:139
  (34 shorter events, 1.2 us)
Async XLA Ops:
  0.0 4.1 %copy-start = (bf16[1,64,4,3,512]{4,2,3,1,0:T(4,128)(2,1)S(1)}, bf16[1,64,4,3,512]{4,2,3,1,0:T(4,128)(2,1)}, u32[]{:S(2)}) copy-start(bf16[1,64,4,3,512]{4,2,3,1,0:T(4,128)(2,1)} %param.5) | copy-start | bytes 2359300
  0.0 3.9 %copy-start.1 = (s32[1,64,4,3]{1,2,3,0:T(4,128)S(1)}, s32[1,64,4,3]{1,2,3,0:T(4,128)}, u32[]{:S(2)}) copy-start(s32[1,64,4,3]{1,2,3,0:T(4,128)} %param.6) | copy-start | bytes 9220
  0.9 6.1 %collective-permute-start = (bf16[2,3,512]{2,0,1:T(2,128)(2,1)S(1)}, bf16[2,3,512]{2,0,1:T(2,128)(2,1)S(1)}, u32[]{:S(2)}, u32[]{:S(2)}) collective-permute-start(bf16[2,3,512]{2,0,1:T(2,128)(2,1)S(1)} %reshape.123), channel_id=1, source_target_pairs={{2,0},{3,1},{6,4},{7,5},{10,8},{11,9},{14,12},{15,13},{18,16},{19,... | collective-permute-start | bytes 18440 | tf_op jit(solution)/shard_map/ppermute | solution.py:82
  5.2 1.9 %copy-start.2 = (s32[2]{0:T(128)S(1)}, s32[2]{0:T(128)}, u32[]{:S(2)}) copy-start(s32[2]{0:T(128)} %param.7) | copy-start | bytes 28
  7.2 4.8 %collective-permute-start.1 = (bf16[2,4,1024]{2,1,0:T(4,128)(2,1)S(1)}, bf16[2,4,1024]{2,1,0:T(4,128)(2,1)S(1)}, u32[]{:S(2)}, u32[]{:S(2)}) collective-permute-start(bf16[2,4,1024]{2,1,0:T(4,128)(2,1)S(1)} %pad_maximum_fusion.3), channel_id=1, source_target_pairs={{0,4},{4,0},{8,12},{12,8},{1,5},{5,1},{9,13},{13,9},{2,6},{6,2},{1... | collective-permute-start | bytes 49160 | tf_op jit(solution)/shard_map/ppermute | solution.py:96
  12.0 5.0 %collective-permute-start.2 = (bf16[4,4,1024]{2,1,0:T(4,128)(2,1)S(1)}, bf16[4,4,1024]{2,1,0:T(4,128)(2,1)S(1)}, u32[]{:S(2)}, u32[]{:S(2)}) collective-permute-start(bf16[4,4,1024]{2,1,0:T(4,128)(2,1)S(1)} %pad_maximum_fusion.2), channel_id=1, source_target_pairs={{0,8},{4,12},{8,0},{12,4},{1,9},{5,13},{9,1},{13,5},{2,10},{6,14},... | collective-permute-start | bytes 98312 | tf_op jit(solution)/shard_map/ppermute | solution.py:96
  25.1 5.2 %collective-permute-start.3 = (f32[64,512]{1,0:T(8,128)}, f32[64,512]{1,0:T(8,128)S(1)}, u32[]{:S(2)}, u32[]{:S(2)}) collective-permute-start(f32[64,512]{1,0:T(8,128)} %shard_map.46), channel_id=1, source_target_pairs={{0,4},{4,0},{8,12},{12,8},{1,5},{5,1},{9,13},{13,9},{2,6},{6,2},{1... | collective-permute-start | bytes 393224 | tf_op jit(solution)/shard_map/ppermute | solution.py:65
  31.2 6.0 %collective-permute-start.4 = (f32[64,512]{1,0:T(8,128)S(1)}, f32[64,512]{1,0:T(8,128)S(1)}, u32[]{:S(2)}, u32[]{:S(2)}) collective-permute-start(f32[64,512]{1,0:T(8,128)S(1)} %add.56), channel_id=1, source_target_pairs={{0,8},{4,12},{8,0},{12,4},{1,9},{5,13},{9,1},{13,5},{2,10},{6,14},... | collective-permute-start | bytes 393224 | tf_op jit(solution)/shard_map/ppermute | solution.py:65
  37.3 5.9 %collective-permute-start.5 = (f32[64]{0:T(128)S(1)}, f32[64]{0:T(128)S(1)}, u32[]{:S(2)}, u32[]{:S(2)}) collective-permute-start(f32[64]{0:T(128)S(1)} %get-tuple-element.9), channel_id=1, source_target_pairs={{0,2},{2,0},{1,3},{3,1},{4,6},{6,4},{5,7},{7,5},{8,10},{10,8},{9,1... | collective-permute-start | bytes 776 | tf_op jit(solution)/shard_map/ppermute | solution.py:65

commit v12 on v9

--- a/solution.py
+++ b/solution.py
@@ -7,7 +7,7 @@
 
 
 def hankel_kernel(x_ref, n_ref, o_ref, h_ref):
-    width = h_ref.shape[0]
+    width = h_ref.shape[1]
     channels = n_ref.shape[1] // width
     taps_blocks = width // 128
     out_blocks = o_ref.shape[1] // 128
@@ -16,7 +16,7 @@
     lane = lax.broadcasted_iota(jnp.int32, (128, 128), 1)
     low = lane >= row
 
-    def one_channel(c, acc):
+    def one_channel(c, slot, acc):
         rolled = [
             pltpu.roll(x_ref[pl.ds(c * blocks + m, 128, stride=0), :], 0, 1, stride=1, stride_axis=0)
             for m in range(blocks)
@@ -29,15 +29,24 @@
             for p in range(taps_blocks):
                 a = m - p
                 if 0 <= a < out_blocks:
-                    h_ref[p * 128 : (p + 1) * 128, a * 128 : (a + 1) * 128] = window
+                    h_ref[slot, p * 128 : (p + 1) * 128, a * 128 : (a + 1) * 128] = window
         energy = jnp.concatenate(
             [sum(squares[a + p] for p in range(taps_blocks)) for a in range(out_blocks)], axis=1
         )
         start = pl.multiple_of(c * width, 128)
-        part = jnp.dot(n_ref[:, pl.ds(start, width)], h_ref[...], preferred_element_type=jnp.float32)
+        part = jnp.dot(n_ref[:, pl.ds(start, width)], h_ref[slot], preferred_element_type=jnp.float32)
         return acc + part * (1.0 / jnp.sqrt(jnp.maximum(energy, 1.0)))
 
-    o_ref[...] = lax.fori_loop(0, channels, one_channel, jnp.zeros(o_ref.shape, jnp.float32))
+    def two_channels(i, acc):
+        acc = one_channel(2 * i, 0, acc)
+        return one_channel(2 * i + 1, 1, acc)
+
+    acc = jnp.zeros(o_ref.shape, jnp.float32)
+    pairs = channels // 2
+    acc = lax.fori_loop(0, pairs, two_channels, acc, unroll=2 if pairs % 2 == 0 else 1)
+    if channels % 2:
+        acc = one_channel(channels - 1, 0, acc)
+    o_ref[...] = acc
 
 
 def unflip(stacked):
@@ -51,7 +60,7 @@
     return pl.pallas_call(
         hankel_kernel,
         out_shape=jax.ShapeDtypeStruct((rows, seg_len), jnp.float32),
-        scratch_shapes=[pltpu.VMEM((filter_taps, seg_len), jnp.bfloat16)],
+        scratch_shapes=[pltpu.VMEM((2, filter_taps, seg_len), jnp.bfloat16)],
     )(blocks, normed.reshape(rows, channels * filter_taps))
 
 

time: 42.2 us -> 40.3 us (0.955)
  Pallas kernels: 6.68 us -> 4.75 us
    pallas_call x1, Pallas kernels: 6.68 us -> 4.75 us  [correlate(): pl.pallas_call(hankel_kernel, out_shape=jax.ShapeDtypeStruct((rows, seg_l...]
  transfers between devices with their start and end apart: 6 -> 6, of which waited for: 5 -> 5; matrix products, arithmetic and copies ran while one was open for 14% -> 15% of each run, Pallas kernels for 0% -> 0%
where the time goes in v12:
time: 40.3 us; the launch traced here: 40 us
  starting transfers between devices  14.1 us (35%)
  waiting for transfers between devices  11.6 us (29%)
  other arithmetic  5.37 us (13%)
  Pallas kernels  4.75 us (12%)
  local copies, waits for them, and re-layouts  3.81 us (9%)
    ppermute x3, waiting for transfers between devices, ordered_sum(): part = part + lax.ppermute(part, axis, [(i, i ^ step) for i in range(size)])  8.34 us
    ppermute x3, starting transfers between devices, ordered_sum(): part = part + lax.ppermute(part, axis, [(i, i ^ step) for i in range(size)])  6.83 us
    ppermute x2, starting transfers between devices, gather_owned(): lax.ppermute(here, 'region', [(r, r ^ step) for r in range(regions)])  5.89 us
    pallas_call x1, Pallas kernels, correlate(): pl.pallas_call(hankel_kernel, out_shape=jax.ShapeDtypeStruct((rows, seg_l...  4.75 us
    another operation x1, local copies, waits for them, and re-layouts, correlate(): normed.reshape(rows, channels * filter_taps)  1.84 us
    ppermute x2, waiting for transfers between devices, gather_owned(): lax.ppermute(here, 'region', [(r, r ^ step) for r in range(regions)])  1.72 us
    reduce_sum x1, other arithmetic, per_device(): jnp.sum(widened_templates * widened_templates, axis=4, keepdims=True)  1.65 us
    ppermute x1, waiting for transfers between devices, gather_owned(): lax.ppermute(records[:, :, :filter_taps], 'seg', [(s + 1, s) for s in ran...  1.57 us
  transfers between devices with their start and end apart: 6, of which 5 were waited for; matrix products, arithmetic and copies ran while one was open for 15% of the time, Pallas kernels for 0%

profile of v12, /device:TPU:0, one launch (start us, length us, event | category | flops | bytes accessed | tf_op | source)
XLA Modules:
  0.0 40.0 jit_solution(7580505677737974313)
XLA Ops:
  0.0 1.4 %collective-permute-start = (bf16[2,3,512]{2,0,1:T(2,128)(2,1)}, bf16[2,3,512]{2,0,1:T(2,128)(2,1)S(1)}, u32[]{:S(2)}, u32[]{:S(2)}) collective-permute-start(bf16[2,3,512]{2,0,1:T(2,128)(2,1)} %param.4), channel_id=1, source_target_pairs={{2,0},{3,1},{6,4},{7,5},{10,8},{11,9},{14,12},{15,13},{18,16},{19,... | collective-permute-start | bytes 18440 | tf_op jit(solution)/shard_map/ppermute | solution.py:87
  1.4 0.7 %convert_bitcast_fusion = f32[64,4,3]{0,1,2:T(4,128)S(1)} fusion(s32[1,64,4,3]{1,2,3,0:T(4,128)} %param.6), kind=kLoop, calls=%fused_computation.16 | loop fusion | flops 768 | bytes 6144 | tf_op jit(solution)/shard_map/mul | solution.py:138
  2.1 0.1 copy.9
  2.3 1.7 %fusion.3 = f32[64,4,3]{1,2,0:T(4,128)S(1)} fusion(bf16[1,64,4,3,512]{4,2,3,1,0:T(4,128)(2,1)} %param.5), kind=kLoop, calls=%fused_computation.6 | loop fusion | flops 1178880 | bytes 789504 | tf_op jit(solution)/shard_map/reduce_sum | solution.py:136
  4.0 0.5 %fusion.2 = bf16[1,64,4,3,512]{4,2,3,1,0:T(4,128)(2,1)S(1)} fusion(bf16[1,64,4,3,512]{4,2,3,1,0:T(4,128)(2,1)S(1)} %copy-done, f32[64,4,3]{1,2,0:T(4,128)S(1)} %add_sqrt_fusion, f32[64,4,3]{1,2,0:T(4,128)S(1)} %copy.9), kind=kLoop, calls=%fused_computation.5 | loop fusion | flops 1572864 | bytes 1579008 | tf_op jit(solution)/shard_map/convert_element_type | solution.py:138
  4.6 1.6 %collective-permute-done = bf16[2,3,512]{2,0,1:T(2,128)(2,1)S(1)} collective-permute-done((bf16[2,3,512]{2,0,1:T(2,128)(2,1)}, bf16[2,3,512]{2,0,1:T(2,128)(2,1)S(1)}, u32[]{:S(2)}, u32[]{:S(2)}) %collective-permute-start) | collective-permute-done | bytes 6176 | tf_op jit(solution)/shard_map/ppermute | solution.py:87
  6.3 2.8 %collective-permute-start.1 = (bf16[2,4,1024]{2,0,1:T(2,128)(2,1)S(1)}, bf16[2,4,1024]{2,0,1:T(2,128)(2,1)S(1)}, u32[]{:S(2)}, u32[]{:S(2)}) collective-permute-start(bf16[2,4,1024]{2,0,1:T(2,128)(2,1)S(1)} %pad_maximum_fusion.5), channel_id=1, source_target_pairs={{0,4},{4,0},{8,12},{12,8},{1,5},{5,1},{9,13},{13,9},{2,6},{6,2},{1... | collective-permute-start | bytes 49160 | tf_op jit(solution)/shard_map/ppermute | solution.py:100
  9.1 1.7 %collective-permute-done.1 = bf16[2,4,1024]{2,0,1:T(2,128)(2,1)S(1)} collective-permute-done((bf16[2,4,1024]{2,0,1:T(2,128)(2,1)S(1)}, bf16[2,4,1024]{2,0,1:T(2,128)(2,1)S(1)}, u32[]{:S(2)}, u32[]{:S(2)}) %collective-permute-start.1) | collective-permute-done | bytes 16416 | tf_op jit(solution)/shard_map/ppermute | solution.py:100
  10.8 3.1 %collective-permute-start.2 = (bf16[4,4,1024]{2,0,1:T(4,128)(2,1)S(1)}, bf16[4,4,1024]{2,0,1:T(4,128)(2,1)S(1)}, u32[]{:S(2)}, u32[]{:S(2)}) collective-permute-start(bf16[4,4,1024]{2,0,1:T(4,128)(2,1)S(1)} %pad_maximum_fusion.4), channel_id=1, source_target_pairs={{0,8},{4,12},{8,0},{12,4},{1,9},{5,13},{9,1},{13,5},{2,10},{6,14},... | collective-permute-start | bytes 98312 | tf_op jit(solution)/shard_map/ppermute | solution.py:100
  14.1 0.6 %copy.10 = bf16[1,64,4,3,512]{4,3,2,1,0:T(4,128)(2,1)S(1)} copy(bf16[1,64,4,3,512]{4,2,3,1,0:T(4,128)(2,1)S(1)} %fusion.2) | data formatting | bytes 1572864 | tf_op jit(solution)/shard_map/convert_element_type | solution.py:138
  14.6 1.8 %reshape_reshape.4.n_ref = bf16[64,6144]{1,0:T(8,128)(2,1)} reshape(bf16[1,64,4,3,512]{4,3,2,1,0:T(4,128)(2,1)S(1)} %copy.10) | data formatting | bytes 1572864 | tf_op jit(solution)/shard_map/reshape;reshape | solution.py:64
  16.6 0.2 convert_reduce_fusion.1
  17.0 0.1 fusion
  17.2 0.7 %rev.6.x_ref = f32[96,128]{1,0:T(8,128)} reverse(f32[96,128]{1,0:T(8,128)S(1)} %mul.38), dimensions={1} | reverse | bytes 98304 | tf_op jit(solution)/shard_map/rev | solution.py:59
  17.9 4.8 %shard_map.46 = f32[64,512]{1,0:T(8,128)} custom-call(f32[96,128]{1,0:T(8,128)} %rev.6.x_ref, bf16[64,6144]{1,0:T(8,128)(2,1)} %reshape_reshape.4.n_ref), custom_call_target="tpu_custom_call" | custom-call | tf_op jit(solution)/shard_map/pallas_call | solution.py:60
  22.7 1.6 %collective-permute-start.3 = (f32[64,512]{1,0:T(8,128)}, f32[64,512]{1,0:T(8,128)S(1)}, u32[]{:S(2)}, u32[]{:S(2)}) collective-permute-start(f32[64,512]{1,0:T(8,128)} %shard_map.46), channel_id=1, source_target_pairs={{0,4},{4,0},{8,12},{12,8},{1,5},{5,1},{9,13},{13,9},{2,6},{6,2},{1... | collective-permute-start | bytes 393224 | tf_op jit(solution)/shard_map/ppermute | solution.py:72
  24.3 3.6 %collective-permute-done.3 = f32[64,512]{1,0:T(8,128)S(1)} collective-permute-done((f32[64,512]{1,0:T(8,128)}, f32[64,512]{1,0:T(8,128)S(1)}, u32[]{:S(2)}, u32[]{:S(2)}) %collective-permute-start.3) | collective-permute-done | bytes 131104 | tf_op jit(solution)/shard_map/ppermute | solution.py:72
  27.9 0.9 %add.56 = f32[64,512]{1,0:T(8,128)S(1)} add(f32[64,512]{1,0:T(8,128)} %shard_map.46, f32[64,512]{1,0:T(8,128)S(1)} %collective-permute-done.3) | non-fusion elementwise | flops 32768 | bytes 393216 | tf_op jit(solution)/shard_map/add | solution.py:72
  28.8 2.4 %collective-permute-start.4 = (f32[64,512]{1,0:T(8,128)S(1)}, f32[64,512]{1,0:T(8,128)S(1)}, u32[]{:S(2)}, u32[]{:S(2)}) collective-permute-start(f32[64,512]{1,0:T(8,128)S(1)} %add.56), channel_id=1, source_target_pairs={{0,8},{4,12},{8,0},{12,4},{1,9},{5,13},{9,1},{13,5},{2,10},{6,14},... | collective-permute-start | bytes 393224 | tf_op jit(solution)/shard_map/ppermute | solution.py:72
  31.2 3.5 %collective-permute-done.4 = f32[64,512]{1,0:T(8,128)S(1)} collective-permute-done((f32[64,512]{1,0:T(8,128)S(1)}, f32[64,512]{1,0:T(8,128)S(1)}, u32[]{:S(2)}, u32[]{:S(2)}) %collective-permute-start.4) | collective-permute-done | bytes 131104 | tf_op jit(solution)/shard_map/ppermute | solution.py:72
  34.9 2.8 %collective-permute-start.5 = (f32[64]{0:T(128)S(1)}, f32[64]{0:T(128)S(1)}, u32[]{:S(2)}, u32[]{:S(2)}) collective-permute-start(f32[64]{0:T(128)S(1)} %get-tuple-element.5), channel_id=1, source_target_pairs={{0,2},{2,0},{1,3},{3,1},{4,6},{6,4},{5,7},{7,5},{8,10},{10,8},{9,1... | collective-permute-start | bytes 776 | tf_op jit(solution)/shard_map/ppermute | solution.py:72
  37.7 0.2 rev.7
  38.0 1.2 %collective-permute-done.5 = f32[64]{0:T(128)S(1)} collective-permute-done((f32[64]{0:T(128)S(1)}, f32[64]{0:T(128)S(1)}, u32[]{:S(2)}, u32[]{:S(2)}) %collective-permute-start.5) | collective-permute-done | bytes 288 | tf_op jit(solution)/shard_map/ppermute | solution.py:72
  39.2 0.7 %broadcast_divide_fusion = f32[1,64,512]{2,1,0:T(8,128)} fusion(f32[1,64,512]{2,1,0:T(8,128)S(1)} %reshape.115, f32[64]{0:T(128)S(1)} %add_sqrt_fusion.1), kind=kLoop, calls=%fused_computation.9 | loop fusion | flops 32768 | bytes 262400 | tf_op jit(solution)/shard_map/div | solution.py:143
  (27 shorter events, 1.1 us)
Async XLA Ops:
  0.0 4.0 %copy-start = (bf16[1,64,4,3,512]{4,2,3,1,0:T(4,128)(2,1)S(1)}, bf16[1,64,4,3,512]{4,2,3,1,0:T(4,128)(2,1)}, u32[]{:S(2)}) copy-start(bf16[1,64,4,3,512]{4,2,3,1,0:T(4,128)(2,1)} %param.5) | copy-start | bytes 2359300
  0.0 6.2 %collective-permute-start = (bf16[2,3,512]{2,0,1:T(2,128)(2,1)}, bf16[2,3,512]{2,0,1:T(2,128)(2,1)S(1)}, u32[]{:S(2)}, u32[]{:S(2)}) collective-permute-start(bf16[2,3,512]{2,0,1:T(2,128)(2,1)} %param.4), channel_id=1, source_target_pairs={{2,0},{3,1},{6,4},{7,5},{10,8},{11,9},{14,12},{15,13},{18,16},{19,... | collective-permute-start | bytes 18440 | tf_op jit(solution)/shard_map/ppermute | solution.py:87
  3.9 0.7 %copy-start.2 = (s32[2]{0:T(128)S(1)}, s32[2]{0:T(128)}, u32[]{:S(2)}) copy-start(s32[2]{0:T(128)} %param.7) | copy-start | bytes 28
  3.9 2.3 %copy-start.1 = (bf16[2,3,512]{2,0,1:T(2,128)(2,1)S(1)}, bf16[2,3,512]{2,0,1:T(2,128)(2,1)}, u32[]{:S(2)}) copy-start(bf16[2,3,512]{2,0,1:T(2,128)(2,1)} %param.4) | copy-start | bytes 18436
  6.3 4.5 %collective-permute-start.1 = (bf16[2,4,1024]{2,0,1:T(2,128)(2,1)S(1)}, bf16[2,4,1024]{2,0,1:T(2,128)(2,1)S(1)}, u32[]{:S(2)}, u32[]{:S(2)}) collective-permute-start(bf16[2,4,1024]{2,0,1:T(2,128)(2,1)S(1)} %pad_maximum_fusion.5), channel_id=1, source_target_pairs={{0,4},{4,0},{8,12},{12,8},{1,5},{5,1},{9,13},{13,9},{2,6},{6,2},{1... | collective-permute-start | bytes 49160 | tf_op jit(solution)/shard_map/ppermute | solution.py:100
  10.8 5.7 %collective-permute-start.2 = (bf16[4,4,1024]{2,0,1:T(4,128)(2,1)S(1)}, bf16[4,4,1024]{2,0,1:T(4,128)(2,1)S(1)}, u32[]{:S(2)}, u32[]{:S(2)}) collective-permute-start(bf16[4,4,1024]{2,0,1:T(4,128)(2,1)S(1)} %pad_maximum_fusion.4), channel_id=1, source_target_pairs={{0,8},{4,12},{8,0},{12,4},{1,9},{5,13},{9,1},{13,5},{2,10},{6,14},... | collective-permute-start | bytes 98312 | tf_op jit(solution)/shard_map/ppermute | solution.py:100
  22.7 5.2 %collective-permute-start.3 = (f32[64,512]{1,0:T(8,128)}, f32[64,512]{1,0:T(8,128)S(1)}, u32[]{:S(2)}, u32[]{:S(2)}) collective-permute-start(f32[64,512]{1,0:T(8,128)} %shard_map.46), channel_id=1, source_target_pairs={{0,4},{4,0},{8,12},{12,8},{1,5},{5,1},{9,13},{13,9},{2,6},{6,2},{1... | collective-permute-start | bytes 393224 | tf_op jit(solution)/shard_map/ppermute | solution.py:72
  28.8 5.9 %collective-permute-start.4 = (f32[64,512]{1,0:T(8,128)S(1)}, f32[64,512]{1,0:T(8,128)S(1)}, u32[]{:S(2)}, u32[]{:S(2)}) collective-permute-start(f32[64,512]{1,0:T(8,128)S(1)} %add.56), channel_id=1, source_target_pairs={{0,8},{4,12},{8,0},{12,4},{1,9},{5,13},{9,1},{13,5},{2,10},{6,14},... | collective-permute-start | bytes 393224 | tf_op jit(solution)/shard_map/ppermute | solution.py:72
  34.9 4.4 %collective-permute-start.5 = (f32[64]{0:T(128)S(1)}, f32[64]{0:T(128)S(1)}, u32[]{:S(2)}, u32[]{:S(2)}) collective-permute-start(f32[64]{0:T(128)S(1)} %get-tuple-element.5), channel_id=1, source_target_pairs={{0,2},{2,0},{1,3},{3,1},{4,6},{6,4},{5,7},{7,5},{8,10},{10,8},{9,1... | collective-permute-start | bytes 776 | tf_op jit(solution)/shard_map/ppermute | solution.py:72

commit v13 on v12

--- a/solution.py
+++ b/solution.py
@@ -6,7 +6,7 @@
 from jax.experimental.pallas import tpu as pltpu
 
 
-def hankel_kernel(x_ref, n_ref, o_ref, h_ref):
+def hankel_kernel(x_ref, n_ref, o_ref, h_ref, r_ref):
     width = h_ref.shape[1]
     channels = n_ref.shape[1] // width
     taps_blocks = width // 128
@@ -15,10 +15,12 @@
     row = lax.broadcasted_iota(jnp.int32, (128, 128), 0)
     lane = lax.broadcasted_iota(jnp.int32, (128, 128), 1)
     low = lane >= row
+    exchange = (row + lane == 127).astype(jnp.bfloat16)
+    r_ref[...] = jnp.dot(x_ref[...], exchange, preferred_element_type=jnp.float32)
 
     def one_channel(c, slot, acc):
         rolled = [
-            pltpu.roll(x_ref[pl.ds(c * blocks + m, 128, stride=0), :], 0, 1, stride=1, stride_axis=0)
+            pltpu.roll(r_ref[pl.ds(c * blocks + m, 128, stride=0), :], 0, 1, stride=1, stride_axis=0)
             for m in range(blocks)
         ]
         squares = []
@@ -56,11 +58,14 @@
 
 def correlate(normed, flat_owned, seg_len):
     rows, channels, filter_taps = normed.shape
-    blocks = flat_owned.reshape(channels * (flat_owned.shape[1] // 128), 128)[:, ::-1]
+    blocks = flat_owned.reshape(channels * (flat_owned.shape[1] // 128), 128)
     return pl.pallas_call(
         hankel_kernel,
         out_shape=jax.ShapeDtypeStruct((rows, seg_len), jnp.float32),
-        scratch_shapes=[pltpu.VMEM((2, filter_taps, seg_len), jnp.bfloat16)],
+        scratch_shapes=[
+            pltpu.VMEM((2, filter_taps, seg_len), jnp.bfloat16),
+            pltpu.VMEM(blocks.shape, jnp.float32),
+        ],
     )(blocks, normed.reshape(rows, channels * filter_taps))
 
 
@@ -128,7 +133,7 @@
     local_batches, kept, capacity, components, filter_taps = templates.shape
     seg_len = records.shape[2]
     owned_rows, filled = gather_owned(records, station_region, capacity, filter_taps)
-    owned_rows = owned_rows.astype(jnp.float32) * filled[:, None, None]
+    owned_rows = owned_rows * filled.astype(jnp.bfloat16)[:, None, None]
     flat_owned = owned_rows.reshape(capacity * components, seg_len + filter_taps)
     weight = channel_mask.astype(jnp.float32)
     widened_templates = templates.astype(jnp.float32)

time: 40.3 us -> 40.3 us (level)
  local copies, waits for them, and re-layouts: 3.81 us -> 3.11 us
  other arithmetic: 5.37 us -> 5.97 us
    rev x1 -> x0, local copies, waits for them, and re-layouts: 0.7 us -> none  [correlate(): flat_owned.reshape(channels * (flat_owned.shape[1] // 128), 128)[:, ::-1]]
    mul x1, other arithmetic: 0.01 us -> 0.61 us  [per_device(): owned_rows = owned_rows * filled.astype(jnp.bfloat16)[:, None, None]]
where the time goes in v13:
time: 40.3 us; the launch traced here: 40 us
  starting transfers between devices  14.1 us (35%)
  waiting for transfers between devices  11.6 us (29%)
  other arithmetic  5.97 us (15%)
  Pallas kernels  4.87 us (12%)
  local copies, waits for them, and re-layouts  3.11 us (8%)
    ppermute x3, waiting for transfers between devices, ordered_sum(): part = part + lax.ppermute(part, axis, [(i, i ^ step) for i in range(size)])  8.34 us
    ppermute x3, starting transfers between devices, ordered_sum(): part = part + lax.ppermute(part, axis, [(i, i ^ step) for i in range(size)])  6.83 us
    ppermute x2, starting transfers between devices, gather_owned(): lax.ppermute(here, 'region', [(r, r ^ step) for r in range(regions)])  5.89 us
    pallas_call x1, Pallas kernels, correlate(): pl.pallas_call(hankel_kernel, out_shape=jax.ShapeDtypeStruct((rows, seg_l...  4.87 us
    another operation x1, local copies, waits for them, and re-layouts, correlate(): normed.reshape(rows, channels * filter_taps)  1.84 us
    ppermute x2, waiting for transfers between devices, gather_owned(): lax.ppermute(here, 'region', [(r, r ^ step) for r in range(regions)])  1.72 us
    reduce_sum x1, other arithmetic, per_device(): jnp.sum(widened_templates * widened_templates, axis=4, keepdims=True)  1.65 us
    ppermute x1, waiting for transfers between devices, gather_owned(): lax.ppermute(records[:, :, :filter_taps], 'seg', [(s + 1, s) for s in ran...  1.57 us
  transfers between devices with their start and end apart: 6, of which 5 were waited for; matrix products, arithmetic and copies ran while one was open for 15% of the time, Pallas kernels for 0%

profile of v13, /device:TPU:0, one launch (start us, length us, event | category | flops | bytes accessed | tf_op | source)
XLA Modules:
  0.0 40.0 jit_solution(10472845047853042241)
XLA Ops:
  0.0 1.4 %collective-permute-start = (bf16[2,3,512]{2,0,1:T(2,128)(2,1)}, bf16[2,3,512]{2,0,1:T(2,128)(2,1)S(1)}, u32[]{:S(2)}, u32[]{:S(2)}) collective-permute-start(bf16[2,3,512]{2,0,1:T(2,128)(2,1)} %param.4), channel_id=1, source_target_pairs={{2,0},{3,1},{6,4},{7,5},{10,8},{11,9},{14,12},{15,13},{18,16},{19,... | collective-permute-start | bytes 18440 | tf_op jit(solution)/shard_map/ppermute | solution.py:92
  1.4 0.7 %convert_bitcast_fusion = f32[64,4,3]{0,1,2:T(4,128)S(1)} fusion(s32[1,64,4,3]{1,2,3,0:T(4,128)} %param.6), kind=kLoop, calls=%fused_computation.15 | loop fusion | flops 768 | bytes 6144 | tf_op jit(solution)/shard_map/mul | solution.py:143
  2.1 0.1 copy.9
  2.3 1.7 %fusion.2 = f32[64,4,3]{1,2,0:T(4,128)S(1)} fusion(bf16[1,64,4,3,512]{4,2,3,1,0:T(4,128)(2,1)} %param.5), kind=kLoop, calls=%fused_computation.5 | loop fusion | flops 1178880 | bytes 789504 | tf_op jit(solution)/shard_map/reduce_sum | solution.py:141
  4.0 0.5 %fusion.1 = bf16[1,64,4,3,512]{4,2,3,1,0:T(4,128)(2,1)S(1)} fusion(bf16[1,64,4,3,512]{4,2,3,1,0:T(4,128)(2,1)S(1)} %copy-done, f32[64,4,3]{1,2,0:T(4,128)S(1)} %add_sqrt_fusion, f32[64,4,3]{1,2,0:T(4,128)S(1)} %copy.9), kind=kLoop, calls=%fused_computation.4 | loop fusion | flops 1572864 | bytes 1579008 | tf_op jit(solution)/shard_map/convert_element_type | solution.py:143
  4.6 1.6 %collective-permute-done = bf16[2,3,512]{2,0,1:T(2,128)(2,1)S(1)} collective-permute-done((bf16[2,3,512]{2,0,1:T(2,128)(2,1)}, bf16[2,3,512]{2,0,1:T(2,128)(2,1)S(1)}, u32[]{:S(2)}, u32[]{:S(2)}) %collective-permute-start) | collective-permute-done | bytes 6176 | tf_op jit(solution)/shard_map/ppermute | solution.py:92
  6.3 2.8 %collective-permute-start.1 = (bf16[2,4,1024]{2,0,1:T(2,128)(2,1)S(1)}, bf16[2,4,1024]{2,0,1:T(2,128)(2,1)S(1)}, u32[]{:S(2)}, u32[]{:S(2)}) collective-permute-start(bf16[2,4,1024]{2,0,1:T(2,128)(2,1)S(1)} %pad_maximum_fusion.5), channel_id=1, source_target_pairs={{0,4},{4,0},{8,12},{12,8},{1,5},{5,1},{9,13},{13,9},{2,6},{6,2},{1... | collective-permute-start | bytes 49160 | tf_op jit(solution)/shard_map/ppermute | solution.py:105
  9.1 1.7 %collective-permute-done.1 = bf16[2,4,1024]{2,0,1:T(2,128)(2,1)S(1)} collective-permute-done((bf16[2,4,1024]{2,0,1:T(2,128)(2,1)S(1)}, bf16[2,4,1024]{2,0,1:T(2,128)(2,1)S(1)}, u32[]{:S(2)}, u32[]{:S(2)}) %collective-permute-start.1) | collective-permute-done | bytes 16416 | tf_op jit(solution)/shard_map/ppermute | solution.py:105
  10.8 3.1 %collective-permute-start.2 = (bf16[4,4,1024]{2,0,1:T(4,128)(2,1)S(1)}, bf16[4,4,1024]{2,0,1:T(4,128)(2,1)S(1)}, u32[]{:S(2)}, u32[]{:S(2)}) collective-permute-start(bf16[4,4,1024]{2,0,1:T(4,128)(2,1)S(1)} %pad_maximum_fusion.4), channel_id=1, source_target_pairs={{0,8},{4,12},{8,0},{12,4},{1,9},{5,13},{9,1},{13,5},{2,10},{6,14},... | collective-permute-start | bytes 98312 | tf_op jit(solution)/shard_map/ppermute | solution.py:105
  14.1 0.6 %copy.10 = bf16[1,64,4,3,512]{4,3,2,1,0:T(4,128)(2,1)S(1)} copy(bf16[1,64,4,3,512]{4,2,3,1,0:T(4,128)(2,1)S(1)} %fusion.1) | data formatting | bytes 1572864 | tf_op jit(solution)/shard_map/convert_element_type | solution.py:143
  14.6 1.8 %reshape_reshape.4.n_ref = bf16[64,6144]{1,0:T(8,128)(2,1)} reshape(bf16[1,64,4,3,512]{4,3,2,1,0:T(4,128)(2,1)S(1)} %copy.10) | data formatting | bytes 1572864 | tf_op jit(solution)/shard_map/reshape;reshape | solution.py:69
  16.6 0.2 convert_reduce_fusion.1
  17.0 0.1 convolution_convert_fusion
  17.2 0.6 %mul.38.x_ref = bf16[96,128]{1,0:T(8,128)(2,1)} multiply(bf16[96,128]{1,0:T(8,128)(2,1)S(1)} %reshape.116, bf16[96,128]{1,0:T(8,128)(2,1)S(1)} %mul.37) | non-fusion elementwise | flops 12288 | bytes 73728 | tf_op jit(solution)/shard_map/mul | solution.py:136
  17.8 4.9 %shard_map.46 = f32[64,512]{1,0:T(8,128)} custom-call(bf16[96,128]{1,0:T(8,128)(2,1)} %mul.38.x_ref, bf16[64,6144]{1,0:T(8,128)(2,1)} %reshape_reshape.4.n_ref), custom_call_target="tpu_custom_call" | custom-call | tf_op jit(solution)/shard_map/pallas_call | solution.py:62
  22.7 1.6 %collective-permute-start.3 = (f32[64,512]{1,0:T(8,128)}, f32[64,512]{1,0:T(8,128)S(1)}, u32[]{:S(2)}, u32[]{:S(2)}) collective-permute-start(f32[64,512]{1,0:T(8,128)} %shard_map.46), channel_id=1, source_target_pairs={{0,4},{4,0},{8,12},{12,8},{1,5},{5,1},{9,13},{13,9},{2,6},{6,2},{1... | collective-permute-start | bytes 393224 | tf_op jit(solution)/shard_map/ppermute | solution.py:77
  24.3 3.6 %collective-permute-done.3 = f32[64,512]{1,0:T(8,128)S(1)} collective-permute-done((f32[64,512]{1,0:T(8,128)}, f32[64,512]{1,0:T(8,128)S(1)}, u32[]{:S(2)}, u32[]{:S(2)}) %collective-permute-start.3) | collective-permute-done | bytes 131104 | tf_op jit(solution)/shard_map/ppermute | solution.py:77
  27.9 0.9 %add.56 = f32[64,512]{1,0:T(8,128)S(1)} add(f32[64,512]{1,0:T(8,128)} %shard_map.46, f32[64,512]{1,0:T(8,128)S(1)} %collective-permute-done.3) | non-fusion elementwise | flops 32768 | bytes 393216 | tf_op jit(solution)/shard_map/add | solution.py:77
  28.8 2.4 %collective-permute-start.4 = (f32[64,512]{1,0:T(8,128)S(1)}, f32[64,512]{1,0:T(8,128)S(1)}, u32[]{:S(2)}, u32[]{:S(2)}) collective-permute-start(f32[64,512]{1,0:T(8,128)S(1)} %add.56), channel_id=1, source_target_pairs={{0,8},{4,12},{8,0},{12,4},{1,9},{5,13},{9,1},{13,5},{2,10},{6,14},... | collective-permute-start | bytes 393224 | tf_op jit(solution)/shard_map/ppermute | solution.py:77
  31.2 3.5 %collective-permute-done.4 = f32[64,512]{1,0:T(8,128)S(1)} collective-permute-done((f32[64,512]{1,0:T(8,128)S(1)}, f32[64,512]{1,0:T(8,128)S(1)}, u32[]{:S(2)}, u32[]{:S(2)}) %collective-permute-start.4) | collective-permute-done | bytes 131104 | tf_op jit(solution)/shard_map/ppermute | solution.py:77
  34.9 2.8 %collective-permute-start.5 = (f32[64]{0:T(128)S(1)}, f32[64]{0:T(128)S(1)}, u32[]{:S(2)}, u32[]{:S(2)}) collective-permute-start(f32[64]{0:T(128)S(1)} %get-tuple-element.5), channel_id=1, source_target_pairs={{0,2},{2,0},{1,3},{3,1},{4,6},{6,4},{5,7},{7,5},{8,10},{10,8},{9,1... | collective-permute-start | bytes 776 | tf_op jit(solution)/shard_map/ppermute | solution.py:77
  37.8 0.2 rev.3
  38.0 1.2 %collective-permute-done.5 = f32[64]{0:T(128)S(1)} collective-permute-done((f32[64]{0:T(128)S(1)}, f32[64]{0:T(128)S(1)}, u32[]{:S(2)}, u32[]{:S(2)}) %collective-permute-start.5) | collective-permute-done | bytes 288 | tf_op jit(solution)/shard_map/ppermute | solution.py:77
  39.2 0.7 %broadcast_divide_fusion = f32[1,64,512]{2,1,0:T(8,128)} fusion(f32[1,64,512]{2,1,0:T(8,128)S(1)} %reshape.118, f32[64]{0:T(128)S(1)} %add_sqrt_fusion.1), kind=kLoop, calls=%fused_computation.8 | loop fusion | flops 32768 | bytes 262400 | tf_op jit(solution)/shard_map/div | solution.py:148
  (26 shorter events, 1.0 us)
Async XLA Ops:
  0.0 4.0 %copy-start = (bf16[1,64,4,3,512]{4,2,3,1,0:T(4,128)(2,1)S(1)}, bf16[1,64,4,3,512]{4,2,3,1,0:T(4,128)(2,1)}, u32[]{:S(2)}) copy-start(bf16[1,64,4,3,512]{4,2,3,1,0:T(4,128)(2,1)} %param.5) | copy-start | bytes 2359300
  0.0 6.2 %collective-permute-start = (bf16[2,3,512]{2,0,1:T(2,128)(2,1)}, bf16[2,3,512]{2,0,1:T(2,128)(2,1)S(1)}, u32[]{:S(2)}, u32[]{:S(2)}) collective-permute-start(bf16[2,3,512]{2,0,1:T(2,128)(2,1)} %param.4), channel_id=1, source_target_pairs={{2,0},{3,1},{6,4},{7,5},{10,8},{11,9},{14,12},{15,13},{18,16},{19,... | collective-permute-start | bytes 18440 | tf_op jit(solution)/shard_map/ppermute | solution.py:92
  3.9 0.7 %copy-start.2 = (s32[2]{0:T(128)S(1)}, s32[2]{0:T(128)}, u32[]{:S(2)}) copy-start(s32[2]{0:T(128)} %param.7) | copy-start | bytes 28
  3.9 2.3 %copy-start.1 = (bf16[2,3,512]{2,0,1:T(2,128)(2,1)S(1)}, bf16[2,3,512]{2,0,1:T(2,128)(2,1)}, u32[]{:S(2)}) copy-start(bf16[2,3,512]{2,0,1:T(2,128)(2,1)} %param.4) | copy-start | bytes 18436
  6.3 4.5 %collective-permute-start.1 = (bf16[2,4,1024]{2,0,1:T(2,128)(2,1)S(1)}, bf16[2,4,1024]{2,0,1:T(2,128)(2,1)S(1)}, u32[]{:S(2)}, u32[]{:S(2)}) collective-permute-start(bf16[2,4,1024]{2,0,1:T(2,128)(2,1)S(1)} %pad_maximum_fusion.5), channel_id=1, source_target_pairs={{0,4},{4,0},{8,12},{12,8},{1,5},{5,1},{9,13},{13,9},{2,6},{6,2},{1... | collective-permute-start | bytes 49160 | tf_op jit(solution)/shard_map/ppermute | solution.py:105
  10.8 5.7 %collective-permute-start.2 = (bf16[4,4,1024]{2,0,1:T(4,128)(2,1)S(1)}, bf16[4,4,1024]{2,0,1:T(4,128)(2,1)S(1)}, u32[]{:S(2)}, u32[]{:S(2)}) collective-permute-start(bf16[4,4,1024]{2,0,1:T(4,128)(2,1)S(1)} %pad_maximum_fusion.4), channel_id=1, source_target_pairs={{0,8},{4,12},{8,0},{12,4},{1,9},{5,13},{9,1},{13,5},{2,10},{6,14},... | collective-permute-start | bytes 98312 | tf_op jit(solution)/shard_map/ppermute | solution.py:105
  22.7 5.2 %collective-permute-start.3 = (f32[64,512]{1,0:T(8,128)}, f32[64,512]{1,0:T(8,128)S(1)}, u32[]{:S(2)}, u32[]{:S(2)}) collective-permute-start(f32[64,512]{1,0:T(8,128)} %shard_map.46), channel_id=1, source_target_pairs={{0,4},{4,0},{8,12},{12,8},{1,5},{5,1},{9,13},{13,9},{2,6},{6,2},{1... | collective-permute-start | bytes 393224 | tf_op jit(solution)/shard_map/ppermute | solution.py:77
  28.8 5.9 %collective-permute-start.4 = (f32[64,512]{1,0:T(8,128)S(1)}, f32[64,512]{1,0:T(8,128)S(1)}, u32[]{:S(2)}, u32[]{:S(2)}) collective-permute-start(f32[64,512]{1,0:T(8,128)S(1)} %add.56), channel_id=1, source_target_pairs={{0,8},{4,12},{8,0},{12,4},{1,9},{5,13},{9,1},{13,5},{2,10},{6,14},... | collective-permute-start | bytes 393224 | tf_op jit(solution)/shard_map/ppermute | solution.py:77
  34.9 4.4 %collective-permute-start.5 = (f32[64]{0:T(128)S(1)}, f32[64]{0:T(128)S(1)}, u32[]{:S(2)}, u32[]{:S(2)}) collective-permute-start(f32[64]{0:T(128)S(1)} %get-tuple-element.5), channel_id=1, source_target_pairs={{0,2},{2,0},{1,3},{3,1},{4,6},{6,4},{5,7},{7,5},{8,10},{10,8},{9,1... | collective-permute-start | bytes 776 | tf_op jit(solution)/shard_map/ppermute | solution.py:77

commit v14 on v12

--- a/solution.py
+++ b/solution.py
@@ -55,13 +55,15 @@
 
 
 def correlate(normed, flat_owned, seg_len):
-    rows, channels, filter_taps = normed.shape
+    channels = flat_owned.shape[0]
+    rows = normed.shape[0]
+    filter_taps = normed.shape[1] // channels
     blocks = flat_owned.reshape(channels * (flat_owned.shape[1] // 128), 128)[:, ::-1]
     return pl.pallas_call(
         hankel_kernel,
         out_shape=jax.ShapeDtypeStruct((rows, seg_len), jnp.float32),
         scratch_shapes=[pltpu.VMEM((2, filter_taps, seg_len), jnp.bfloat16)],
-    )(blocks, normed.reshape(rows, channels * filter_taps))
+    )(blocks, normed)
 
 
 def ordered_sum(part, axis):
@@ -80,7 +82,7 @@
     return jnp.sum(jnp.take(jnp.stack(received), order, axis=0), axis=0)
 
 
-def gather_owned(records, station_region, capacity, filter_taps):
+def gather_owned(records, station_region, capacity, filter_taps, prepared):
     local_count, components, seg_len = records.shape
     regions = lax.axis_size("region")
     segs = lax.axis_size("seg")
@@ -98,6 +100,8 @@
         step = 1
         while step < regions:
             theirs = lax.ppermute(here, "region", [(r, r ^ step) for r in range(regions)])
+            if step == 1:
+                theirs, prepared = lax.optimization_barrier((theirs, prepared))
             here = jnp.concatenate([here, theirs], axis=0)
             step *= 2
         source = me ^ jnp.arange(regions, dtype=jnp.int32)[:, None]
@@ -121,22 +125,22 @@
     ).astype(jnp.bfloat16)
     owned_rows = owned_rows.reshape(capacity, components, seg_len + filter_taps)
     filled = jnp.sum(placing.astype(jnp.float32), axis=1)
-    return owned_rows, filled
+    return owned_rows, filled, prepared
 
 
 def per_device(records, templates, channel_mask, station_region):
     local_batches, kept, capacity, components, filter_taps = templates.shape
     seg_len = records.shape[2]
-    owned_rows, filled = gather_owned(records, station_region, capacity, filter_taps)
-    owned_rows = owned_rows.astype(jnp.float32) * filled[:, None, None]
-    flat_owned = owned_rows.reshape(capacity * components, seg_len + filter_taps)
     weight = channel_mask.astype(jnp.float32)
     widened_templates = templates.astype(jnp.float32)
     template_norm = jnp.sqrt(
         jnp.sum(widened_templates * widened_templates, axis=4, keepdims=True) + 1e-06
     )
     normed = (widened_templates * weight[..., None] / template_norm).astype(jnp.bfloat16)
-    normed = normed.reshape(local_batches * kept, capacity * components, filter_taps)
+    normed = normed.reshape(local_batches * kept, capacity * components * filter_taps)
+    owned_rows, filled, normed = gather_owned(records, station_region, capacity, filter_taps, normed)
+    owned_rows = owned_rows.astype(jnp.float32) * filled[:, None, None]
+    flat_owned = owned_rows.reshape(capacity * components, seg_len + filter_taps)
     total_len = seg_len * lax.axis_size("seg")
     stacked = ordered_sum(correlate(normed, flat_owned, seg_len), "region")
     power_sum = ordered_sum(jnp.sum(stacked * stacked, axis=1), "seg")

time: 40.3 us -> 41.8 us (1.037)
  waiting for transfers between devices: 11.6 us -> 15.6 us
  starting transfers between devices: 14.1 us -> 12.4 us
  other arithmetic: 5.37 us -> 4.66 us
    ppermute x3, waiting for transfers between devices: 8.34 us -> 11.2 us  [ordered_sum(): part = part + lax.ppermute(part, axis, [(i, i ^ step) for i in range(size)])]
    another operation x1 -> x0, local copies, waits for them, and re-layouts: 1.84 us -> none  [correlate(): normed.reshape(rows, channels * filter_taps)]
    reshape x0 -> x1, local copies, waits for them, and re-layouts: none -> 1.84 us  [per_device(): normed.reshape(local_batches * kept, capacity * components * filter_taps)]
    ppermute x3, starting transfers between devices: 6.83 us -> 5.59 us  [ordered_sum(): part = part + lax.ppermute(part, axis, [(i, i ^ step) for i in range(size)])]
    mul x1, other arithmetic: 0.7 us -> 0.01 us  [per_device(): widened_templates * weight[..., None] / template_norm]
    ppermute x1, waiting for transfers between devices: 1.57 us -> 2.26 us  [gather_owned(): lax.ppermute(records[:, :, :filter_taps], 'seg', [(s + 1, s) for s in ran...]
    ppermute x2, starting transfers between devices: 5.89 us -> 5.44 us  [gather_owned(): lax.ppermute(here, 'region', [(r, r ^ step) for r in range(regions)])]
  transfers between devices with their start and end apart: 6 -> 6, of which waited for: 5 -> 5; matrix products, arithmetic and copies ran while one was open for 15% -> 13% of each run, Pallas kernels for 0% -> 0%
where the time goes in v14:
time: 41.8 us; the launch traced here: 41.6 us
  waiting for transfers between devices  15.6 us (37%)
  starting transfers between devices  12.4 us (30%)
  Pallas kernels  4.75 us (11%)
  other arithmetic  4.66 us (11%)
  local copies, waits for them, and re-layouts  3.81 us (9%)
    ppermute x3, waiting for transfers between devices, ordered_sum(): part = part + lax.ppermute(part, axis, [(i, i ^ step) for i in range(size)])  11.2 us
    ppermute x3, starting transfers between devices, ordered_sum(): part = part + lax.ppermute(part, axis, [(i, i ^ step) for i in range(size)])  5.59 us
    ppermute x2, starting transfers between devices, gather_owned(): lax.ppermute(here, 'region', [(r, r ^ step) for r in range(regions)])  5.44 us
    pallas_call x1, Pallas kernels, correlate(): pl.pallas_call(hankel_kernel, out_shape=jax.ShapeDtypeStruct((rows, seg_l...  4.75 us
    ppermute x1, waiting for transfers between devices, gather_owned(): lax.ppermute(records[:, :, :filter_taps], 'seg', [(s + 1, s) for s in ran...  2.26 us
    ppermute x2, waiting for transfers between devices, gather_owned(): lax.ppermute(here, 'region', [(r, r ^ step) for r in range(regions)])  2.07 us
    reshape x1, local copies, waits for them, and re-layouts, per_device(): normed.reshape(local_batches * kept, capacity * components * filter_taps)  1.84 us
    reduce_sum x1, other arithmetic, per_device(): jnp.sum(widened_templates * widened_templates, axis=4, keepdims=True)  1.65 us
  transfers between devices with their start and end apart: 6, of which 5 were waited for; matrix products, arithmetic and copies ran while one was open for 13% of the time, Pallas kernels for 0%

profile of v14, /device:TPU:0, one launch (start us, length us, event | category | flops | bytes accessed | tf_op | source)
XLA Modules:
  0.0 41.6 jit_solution(11794795708960348978)
XLA Ops:
  0.0 1.4 %collective-permute-start = (bf16[2,3,512]{2,0,1:T(2,128)(2,1)}, bf16[2,3,512]{2,0,1:T(2,128)(2,1)S(1)}, u32[]{:S(2)}, u32[]{:S(2)}) collective-permute-start(bf16[2,3,512]{2,0,1:T(2,128)(2,1)} %param.4), channel_id=1, source_target_pairs={{2,0},{3,1},{6,4},{7,5},{10,8},{11,9},{14,12},{15,13},{18,16},{19,... | collective-permute-start | bytes 18440 | tf_op jit(solution)/shard_map/ppermute | solution.py:89
  1.4 1.6 %fusion.3 = f32[64,4,3]{1,2,0:T(4,128)S(1)} fusion(bf16[1,64,4,3,512]{4,2,3,1,0:T(4,128)(2,1)} %param.5), kind=kLoop, calls=%fused_computation.6 | loop fusion | flops 1178880 | bytes 789504 | tf_op jit(solution)/shard_map/reduce_sum | solution.py:137
  3.2 0.1 copy.9
  3.4 0.5 %fusion.2 = bf16[1,64,4,3,512]{4,2,3,1,0:T(4,128)(2,1)S(1)} fusion(bf16[1,64,4,3,512]{4,2,3,1,0:T(4,128)(2,1)S(1)} %copy-done, f32[64,4,3]{1,2,0:T(4,128)S(1)} %add_sqrt_fusion, f32[64,4,3]{1,2,0:T(4,128)S(1)} %copy.9), kind=kLoop, calls=%fused_computation.5 | loop fusion | flops 1572864 | bytes 1579008 | tf_op jit(solution)/shard_map/convert_element_type | solution.py:139
  3.9 2.3 %collective-permute-done = bf16[2,3,512]{2,0,1:T(2,128)(2,1)S(1)} collective-permute-done((bf16[2,3,512]{2,0,1:T(2,128)(2,1)}, bf16[2,3,512]{2,0,1:T(2,128)(2,1)S(1)}, u32[]{:S(2)}, u32[]{:S(2)}) %collective-permute-start) | collective-permute-done | bytes 6176 | tf_op jit(solution)/shard_map/ppermute | solution.py:89
  6.3 2.8 %collective-permute-start.1 = (bf16[2,4,1024]{2,0,1:T(2,128)(2,1)S(1)}, bf16[2,4,1024]{2,0,1:T(2,128)(2,1)S(1)}, u32[]{:S(2)}, u32[]{:S(2)}) collective-permute-start(bf16[2,4,1024]{2,0,1:T(2,128)(2,1)S(1)} %pad_maximum_fusion.5), channel_id=1, source_target_pairs={{0,4},{4,0},{8,12},{12,8},{1,5},{5,1},{9,13},{13,9},{2,6},{6,2},{1... | collective-permute-start | bytes 49160 | tf_op jit(solution)/shard_map/ppermute | solution.py:102
  9.1 0.6 %copy.10 = bf16[1,64,4,3,512]{4,3,2,1,0:T(4,128)(2,1)S(1)} copy(bf16[1,64,4,3,512]{4,2,3,1,0:T(4,128)(2,1)S(1)} %fusion.2) | data formatting | bytes 1572864 | tf_op jit(solution)/shard_map/convert_element_type | solution.py:139
  9.6 1.8 %reshape.116.n_ref = bf16[64,6144]{1,0:T(8,128)(2,1)} reshape(bf16[1,64,4,3,512]{4,3,2,1,0:T(4,128)(2,1)S(1)} %copy.10) | data formatting | bytes 1572864 | tf_op jit(solution)/shard_map/reshape | solution.py:140
  11.5 2.7 %collective-permute-start.2 = (bf16[4,4,1024]{2,0,1:T(4,128)(2,1)S(1)}, bf16[4,4,1024]{2,0,1:T(4,128)(2,1)S(1)}, u32[]{:S(2)}, u32[]{:S(2)}) collective-permute-start(bf16[4,4,1024]{2,0,1:T(4,128)(2,1)S(1)} %pad_maximum_fusion.4), channel_id=1, source_target_pairs={{0,8},{4,12},{8,0},{12,4},{1,9},{5,13},{9,1},{13,5},{2,10},{6,14},... | collective-permute-start | bytes 98312 | tf_op jit(solution)/shard_map/ppermute | solution.py:102
  14.3 2.1 %collective-permute-done.2 = bf16[4,4,1024]{2,0,1:T(4,128)(2,1)S(1)} collective-permute-done((bf16[4,4,1024]{2,0,1:T(4,128)(2,1)S(1)}, bf16[4,4,1024]{2,0,1:T(4,128)(2,1)S(1)}, u32[]{:S(2)}, u32[]{:S(2)}) %collective-permute-start.2) | collective-permute-done | bytes 32800 | tf_op jit(solution)/shard_map/ppermute | solution.py:102
  16.4 0.1 convert_reduce_fusion
  16.5 0.2 convert_reduce_fusion.1
  17.0 0.1 fusion
  17.2 0.7 %rev.6.x_ref = f32[96,128]{1,0:T(8,128)} reverse(f32[96,128]{1,0:T(8,128)S(1)} %mul.42), dimensions={1} | reverse | bytes 98304 | tf_op jit(solution)/shard_map/rev | solution.py:61
  17.9 4.8 %shard_map.46 = f32[64,512]{1,0:T(8,128)} custom-call(f32[96,128]{1,0:T(8,128)} %rev.6.x_ref, bf16[64,6144]{1,0:T(8,128)(2,1)} %reshape.116.n_ref), custom_call_target="tpu_custom_call" | custom-call | tf_op jit(solution)/shard_map/pallas_call | solution.py:62
  22.6 1.3 %collective-permute-start.3 = (f32[64,512]{1,0:T(8,128)}, f32[64,512]{1,0:T(8,128)S(1)}, u32[]{:S(2)}, u32[]{:S(2)}) collective-permute-start(f32[64,512]{1,0:T(8,128)} %shard_map.46), channel_id=1, source_target_pairs={{0,4},{4,0},{8,12},{12,8},{1,5},{5,1},{9,13},{13,9},{2,6},{6,2},{1... | collective-permute-start | bytes 393224 | tf_op jit(solution)/shard_map/ppermute | solution.py:74
  24.0 3.8 %collective-permute-done.3 = f32[64,512]{1,0:T(8,128)S(1)} collective-permute-done((f32[64,512]{1,0:T(8,128)}, f32[64,512]{1,0:T(8,128)S(1)}, u32[]{:S(2)}, u32[]{:S(2)}) %collective-permute-start.3) | collective-permute-done | bytes 131104 | tf_op jit(solution)/shard_map/ppermute | solution.py:74
  27.8 0.9 %add.56 = f32[64,512]{1,0:T(8,128)S(1)} add(f32[64,512]{1,0:T(8,128)} %shard_map.46, f32[64,512]{1,0:T(8,128)S(1)} %collective-permute-done.3) | non-fusion elementwise | flops 32768 | bytes 393216 | tf_op jit(solution)/shard_map/add | solution.py:74
  28.7 4.0 %collective-permute-start.4 = (f32[64,512]{1,0:T(8,128)S(1)}, f32[64,512]{1,0:T(8,128)S(1)}, u32[]{:S(2)}, u32[]{:S(2)}) collective-permute-start(f32[64,512]{1,0:T(8,128)S(1)} %add.56), channel_id=1, source_target_pairs={{0,8},{4,12},{8,0},{12,4},{1,9},{5,13},{9,1},{13,5},{2,10},{6,14},... | collective-permute-start | bytes 393224 | tf_op jit(solution)/shard_map/ppermute | solution.py:74
  32.7 4.4 %collective-permute-done.4 = f32[64,512]{1,0:T(8,128)S(1)} collective-permute-done((f32[64,512]{1,0:T(8,128)S(1)}, f32[64,512]{1,0:T(8,128)S(1)}, u32[]{:S(2)}, u32[]{:S(2)}) %collective-permute-start.4) | collective-permute-done | bytes 131104 | tf_op jit(solution)/shard_map/ppermute | solution.py:74
  37.2 0.2 collective-permute-start.5
  37.5 0.2 rev.7
  37.7 3.1 %collective-permute-done.5 = f32[64]{0:T(128)S(1)} collective-permute-done((f32[64]{0:T(128)S(1)}, f32[64]{0:T(128)S(1)}, u32[]{:S(2)}, u32[]{:S(2)}) %collective-permute-start.5) | collective-permute-done | bytes 288 | tf_op jit(solution)/shard_map/ppermute | solution.py:74
  40.8 0.7 %broadcast_divide_fusion = f32[1,64,512]{2,1,0:T(8,128)} fusion(f32[1,64,512]{2,1,0:T(8,128)S(1)} %reshape.119, f32[64]{0:T(128)S(1)} %add_sqrt_fusion.1), kind=kLoop, calls=%fused_computation.9 | loop fusion | flops 32768 | bytes 262400 | tf_op jit(solution)/shard_map/div | solution.py:147
  (29 shorter events, 0.9 us)
Async XLA Ops:
  0.0 3.3 %copy-start = (bf16[1,64,4,3,512]{4,2,3,1,0:T(4,128)(2,1)S(1)}, bf16[1,64,4,3,512]{4,2,3,1,0:T(4,128)(2,1)}, u32[]{:S(2)}) copy-start(bf16[1,64,4,3,512]{4,2,3,1,0:T(4,128)(2,1)} %param.5) | copy-start | bytes 2359300
  0.0 3.2 %copy-start.2 = (s32[1,64,4,3]{1,2,3,0:T(4,128)S(1)}, s32[1,64,4,3]{1,2,3,0:T(4,128)}, u32[]{:S(2)}) copy-start(s32[1,64,4,3]{1,2,3,0:T(4,128)} %param.6) | copy-start | bytes 9220
  0.0 6.2 %collective-permute-start = (bf16[2,3,512]{2,0,1:T(2,128)(2,1)}, bf16[2,3,512]{2,0,1:T(2,128)(2,1)S(1)}, u32[]{:S(2)}, u32[]{:S(2)}) collective-permute-start(bf16[2,3,512]{2,0,1:T(2,128)(2,1)} %param.4), channel_id=1, source_target_pairs={{2,0},{3,1},{6,4},{7,5},{10,8},{11,9},{14,12},{15,13},{18,16},{19,... | collective-permute-start | bytes 18440 | tf_op jit(solution)/shard_map/ppermute | solution.py:89
  3.2 0.7 %copy-start.3 = (s32[2]{0:T(128)S(1)}, s32[2]{0:T(128)}, u32[]{:S(2)}) copy-start(s32[2]{0:T(128)} %param.7) | copy-start | bytes 28
  3.2 3.1 %copy-start.1 = (bf16[2,3,512]{2,0,1:T(2,128)(2,1)S(1)}, bf16[2,3,512]{2,0,1:T(2,128)(2,1)}, u32[]{:S(2)}) copy-start(bf16[2,3,512]{2,0,1:T(2,128)(2,1)} %param.4) | copy-start | bytes 18436
  6.3 5.2 %collective-permute-start.1 = (bf16[2,4,1024]{2,0,1:T(2,128)(2,1)S(1)}, bf16[2,4,1024]{2,0,1:T(2,128)(2,1)S(1)}, u32[]{:S(2)}, u32[]{:S(2)}) collective-permute-start(bf16[2,4,1024]{2,0,1:T(2,128)(2,1)S(1)} %pad_maximum_fusion.5), channel_id=1, source_target_pairs={{0,4},{4,0},{8,12},{12,8},{1,5},{5,1},{9,13},{13,9},{2,6},{6,2},{1... | collective-permute-start | bytes 49160 | tf_op jit(solution)/shard_map/ppermute | solution.py:102
  11.5 4.9 %collective-permute-start.2 = (bf16[4,4,1024]{2,0,1:T(4,128)(2,1)S(1)}, bf16[4,4,1024]{2,0,1:T(4,128)(2,1)S(1)}, u32[]{:S(2)}, u32[]{:S(2)}) collective-permute-start(bf16[4,4,1024]{2,0,1:T(4,128)(2,1)S(1)} %pad_maximum_fusion.4), channel_id=1, source_target_pairs={{0,8},{4,12},{8,0},{12,4},{1,9},{5,13},{9,1},{13,5},{2,10},{6,14},... | collective-permute-start | bytes 98312 | tf_op jit(solution)/shard_map/ppermute | solution.py:102
  22.6 5.2 %collective-permute-start.3 = (f32[64,512]{1,0:T(8,128)}, f32[64,512]{1,0:T(8,128)S(1)}, u32[]{:S(2)}, u32[]{:S(2)}) collective-permute-start(f32[64,512]{1,0:T(8,128)} %shard_map.46), channel_id=1, source_target_pairs={{0,4},{4,0},{8,12},{12,8},{1,5},{5,1},{9,13},{13,9},{2,6},{6,2},{1... | collective-permute-start | bytes 393224 | tf_op jit(solution)/shard_map/ppermute | solution.py:74
  28.7 8.4 %collective-permute-start.4 = (f32[64,512]{1,0:T(8,128)S(1)}, f32[64,512]{1,0:T(8,128)S(1)}, u32[]{:S(2)}, u32[]{:S(2)}) collective-permute-start(f32[64,512]{1,0:T(8,128)S(1)} %add.56), channel_id=1, source_target_pairs={{0,8},{4,12},{8,0},{12,4},{1,9},{5,13},{9,1},{13,5},{2,10},{6,14},... | collective-permute-start | bytes 393224 | tf_op jit(solution)/shard_map/ppermute | solution.py:74
  37.2 3.6 %collective-permute-start.5 = (f32[64]{0:T(128)S(1)}, f32[64]{0:T(128)S(1)}, u32[]{:S(2)}, u32[]{:S(2)}) collective-permute-start(f32[64]{0:T(128)S(1)} %get-tuple-element.9), channel_id=1, source_target_pairs={{0,2},{2,0},{1,3},{3,1},{4,6},{6,4},{5,7},{7,5},{8,10},{10,8},{9,1... | collective-permute-start | bytes 776 | tf_op jit(solution)/shard_map/ppermute | solution.py:74

commit v15 on v12

--- a/solution.py
+++ b/solution.py
@@ -84,34 +84,25 @@
     local_count, components, seg_len = records.shape
     regions = lax.axis_size("region")
     segs = lax.axis_size("seg")
-    ahead = lax.ppermute(
-        records[:, :, :filter_taps], "seg", [(s + 1, s) for s in range(segs - 1)]
-    )
-    tag = jnp.broadcast_to(station_region.astype(jnp.bfloat16)[:, None, None], (local_count, 1, seg_len + filter_taps))
-    payload = jnp.concatenate(
-        [jnp.concatenate([records, ahead], axis=2), tag], axis=1
-    )
+    tag = jnp.broadcast_to(station_region.astype(jnp.bfloat16)[:, None, None], (local_count, 1, seg_len))
+    payload = jnp.concatenate([records, tag], axis=1)
+    everyone = regions * segs
+    spread = jnp.broadcast_to(payload[None], (everyone,) + payload.shape)
+    arrived = lax.all_to_all(spread, ("region", "seg"), 0, 0, tiled=True)
+    arrived = arrived.reshape(regions, segs, local_count, components + 1, seg_len)
     me = lax.axis_index("region")
+    seg_index = lax.axis_index("seg")
     stations = regions * local_count
-    if regions & (regions - 1) == 0:
-        here = payload
-        step = 1
-        while step < regions:
-            theirs = lax.ppermute(here, "region", [(r, r ^ step) for r in range(regions)])
-            here = jnp.concatenate([here, theirs], axis=0)
-            step *= 2
-        source = me ^ jnp.arange(regions, dtype=jnp.int32)[:, None]
-    else:
-        gathered = [payload] + [
-            lax.ppermute(payload, "region", [(r, (r + k) % regions) for r in range(regions)])
-            for k in range(1, regions)
-        ]
-        here = jnp.concatenate(gathered, axis=0)
-        source = (me - jnp.arange(regions, dtype=jnp.int32)[:, None]) % regions
+    here = jnp.take(arrived, seg_index, axis=1)
+    following = jnp.take(arrived, jnp.minimum(seg_index + 1, segs - 1), axis=1)[:, :, :components, :filter_taps]
+    following = jnp.where(seg_index + 1 < segs, following, jnp.zeros_like(following))
+    here = here.reshape(stations, components + 1, seg_len)
+    following = following.reshape(stations, components, filter_taps)
     local = jnp.arange(local_count, dtype=jnp.int32)[None, :]
+    source = jnp.arange(regions, dtype=jnp.int32)[:, None]
     station_ids = (source * local_count + local).reshape(stations)
     region_of = here[:, components, 0].astype(jnp.int32)
-    rows = here[:, :components, :]
+    rows = jnp.concatenate([here[:, :components, :], following], axis=2)
     earlier = (region_of[None, :] == region_of[:, None]) & (station_ids[None, :] < station_ids[:, None])
     ranks = jnp.sum(earlier.astype(jnp.int32), axis=1)
     slot_index = jnp.arange(capacity, dtype=jnp.int32)

time: 40.3 us -> 41 us (1.017)
  starting transfers between devices: 14.1 us -> 10.6 us
  waiting for transfers between devices: 11.6 us -> 13.6 us
  other arithmetic: 5.37 us -> 6.9 us
  local copies, waits for them, and re-layouts: 3.81 us -> 4.47 us
    ppermute x3 -> x0, starting transfers between devices: 7.3 us -> none  [the longest x2 5.89 us: gather_owned(): lax.ppermute(here, 'region', [(r, r ^ step) for r in range(regions)])]
    all_to_all x0 -> x1, starting transfers between devices: none -> 7.25 us  [gather_owned(): arrived = lax.all_to_all(spread, ('region', 'seg'), 0, 0, tiled=True)]
    ppermute x3, waiting for transfers between devices: 8.34 us -> 12.4 us  [ordered_sum(): part = part + lax.ppermute(part, axis, [(i, i ^ step) for i in range(size)])]
    ppermute x3, starting transfers between devices: 6.83 us -> 3.39 us  [ordered_sum(): part = part + lax.ppermute(part, axis, [(i, i ^ step) for i in range(size)])]
    ppermute x3 -> x0, waiting for transfers between devices: 3.29 us -> none  [the longest x2 1.72 us: gather_owned(): lax.ppermute(here, 'region', [(r, r ^ step) for r in range(regions)])]
    all_to_all x0 -> x1, waiting for transfers between devices: none -> 1.23 us  [gather_owned(): arrived = lax.all_to_all(spread, ('region', 'seg'), 0, 0, tiled=True)]
    convert_element_type x1, other arithmetic: 0.01 us -> 0.73 us  [gather_owned(): station_region.astype(jnp.bfloat16)[:, None, None]]
    broadcast_in_dim x0 -> x1, local copies, waits for them, and re-layouts: none -> 0.65 us  [gather_owned(): spread = jnp.broadcast_to(payload[None], (everyone,) + payload.shape)]
  transfers between devices with their start and end apart: 6 -> 4, of which waited for: 5 -> 4; matrix products, arithmetic and copies ran while one was open for 15% -> 15% of each run, Pallas kernels for 0% -> 0%
where the time goes in v15:
time: 41 us; the launch traced here: 40.7 us
  waiting for transfers between devices  13.6 us (33%)
  starting transfers between devices  10.6 us (26%)
  other arithmetic  6.9 us (17%)
  Pallas kernels  4.75 us (12%)
  local copies, waits for them, and re-layouts  4.47 us (11%)
    ppermute x3, waiting for transfers between devices, ordered_sum(): part = part + lax.ppermute(part, axis, [(i, i ^ step) for i in range(size)])  12.4 us
    all_to_all x1, starting transfers between devices, gather_owned(): arrived = lax.all_to_all(spread, ('region', 'seg'), 0, 0, tiled=True)  7.25 us
    pallas_call x1, Pallas kernels, correlate(): pl.pallas_call(hankel_kernel, out_shape=jax.ShapeDtypeStruct((rows, seg_l...  4.75 us
    ppermute x3, starting transfers between devices, ordered_sum(): part = part + lax.ppermute(part, axis, [(i, i ^ step) for i in range(size)])  3.39 us
    another operation x1, local copies, waits for them, and re-layouts, correlate(): normed.reshape(rows, channels * filter_taps)  1.84 us
    reduce_sum x1, other arithmetic, per_device(): jnp.sum(widened_templates * widened_templates, axis=4, keepdims=True)  1.65 us
    all_to_all x1, waiting for transfers between devices, gather_owned(): arrived = lax.all_to_all(spread, ('region', 'seg'), 0, 0, tiled=True)  1.23 us
    add x1, other arithmetic, ordered_sum(): part = part + lax.ppermute(part, axis, [(i, i ^ step) for i in range(size)])  0.93 us
  transfers between devices with their start and end apart: 4, of which 4 were waited for; matrix products, arithmetic and copies ran while one was open for 15% of the time, Pallas kernels for 0%

profile of v15, /device:TPU:0, one launch (start us, length us, event | category | flops | bytes accessed | tf_op | source)
XLA Modules:
  0.0 40.7 jit_solution(7686211014012168828)
XLA Ops:
  0.0 0.7 %convert_element_type.46 = bf16[2]{0:T(256)(128)(2,1)S(1)} convert(s32[2]{0:T(128)} %param.9) | non-fusion elementwise | flops 2 | bytes 12 | tf_op jit(solution)/shard_map/convert_element_type | solution.py:87
  0.8 0.7 %pad_maximum_fusion = bf16[2,4,512]{2,0,1:T(2,128)(2,1)S(1)} fusion(bf16[2,1,512]{2,0,1:T(2,128)(2,1)S(1)} %broadcast_in_dim.15, bf16[2,3,512]{2,0,1:T(2,128)(2,1)} %param.6), kind=kLoop, calls=%fused_computation.14 | loop fusion | flops 4096 | bytes 16384 | tf_op jit(solution)/shard_map/concatenate | solution.py:88
  1.5 0.6 %broadcast_in_dim.16 = bf16[8,2,4,512]{3,2,1,0:T(4,128)(2,1)} broadcast(bf16[2,4,512]{2,1,0:T(4,128)(2,1)S(1)} %copy.18), dimensions={1,2,3} | broadcast | bytes 73728 | tf_op jit(solution)/shard_map/broadcast_in_dim | solution.py:90
  2.2 7.3 %all-to-all-start = ((bf16[8,2,4,512]{3,2,1,0:T(4,128)(2,1)}), bf16[8,2,4,512]{3,2,1,0:T(4,128)(2,1)S(1)}, u32[]{:S(2)}, u32[]{:S(2)}) async-start(bf16[8,2,4,512]{3,2,1,0:T(4,128)(2,1)} %broadcast_in_dim.16), calls=%async_computation | async-start | bytes 131072 | tf_op jit(solution)/shard_map/all_to_all | solution.py:91
  9.4 0.7 %convert_bitcast_fusion = f32[64,4,3]{0,1,2:T(4,128)S(1)} fusion(s32[1,64,4,3]{1,2,3,0:T(4,128)} %param.8), kind=kLoop, calls=%fused_computation.15 | loop fusion | flops 768 | bytes 6144 | tf_op jit(solution)/shard_map/mul | solution.py:129
  10.3 1.7 %fusion.3 = f32[64,4,3]{1,2,0:T(4,128)S(1)} fusion(bf16[1,64,4,3,512]{4,2,3,1,0:T(4,128)(2,1)} %param.7), kind=kLoop, calls=%fused_computation.6 | loop fusion | flops 1178880 | bytes 789504 | tf_op jit(solution)/shard_map/reduce_sum | solution.py:127
  12.0 0.5 %fusion.2 = bf16[1,64,4,3,512]{4,2,3,1,0:T(4,128)(2,1)S(1)} fusion(bf16[1,64,4,3,512]{4,2,3,1,0:T(4,128)(2,1)S(1)} %copy-done, f32[64,4,3]{1,2,0:T(4,128)S(1)} %add_sqrt_fusion, f32[64,4,3]{1,2,0:T(4,128)S(1)} %copy.21), kind=kLoop, calls=%fused_computation.5 | loop fusion | flops 1572864 | bytes 1579008 | tf_op jit(solution)/shard_map/convert_element_type | solution.py:129
  12.7 0.6 %copy.22 = bf16[1,64,4,3,512]{4,3,2,1,0:T(4,128)(2,1)S(1)} copy(bf16[1,64,4,3,512]{4,2,3,1,0:T(4,128)(2,1)S(1)} %fusion.2) | data formatting | bytes 1572864 | tf_op jit(solution)/shard_map/convert_element_type | solution.py:129
  13.3 1.8 %reshape_reshape.4.n_ref = bf16[64,6144]{1,0:T(8,128)(2,1)} reshape(bf16[1,64,4,3,512]{4,3,2,1,0:T(4,128)(2,1)S(1)} %copy.22) | data formatting | bytes 1572864 | tf_op jit(solution)/shard_map/reshape;reshape | solution.py:64
  15.1 1.2 %all-to-all-done = bf16[8,2,4,512]{3,2,1,0:T(4,128)(2,1)S(1)} async-done(((bf16[8,2,4,512]{3,2,1,0:T(4,128)(2,1)}), bf16[8,2,4,512]{3,2,1,0:T(4,128)(2,1)S(1)}, u32[]{:S(2)}, u32[]{:S(2)}) %all-to-all-start) | async-done | bytes 65568 | tf_op jit(solution)/shard_map/all_to_all | solution.py:91
  16.4 0.2 fusion.4
  16.6 0.2 convert_reduce_fusion
  17.0 0.1 fusion
  17.3 0.7 %rev.6.x_ref = f32[96,128]{1,0:T(8,128)} reverse(f32[96,128]{1,0:T(8,128)S(1)} %mul.38), dimensions={1} | reverse | bytes 98304 | tf_op jit(solution)/shard_map/rev | solution.py:59
  18.0 4.8 %shard_map.46 = f32[64,512]{1,0:T(8,128)} custom-call(f32[96,128]{1,0:T(8,128)} %rev.6.x_ref, bf16[64,6144]{1,0:T(8,128)(2,1)} %reshape_reshape.4.n_ref), custom_call_target="tpu_custom_call" | custom-call | tf_op jit(solution)/shard_map/pallas_call | solution.py:60
  22.8 0.8 %collective-permute-start = (f32[64,512]{1,0:T(8,128)}, f32[64,512]{1,0:T(8,128)S(1)}, u32[]{:S(2)}, u32[]{:S(2)}) collective-permute-start(f32[64,512]{1,0:T(8,128)} %shard_map.46), channel_id=1, source_target_pairs={{0,4},{4,0},{8,12},{12,8},{1,5},{5,1},{9,13},{13,9},{2,6},{6,2},{1... | collective-permute-start | bytes 393224 | tf_op jit(solution)/shard_map/ppermute | solution.py:72
  23.6 4.4 %collective-permute-done = f32[64,512]{1,0:T(8,128)S(1)} collective-permute-done((f32[64,512]{1,0:T(8,128)}, f32[64,512]{1,0:T(8,128)S(1)}, u32[]{:S(2)}, u32[]{:S(2)}) %collective-permute-start) | collective-permute-done | bytes 131104 | tf_op jit(solution)/shard_map/ppermute | solution.py:72
  28.0 0.9 %add.64 = f32[64,512]{1,0:T(8,128)S(1)} add(f32[64,512]{1,0:T(8,128)} %shard_map.46, f32[64,512]{1,0:T(8,128)S(1)} %collective-permute-done) | non-fusion elementwise | flops 32768 | bytes 393216 | tf_op jit(solution)/shard_map/add | solution.py:72
  28.9 1.8 %collective-permute-start.1 = (f32[64,512]{1,0:T(8,128)S(1)}, f32[64,512]{1,0:T(8,128)S(1)}, u32[]{:S(2)}, u32[]{:S(2)}) collective-permute-start(f32[64,512]{1,0:T(8,128)S(1)} %add.64), channel_id=1, source_target_pairs={{0,8},{4,12},{8,0},{12,4},{1,9},{5,13},{9,1},{13,5},{2,10},{6,14},... | collective-permute-start | bytes 393224 | tf_op jit(solution)/shard_map/ppermute | solution.py:72
  30.6 5.6 %collective-permute-done.1 = f32[64,512]{1,0:T(8,128)S(1)} collective-permute-done((f32[64,512]{1,0:T(8,128)S(1)}, f32[64,512]{1,0:T(8,128)S(1)}, u32[]{:S(2)}, u32[]{:S(2)}) %collective-permute-start.1) | collective-permute-done | bytes 131104 | tf_op jit(solution)/shard_map/ppermute | solution.py:72
  36.3 0.8 %collective-permute-start.2 = (f32[64]{0:T(128)S(1)}, f32[64]{0:T(128)S(1)}, u32[]{:S(2)}, u32[]{:S(2)}) collective-permute-start(f32[64]{0:T(128)S(1)} %get-tuple-element.17), channel_id=1, source_target_pairs={{0,2},{2,0},{1,3},{3,1},{4,6},{6,4},{5,7},{7,5},{8,10},{10,8},{9,1... | collective-permute-start | bytes 776 | tf_op jit(solution)/shard_map/ppermute | solution.py:72
  37.2 0.2 rev.7
  37.5 2.5 %collective-permute-done.2 = f32[64]{0:T(128)S(1)} collective-permute-done((f32[64]{0:T(128)S(1)}, f32[64]{0:T(128)S(1)}, u32[]{:S(2)}, u32[]{:S(2)}) %collective-permute-start.2) | collective-permute-done | bytes 288 | tf_op jit(solution)/shard_map/ppermute | solution.py:72
  40.0 0.7 %broadcast_divide_fusion = f32[1,64,512]{2,1,0:T(8,128)} fusion(f32[1,64,512]{2,1,0:T(8,128)S(1)} %reshape.127, f32[64]{0:T(128)S(1)} %add_sqrt_fusion.1), kind=kLoop, calls=%fused_computation.10 | loop fusion | flops 32768 | bytes 262400 | tf_op jit(solution)/shard_map/div | solution.py:134
  (23 shorter events, 1.1 us)
Async XLA Ops:
  0.0 12.0 %copy-start = (bf16[1,64,4,3,512]{4,2,3,1,0:T(4,128)(2,1)S(1)}, bf16[1,64,4,3,512]{4,2,3,1,0:T(4,128)(2,1)}, u32[]{:S(2)}) copy-start(bf16[1,64,4,3,512]{4,2,3,1,0:T(4,128)(2,1)} %param.7) | copy-start | bytes 2359300
  2.2 14.2 %all-to-all-start = ((bf16[8,2,4,512]{3,2,1,0:T(4,128)(2,1)}), bf16[8,2,4,512]{3,2,1,0:T(4,128)(2,1)S(1)}, u32[]{:S(2)}, u32[]{:S(2)}) async-start(bf16[8,2,4,512]{3,2,1,0:T(4,128)(2,1)} %broadcast_in_dim.16), calls=%async_computation | async-start | bytes 131072 | tf_op jit(solution)/shard_map/all_to_all | solution.py:91
  22.8 5.2 %collective-permute-start = (f32[64,512]{1,0:T(8,128)}, f32[64,512]{1,0:T(8,128)S(1)}, u32[]{:S(2)}, u32[]{:S(2)}) collective-permute-start(f32[64,512]{1,0:T(8,128)} %shard_map.46), channel_id=1, source_target_pairs={{0,4},{4,0},{8,12},{12,8},{1,5},{5,1},{9,13},{13,9},{2,6},{6,2},{1... | collective-permute-start | bytes 393224 | tf_op jit(solution)/shard_map/ppermute | solution.py:72
  28.9 7.3 %collective-permute-start.1 = (f32[64,512]{1,0:T(8,128)S(1)}, f32[64,512]{1,0:T(8,128)S(1)}, u32[]{:S(2)}, u32[]{:S(2)}) collective-permute-start(f32[64,512]{1,0:T(8,128)S(1)} %add.64), channel_id=1, source_target_pairs={{0,8},{4,12},{8,0},{12,4},{1,9},{5,13},{9,1},{13,5},{2,10},{6,14},... | collective-permute-start | bytes 393224 | tf_op jit(solution)/shard_map/ppermute | solution.py:72
  36.3 3.6 %collective-permute-start.2 = (f32[64]{0:T(128)S(1)}, f32[64]{0:T(128)S(1)}, u32[]{:S(2)}, u32[]{:S(2)}) collective-permute-start(f32[64]{0:T(128)S(1)} %get-tuple-element.17), channel_id=1, source_target_pairs={{0,2},{2,0},{1,3},{3,1},{4,6},{6,4},{5,7},{7,5},{8,10},{10,8},{9,1... | collective-permute-start | bytes 776 | tf_op jit(solution)/shard_map/ppermute | solution.py:72

commit v16 on v12

--- a/solution.py
+++ b/solution.py
@@ -42,10 +42,14 @@
         return one_channel(2 * i + 1, 1, acc)
 
     acc = jnp.zeros(o_ref.shape, jnp.float32)
-    pairs = channels // 2
-    acc = lax.fori_loop(0, pairs, two_channels, acc, unroll=2 if pairs % 2 == 0 else 1)
-    if channels % 2:
-        acc = one_channel(channels - 1, 0, acc)
+    if channels <= 16:
+        for c in range(channels):
+            acc = one_channel(c, c % 2, acc)
+    else:
+        pairs = channels // 2
+        acc = lax.fori_loop(0, pairs, two_channels, acc, unroll=2 if pairs % 2 == 0 else 1)
+        if channels % 2:
+            acc = one_channel(channels - 1, 0, acc)
     o_ref[...] = acc
 
 

time: 40.3 us -> 39.8 us (0.988)
  Pallas kernels: 4.75 us -> 4.33 us
    pallas_call x1, Pallas kernels: 4.75 us -> 4.33 us  [correlate(): pl.pallas_call(hankel_kernel, out_shape=jax.ShapeDtypeStruct((rows, seg_l...]
where the time goes in v16:
time: 39.8 us; the launch traced here: 39.5 us
  starting transfers between devices  14.1 us (35%)
  waiting for transfers between devices  11.6 us (29%)
  other arithmetic  5.37 us (13%)
  Pallas kernels  4.33 us (11%)
  local copies, waits for them, and re-layouts  3.81 us (10%)
    ppermute x3, waiting for transfers between devices, ordered_sum(): part = part + lax.ppermute(part, axis, [(i, i ^ step) for i in range(size)])  8.34 us
    ppermute x3, starting transfers between devices, ordered_sum(): part = part + lax.ppermute(part, axis, [(i, i ^ step) for i in range(size)])  6.83 us
    ppermute x2, starting transfers between devices, gather_owned(): lax.ppermute(here, 'region', [(r, r ^ step) for r in range(regions)])  5.89 us
    pallas_call x1, Pallas kernels, correlate(): pl.pallas_call(hankel_kernel, out_shape=jax.ShapeDtypeStruct((rows, seg_l...  4.33 us
    another operation x1, local copies, waits for them, and re-layouts, correlate(): normed.reshape(rows, channels * filter_taps)  1.84 us
    ppermute x2, waiting for transfers between devices, gather_owned(): lax.ppermute(here, 'region', [(r, r ^ step) for r in range(regions)])  1.72 us
    reduce_sum x1, other arithmetic, per_device(): jnp.sum(widened_templates * widened_templates, axis=4, keepdims=True)  1.65 us
    ppermute x1, waiting for transfers between devices, gather_owned(): lax.ppermute(records[:, :, :filter_taps], 'seg', [(s + 1, s) for s in ran...  1.57 us
  transfers between devices with their start and end apart: 6, of which 5 were waited for; matrix products, arithmetic and copies ran while one was open for 15% of the time, Pallas kernels for 0%

profile of v16, /device:TPU:0, one launch (start us, length us, event | category | flops | bytes accessed | tf_op | source)
XLA Modules:
  0.0 39.5 jit_solution(10461793445264020986)
XLA Ops:
  0.0 1.4 %collective-permute-start = (bf16[2,3,512]{2,0,1:T(2,128)(2,1)}, bf16[2,3,512]{2,0,1:T(2,128)(2,1)S(1)}, u32[]{:S(2)}, u32[]{:S(2)}) collective-permute-start(bf16[2,3,512]{2,0,1:T(2,128)(2,1)} %param.4), channel_id=1, source_target_pairs={{2,0},{3,1},{6,4},{7,5},{10,8},{11,9},{14,12},{15,13},{18,16},{19,... | collective-permute-start | bytes 18440 | tf_op jit(solution)/shard_map/ppermute | solution.py:91
  1.4 0.7 %convert_bitcast_fusion = f32[64,4,3]{0,1,2:T(4,128)S(1)} fusion(s32[1,64,4,3]{1,2,3,0:T(4,128)} %param.6), kind=kLoop, calls=%fused_computation.16 | loop fusion | flops 768 | bytes 6144 | tf_op jit(solution)/shard_map/mul | solution.py:142
  2.1 0.1 copy.9
  2.3 1.7 %fusion.3 = f32[64,4,3]{1,2,0:T(4,128)S(1)} fusion(bf16[1,64,4,3,512]{4,2,3,1,0:T(4,128)(2,1)} %param.5), kind=kLoop, calls=%fused_computation.6 | loop fusion | flops 1178880 | bytes 789504 | tf_op jit(solution)/shard_map/reduce_sum | solution.py:140
  4.0 0.5 %fusion.2 = bf16[1,64,4,3,512]{4,2,3,1,0:T(4,128)(2,1)S(1)} fusion(bf16[1,64,4,3,512]{4,2,3,1,0:T(4,128)(2,1)S(1)} %copy-done, f32[64,4,3]{1,2,0:T(4,128)S(1)} %add_sqrt_fusion, f32[64,4,3]{1,2,0:T(4,128)S(1)} %copy.9), kind=kLoop, calls=%fused_computation.5 | loop fusion | flops 1572864 | bytes 1579008 | tf_op jit(solution)/shard_map/convert_element_type | solution.py:142
  4.6 1.6 %collective-permute-done = bf16[2,3,512]{2,0,1:T(2,128)(2,1)S(1)} collective-permute-done((bf16[2,3,512]{2,0,1:T(2,128)(2,1)}, bf16[2,3,512]{2,0,1:T(2,128)(2,1)S(1)}, u32[]{:S(2)}, u32[]{:S(2)}) %collective-permute-start) | collective-permute-done | bytes 6176 | tf_op jit(solution)/shard_map/ppermute | solution.py:91
  6.3 2.8 %collective-permute-start.1 = (bf16[2,4,1024]{2,0,1:T(2,128)(2,1)S(1)}, bf16[2,4,1024]{2,0,1:T(2,128)(2,1)S(1)}, u32[]{:S(2)}, u32[]{:S(2)}) collective-permute-start(bf16[2,4,1024]{2,0,1:T(2,128)(2,1)S(1)} %pad_maximum_fusion.5), channel_id=1, source_target_pairs={{0,4},{4,0},{8,12},{12,8},{1,5},{5,1},{9,13},{13,9},{2,6},{6,2},{1... | collective-permute-start | bytes 49160 | tf_op jit(solution)/shard_map/ppermute | solution.py:104
  9.1 1.7 %collective-permute-done.1 = bf16[2,4,1024]{2,0,1:T(2,128)(2,1)S(1)} collective-permute-done((bf16[2,4,1024]{2,0,1:T(2,128)(2,1)S(1)}, bf16[2,4,1024]{2,0,1:T(2,128)(2,1)S(1)}, u32[]{:S(2)}, u32[]{:S(2)}) %collective-permute-start.1) | collective-permute-done | bytes 16416 | tf_op jit(solution)/shard_map/ppermute | solution.py:104
  10.8 3.1 %collective-permute-start.2 = (bf16[4,4,1024]{2,0,1:T(4,128)(2,1)S(1)}, bf16[4,4,1024]{2,0,1:T(4,128)(2,1)S(1)}, u32[]{:S(2)}, u32[]{:S(2)}) collective-permute-start(bf16[4,4,1024]{2,0,1:T(4,128)(2,1)S(1)} %pad_maximum_fusion.4), channel_id=1, source_target_pairs={{0,8},{4,12},{8,0},{12,4},{1,9},{5,13},{9,1},{13,5},{2,10},{6,14},... | collective-permute-start | bytes 98312 | tf_op jit(solution)/shard_map/ppermute | solution.py:104
  14.1 0.6 %copy.10 = bf16[1,64,4,3,512]{4,3,2,1,0:T(4,128)(2,1)S(1)} copy(bf16[1,64,4,3,512]{4,2,3,1,0:T(4,128)(2,1)S(1)} %fusion.2) | data formatting | bytes 1572864 | tf_op jit(solution)/shard_map/convert_element_type | solution.py:142
  14.6 1.8 %reshape_reshape.4.n_ref = bf16[64,6144]{1,0:T(8,128)(2,1)} reshape(bf16[1,64,4,3,512]{4,3,2,1,0:T(4,128)(2,1)S(1)} %copy.10) | data formatting | bytes 1572864 | tf_op jit(solution)/shard_map/reshape;reshape | solution.py:68
  16.6 0.2 convert_reduce_fusion.1
  17.0 0.1 fusion
  17.2 0.7 %rev.6.x_ref = f32[96,128]{1,0:T(8,128)} reverse(f32[96,128]{1,0:T(8,128)S(1)} %mul.38), dimensions={1} | reverse | bytes 98304 | tf_op jit(solution)/shard_map/rev | solution.py:63
  17.9 4.3 %shard_map.46 = f32[64,512]{1,0:T(8,128)} custom-call(f32[96,128]{1,0:T(8,128)} %rev.6.x_ref, bf16[64,6144]{1,0:T(8,128)(2,1)} %reshape_reshape.4.n_ref), custom_call_target="tpu_custom_call" | custom-call | tf_op jit(solution)/shard_map/pallas_call | solution.py:64
  22.3 1.6 %collective-permute-start.3 = (f32[64,512]{1,0:T(8,128)}, f32[64,512]{1,0:T(8,128)S(1)}, u32[]{:S(2)}, u32[]{:S(2)}) collective-permute-start(f32[64,512]{1,0:T(8,128)} %shard_map.46), channel_id=1, source_target_pairs={{0,4},{4,0},{8,12},{12,8},{1,5},{5,1},{9,13},{13,9},{2,6},{6,2},{1... | collective-permute-start | bytes 393224 | tf_op jit(solution)/shard_map/ppermute | solution.py:76
  23.8 3.6 %collective-permute-done.3 = f32[64,512]{1,0:T(8,128)S(1)} collective-permute-done((f32[64,512]{1,0:T(8,128)}, f32[64,512]{1,0:T(8,128)S(1)}, u32[]{:S(2)}, u32[]{:S(2)}) %collective-permute-start.3) | collective-permute-done | bytes 131104 | tf_op jit(solution)/shard_map/ppermute | solution.py:76
  27.4 0.9 %add.56 = f32[64,512]{1,0:T(8,128)S(1)} add(f32[64,512]{1,0:T(8,128)} %shard_map.46, f32[64,512]{1,0:T(8,128)S(1)} %collective-permute-done.3) | non-fusion elementwise | flops 32768 | bytes 393216 | tf_op jit(solution)/shard_map/add | solution.py:76
  28.4 2.4 %collective-permute-start.4 = (f32[64,512]{1,0:T(8,128)S(1)}, f32[64,512]{1,0:T(8,128)S(1)}, u32[]{:S(2)}, u32[]{:S(2)}) collective-permute-start(f32[64,512]{1,0:T(8,128)S(1)} %add.56), channel_id=1, source_target_pairs={{0,8},{4,12},{8,0},{12,4},{1,9},{5,13},{9,1},{13,5},{2,10},{6,14},... | collective-permute-start | bytes 393224 | tf_op jit(solution)/shard_map/ppermute | solution.py:76
  30.8 3.5 %collective-permute-done.4 = f32[64,512]{1,0:T(8,128)S(1)} collective-permute-done((f32[64,512]{1,0:T(8,128)S(1)}, f32[64,512]{1,0:T(8,128)S(1)}, u32[]{:S(2)}, u32[]{:S(2)}) %collective-permute-start.4) | collective-permute-done | bytes 131104 | tf_op jit(solution)/shard_map/ppermute | solution.py:76
  34.4 2.8 %collective-permute-start.5 = (f32[64]{0:T(128)S(1)}, f32[64]{0:T(128)S(1)}, u32[]{:S(2)}, u32[]{:S(2)}) collective-permute-start(f32[64]{0:T(128)S(1)} %get-tuple-element.5), channel_id=1, source_target_pairs={{0,2},{2,0},{1,3},{3,1},{4,6},{6,4},{5,7},{7,5},{8,10},{10,8},{9,1... | collective-permute-start | bytes 776 | tf_op jit(solution)/shard_map/ppermute | solution.py:76
  37.3 0.2 rev.7
  37.6 1.2 %collective-permute-done.5 = f32[64]{0:T(128)S(1)} collective-permute-done((f32[64]{0:T(128)S(1)}, f32[64]{0:T(128)S(1)}, u32[]{:S(2)}, u32[]{:S(2)}) %collective-permute-start.5) | collective-permute-done | bytes 288 | tf_op jit(solution)/shard_map/ppermute | solution.py:76
  38.8 0.7 %broadcast_divide_fusion = f32[1,64,512]{2,1,0:T(8,128)} fusion(f32[1,64,512]{2,1,0:T(8,128)S(1)} %reshape.115, f32[64]{0:T(128)S(1)} %add_sqrt_fusion.1), kind=kLoop, calls=%fused_computation.9 | loop fusion | flops 32768 | bytes 262400 | tf_op jit(solution)/shard_map/div | solution.py:147
  (27 shorter events, 1.1 us)
Async XLA Ops:
  0.0 4.0 %copy-start = (bf16[1,64,4,3,512]{4,2,3,1,0:T(4,128)(2,1)S(1)}, bf16[1,64,4,3,512]{4,2,3,1,0:T(4,128)(2,1)}, u32[]{:S(2)}) copy-start(bf16[1,64,4,3,512]{4,2,3,1,0:T(4,128)(2,1)} %param.5) | copy-start | bytes 2359300
  0.0 6.2 %collective-permute-start = (bf16[2,3,512]{2,0,1:T(2,128)(2,1)}, bf16[2,3,512]{2,0,1:T(2,128)(2,1)S(1)}, u32[]{:S(2)}, u32[]{:S(2)}) collective-permute-start(bf16[2,3,512]{2,0,1:T(2,128)(2,1)} %param.4), channel_id=1, source_target_pairs={{2,0},{3,1},{6,4},{7,5},{10,8},{11,9},{14,12},{15,13},{18,16},{19,... | collective-permute-start | bytes 18440 | tf_op jit(solution)/shard_map/ppermute | solution.py:91
  3.9 0.7 %copy-start.2 = (s32[2]{0:T(128)S(1)}, s32[2]{0:T(128)}, u32[]{:S(2)}) copy-start(s32[2]{0:T(128)} %param.7) | copy-start | bytes 28
  3.9 2.3 %copy-start.1 = (bf16[2,3,512]{2,0,1:T(2,128)(2,1)S(1)}, bf16[2,3,512]{2,0,1:T(2,128)(2,1)}, u32[]{:S(2)}) copy-start(bf16[2,3,512]{2,0,1:T(2,128)(2,1)} %param.4) | copy-start | bytes 18436
  6.3 4.5 %collective-permute-start.1 = (bf16[2,4,1024]{2,0,1:T(2,128)(2,1)S(1)}, bf16[2,4,1024]{2,0,1:T(2,128)(2,1)S(1)}, u32[]{:S(2)}, u32[]{:S(2)}) collective-permute-start(bf16[2,4,1024]{2,0,1:T(2,128)(2,1)S(1)} %pad_maximum_fusion.5), channel_id=1, source_target_pairs={{0,4},{4,0},{8,12},{12,8},{1,5},{5,1},{9,13},{13,9},{2,6},{6,2},{1... | collective-permute-start | bytes 49160 | tf_op jit(solution)/shard_map/ppermute | solution.py:104
  10.8 5.7 %collective-permute-start.2 = (bf16[4,4,1024]{2,0,1:T(4,128)(2,1)S(1)}, bf16[4,4,1024]{2,0,1:T(4,128)(2,1)S(1)}, u32[]{:S(2)}, u32[]{:S(2)}) collective-permute-start(bf16[4,4,1024]{2,0,1:T(4,128)(2,1)S(1)} %pad_maximum_fusion.4), channel_id=1, source_target_pairs={{0,8},{4,12},{8,0},{12,4},{1,9},{5,13},{9,1},{13,5},{2,10},{6,14},... | collective-permute-start | bytes 98312 | tf_op jit(solution)/shard_map/ppermute | solution.py:104
  22.3 5.2 %collective-permute-start.3 = (f32[64,512]{1,0:T(8,128)}, f32[64,512]{1,0:T(8,128)S(1)}, u32[]{:S(2)}, u32[]{:S(2)}) collective-permute-start(f32[64,512]{1,0:T(8,128)} %shard_map.46), channel_id=1, source_target_pairs={{0,4},{4,0},{8,12},{12,8},{1,5},{5,1},{9,13},{13,9},{2,6},{6,2},{1... | collective-permute-start | bytes 393224 | tf_op jit(solution)/shard_map/ppermute | solution.py:76
  28.4 5.9 %collective-permute-start.4 = (f32[64,512]{1,0:T(8,128)S(1)}, f32[64,512]{1,0:T(8,128)S(1)}, u32[]{:S(2)}, u32[]{:S(2)}) collective-permute-start(f32[64,512]{1,0:T(8,128)S(1)} %add.56), channel_id=1, source_target_pairs={{0,8},{4,12},{8,0},{12,4},{1,9},{5,13},{9,1},{13,5},{2,10},{6,14},... | collective-permute-start | bytes 393224 | tf_op jit(solution)/shard_map/ppermute | solution.py:76
  34.4 4.4 %collective-permute-start.5 = (f32[64]{0:T(128)S(1)}, f32[64]{0:T(128)S(1)}, u32[]{:S(2)}, u32[]{:S(2)}) collective-permute-start(f32[64]{0:T(128)S(1)} %get-tuple-element.5), channel_id=1, source_target_pairs={{0,2},{2,0},{1,3},{3,1},{4,6},{6,4},{5,7},{7,5},{8,10},{10,8},{9,1... | collective-permute-start | bytes 776 | tf_op jit(solution)/shard_map/ppermute | solution.py:76

commit v17 on v16

--- a/solution.py
+++ b/solution.py
@@ -97,21 +97,9 @@
     )
     me = lax.axis_index("region")
     stations = regions * local_count
-    if regions & (regions - 1) == 0:
-        here = payload
-        step = 1
-        while step < regions:
-            theirs = lax.ppermute(here, "region", [(r, r ^ step) for r in range(regions)])
-            here = jnp.concatenate([here, theirs], axis=0)
-            step *= 2
-        source = me ^ jnp.arange(regions, dtype=jnp.int32)[:, None]
-    else:
-        gathered = [payload] + [
-            lax.ppermute(payload, "region", [(r, (r + k) % regions) for r in range(regions)])
-            for k in range(1, regions)
-        ]
-        here = jnp.concatenate(gathered, axis=0)
-        source = (me - jnp.arange(regions, dtype=jnp.int32)[:, None]) % regions
+    spread = jnp.broadcast_to(payload[None], (regions,) + payload.shape)
+    here = lax.all_to_all(spread, "region", 0, 0, tiled=True).reshape((stations,) + payload.shape[1:])
+    source = jnp.arange(regions, dtype=jnp.int32)[:, None]
     local = jnp.arange(local_count, dtype=jnp.int32)[None, :]
     station_ids = (source * local_count + local).reshape(stations)
     region_of = here[:, components, 0].astype(jnp.int32)

time: 39.8 us -> 42.9 us (1.078)
  waiting for transfers between devices: 11.6 us -> 17.4 us
  starting transfers between devices: 14.1 us -> 10.6 us
  local copies, waits for them, and re-layouts: 3.81 us -> 4.52 us
    all_to_all x0 -> x1, starting transfers between devices: none -> 6.02 us  [gather_owned(): lax.all_to_all(spread, 'region', 0, 0, tiled=True)]
    ppermute x2 -> x0, starting transfers between devices: 5.89 us -> none  [gather_owned(): lax.ppermute(here, 'region', [(r, r ^ step) for r in range(regions)])]
    ppermute x3, waiting for transfers between devices: 8.34 us -> 12.7 us  [ordered_sum(): part = part + lax.ppermute(part, axis, [(i, i ^ step) for i in range(size)])]
    ppermute x3, starting transfers between devices: 6.83 us -> 3.16 us  [ordered_sum(): part = part + lax.ppermute(part, axis, [(i, i ^ step) for i in range(size)])]
    all_to_all x0 -> x1, waiting for transfers between devices: none -> 3.19 us  [gather_owned(): lax.all_to_all(spread, 'region', 0, 0, tiled=True)]
    ppermute x2 -> x0, waiting for transfers between devices: 1.72 us -> none  [gather_owned(): lax.ppermute(here, 'region', [(r, r ^ step) for r in range(regions)])]
    broadcast_in_dim x0 -> x1, local copies, waits for them, and re-layouts: none -> 0.65 us  [gather_owned(): spread = jnp.broadcast_to(payload[None], (regions,) + payload.shape)]
  transfers between devices with their start and end apart: 6 -> 5, of which waited for: 5 -> 5; matrix products, arithmetic and copies ran while one was open for 15% -> 14% of each run, Pallas kernels for 0% -> 0%
where the time goes in v17:
time: 42.9 us; the launch traced here: 42.5 us
  waiting for transfers between devices  17.4 us (41%)
  starting transfers between devices  10.6 us (25%)
  other arithmetic  5.39 us (13%)
  local copies, waits for them, and re-layouts  4.52 us (11%)
  Pallas kernels  4.33 us (10%)
    ppermute x3, waiting for transfers between devices, ordered_sum(): part = part + lax.ppermute(part, axis, [(i, i ^ step) for i in range(size)])  12.7 us
    all_to_all x1, starting transfers between devices, gather_owned(): lax.all_to_all(spread, 'region', 0, 0, tiled=True)  6.02 us
    pallas_call x1, Pallas kernels, correlate(): pl.pallas_call(hankel_kernel, out_shape=jax.ShapeDtypeStruct((rows, seg_l...  4.33 us
    all_to_all x1, waiting for transfers between devices, gather_owned(): lax.all_to_all(spread, 'region', 0, 0, tiled=True)  3.19 us
    ppermute x3, starting transfers between devices, ordered_sum(): part = part + lax.ppermute(part, axis, [(i, i ^ step) for i in range(size)])  3.16 us
    another operation x1, local copies, waits for them, and re-layouts, correlate(): normed.reshape(rows, channels * filter_taps)  1.84 us
    reduce_sum x1, other arithmetic, per_device(): jnp.sum(widened_templates * widened_templates, axis=4, keepdims=True)  1.65 us
    ppermute x1, waiting for transfers between devices, gather_owned(): lax.ppermute(records[:, :, :filter_taps], 'seg', [(s + 1, s) for s in ran...  1.57 us
  transfers between devices with their start and end apart: 5, of which 5 were waited for; matrix products, arithmetic and copies ran while one was open for 14% of the time, Pallas kernels for 0%

profile of v17, /device:TPU:0, one launch (start us, length us, event | category | flops | bytes accessed | tf_op | source)
XLA Modules:
  0.0 42.5 jit_solution(8648369898587487870)
XLA Ops:
  0.0 1.4 %collective-permute-start = (bf16[2,3,512]{2,0,1:T(2,128)(2,1)}, bf16[2,3,512]{2,0,1:T(2,128)(2,1)S(1)}, u32[]{:S(2)}, u32[]{:S(2)}) collective-permute-start(bf16[2,3,512]{2,0,1:T(2,128)(2,1)} %param.4), channel_id=1, source_target_pairs={{2,0},{3,1},{6,4},{7,5},{10,8},{11,9},{14,12},{15,13},{18,16},{19,... | collective-permute-start | bytes 18440 | tf_op jit(solution)/shard_map/ppermute | solution.py:91
  1.4 0.7 %convert_bitcast_fusion = f32[64,4,3]{0,1,2:T(4,128)S(1)} fusion(s32[1,64,4,3]{1,2,3,0:T(4,128)} %param.6), kind=kLoop, calls=%fused_computation.12 | loop fusion | flops 768 | bytes 6144 | tf_op jit(solution)/shard_map/mul | solution.py:130
  2.3 1.7 %fusion.3 = f32[64,4,3]{1,2,0:T(4,128)S(1)} fusion(bf16[1,64,4,3,512]{4,2,3,1,0:T(4,128)(2,1)} %param.5), kind=kLoop, calls=%fused_computation.6 | loop fusion | flops 1178880 | bytes 789504 | tf_op jit(solution)/shard_map/reduce_sum | solution.py:128
  4.0 0.5 %fusion.2 = bf16[1,64,4,3,512]{4,2,3,1,0:T(4,128)(2,1)S(1)} fusion(bf16[1,64,4,3,512]{4,2,3,1,0:T(4,128)(2,1)S(1)} %copy-done, f32[64,4,3]{1,2,0:T(4,128)S(1)} %add_sqrt_fusion, f32[64,4,3]{1,2,0:T(4,128)S(1)} %copy.15), kind=kLoop, calls=%fused_computation.5 | loop fusion | flops 1572864 | bytes 1579008 | tf_op jit(solution)/shard_map/convert_element_type | solution.py:130
  4.6 1.6 %collective-permute-done = bf16[2,3,512]{2,0,1:T(2,128)(2,1)S(1)} collective-permute-done((bf16[2,3,512]{2,0,1:T(2,128)(2,1)}, bf16[2,3,512]{2,0,1:T(2,128)(2,1)S(1)}, u32[]{:S(2)}, u32[]{:S(2)}) %collective-permute-start) | collective-permute-done | bytes 6176 | tf_op jit(solution)/shard_map/ppermute | solution.py:91
  6.3 0.6 %broadcast_in_dim.5 = bf16[4,2,4,1024]{3,2,1,0:T(4,128)(2,1)} broadcast(bf16[2,4,1024]{2,1,0:T(4,128)(2,1)S(1)} %copy.14), dimensions={1,2,3} | broadcast | bytes 81920 | tf_op jit(solution)/shard_map/broadcast_in_dim | solution.py:100
  6.9 6.0 %all-to-all-start = ((bf16[4,2,4,1024]{3,2,1,0:T(4,128)(2,1)}), bf16[4,2,4,1024]{3,2,1,0:T(4,128)(2,1)S(1)}, u32[]{:S(2)}, u32[]{:S(2)}) async-start(bf16[4,2,4,1024]{3,2,1,0:T(4,128)(2,1)} %broadcast_in_dim.5), calls=%async_computation | async-start | bytes 131072 | tf_op jit(solution)/shard_map/all_to_all | solution.py:101
  13.1 0.6 %copy.16 = bf16[1,64,4,3,512]{4,3,2,1,0:T(4,128)(2,1)S(1)} copy(bf16[1,64,4,3,512]{4,2,3,1,0:T(4,128)(2,1)S(1)} %fusion.2) | data formatting | bytes 1572864 | tf_op jit(solution)/shard_map/convert_element_type | solution.py:130
  13.7 1.8 %reshape_reshape.4.n_ref = bf16[64,6144]{1,0:T(8,128)(2,1)} reshape(bf16[1,64,4,3,512]{4,3,2,1,0:T(4,128)(2,1)S(1)} %copy.16) | data formatting | bytes 1572864 | tf_op jit(solution)/shard_map/reshape;reshape | solution.py:68
  15.5 3.2 %all-to-all-done = bf16[4,2,4,1024]{3,2,1,0:T(4,128)(2,1)S(1)} async-done(((bf16[4,2,4,1024]{3,2,1,0:T(4,128)(2,1)}), bf16[4,2,4,1024]{3,2,1,0:T(4,128)(2,1)S(1)}, u32[]{:S(2)}, u32[]{:S(2)}) %all-to-all-start) | async-done | bytes 65568 | tf_op jit(solution)/shard_map/all_to_all | solution.py:101
  18.7 0.2 fusion.4
  19.0 0.2 convert_reduce_fusion
  19.3 0.1 fusion
  19.6 0.7 %rev.6.x_ref = f32[96,128]{1,0:T(8,128)} reverse(f32[96,128]{1,0:T(8,128)S(1)} %mul.38), dimensions={1} | reverse | bytes 98304 | tf_op jit(solution)/shard_map/rev | solution.py:63
  20.3 4.3 %shard_map.46 = f32[64,512]{1,0:T(8,128)} custom-call(f32[96,128]{1,0:T(8,128)} %rev.6.x_ref, bf16[64,6144]{1,0:T(8,128)(2,1)} %reshape_reshape.4.n_ref), custom_call_target="tpu_custom_call" | custom-call | tf_op jit(solution)/shard_map/pallas_call | solution.py:64
  24.6 0.9 %collective-permute-start.1 = (f32[64,512]{1,0:T(8,128)}, f32[64,512]{1,0:T(8,128)S(1)}, u32[]{:S(2)}, u32[]{:S(2)}) collective-permute-start(f32[64,512]{1,0:T(8,128)} %shard_map.46), channel_id=1, source_target_pairs={{0,4},{4,0},{8,12},{12,8},{1,5},{5,1},{9,13},{13,9},{2,6},{6,2},{1... | collective-permute-start | bytes 393224 | tf_op jit(solution)/shard_map/ppermute | solution.py:76
  25.5 4.3 %collective-permute-done.1 = f32[64,512]{1,0:T(8,128)S(1)} collective-permute-done((f32[64,512]{1,0:T(8,128)}, f32[64,512]{1,0:T(8,128)S(1)}, u32[]{:S(2)}, u32[]{:S(2)}) %collective-permute-start.1) | collective-permute-done | bytes 131104 | tf_op jit(solution)/shard_map/ppermute | solution.py:76
  29.8 0.9 %add.56 = f32[64,512]{1,0:T(8,128)S(1)} add(f32[64,512]{1,0:T(8,128)} %shard_map.46, f32[64,512]{1,0:T(8,128)S(1)} %collective-permute-done.1) | non-fusion elementwise | flops 32768 | bytes 393216 | tf_op jit(solution)/shard_map/add | solution.py:76
  30.7 0.8 %collective-permute-start.2 = (f32[64,512]{1,0:T(8,128)S(1)}, f32[64,512]{1,0:T(8,128)S(1)}, u32[]{:S(2)}, u32[]{:S(2)}) collective-permute-start(f32[64,512]{1,0:T(8,128)S(1)} %add.56), channel_id=1, source_target_pairs={{0,8},{4,12},{8,0},{12,4},{1,9},{5,13},{9,1},{13,5},{2,10},{6,14},... | collective-permute-start | bytes 393224 | tf_op jit(solution)/shard_map/ppermute | solution.py:76
  31.5 6.5 %collective-permute-done.2 = f32[64,512]{1,0:T(8,128)S(1)} collective-permute-done((f32[64,512]{1,0:T(8,128)S(1)}, f32[64,512]{1,0:T(8,128)S(1)}, u32[]{:S(2)}, u32[]{:S(2)}) %collective-permute-start.2) | collective-permute-done | bytes 131104 | tf_op jit(solution)/shard_map/ppermute | solution.py:76
  38.2 1.4 %collective-permute-start.3 = (f32[64]{0:T(128)S(1)}, f32[64]{0:T(128)S(1)}, u32[]{:S(2)}, u32[]{:S(2)}) collective-permute-start(f32[64]{0:T(128)S(1)} %get-tuple-element.5), channel_id=1, source_target_pairs={{0,2},{2,0},{1,3},{3,1},{4,6},{6,4},{5,7},{7,5},{8,10},{10,8},{9,1... | collective-permute-start | bytes 776 | tf_op jit(solution)/shard_map/ppermute | solution.py:76
  39.7 0.2 rev.7
  39.9 1.9 %collective-permute-done.3 = f32[64]{0:T(128)S(1)} collective-permute-done((f32[64]{0:T(128)S(1)}, f32[64]{0:T(128)S(1)}, u32[]{:S(2)}, u32[]{:S(2)}) %collective-permute-start.3) | collective-permute-done | bytes 288 | tf_op jit(solution)/shard_map/ppermute | solution.py:76
  41.8 0.7 %broadcast_divide_fusion = f32[1,64,512]{2,1,0:T(8,128)} fusion(f32[1,64,512]{2,1,0:T(8,128)S(1)} %reshape.118, f32[64]{0:T(128)S(1)} %add_sqrt_fusion.1), kind=kLoop, calls=%fused_computation.10 | loop fusion | flops 32768 | bytes 262400 | tf_op jit(solution)/shard_map/div | solution.py:135
  (27 shorter events, 1.0 us)
Async XLA Ops:
  0.0 4.0 %copy-start = (bf16[1,64,4,3,512]{4,2,3,1,0:T(4,128)(2,1)S(1)}, bf16[1,64,4,3,512]{4,2,3,1,0:T(4,128)(2,1)}, u32[]{:S(2)}) copy-start(bf16[1,64,4,3,512]{4,2,3,1,0:T(4,128)(2,1)} %param.5) | copy-start | bytes 2359300
  0.0 6.2 %collective-permute-start = (bf16[2,3,512]{2,0,1:T(2,128)(2,1)}, bf16[2,3,512]{2,0,1:T(2,128)(2,1)S(1)}, u32[]{:S(2)}, u32[]{:S(2)}) collective-permute-start(bf16[2,3,512]{2,0,1:T(2,128)(2,1)} %param.4), channel_id=1, source_target_pairs={{2,0},{3,1},{6,4},{7,5},{10,8},{11,9},{14,12},{15,13},{18,16},{19,... | collective-permute-start | bytes 18440 | tf_op jit(solution)/shard_map/ppermute | solution.py:91
  3.9 0.7 %copy-start.2 = (s32[2]{0:T(128)S(1)}, s32[2]{0:T(128)}, u32[]{:S(2)}) copy-start(s32[2]{0:T(128)} %param.7) | copy-start | bytes 28
  3.9 2.3 %copy-start.1 = (bf16[2,3,512]{2,0,1:T(2,128)(2,1)S(1)}, bf16[2,3,512]{2,0,1:T(2,128)(2,1)}, u32[]{:S(2)}) copy-start(bf16[2,3,512]{2,0,1:T(2,128)(2,1)} %param.4) | copy-start | bytes 18436
  6.9 11.8 %all-to-all-start = ((bf16[4,2,4,1024]{3,2,1,0:T(4,128)(2,1)}), bf16[4,2,4,1024]{3,2,1,0:T(4,128)(2,1)S(1)}, u32[]{:S(2)}, u32[]{:S(2)}) async-start(bf16[4,2,4,1024]{3,2,1,0:T(4,128)(2,1)} %broadcast_in_dim.5), calls=%async_computation | async-start | bytes 131072 | tf_op jit(solution)/shard_map/all_to_all | solution.py:101
  24.6 5.2 %collective-permute-start.1 = (f32[64,512]{1,0:T(8,128)}, f32[64,512]{1,0:T(8,128)S(1)}, u32[]{:S(2)}, u32[]{:S(2)}) collective-permute-start(f32[64,512]{1,0:T(8,128)} %shard_map.46), channel_id=1, source_target_pairs={{0,4},{4,0},{8,12},{12,8},{1,5},{5,1},{9,13},{13,9},{2,6},{6,2},{1... | collective-permute-start | bytes 393224 | tf_op jit(solution)/shard_map/ppermute | solution.py:76
  30.7 7.3 %collective-permute-start.2 = (f32[64,512]{1,0:T(8,128)S(1)}, f32[64,512]{1,0:T(8,128)S(1)}, u32[]{:S(2)}, u32[]{:S(2)}) collective-permute-start(f32[64,512]{1,0:T(8,128)S(1)} %add.56), channel_id=1, source_target_pairs={{0,8},{4,12},{8,0},{12,4},{1,9},{5,13},{9,1},{13,5},{2,10},{6,14},... | collective-permute-start | bytes 393224 | tf_op jit(solution)/shard_map/ppermute | solution.py:76
  38.2 3.6 %collective-permute-start.3 = (f32[64]{0:T(128)S(1)}, f32[64]{0:T(128)S(1)}, u32[]{:S(2)}, u32[]{:S(2)}) collective-permute-start(f32[64]{0:T(128)S(1)} %get-tuple-element.5), channel_id=1, source_target_pairs={{0,2},{2,0},{1,3},{3,1},{4,6},{6,4},{5,7},{7,5},{8,10},{10,8},{9,1... | collective-permute-start | bytes 776 | tf_op jit(solution)/shard_map/ppermute | solution.py:76

commit v18 on v16

--- a/solution.py
+++ b/solution.py
@@ -53,6 +53,11 @@
     o_ref[...] = acc
 
 
+def reverse_blocks(rows):
+    shape = rows.shape
+    return rows.reshape(shape[:-1] + (shape[-1] // 128, 128))[..., ::-1].reshape(shape)
+
+
 def unflip(stacked):
     rows, seg_len = stacked.shape
     return stacked.reshape(rows, seg_len // 128, 128)[..., ::-1].reshape(rows, seg_len)
@@ -60,7 +65,7 @@
 
 def correlate(normed, flat_owned, seg_len):
     rows, channels, filter_taps = normed.shape
-    blocks = flat_owned.reshape(channels * (flat_owned.shape[1] // 128), 128)[:, ::-1]
+    blocks = flat_owned.reshape(channels * (flat_owned.shape[1] // 128), 128)
     return pl.pallas_call(
         hankel_kernel,
         out_shape=jax.ShapeDtypeStruct((rows, seg_len), jnp.float32),
@@ -92,9 +97,8 @@
         records[:, :, :filter_taps], "seg", [(s + 1, s) for s in range(segs - 1)]
     )
     tag = jnp.broadcast_to(station_region.astype(jnp.bfloat16)[:, None, None], (local_count, 1, seg_len + filter_taps))
-    payload = jnp.concatenate(
-        [jnp.concatenate([records, ahead], axis=2), tag], axis=1
-    )
+    window = jnp.concatenate([reverse_blocks(records), reverse_blocks(ahead)], axis=2)
+    payload = jnp.concatenate([window, tag], axis=1)
     me = lax.axis_index("region")
     stations = regions * local_count
     if regions & (regions - 1) == 0:

time: 39.8 us -> 40.2 us (1.010)
  other arithmetic: 5.37 us -> 5.98 us
    mul x1, other arithmetic: 0.01 us -> 0.62 us  [per_device(): owned_rows = owned_rows.astype(jnp.float32) * filled[:, None, None]]
    rev x1 -> x2, local copies, waits for them, and re-layouts: 0.7 us -> 0.2 us  [reverse_blocks(): rows.reshape(shape[:-1] + (shape[-1] // 128, 128))[..., ::-1].reshape(shape)]
where the time goes in v18:
time: 40.2 us; the launch traced here: 39.9 us
  starting transfers between devices  14.2 us (35%)
  waiting for transfers between devices  11.6 us (29%)
  other arithmetic  5.98 us (15%)
  Pallas kernels  4.32 us (11%)
  local copies, waits for them, and re-layouts  3.46 us (9%)
    ppermute x3, waiting for transfers between devices, ordered_sum(): part = part + lax.ppermute(part, axis, [(i, i ^ step) for i in range(size)])  8.46 us
    ppermute x3, starting transfers between devices, ordered_sum(): part = part + lax.ppermute(part, axis, [(i, i ^ step) for i in range(size)])  6.89 us
    ppermute x2, starting transfers between devices, gather_owned(): lax.ppermute(here, 'region', [(r, r ^ step) for r in range(regions)])  5.89 us
    pallas_call x1, Pallas kernels, correlate(): pl.pallas_call(hankel_kernel, out_shape=jax.ShapeDtypeStruct((rows, seg_l...  4.32 us
    another operation x1, local copies, waits for them, and re-layouts, correlate(): normed.reshape(rows, channels * filter_taps)  1.84 us
    ppermute x2, waiting for transfers between devices, gather_owned(): lax.ppermute(here, 'region', [(r, r ^ step) for r in range(regions)])  1.72 us
    reduce_sum x1, other arithmetic, per_device(): jnp.sum(widened_templates * widened_templates, axis=4, keepdims=True)  1.65 us
    ppermute x1, starting transfers between devices, gather_owned(): lax.ppermute(records[:, :, :filter_taps], 'seg', [(s + 1, s) for s in ran...  1.41 us
  transfers between devices with their start and end apart: 6, of which 5 were waited for; matrix products, arithmetic and copies ran while one was open for 15% of the time, Pallas kernels for 0%

profile of v18, /device:TPU:0, one launch (start us, length us, event | category | flops | bytes accessed | tf_op | source)
XLA Modules:
  0.0 39.9 jit_solution(8486593522774661300)
XLA Ops:
  0.0 1.4 %collective-permute-start = (bf16[2,3,512]{2,0,1:T(2,128)(2,1)}, bf16[2,3,512]{2,0,1:T(2,128)(2,1)S(1)}, u32[]{:S(2)}, u32[]{:S(2)}) collective-permute-start(bf16[2,3,512]{2,0,1:T(2,128)(2,1)} %param.4), channel_id=1, source_target_pairs={{2,0},{3,1},{6,4},{7,5},{10,8},{11,9},{14,12},{15,13},{18,16},{19,... | collective-permute-start | bytes 18440 | tf_op jit(solution)/shard_map/ppermute | solution.py:96
  1.4 0.7 %convert_bitcast_fusion = f32[64,4,3]{0,1,2:T(4,128)S(1)} fusion(s32[1,64,4,3]{1,2,3,0:T(4,128)} %param.6), kind=kLoop, calls=%fused_computation.15 | loop fusion | flops 768 | bytes 6144 | tf_op jit(solution)/shard_map/mul | solution.py:146
  2.1 0.1 copy.29
  2.3 1.7 %fusion.3 = f32[64,4,3]{1,2,0:T(4,128)S(1)} fusion(bf16[1,64,4,3,512]{4,2,3,1,0:T(4,128)(2,1)} %param.5), kind=kLoop, calls=%fused_computation.6 | loop fusion | flops 1178880 | bytes 789504 | tf_op jit(solution)/shard_map/reduce_sum | solution.py:144
  4.0 0.5 %fusion.2 = bf16[1,64,4,3,512]{4,2,3,1,0:T(4,128)(2,1)S(1)} fusion(bf16[1,64,4,3,512]{4,2,3,1,0:T(4,128)(2,1)S(1)} %copy-done, f32[64,4,3]{1,2,0:T(4,128)S(1)} %add_sqrt_fusion, f32[64,4,3]{1,2,0:T(4,128)S(1)} %copy.29), kind=kLoop, calls=%fused_computation.5 | loop fusion | flops 1572864 | bytes 1579008 | tf_op jit(solution)/shard_map/convert_element_type | solution.py:146
  4.8 1.4 %collective-permute-done = bf16[2,3,512]{2,0,1:T(2,128)(2,1)S(1)} collective-permute-done((bf16[2,3,512]{2,0,1:T(2,128)(2,1)}, bf16[2,3,512]{2,0,1:T(2,128)(2,1)S(1)}, u32[]{:S(2)}, u32[]{:S(2)}) %collective-permute-start) | collective-permute-done | bytes 6176 | tf_op jit(solution)/shard_map/ppermute | solution.py:96
  6.4 2.8 %collective-permute-start.1 = (bf16[2,4,1024]{2,1,0:T(4,128)(2,1)S(1)}, bf16[2,4,1024]{2,1,0:T(4,128)(2,1)S(1)}, u32[]{:S(2)}, u32[]{:S(2)}) collective-permute-start(bf16[2,4,1024]{2,1,0:T(4,128)(2,1)S(1)} %pad_maximum_fusion.3), channel_id=1, source_target_pairs={{0,4},{4,0},{8,12},{12,8},{1,5},{5,1},{9,13},{13,9},{2,6},{6,2},{1... | collective-permute-start | bytes 49160 | tf_op jit(solution)/shard_map/ppermute | solution.py:108
  9.2 1.7 %collective-permute-done.1 = bf16[2,4,1024]{2,1,0:T(4,128)(2,1)S(1)} collective-permute-done((bf16[2,4,1024]{2,1,0:T(4,128)(2,1)S(1)}, bf16[2,4,1024]{2,1,0:T(4,128)(2,1)S(1)}, u32[]{:S(2)}, u32[]{:S(2)}) %collective-permute-start.1) | collective-permute-done | bytes 16416 | tf_op jit(solution)/shard_map/ppermute | solution.py:108
  11.0 3.1 %collective-permute-start.2 = (bf16[4,4,1024]{2,1,0:T(4,128)(2,1)S(1)}, bf16[4,4,1024]{2,1,0:T(4,128)(2,1)S(1)}, u32[]{:S(2)}, u32[]{:S(2)}) collective-permute-start(bf16[4,4,1024]{2,1,0:T(4,128)(2,1)S(1)} %pad_maximum_fusion.2), channel_id=1, source_target_pairs={{0,8},{4,12},{8,0},{12,4},{1,9},{5,13},{9,1},{13,5},{2,10},{6,14},... | collective-permute-start | bytes 98312 | tf_op jit(solution)/shard_map/ppermute | solution.py:108
  14.2 0.6 %copy.30 = bf16[1,64,4,3,512]{4,3,2,1,0:T(4,128)(2,1)S(1)} copy(bf16[1,64,4,3,512]{4,2,3,1,0:T(4,128)(2,1)S(1)} %fusion.2) | data formatting | bytes 1572864 | tf_op jit(solution)/shard_map/convert_element_type | solution.py:146
  14.8 1.8 %reshape_reshape.4.n_ref = bf16[64,6144]{1,0:T(8,128)(2,1)} reshape(bf16[1,64,4,3,512]{4,3,2,1,0:T(4,128)(2,1)S(1)} %copy.30) | data formatting | bytes 1572864 | tf_op jit(solution)/shard_map/reshape;reshape | solution.py:73
  16.9 0.2 convert_reduce_fusion.1
  17.2 0.1 fusion
  17.5 0.6 %mul.38.x_ref = f32[96,128]{1,0:T(8,128)} multiply(f32[96,128]{1,0:T(8,128)S(1)} %reshape.133, f32[96,128]{1,0:T(8,128)S(1)} %mul.37) | non-fusion elementwise | flops 12288 | bytes 147456 | tf_op jit(solution)/shard_map/mul | solution.py:139
  18.1 4.3 %shard_map.46 = f32[64,512]{1,0:T(8,128)} custom-call(f32[96,128]{1,0:T(8,128)} %mul.38.x_ref, bf16[64,6144]{1,0:T(8,128)(2,1)} %reshape_reshape.4.n_ref), custom_call_target="tpu_custom_call" | custom-call | tf_op jit(solution)/shard_map/pallas_call | solution.py:69
  22.4 1.6 %collective-permute-start.3 = (f32[64,512]{1,0:T(8,128)}, f32[64,512]{1,0:T(8,128)S(1)}, u32[]{:S(2)}, u32[]{:S(2)}) collective-permute-start(f32[64,512]{1,0:T(8,128)} %shard_map.46), channel_id=1, source_target_pairs={{0,4},{4,0},{8,12},{12,8},{1,5},{5,1},{9,13},{13,9},{2,6},{6,2},{1... | collective-permute-start | bytes 393224 | tf_op jit(solution)/shard_map/ppermute | solution.py:81
  24.0 3.6 %collective-permute-done.3 = f32[64,512]{1,0:T(8,128)S(1)} collective-permute-done((f32[64,512]{1,0:T(8,128)}, f32[64,512]{1,0:T(8,128)S(1)}, u32[]{:S(2)}, u32[]{:S(2)}) %collective-permute-start.3) | collective-permute-done | bytes 131104 | tf_op jit(solution)/shard_map/ppermute | solution.py:81
  27.6 0.9 %add.56 = f32[64,512]{1,0:T(8,128)S(1)} add(f32[64,512]{1,0:T(8,128)} %shard_map.46, f32[64,512]{1,0:T(8,128)S(1)} %collective-permute-done.3) | non-fusion elementwise | flops 32768 | bytes 393216 | tf_op jit(solution)/shard_map/add | solution.py:81
  28.5 2.3 %collective-permute-start.4 = (f32[64,512]{1,0:T(8,128)S(1)}, f32[64,512]{1,0:T(8,128)S(1)}, u32[]{:S(2)}, u32[]{:S(2)}) collective-permute-start(f32[64,512]{1,0:T(8,128)S(1)} %add.56), channel_id=1, source_target_pairs={{0,8},{4,12},{8,0},{12,4},{1,9},{5,13},{9,1},{13,5},{2,10},{6,14},... | collective-permute-start | bytes 393224 | tf_op jit(solution)/shard_map/ppermute | solution.py:81
  30.8 3.6 %collective-permute-done.4 = f32[64,512]{1,0:T(8,128)S(1)} collective-permute-done((f32[64,512]{1,0:T(8,128)S(1)}, f32[64,512]{1,0:T(8,128)S(1)}, u32[]{:S(2)}, u32[]{:S(2)}) %collective-permute-start.4) | collective-permute-done | bytes 131104 | tf_op jit(solution)/shard_map/ppermute | solution.py:81
  34.6 3.0 %collective-permute-start.5 = (f32[64]{0:T(128)S(1)}, f32[64]{0:T(128)S(1)}, u32[]{:S(2)}, u32[]{:S(2)}) collective-permute-start(f32[64]{0:T(128)S(1)} %get-tuple-element.5), channel_id=1, source_target_pairs={{0,2},{2,0},{1,3},{3,1},{4,6},{6,4},{5,7},{7,5},{8,10},{10,8},{9,1... | collective-permute-start | bytes 776 | tf_op jit(solution)/shard_map/ppermute | solution.py:81
  37.6 0.2 rev.11
  37.9 1.2 %collective-permute-done.5 = f32[64]{0:T(128)S(1)} collective-permute-done((f32[64]{0:T(128)S(1)}, f32[64]{0:T(128)S(1)}, u32[]{:S(2)}, u32[]{:S(2)}) %collective-permute-start.5) | collective-permute-done | bytes 288 | tf_op jit(solution)/shard_map/ppermute | solution.py:81
  39.1 0.7 %broadcast_divide_fusion = f32[1,64,512]{2,1,0:T(8,128)} fusion(f32[1,64,512]{2,1,0:T(8,128)S(1)} %reshape.131, f32[64]{0:T(128)S(1)} %add_sqrt_fusion.1), kind=kLoop, calls=%fused_computation.9 | loop fusion | flops 32768 | bytes 262400 | tf_op jit(solution)/shard_map/div | solution.py:151
  (37 shorter events, 1.4 us)
Async XLA Ops:
  0.0 4.0 %copy-start = (bf16[1,64,4,3,512]{4,2,3,1,0:T(4,128)(2,1)S(1)}, bf16[1,64,4,3,512]{4,2,3,1,0:T(4,128)(2,1)}, u32[]{:S(2)}) copy-start(bf16[1,64,4,3,512]{4,2,3,1,0:T(4,128)(2,1)} %param.5) | copy-start | bytes 2359300
  0.0 6.2 %collective-permute-start = (bf16[2,3,512]{2,0,1:T(2,128)(2,1)}, bf16[2,3,512]{2,0,1:T(2,128)(2,1)S(1)}, u32[]{:S(2)}, u32[]{:S(2)}) collective-permute-start(bf16[2,3,512]{2,0,1:T(2,128)(2,1)} %param.4), channel_id=1, source_target_pairs={{2,0},{3,1},{6,4},{7,5},{10,8},{11,9},{14,12},{15,13},{18,16},{19,... | collective-permute-start | bytes 18440 | tf_op jit(solution)/shard_map/ppermute | solution.py:96
  3.9 0.7 %copy-start.1 = (bf16[2,3,512]{2,0,1:T(2,128)(2,1)S(1)}, bf16[2,3,512]{2,0,1:T(2,128)(2,1)}, u32[]{:S(2)}) copy-start(bf16[2,3,512]{2,0,1:T(2,128)(2,1)} %param.4) | copy-start | bytes 18436
  3.9 0.7 %copy-start.2 = (s32[2]{0:T(128)S(1)}, s32[2]{0:T(128)}, u32[]{:S(2)}) copy-start(s32[2]{0:T(128)} %param.7) | copy-start | bytes 28
  6.4 4.5 %collective-permute-start.1 = (bf16[2,4,1024]{2,1,0:T(4,128)(2,1)S(1)}, bf16[2,4,1024]{2,1,0:T(4,128)(2,1)S(1)}, u32[]{:S(2)}, u32[]{:S(2)}) collective-permute-start(bf16[2,4,1024]{2,1,0:T(4,128)(2,1)S(1)} %pad_maximum_fusion.3), channel_id=1, source_target_pairs={{0,4},{4,0},{8,12},{12,8},{1,5},{5,1},{9,13},{13,9},{2,6},{6,2},{1... | collective-permute-start | bytes 49160 | tf_op jit(solution)/shard_map/ppermute | solution.py:108
  11.0 5.7 %collective-permute-start.2 = (bf16[4,4,1024]{2,1,0:T(4,128)(2,1)S(1)}, bf16[4,4,1024]{2,1,0:T(4,128)(2,1)S(1)}, u32[]{:S(2)}, u32[]{:S(2)}) collective-permute-start(bf16[4,4,1024]{2,1,0:T(4,128)(2,1)S(1)} %pad_maximum_fusion.2), channel_id=1, source_target_pairs={{0,8},{4,12},{8,0},{12,4},{1,9},{5,13},{9,1},{13,5},{2,10},{6,14},... | collective-permute-start | bytes 98312 | tf_op jit(solution)/shard_map/ppermute | solution.py:108
  22.4 5.2 %collective-permute-start.3 = (f32[64,512]{1,0:T(8,128)}, f32[64,512]{1,0:T(8,128)S(1)}, u32[]{:S(2)}, u32[]{:S(2)}) collective-permute-start(f32[64,512]{1,0:T(8,128)} %shard_map.46), channel_id=1, source_target_pairs={{0,4},{4,0},{8,12},{12,8},{1,5},{5,1},{9,13},{13,9},{2,6},{6,2},{1... | collective-permute-start | bytes 393224 | tf_op jit(solution)/shard_map/ppermute | solution.py:81
  28.5 5.9 %collective-permute-start.4 = (f32[64,512]{1,0:T(8,128)S(1)}, f32[64,512]{1,0:T(8,128)S(1)}, u32[]{:S(2)}, u32[]{:S(2)}) collective-permute-start(f32[64,512]{1,0:T(8,128)S(1)} %add.56), channel_id=1, source_target_pairs={{0,8},{4,12},{8,0},{12,4},{1,9},{5,13},{9,1},{13,5},{2,10},{6,14},... | collective-permute-start | bytes 393224 | tf_op jit(solution)/shard_map/ppermute | solution.py:81
  34.6 4.5 %collective-permute-start.5 = (f32[64]{0:T(128)S(1)}, f32[64]{0:T(128)S(1)}, u32[]{:S(2)}, u32[]{:S(2)}) collective-permute-start(f32[64]{0:T(128)S(1)} %get-tuple-element.5), channel_id=1, source_target_pairs={{0,2},{2,0},{1,3},{3,1},{4,6},{6,4},{5,7},{7,5},{8,10},{10,8},{9,1... | collective-permute-start | bytes 776 | tf_op jit(solution)/shard_map/ppermute | solution.py:81

commit v19 on v16

--- a/solution.py
+++ b/solution.py
@@ -84,6 +84,23 @@
     return jnp.sum(jnp.take(jnp.stack(received), order, axis=0), axis=0)
 
 
+def region_sum(part):
+    regions = lax.axis_size("region")
+    cores = lax.axis_size("tb")
+    if regions & (regions - 1) or cores != 2:
+        return ordered_sum(part, "region")
+    steps = []
+    step = 1
+    while step < regions:
+        steps.append(step)
+        step *= 2
+    for first, second in zip(steps, steps[::-1]):
+        pairs = [(r * 2, (r ^ first) * 2) for r in range(regions)]
+        pairs += [(r * 2 + 1, (r ^ second) * 2 + 1) for r in range(regions)]
+        part = part + lax.ppermute(part, ("region", "tb"), pairs)
+    return part
+
+
 def gather_owned(records, station_region, capacity, filter_taps):
     local_count, components, seg_len = records.shape
     regions = lax.axis_size("region")
@@ -142,7 +159,7 @@
     normed = (widened_templates * weight[..., None] / template_norm).astype(jnp.bfloat16)
     normed = normed.reshape(local_batches * kept, capacity * components, filter_taps)
     total_len = seg_len * lax.axis_size("seg")
-    stacked = ordered_sum(correlate(normed, flat_owned, seg_len), "region")
+    stacked = region_sum(correlate(normed, flat_owned, seg_len))
     power_sum = ordered_sum(jnp.sum(stacked * stacked, axis=1), "seg")
     detect = unflip(stacked) / jnp.sqrt(power_sum / total_len + 1e-06)[:, None]
     return detect.reshape(local_batches, kept, seg_len)

time: 39.8 us -> 40.5 us (1.018)
  waiting for transfers between devices: 11.6 us -> 13.5 us
  starting transfers between devices: 14.1 us -> 12.9 us
    ppermute x0 -> x2, waiting for transfers between devices: none -> 8.59 us  [region_sum(): part = part + lax.ppermute(part, ('region', 'tb'), pairs)]
    ppermute x3 -> x1, waiting for transfers between devices: 8.34 us -> 1.57 us  [ordered_sum(): part = part + lax.ppermute(part, axis, [(i, i ^ step) for i in range(size)])]
    ppermute x3 -> x1, starting transfers between devices: 6.83 us -> 1.73 us  [ordered_sum(): part = part + lax.ppermute(part, axis, [(i, i ^ step) for i in range(size)])]
    ppermute x0 -> x2, starting transfers between devices: none -> 3.92 us  [region_sum(): part = part + lax.ppermute(part, ('region', 'tb'), pairs)]
where the time goes in v19:
time: 40.5 us; the launch traced here: 40.2 us
  waiting for transfers between devices  13.5 us (33%)
  starting transfers between devices  12.9 us (32%)
  other arithmetic  5.37 us (13%)
  Pallas kernels  4.33 us (11%)
  local copies, waits for them, and re-layouts  3.81 us (9%)
    ppermute x2, waiting for transfers between devices, region_sum(): part = part + lax.ppermute(part, ('region', 'tb'), pairs)  8.59 us
    ppermute x2, starting transfers between devices, gather_owned(): lax.ppermute(here, 'region', [(r, r ^ step) for r in range(regions)])  5.89 us
    pallas_call x1, Pallas kernels, correlate(): pl.pallas_call(hankel_kernel, out_shape=jax.ShapeDtypeStruct((rows, seg_l...  4.33 us
    ppermute x2, starting transfers between devices, region_sum(): part = part + lax.ppermute(part, ('region', 'tb'), pairs)  3.92 us
    another operation x1, local copies, waits for them, and re-layouts, correlate(): normed.reshape(rows, channels * filter_taps)  1.84 us
    ppermute x1, starting transfers between devices, ordered_sum(): part = part + lax.ppermute(part, axis, [(i, i ^ step) for i in range(size)])  1.73 us
    ppermute x2, waiting for transfers between devices, gather_owned(): lax.ppermute(here, 'region', [(r, r ^ step) for r in range(regions)])  1.72 us
    reduce_sum x1, other arithmetic, per_device(): jnp.sum(widened_templates * widened_templates, axis=4, keepdims=True)  1.65 us
  transfers between devices with their start and end apart: 6, of which 5 were waited for; matrix products, arithmetic and copies ran while one was open for 15% of the time, Pallas kernels for 0%

profile of v19, /device:TPU:0, one launch (start us, length us, event | category | flops | bytes accessed | tf_op | source)
XLA Modules:
  0.0 40.2 jit_solution(14643774878315071911)
XLA Ops:
  0.0 1.4 %collective-permute-start = (bf16[2,3,512]{2,0,1:T(2,128)(2,1)}, bf16[2,3,512]{2,0,1:T(2,128)(2,1)S(1)}, u32[]{:S(2)}, u32[]{:S(2)}) collective-permute-start(bf16[2,3,512]{2,0,1:T(2,128)(2,1)} %param.4), channel_id=1, source_target_pairs={{2,0},{3,1},{6,4},{7,5},{10,8},{11,9},{14,12},{15,13},{18,16},{19,... | collective-permute-start | bytes 18440 | tf_op jit(solution)/shard_map/ppermute | solution.py:108
  1.4 0.7 %convert_bitcast_fusion = f32[64,4,3]{0,1,2:T(4,128)S(1)} fusion(s32[1,64,4,3]{1,2,3,0:T(4,128)} %param.6), kind=kLoop, calls=%fused_computation.16 | loop fusion | flops 768 | bytes 6144 | tf_op jit(solution)/shard_map/mul | solution.py:159
  2.1 0.1 copy.9
  2.3 1.7 %fusion.3 = f32[64,4,3]{1,2,0:T(4,128)S(1)} fusion(bf16[1,64,4,3,512]{4,2,3,1,0:T(4,128)(2,1)} %param.5), kind=kLoop, calls=%fused_computation.6 | loop fusion | flops 1178880 | bytes 789504 | tf_op jit(solution)/shard_map/reduce_sum | solution.py:157
  4.0 0.5 %fusion.2 = bf16[1,64,4,3,512]{4,2,3,1,0:T(4,128)(2,1)S(1)} fusion(bf16[1,64,4,3,512]{4,2,3,1,0:T(4,128)(2,1)S(1)} %copy-done, f32[64,4,3]{1,2,0:T(4,128)S(1)} %add_sqrt_fusion, f32[64,4,3]{1,2,0:T(4,128)S(1)} %copy.9), kind=kLoop, calls=%fused_computation.5 | loop fusion | flops 1572864 | bytes 1579008 | tf_op jit(solution)/shard_map/convert_element_type | solution.py:159
  4.6 1.6 %collective-permute-done = bf16[2,3,512]{2,0,1:T(2,128)(2,1)S(1)} collective-permute-done((bf16[2,3,512]{2,0,1:T(2,128)(2,1)}, bf16[2,3,512]{2,0,1:T(2,128)(2,1)S(1)}, u32[]{:S(2)}, u32[]{:S(2)}) %collective-permute-start) | collective-permute-done | bytes 6176 | tf_op jit(solution)/shard_map/ppermute | solution.py:108
  6.3 2.8 %collective-permute-start.1 = (bf16[2,4,1024]{2,0,1:T(2,128)(2,1)S(1)}, bf16[2,4,1024]{2,0,1:T(2,128)(2,1)S(1)}, u32[]{:S(2)}, u32[]{:S(2)}) collective-permute-start(bf16[2,4,1024]{2,0,1:T(2,128)(2,1)S(1)} %pad_maximum_fusion.5), channel_id=1, source_target_pairs={{0,4},{4,0},{8,12},{12,8},{1,5},{5,1},{9,13},{13,9},{2,6},{6,2},{1... | collective-permute-start | bytes 49160 | tf_op jit(solution)/shard_map/ppermute | solution.py:121
  9.1 1.7 %collective-permute-done.1 = bf16[2,4,1024]{2,0,1:T(2,128)(2,1)S(1)} collective-permute-done((bf16[2,4,1024]{2,0,1:T(2,128)(2,1)S(1)}, bf16[2,4,1024]{2,0,1:T(2,128)(2,1)S(1)}, u32[]{:S(2)}, u32[]{:S(2)}) %collective-permute-start.1) | collective-permute-done | bytes 16416 | tf_op jit(solution)/shard_map/ppermute | solution.py:121
  10.8 3.1 %collective-permute-start.2 = (bf16[4,4,1024]{2,0,1:T(4,128)(2,1)S(1)}, bf16[4,4,1024]{2,0,1:T(4,128)(2,1)S(1)}, u32[]{:S(2)}, u32[]{:S(2)}) collective-permute-start(bf16[4,4,1024]{2,0,1:T(4,128)(2,1)S(1)} %pad_maximum_fusion.4), channel_id=1, source_target_pairs={{0,8},{4,12},{8,0},{12,4},{1,9},{5,13},{9,1},{13,5},{2,10},{6,14},... | collective-permute-start | bytes 98312 | tf_op jit(solution)/shard_map/ppermute | solution.py:121
  14.1 0.6 %copy.10 = bf16[1,64,4,3,512]{4,3,2,1,0:T(4,128)(2,1)S(1)} copy(bf16[1,64,4,3,512]{4,2,3,1,0:T(4,128)(2,1)S(1)} %fusion.2) | data formatting | bytes 1572864 | tf_op jit(solution)/shard_map/convert_element_type | solution.py:159
  14.6 1.8 %reshape_reshape.4.n_ref = bf16[64,6144]{1,0:T(8,128)(2,1)} reshape(bf16[1,64,4,3,512]{4,3,2,1,0:T(4,128)(2,1)S(1)} %copy.10) | data formatting | bytes 1572864 | tf_op jit(solution)/shard_map/reshape;reshape | solution.py:68
  16.6 0.2 convert_reduce_fusion.1
  17.0 0.1 fusion
  17.2 0.7 %rev.6.x_ref = f32[96,128]{1,0:T(8,128)} reverse(f32[96,128]{1,0:T(8,128)S(1)} %mul.38), dimensions={1} | reverse | bytes 98304 | tf_op jit(solution)/shard_map/rev | solution.py:63
  17.9 4.3 %shard_map.46 = f32[64,512]{1,0:T(8,128)} custom-call(f32[96,128]{1,0:T(8,128)} %rev.6.x_ref, bf16[64,6144]{1,0:T(8,128)(2,1)} %reshape_reshape.4.n_ref), custom_call_target="tpu_custom_call" | custom-call | tf_op jit(solution)/shard_map/pallas_call | solution.py:64
  22.3 1.6 %collective-permute-start.3 = (f32[64,512]{1,0:T(8,128)}, f32[64,512]{1,0:T(8,128)S(1)}, u32[]{:S(2)}, u32[]{:S(2)}) collective-permute-start(f32[64,512]{1,0:T(8,128)} %shard_map.46), channel_id=1, source_target_pairs={{0,4},{4,0},{8,12},{12,8},{1,9},{5,13},{9,1},{13,5},{2,6},{6,2},{1... | collective-permute-start | bytes 393224 | tf_op jit(solution)/shard_map/ppermute | solution.py:100
  23.8 3.6 %collective-permute-done.3 = f32[64,512]{1,0:T(8,128)S(1)} collective-permute-done((f32[64,512]{1,0:T(8,128)}, f32[64,512]{1,0:T(8,128)S(1)}, u32[]{:S(2)}, u32[]{:S(2)}) %collective-permute-start.3) | collective-permute-done | bytes 131104 | tf_op jit(solution)/shard_map/ppermute | solution.py:100
  27.4 0.9 %add.56 = f32[64,512]{1,0:T(8,128)S(1)} add(f32[64,512]{1,0:T(8,128)} %shard_map.46, f32[64,512]{1,0:T(8,128)S(1)} %collective-permute-done.3) | non-fusion elementwise | flops 32768 | bytes 393216 | tf_op jit(solution)/shard_map/add | solution.py:100
  28.4 2.3 %collective-permute-start.4 = (f32[64,512]{1,0:T(8,128)S(1)}, f32[64,512]{1,0:T(8,128)S(1)}, u32[]{:S(2)}, u32[]{:S(2)}) collective-permute-start(f32[64,512]{1,0:T(8,128)S(1)} %add.56), channel_id=1, source_target_pairs={{0,8},{4,12},{8,0},{12,4},{1,5},{5,1},{9,13},{13,9},{2,10},{6,14},... | collective-permute-start | bytes 393224 | tf_op jit(solution)/shard_map/ppermute | solution.py:100
  30.7 5.0 %collective-permute-done.4 = f32[64,512]{1,0:T(8,128)S(1)} collective-permute-done((f32[64,512]{1,0:T(8,128)S(1)}, f32[64,512]{1,0:T(8,128)S(1)}, u32[]{:S(2)}, u32[]{:S(2)}) %collective-permute-start.4) | collective-permute-done | bytes 131104 | tf_op jit(solution)/shard_map/ppermute | solution.py:100
  35.8 1.7 %collective-permute-start.5 = (f32[64]{0:T(128)S(1)}, f32[64]{0:T(128)S(1)}, u32[]{:S(2)}, u32[]{:S(2)}) collective-permute-start(f32[64]{0:T(128)S(1)} %get-tuple-element.5), channel_id=1, source_target_pairs={{0,2},{2,0},{1,3},{3,1},{4,6},{6,4},{5,7},{7,5},{8,10},{10,8},{9,1... | collective-permute-start | bytes 776 | tf_op jit(solution)/shard_map/ppermute | solution.py:76
  37.6 0.2 rev.7
  37.9 1.6 %collective-permute-done.5 = f32[64]{0:T(128)S(1)} collective-permute-done((f32[64]{0:T(128)S(1)}, f32[64]{0:T(128)S(1)}, u32[]{:S(2)}, u32[]{:S(2)}) %collective-permute-start.5) | collective-permute-done | bytes 288 | tf_op jit(solution)/shard_map/ppermute | solution.py:76
  39.4 0.7 %broadcast_divide_fusion = f32[1,64,512]{2,1,0:T(8,128)} fusion(f32[1,64,512]{2,1,0:T(8,128)S(1)} %reshape.115, f32[64]{0:T(128)S(1)} %add_sqrt_fusion.1), kind=kLoop, calls=%fused_computation.9 | loop fusion | flops 32768 | bytes 262400 | tf_op jit(solution)/shard_map/div | solution.py:164
  (27 shorter events, 1.1 us)
Async XLA Ops:
  0.0 4.0 %copy-start = (bf16[1,64,4,3,512]{4,2,3,1,0:T(4,128)(2,1)S(1)}, bf16[1,64,4,3,512]{4,2,3,1,0:T(4,128)(2,1)}, u32[]{:S(2)}) copy-start(bf16[1,64,4,3,512]{4,2,3,1,0:T(4,128)(2,1)} %param.5) | copy-start | bytes 2359300
  0.0 6.2 %collective-permute-start = (bf16[2,3,512]{2,0,1:T(2,128)(2,1)}, bf16[2,3,512]{2,0,1:T(2,128)(2,1)S(1)}, u32[]{:S(2)}, u32[]{:S(2)}) collective-permute-start(bf16[2,3,512]{2,0,1:T(2,128)(2,1)} %param.4), channel_id=1, source_target_pairs={{2,0},{3,1},{6,4},{7,5},{10,8},{11,9},{14,12},{15,13},{18,16},{19,... | collective-permute-start | bytes 18440 | tf_op jit(solution)/shard_map/ppermute | solution.py:108
  3.9 0.7 %copy-start.2 = (s32[2]{0:T(128)S(1)}, s32[2]{0:T(128)}, u32[]{:S(2)}) copy-start(s32[2]{0:T(128)} %param.7) | copy-start | bytes 28
  3.9 2.3 %copy-start.1 = (bf16[2,3,512]{2,0,1:T(2,128)(2,1)S(1)}, bf16[2,3,512]{2,0,1:T(2,128)(2,1)}, u32[]{:S(2)}) copy-start(bf16[2,3,512]{2,0,1:T(2,128)(2,1)} %param.4) | copy-start | bytes 18436
  6.3 4.5 %collective-permute-start.1 = (bf16[2,4,1024]{2,0,1:T(2,128)(2,1)S(1)}, bf16[2,4,1024]{2,0,1:T(2,128)(2,1)S(1)}, u32[]{:S(2)}, u32[]{:S(2)}) collective-permute-start(bf16[2,4,1024]{2,0,1:T(2,128)(2,1)S(1)} %pad_maximum_fusion.5), channel_id=1, source_target_pairs={{0,4},{4,0},{8,12},{12,8},{1,5},{5,1},{9,13},{13,9},{2,6},{6,2},{1... | collective-permute-start | bytes 49160 | tf_op jit(solution)/shard_map/ppermute | solution.py:121
  10.8 5.7 %collective-permute-start.2 = (bf16[4,4,1024]{2,0,1:T(4,128)(2,1)S(1)}, bf16[4,4,1024]{2,0,1:T(4,128)(2,1)S(1)}, u32[]{:S(2)}, u32[]{:S(2)}) collective-permute-start(bf16[4,4,1024]{2,0,1:T(4,128)(2,1)S(1)} %pad_maximum_fusion.4), channel_id=1, source_target_pairs={{0,8},{4,12},{8,0},{12,4},{1,9},{5,13},{9,1},{13,5},{2,10},{6,14},... | collective-permute-start | bytes 98312 | tf_op jit(solution)/shard_map/ppermute | solution.py:121
  22.3 5.2 %collective-permute-start.3 = (f32[64,512]{1,0:T(8,128)}, f32[64,512]{1,0:T(8,128)S(1)}, u32[]{:S(2)}, u32[]{:S(2)}) collective-permute-start(f32[64,512]{1,0:T(8,128)} %shard_map.46), channel_id=1, source_target_pairs={{0,4},{4,0},{8,12},{12,8},{1,9},{5,13},{9,1},{13,5},{2,6},{6,2},{1... | collective-permute-start | bytes 393224 | tf_op jit(solution)/shard_map/ppermute | solution.py:100
  28.4 7.3 %collective-permute-start.4 = (f32[64,512]{1,0:T(8,128)S(1)}, f32[64,512]{1,0:T(8,128)S(1)}, u32[]{:S(2)}, u32[]{:S(2)}) collective-permute-start(f32[64,512]{1,0:T(8,128)S(1)} %add.56), channel_id=1, source_target_pairs={{0,8},{4,12},{8,0},{12,4},{1,5},{5,1},{9,13},{13,9},{2,10},{6,14},... | collective-permute-start | bytes 393224 | tf_op jit(solution)/shard_map/ppermute | solution.py:100
  35.8 3.6 %collective-permute-start.5 = (f32[64]{0:T(128)S(1)}, f32[64]{0:T(128)S(1)}, u32[]{:S(2)}, u32[]{:S(2)}) collective-permute-start(f32[64]{0:T(128)S(1)} %get-tuple-element.5), channel_id=1, source_target_pairs={{0,2},{2,0},{1,3},{3,1},{4,6},{6,4},{5,7},{7,5},{8,10},{10,8},{9,1... | collective-permute-start | bytes 776 | tf_op jit(solution)/shard_map/ppermute | solution.py:76

commit v20 on v16

--- a/solution.py
+++ b/solution.py
@@ -73,7 +73,16 @@
     if size & (size - 1) == 0:
         step = 1
         while step < size:
-            part = part + lax.ppermute(part, axis, [(i, i ^ step) for i in range(size)])
+            pairs = [(i, i ^ step) for i in range(size)]
+            if part.ndim == 2 and part.shape[1] % 256 == 0:
+                half = part.shape[1] // 2
+                theirs = jnp.concatenate(
+                    [lax.ppermute(part[:, :half], axis, pairs), lax.ppermute(part[:, half:], axis, pairs)],
+                    axis=1,
+                )
+            else:
+                theirs = lax.ppermute(part, axis, pairs)
+            part = part + theirs
             step *= 2
         return part
     me = lax.axis_index(axis)

time: 39.8 us -> 43.5 us (1.093)
  waiting for transfers between devices: 11.6 us -> 14.9 us
  local copies, waits for them, and re-layouts: 3.81 us -> 4.7 us
    ppermute x3 -> x5, waiting for transfers between devices: 8.34 us -> 11.6 us  [the longest x2 5.18 us: ordered_sum(): lax.ppermute(part[:, :half], axis, pairs)]
    slice x0 -> x2, local copies, waits for them, and re-layouts: none -> 0.89 us  [ordered_sum(): part[:, :half]]
    ppermute x3 -> x5, starting transfers between devices: 6.83 us -> 6.35 us  [the longest x2 4.5 us: ordered_sum(): lax.ppermute(part[:, :half], axis, pairs)]
  transfers between devices with their start and end apart: 6 -> 8, of which waited for: 5 -> 7; matrix products, arithmetic and copies ran while one was open for 15% -> 14% of each run, Pallas kernels for 0% -> 0%
where the time goes in v20:
time: 43.5 us; the launch traced here: 43.2 us
  waiting for transfers between devices  14.9 us (34%)
  starting transfers between devices  13.7 us (31%)
  other arithmetic  5.36 us (12%)
  local copies, waits for them, and re-layouts  4.7 us (11%)
  Pallas kernels  4.33 us (10%)
    ppermute x2, starting transfers between devices, gather_owned(): lax.ppermute(here, 'region', [(r, r ^ step) for r in range(regions)])  5.89 us
    ppermute x2, waiting for transfers between devices, ordered_sum(): lax.ppermute(part[:, :half], axis, pairs)  5.18 us
    ppermute x2, starting transfers between devices, ordered_sum(): lax.ppermute(part[:, :half], axis, pairs)  4.5 us
    ppermute x2, waiting for transfers between devices, ordered_sum(): lax.ppermute(part[:, half:], axis, pairs)  4.37 us
    pallas_call x1, Pallas kernels, correlate(): pl.pallas_call(hankel_kernel, out_shape=jax.ShapeDtypeStruct((rows, seg_l...  4.33 us
    ppermute x1, waiting for transfers between devices, ordered_sum(): theirs = lax.ppermute(part, axis, pairs)  2.03 us
    another operation x1, local copies, waits for them, and re-layouts, correlate(): normed.reshape(rows, channels * filter_taps)  1.84 us
    ppermute x2, waiting for transfers between devices, gather_owned(): lax.ppermute(here, 'region', [(r, r ^ step) for r in range(regions)])  1.72 us
  transfers between devices with their start and end apart: 8, of which 7 were waited for; matrix products, arithmetic and copies ran while one was open for 14% of the time, Pallas kernels for 0%

profile of v20, /device:TPU:0, one launch (start us, length us, event | category | flops | bytes accessed | tf_op | source)
XLA Modules:
  0.0 43.2 jit_solution(16103386695071950326)
XLA Ops:
  0.0 1.4 %collective-permute-start = (bf16[2,3,512]{2,0,1:T(2,128)(2,1)}, bf16[2,3,512]{2,0,1:T(2,128)(2,1)S(1)}, u32[]{:S(2)}, u32[]{:S(2)}) collective-permute-start(bf16[2,3,512]{2,0,1:T(2,128)(2,1)} %param.4), channel_id=1, source_target_pairs={{2,0},{3,1},{6,4},{7,5},{10,8},{11,9},{14,12},{15,13},{18,16},{19,... | collective-permute-start | bytes 18440 | tf_op jit(solution)/shard_map/ppermute | solution.py:100
  1.4 0.7 %convert_bitcast_fusion = f32[64,4,3]{0,1,2:T(4,128)S(1)} fusion(s32[1,64,4,3]{1,2,3,0:T(4,128)} %param.6), kind=kLoop, calls=%fused_computation.18 | loop fusion | flops 768 | bytes 6144 | tf_op jit(solution)/shard_map/mul | solution.py:151
  2.3 1.7 %fusion.3 = f32[64,4,3]{1,2,0:T(4,128)S(1)} fusion(bf16[1,64,4,3,512]{4,2,3,1,0:T(4,128)(2,1)} %param.5), kind=kLoop, calls=%fused_computation.6 | loop fusion | flops 1178880 | bytes 789504 | tf_op jit(solution)/shard_map/reduce_sum | solution.py:149
  4.0 0.5 %fusion.2 = bf16[1,64,4,3,512]{4,2,3,1,0:T(4,128)(2,1)S(1)} fusion(bf16[1,64,4,3,512]{4,2,3,1,0:T(4,128)(2,1)S(1)} %copy-done, f32[64,4,3]{1,2,0:T(4,128)S(1)} %add_sqrt_fusion, f32[64,4,3]{1,2,0:T(4,128)S(1)} %copy.9), kind=kLoop, calls=%fused_computation.5 | loop fusion | flops 1572864 | bytes 1579008 | tf_op jit(solution)/shard_map/convert_element_type | solution.py:151
  4.6 1.6 %collective-permute-done = bf16[2,3,512]{2,0,1:T(2,128)(2,1)S(1)} collective-permute-done((bf16[2,3,512]{2,0,1:T(2,128)(2,1)}, bf16[2,3,512]{2,0,1:T(2,128)(2,1)S(1)}, u32[]{:S(2)}, u32[]{:S(2)}) %collective-permute-start) | collective-permute-done | bytes 6176 | tf_op jit(solution)/shard_map/ppermute | solution.py:100
  6.3 2.8 %collective-permute-start.1 = (bf16[2,4,1024]{2,0,1:T(2,128)(2,1)S(1)}, bf16[2,4,1024]{2,0,1:T(2,128)(2,1)S(1)}, u32[]{:S(2)}, u32[]{:S(2)}) collective-permute-start(bf16[2,4,1024]{2,0,1:T(2,128)(2,1)S(1)} %pad_maximum_fusion.5), channel_id=1, source_target_pairs={{0,4},{4,0},{8,12},{12,8},{1,5},{5,1},{9,13},{13,9},{2,6},{6,2},{1... | collective-permute-start | bytes 49160 | tf_op jit(solution)/shard_map/ppermute | solution.py:113
  9.1 1.7 %collective-permute-done.1 = bf16[2,4,1024]{2,0,1:T(2,128)(2,1)S(1)} collective-permute-done((bf16[2,4,1024]{2,0,1:T(2,128)(2,1)S(1)}, bf16[2,4,1024]{2,0,1:T(2,128)(2,1)S(1)}, u32[]{:S(2)}, u32[]{:S(2)}) %collective-permute-start.1) | collective-permute-done | bytes 16416 | tf_op jit(solution)/shard_map/ppermute | solution.py:113
  10.8 3.1 %collective-permute-start.2 = (bf16[4,4,1024]{2,0,1:T(4,128)(2,1)S(1)}, bf16[4,4,1024]{2,0,1:T(4,128)(2,1)S(1)}, u32[]{:S(2)}, u32[]{:S(2)}) collective-permute-start(bf16[4,4,1024]{2,0,1:T(4,128)(2,1)S(1)} %pad_maximum_fusion.4), channel_id=1, source_target_pairs={{0,8},{4,12},{8,0},{12,4},{1,9},{5,13},{9,1},{13,5},{2,10},{6,14},... | collective-permute-start | bytes 98312 | tf_op jit(solution)/shard_map/ppermute | solution.py:113
  14.1 0.6 %copy.10 = bf16[1,64,4,3,512]{4,3,2,1,0:T(4,128)(2,1)S(1)} copy(bf16[1,64,4,3,512]{4,2,3,1,0:T(4,128)(2,1)S(1)} %fusion.2) | data formatting | bytes 1572864 | tf_op jit(solution)/shard_map/convert_element_type | solution.py:151
  14.6 1.8 %reshape_reshape.4.n_ref = bf16[64,6144]{1,0:T(8,128)(2,1)} reshape(bf16[1,64,4,3,512]{4,3,2,1,0:T(4,128)(2,1)S(1)} %copy.10) | data formatting | bytes 1572864 | tf_op jit(solution)/shard_map/reshape;reshape | solution.py:68
  17.2 0.7 %rev.6.x_ref = f32[96,128]{1,0:T(8,128)} reverse(f32[96,128]{1,0:T(8,128)S(1)} %mul.38), dimensions={1} | reverse | bytes 98304 | tf_op jit(solution)/shard_map/rev | solution.py:63
  17.9 4.3 %shard_map.46 = f32[64,512]{1,0:T(8,128)} custom-call(f32[96,128]{1,0:T(8,128)} %rev.6.x_ref, bf16[64,6144]{1,0:T(8,128)(2,1)} %reshape_reshape.4.n_ref), custom_call_target="tpu_custom_call" | custom-call | tf_op jit(solution)/shard_map/pallas_call | solution.py:64
  22.3 0.9 %fusion.9 = (f32[64,256]{1,0:T(8,128)S(1)}, f32[64,256]{1,0:T(8,128)S(1)}) fusion(f32[64,512]{1,0:T(8,128)} %shard_map.46), kind=kLoop, calls=%fused_computation.31 | loop fusion | bytes 262144 | tf_op jit(solution)/shard_map/slice | solution.py:80
  23.2 1.6 %collective-permute-start.3 = (f32[64,256]{1,0:T(8,128)S(1)}, f32[64,256]{1,0:T(8,128)S(1)}, u32[]{:S(2)}, u32[]{:S(2)}) collective-permute-start(f32[64,256]{1,0:T(8,128)S(1)} %get-tuple-element.9), channel_id=1, source_target_pairs={{0,4},{4,0},{8,12},{12,8},{1,5},{5,1},{9,13},{13,9},{2,6},{6,2},{1... | collective-permute-start | bytes 196616 | tf_op jit(solution)/shard_map/ppermute | solution.py:80
  24.8 0.4 %collective-permute-start.4 = (f32[64,256]{1,0:T(8,128)S(1)}, f32[64,256]{1,0:T(8,128)S(1)}, u32[]{:S(2)}, u32[]{:S(2)}) collective-permute-start(f32[64,256]{1,0:T(8,128)S(1)} %get-tuple-element.10), channel_id=1, source_target_pairs={{0,4},{4,0},{8,12},{12,8},{1,5},{5,1},{9,13},{13,9},{2,6},{6,2},{1... | collective-permute-start | bytes 196616 | tf_op jit(solution)/shard_map/ppermute | solution.py:80
  25.2 2.2 %collective-permute-done.3 = f32[64,256]{1,0:T(8,128)S(1)} collective-permute-done((f32[64,256]{1,0:T(8,128)S(1)}, f32[64,256]{1,0:T(8,128)S(1)}, u32[]{:S(2)}, u32[]{:S(2)}) %collective-permute-start.3) | collective-permute-done | bytes 65568 | tf_op jit(solution)/shard_map/ppermute | solution.py:80
  27.5 1.6 %collective-permute-done.4 = f32[64,256]{1,0:T(8,128)S(1)} collective-permute-done((f32[64,256]{1,0:T(8,128)S(1)}, f32[64,256]{1,0:T(8,128)S(1)}, u32[]{:S(2)}, u32[]{:S(2)}) %collective-permute-start.4) | collective-permute-done | bytes 65568 | tf_op jit(solution)/shard_map/ppermute | solution.py:80
  29.1 0.9 %maximum_add_fusion = f32[64,512]{1,0:T(8,128)S(1)} fusion(f32[64,512]{1,0:T(8,128)} %shard_map.46, f32[64,256]{1,0:T(8,128)S(1)} %collective-permute-done.4, f32[64,256]{1,0:T(8,128)S(1)} %collective-permute-done.3), kind=kLoop, calls=%fused_computation.7 | loop fusion | flops 65536 | bytes 393216 | tf_op jit(solution)/shard_map/add | solution.py:85
  30.0 2.9 %collective-permute-start.5 = (f32[64,256]{1,0:T(8,128)S(1)}, f32[64,256]{1,0:T(8,128)S(1)}, u32[]{:S(2)}, u32[]{:S(2)}) collective-permute-start(f32[64,256]{1,0:T(8,128)S(1)} %get-tuple-element.7), channel_id=1, source_target_pairs={{0,8},{4,12},{8,0},{12,4},{1,9},{5,13},{9,1},{13,5},{2,10},{6,14},... | collective-permute-start | bytes 196616 | tf_op jit(solution)/shard_map/ppermute | solution.py:80
  33.0 2.9 %collective-permute-done.5 = f32[64,256]{1,0:T(8,128)S(1)} collective-permute-done((f32[64,256]{1,0:T(8,128)S(1)}, f32[64,256]{1,0:T(8,128)S(1)}, u32[]{:S(2)}, u32[]{:S(2)}) %collective-permute-start.5) | collective-permute-done | bytes 65568 | tf_op jit(solution)/shard_map/ppermute | solution.py:80
  35.9 2.8 %collective-permute-done.6 = f32[64,256]{1,0:T(8,128)S(1)} collective-permute-done((f32[64,256]{1,0:T(8,128)S(1)}, f32[64,256]{1,0:T(8,128)S(1)}, u32[]{:S(2)}, u32[]{:S(2)}) %collective-permute-start.6) | collective-permute-done | bytes 65568 | tf_op jit(solution)/shard_map/ppermute | solution.py:80
  38.9 1.3 %collective-permute-start.7 = (f32[64]{0:T(128)S(1)}, f32[64]{0:T(128)S(1)}, u32[]{:S(2)}, u32[]{:S(2)}) collective-permute-start(f32[64]{0:T(128)S(1)} %get-tuple-element.5), channel_id=1, source_target_pairs={{0,2},{2,0},{1,3},{3,1},{4,6},{6,4},{5,7},{7,5},{8,10},{10,8},{9,1... | collective-permute-start | bytes 776 | tf_op jit(solution)/shard_map/ppermute | solution.py:84
  40.4 2.0 %collective-permute-done.7 = f32[64]{0:T(128)S(1)} collective-permute-done((f32[64]{0:T(128)S(1)}, f32[64]{0:T(128)S(1)}, u32[]{:S(2)}, u32[]{:S(2)}) %collective-permute-start.7) | collective-permute-done | bytes 288 | tf_op jit(solution)/shard_map/ppermute | solution.py:84
  42.5 0.7 %broadcast_divide_fusion = f32[1,64,512]{2,1,0:T(8,128)} fusion(f32[1,64,512]{2,1,0:T(8,128)S(1)} %reshape.115, f32[64]{0:T(128)S(1)} %add_sqrt_fusion.1), kind=kLoop, calls=%fused_computation.11 | loop fusion | flops 32768 | bytes 262400 | tf_op jit(solution)/shard_map/div | solution.py:156
  (33 shorter events, 1.8 us)
Async XLA Ops:
  0.0 4.0 %copy-start = (bf16[1,64,4,3,512]{4,2,3,1,0:T(4,128)(2,1)S(1)}, bf16[1,64,4,3,512]{4,2,3,1,0:T(4,128)(2,1)}, u32[]{:S(2)}) copy-start(bf16[1,64,4,3,512]{4,2,3,1,0:T(4,128)(2,1)} %param.5) | copy-start | bytes 2359300
  0.0 6.2 %collective-permute-start = (bf16[2,3,512]{2,0,1:T(2,128)(2,1)}, bf16[2,3,512]{2,0,1:T(2,128)(2,1)S(1)}, u32[]{:S(2)}, u32[]{:S(2)}) collective-permute-start(bf16[2,3,512]{2,0,1:T(2,128)(2,1)} %param.4), channel_id=1, source_target_pairs={{2,0},{3,1},{6,4},{7,5},{10,8},{11,9},{14,12},{15,13},{18,16},{19,... | collective-permute-start | bytes 18440 | tf_op jit(solution)/shard_map/ppermute | solution.py:100
  3.9 0.7 %copy-start.2 = (s32[2]{0:T(128)S(1)}, s32[2]{0:T(128)}, u32[]{:S(2)}) copy-start(s32[2]{0:T(128)} %param.7) | copy-start | bytes 28
  3.9 2.3 %copy-start.1 = (bf16[2,3,512]{2,0,1:T(2,128)(2,1)S(1)}, bf16[2,3,512]{2,0,1:T(2,128)(2,1)}, u32[]{:S(2)}) copy-start(bf16[2,3,512]{2,0,1:T(2,128)(2,1)} %param.4) | copy-start | bytes 18436
  6.3 4.5 %collective-permute-start.1 = (bf16[2,4,1024]{2,0,1:T(2,128)(2,1)S(1)}, bf16[2,4,1024]{2,0,1:T(2,128)(2,1)S(1)}, u32[]{:S(2)}, u32[]{:S(2)}) collective-permute-start(bf16[2,4,1024]{2,0,1:T(2,128)(2,1)S(1)} %pad_maximum_fusion.5), channel_id=1, source_target_pairs={{0,4},{4,0},{8,12},{12,8},{1,5},{5,1},{9,13},{13,9},{2,6},{6,2},{1... | collective-permute-start | bytes 49160 | tf_op jit(solution)/shard_map/ppermute | solution.py:113
  10.8 5.7 %collective-permute-start.2 = (bf16[4,4,1024]{2,0,1:T(4,128)(2,1)S(1)}, bf16[4,4,1024]{2,0,1:T(4,128)(2,1)S(1)}, u32[]{:S(2)}, u32[]{:S(2)}) collective-permute-start(bf16[4,4,1024]{2,0,1:T(4,128)(2,1)S(1)} %pad_maximum_fusion.4), channel_id=1, source_target_pairs={{0,8},{4,12},{8,0},{12,4},{1,9},{5,13},{9,1},{13,5},{2,10},{6,14},... | collective-permute-start | bytes 98312 | tf_op jit(solution)/shard_map/ppermute | solution.py:113
  23.2 4.3 %collective-permute-start.3 = (f32[64,256]{1,0:T(8,128)S(1)}, f32[64,256]{1,0:T(8,128)S(1)}, u32[]{:S(2)}, u32[]{:S(2)}) collective-permute-start(f32[64,256]{1,0:T(8,128)S(1)} %get-tuple-element.9), channel_id=1, source_target_pairs={{0,4},{4,0},{8,12},{12,8},{1,5},{5,1},{9,13},{13,9},{2,6},{6,2},{1... | collective-permute-start | bytes 196616 | tf_op jit(solution)/shard_map/ppermute | solution.py:80
  24.8 4.3 %collective-permute-start.4 = (f32[64,256]{1,0:T(8,128)S(1)}, f32[64,256]{1,0:T(8,128)S(1)}, u32[]{:S(2)}, u32[]{:S(2)}) collective-permute-start(f32[64,256]{1,0:T(8,128)S(1)} %get-tuple-element.10), channel_id=1, source_target_pairs={{0,4},{4,0},{8,12},{12,8},{1,5},{5,1},{9,13},{13,9},{2,6},{6,2},{1... | collective-permute-start | bytes 196616 | tf_op jit(solution)/shard_map/ppermute | solution.py:80
  30.0 5.9 %collective-permute-start.5 = (f32[64,256]{1,0:T(8,128)S(1)}, f32[64,256]{1,0:T(8,128)S(1)}, u32[]{:S(2)}, u32[]{:S(2)}) collective-permute-start(f32[64,256]{1,0:T(8,128)S(1)} %get-tuple-element.7), channel_id=1, source_target_pairs={{0,8},{4,12},{8,0},{12,4},{1,9},{5,13},{9,1},{13,5},{2,10},{6,14},... | collective-permute-start | bytes 196616 | tf_op jit(solution)/shard_map/ppermute | solution.py:80
  32.9 5.9 %collective-permute-start.6 = (f32[64,256]{1,0:T(8,128)S(1)}, f32[64,256]{1,0:T(8,128)S(1)}, u32[]{:S(2)}, u32[]{:S(2)}) collective-permute-start(f32[64,256]{1,0:T(8,128)S(1)} %get-tuple-element.8), channel_id=1, source_target_pairs={{0,8},{4,12},{8,0},{12,4},{1,9},{5,13},{9,1},{13,5},{2,10},{6,14},... | collective-permute-start | bytes 196616 | tf_op jit(solution)/shard_map/ppermute | solution.py:80
  38.9 3.6 %collective-permute-start.7 = (f32[64]{0:T(128)S(1)}, f32[64]{0:T(128)S(1)}, u32[]{:S(2)}, u32[]{:S(2)}) collective-permute-start(f32[64]{0:T(128)S(1)} %get-tuple-element.5), channel_id=1, source_target_pairs={{0,2},{2,0},{1,3},{3,1},{4,6},{6,4},{5,7},{7,5},{8,10},{10,8},{9,1... | collective-permute-start | bytes 776 | tf_op jit(solution)/shard_map/ppermute | solution.py:84

commit v21 on v16

--- a/solution.py
+++ b/solution.py
@@ -21,21 +21,19 @@
             pltpu.roll(x_ref[pl.ds(c * blocks + m, 128, stride=0), :], 0, 1, stride=1, stride_axis=0)
             for m in range(blocks)
         ]
-        squares = []
-        for m in range(blocks - 1):
-            window = jnp.where(low, rolled[m], rolled[m + 1])
-            squares.append(jnp.sum(window * window, axis=0, keepdims=True))
-            window = window.astype(jnp.bfloat16)
-            for p in range(taps_blocks):
-                a = m - p
-                if 0 <= a < out_blocks:
-                    h_ref[slot, p * 128 : (p + 1) * 128, a * 128 : (a + 1) * 128] = window
-        energy = jnp.concatenate(
-            [sum(squares[a + p] for p in range(taps_blocks)) for a in range(out_blocks)], axis=1
-        )
+        windows = [jnp.where(low, rolled[m], rolled[m + 1]) for m in range(blocks - 1)]
+        squares = [jnp.sum(w * w, axis=0, keepdims=True) for w in windows]
+        scale = [
+            1.0 / jnp.sqrt(jnp.maximum(sum(squares[a + p] for p in range(taps_blocks)), 1.0))
+            for a in range(out_blocks)
+        ]
+        for p in range(taps_blocks):
+            for a in range(out_blocks):
+                h_ref[slot, p * 128 : (p + 1) * 128, a * 128 : (a + 1) * 128] = (
+                    windows[a + p] * scale[a]
+                ).astype(jnp.bfloat16)
         start = pl.multiple_of(c * width, 128)
-        part = jnp.dot(n_ref[:, pl.ds(start, width)], h_ref[slot], preferred_element_type=jnp.float32)
-        return acc + part * (1.0 / jnp.sqrt(jnp.maximum(energy, 1.0)))
+        return acc + jnp.dot(n_ref[:, pl.ds(start, width)], h_ref[slot], preferred_element_type=jnp.float32)
 
     def two_channels(i, acc):
         acc = one_channel(2 * i, 0, acc)

time: 39.8 us -> 40.2 us (1.010)
  no operation moved by 1% of the time
where the time goes in v21:
time: 40.2 us; the launch traced here: 39.9 us
  starting transfers between devices  14.1 us (35%)
  waiting for transfers between devices  11.6 us (29%)
  other arithmetic  5.37 us (13%)
  Pallas kernels  4.72 us (12%)
  local copies, waits for them, and re-layouts  3.81 us (9%)
    ppermute x3, waiting for transfers between devices, ordered_sum(): part = part + lax.ppermute(part, axis, [(i, i ^ step) for i in range(size)])  8.34 us
    ppermute x3, starting transfers between devices, ordered_sum(): part = part + lax.ppermute(part, axis, [(i, i ^ step) for i in range(size)])  6.83 us
    ppermute x2, starting transfers between devices, gather_owned(): lax.ppermute(here, 'region', [(r, r ^ step) for r in range(regions)])  5.89 us
    pallas_call x1, Pallas kernels, correlate(): pl.pallas_call(hankel_kernel, out_shape=jax.ShapeDtypeStruct((rows, seg_l...  4.72 us
    another operation x1, local copies, waits for them, and re-layouts, correlate(): normed.reshape(rows, channels * filter_taps)  1.84 us
    ppermute x2, waiting for transfers between devices, gather_owned(): lax.ppermute(here, 'region', [(r, r ^ step) for r in range(regions)])  1.72 us
    reduce_sum x1, other arithmetic, per_device(): jnp.sum(widened_templates * widened_templates, axis=4, keepdims=True)  1.65 us
    ppermute x1, waiting for transfers between devices, gather_owned(): lax.ppermute(records[:, :, :filter_taps], 'seg', [(s + 1, s) for s in ran...  1.57 us
  transfers between devices with their start and end apart: 6, of which 5 were waited for; matrix products, arithmetic and copies ran while one was open for 15% of the time, Pallas kernels for 0%

profile of v21, /device:TPU:0, one launch (start us, length us, event | category | flops | bytes accessed | tf_op | source)
XLA Modules:
  0.0 39.9 jit_solution(15635252233878176782)
XLA Ops:
  0.0 1.4 %collective-permute-start = (bf16[2,3,512]{2,0,1:T(2,128)(2,1)}, bf16[2,3,512]{2,0,1:T(2,128)(2,1)S(1)}, u32[]{:S(2)}, u32[]{:S(2)}) collective-permute-start(bf16[2,3,512]{2,0,1:T(2,128)(2,1)} %param.4), channel_id=1, source_target_pairs={{2,0},{3,1},{6,4},{7,5},{10,8},{11,9},{14,12},{15,13},{18,16},{19,... | collective-permute-start | bytes 18440 | tf_op jit(solution)/shard_map/ppermute | solution.py:89
  1.4 0.7 %convert_bitcast_fusion = f32[64,4,3]{0,1,2:T(4,128)S(1)} fusion(s32[1,64,4,3]{1,2,3,0:T(4,128)} %param.6), kind=kLoop, calls=%fused_computation.16 | loop fusion | flops 768 | bytes 6144 | tf_op jit(solution)/shard_map/mul | solution.py:140
  2.1 0.1 copy.9
  2.3 1.7 %fusion.3 = f32[64,4,3]{1,2,0:T(4,128)S(1)} fusion(bf16[1,64,4,3,512]{4,2,3,1,0:T(4,128)(2,1)} %param.5), kind=kLoop, calls=%fused_computation.6 | loop fusion | flops 1178880 | bytes 789504 | tf_op jit(solution)/shard_map/reduce_sum | solution.py:138
  4.0 0.5 %fusion.2 = bf16[1,64,4,3,512]{4,2,3,1,0:T(4,128)(2,1)S(1)} fusion(bf16[1,64,4,3,512]{4,2,3,1,0:T(4,128)(2,1)S(1)} %copy-done, f32[64,4,3]{1,2,0:T(4,128)S(1)} %add_sqrt_fusion, f32[64,4,3]{1,2,0:T(4,128)S(1)} %copy.9), kind=kLoop, calls=%fused_computation.5 | loop fusion | flops 1572864 | bytes 1579008 | tf_op jit(solution)/shard_map/convert_element_type | solution.py:140
  4.6 1.6 %collective-permute-done = bf16[2,3,512]{2,0,1:T(2,128)(2,1)S(1)} collective-permute-done((bf16[2,3,512]{2,0,1:T(2,128)(2,1)}, bf16[2,3,512]{2,0,1:T(2,128)(2,1)S(1)}, u32[]{:S(2)}, u32[]{:S(2)}) %collective-permute-start) | collective-permute-done | bytes 6176 | tf_op jit(solution)/shard_map/ppermute | solution.py:89
  6.3 2.8 %collective-permute-start.1 = (bf16[2,4,1024]{2,0,1:T(2,128)(2,1)S(1)}, bf16[2,4,1024]{2,0,1:T(2,128)(2,1)S(1)}, u32[]{:S(2)}, u32[]{:S(2)}) collective-permute-start(bf16[2,4,1024]{2,0,1:T(2,128)(2,1)S(1)} %pad_maximum_fusion.5), channel_id=1, source_target_pairs={{0,4},{4,0},{8,12},{12,8},{1,5},{5,1},{9,13},{13,9},{2,6},{6,2},{1... | collective-permute-start | bytes 49160 | tf_op jit(solution)/shard_map/ppermute | solution.py:102
  9.1 1.7 %collective-permute-done.1 = bf16[2,4,1024]{2,0,1:T(2,128)(2,1)S(1)} collective-permute-done((bf16[2,4,1024]{2,0,1:T(2,128)(2,1)S(1)}, bf16[2,4,1024]{2,0,1:T(2,128)(2,1)S(1)}, u32[]{:S(2)}, u32[]{:S(2)}) %collective-permute-start.1) | collective-permute-done | bytes 16416 | tf_op jit(solution)/shard_map/ppermute | solution.py:102
  10.8 3.1 %collective-permute-start.2 = (bf16[4,4,1024]{2,0,1:T(4,128)(2,1)S(1)}, bf16[4,4,1024]{2,0,1:T(4,128)(2,1)S(1)}, u32[]{:S(2)}, u32[]{:S(2)}) collective-permute-start(bf16[4,4,1024]{2,0,1:T(4,128)(2,1)S(1)} %pad_maximum_fusion.4), channel_id=1, source_target_pairs={{0,8},{4,12},{8,0},{12,4},{1,9},{5,13},{9,1},{13,5},{2,10},{6,14},... | collective-permute-start | bytes 98312 | tf_op jit(solution)/shard_map/ppermute | solution.py:102
  14.1 0.6 %copy.10 = bf16[1,64,4,3,512]{4,3,2,1,0:T(4,128)(2,1)S(1)} copy(bf16[1,64,4,3,512]{4,2,3,1,0:T(4,128)(2,1)S(1)} %fusion.2) | data formatting | bytes 1572864 | tf_op jit(solution)/shard_map/convert_element_type | solution.py:140
  14.6 1.8 %reshape_reshape.4.n_ref = bf16[64,6144]{1,0:T(8,128)(2,1)} reshape(bf16[1,64,4,3,512]{4,3,2,1,0:T(4,128)(2,1)S(1)} %copy.10) | data formatting | bytes 1572864 | tf_op jit(solution)/shard_map/reshape;reshape | solution.py:66
  16.6 0.2 convert_reduce_fusion.1
  17.0 0.1 fusion
  17.2 0.7 %rev.6.x_ref = f32[96,128]{1,0:T(8,128)} reverse(f32[96,128]{1,0:T(8,128)S(1)} %mul.38), dimensions={1} | reverse | bytes 98304 | tf_op jit(solution)/shard_map/rev | solution.py:61
  17.9 4.7 %shard_map.46 = f32[64,512]{1,0:T(8,128)} custom-call(f32[96,128]{1,0:T(8,128)} %rev.6.x_ref, bf16[64,6144]{1,0:T(8,128)(2,1)} %reshape_reshape.4.n_ref), custom_call_target="tpu_custom_call" | custom-call | tf_op jit(solution)/shard_map/pallas_call | solution.py:62
  22.7 1.6 %collective-permute-start.3 = (f32[64,512]{1,0:T(8,128)}, f32[64,512]{1,0:T(8,128)S(1)}, u32[]{:S(2)}, u32[]{:S(2)}) collective-permute-start(f32[64,512]{1,0:T(8,128)} %shard_map.46), channel_id=1, source_target_pairs={{0,4},{4,0},{8,12},{12,8},{1,5},{5,1},{9,13},{13,9},{2,6},{6,2},{1... | collective-permute-start | bytes 393224 | tf_op jit(solution)/shard_map/ppermute | solution.py:74
  24.2 3.6 %collective-permute-done.3 = f32[64,512]{1,0:T(8,128)S(1)} collective-permute-done((f32[64,512]{1,0:T(8,128)}, f32[64,512]{1,0:T(8,128)S(1)}, u32[]{:S(2)}, u32[]{:S(2)}) %collective-permute-start.3) | collective-permute-done | bytes 131104 | tf_op jit(solution)/shard_map/ppermute | solution.py:74
  27.8 0.9 %add.56 = f32[64,512]{1,0:T(8,128)S(1)} add(f32[64,512]{1,0:T(8,128)} %shard_map.46, f32[64,512]{1,0:T(8,128)S(1)} %collective-permute-done.3) | non-fusion elementwise | flops 32768 | bytes 393216 | tf_op jit(solution)/shard_map/add | solution.py:74
  28.8 2.4 %collective-permute-start.4 = (f32[64,512]{1,0:T(8,128)S(1)}, f32[64,512]{1,0:T(8,128)S(1)}, u32[]{:S(2)}, u32[]{:S(2)}) collective-permute-start(f32[64,512]{1,0:T(8,128)S(1)} %add.56), channel_id=1, source_target_pairs={{0,8},{4,12},{8,0},{12,4},{1,9},{5,13},{9,1},{13,5},{2,10},{6,14},... | collective-permute-start | bytes 393224 | tf_op jit(solution)/shard_map/ppermute | solution.py:74
  31.2 3.5 %collective-permute-done.4 = f32[64,512]{1,0:T(8,128)S(1)} collective-permute-done((f32[64,512]{1,0:T(8,128)S(1)}, f32[64,512]{1,0:T(8,128)S(1)}, u32[]{:S(2)}, u32[]{:S(2)}) %collective-permute-start.4) | collective-permute-done | bytes 131104 | tf_op jit(solution)/shard_map/ppermute | solution.py:74
  34.8 2.8 %collective-permute-start.5 = (f32[64]{0:T(128)S(1)}, f32[64]{0:T(128)S(1)}, u32[]{:S(2)}, u32[]{:S(2)}) collective-permute-start(f32[64]{0:T(128)S(1)} %get-tuple-element.5), channel_id=1, source_target_pairs={{0,2},{2,0},{1,3},{3,1},{4,6},{6,4},{5,7},{7,5},{8,10},{10,8},{9,1... | collective-permute-start | bytes 776 | tf_op jit(solution)/shard_map/ppermute | solution.py:74
  37.7 0.2 rev.7
  38.0 1.2 %collective-permute-done.5 = f32[64]{0:T(128)S(1)} collective-permute-done((f32[64]{0:T(128)S(1)}, f32[64]{0:T(128)S(1)}, u32[]{:S(2)}, u32[]{:S(2)}) %collective-permute-start.5) | collective-permute-done | bytes 288 | tf_op jit(solution)/shard_map/ppermute | solution.py:74
  39.2 0.7 %broadcast_divide_fusion = f32[1,64,512]{2,1,0:T(8,128)} fusion(f32[1,64,512]{2,1,0:T(8,128)S(1)} %reshape.115, f32[64]{0:T(128)S(1)} %add_sqrt_fusion.1), kind=kLoop, calls=%fused_computation.9 | loop fusion | flops 32768 | bytes 262400 | tf_op jit(solution)/shard_map/div | solution.py:145
  (27 shorter events, 1.1 us)
Async XLA Ops:
  0.0 4.0 %copy-start = (bf16[1,64,4,3,512]{4,2,3,1,0:T(4,128)(2,1)S(1)}, bf16[1,64,4,3,512]{4,2,3,1,0:T(4,128)(2,1)}, u32[]{:S(2)}) copy-start(bf16[1,64,4,3,512]{4,2,3,1,0:T(4,128)(2,1)} %param.5) | copy-start | bytes 2359300
  0.0 6.2 %collective-permute-start = (bf16[2,3,512]{2,0,1:T(2,128)(2,1)}, bf16[2,3,512]{2,0,1:T(2,128)(2,1)S(1)}, u32[]{:S(2)}, u32[]{:S(2)}) collective-permute-start(bf16[2,3,512]{2,0,1:T(2,128)(2,1)} %param.4), channel_id=1, source_target_pairs={{2,0},{3,1},{6,4},{7,5},{10,8},{11,9},{14,12},{15,13},{18,16},{19,... | collective-permute-start | bytes 18440 | tf_op jit(solution)/shard_map/ppermute | solution.py:89
  3.9 0.7 %copy-start.2 = (s32[2]{0:T(128)S(1)}, s32[2]{0:T(128)}, u32[]{:S(2)}) copy-start(s32[2]{0:T(128)} %param.7) | copy-start | bytes 28
  3.9 2.3 %copy-start.1 = (bf16[2,3,512]{2,0,1:T(2,128)(2,1)S(1)}, bf16[2,3,512]{2,0,1:T(2,128)(2,1)}, u32[]{:S(2)}) copy-start(bf16[2,3,512]{2,0,1:T(2,128)(2,1)} %param.4) | copy-start | bytes 18436
  6.3 4.5 %collective-permute-start.1 = (bf16[2,4,1024]{2,0,1:T(2,128)(2,1)S(1)}, bf16[2,4,1024]{2,0,1:T(2,128)(2,1)S(1)}, u32[]{:S(2)}, u32[]{:S(2)}) collective-permute-start(bf16[2,4,1024]{2,0,1:T(2,128)(2,1)S(1)} %pad_maximum_fusion.5), channel_id=1, source_target_pairs={{0,4},{4,0},{8,12},{12,8},{1,5},{5,1},{9,13},{13,9},{2,6},{6,2},{1... | collective-permute-start | bytes 49160 | tf_op jit(solution)/shard_map/ppermute | solution.py:102
  10.8 5.7 %collective-permute-start.2 = (bf16[4,4,1024]{2,0,1:T(4,128)(2,1)S(1)}, bf16[4,4,1024]{2,0,1:T(4,128)(2,1)S(1)}, u32[]{:S(2)}, u32[]{:S(2)}) collective-permute-start(bf16[4,4,1024]{2,0,1:T(4,128)(2,1)S(1)} %pad_maximum_fusion.4), channel_id=1, source_target_pairs={{0,8},{4,12},{8,0},{12,4},{1,9},{5,13},{9,1},{13,5},{2,10},{6,14},... | collective-permute-start | bytes 98312 | tf_op jit(solution)/shard_map/ppermute | solution.py:102
  22.7 5.2 %collective-permute-start.3 = (f32[64,512]{1,0:T(8,128)}, f32[64,512]{1,0:T(8,128)S(1)}, u32[]{:S(2)}, u32[]{:S(2)}) collective-permute-start(f32[64,512]{1,0:T(8,128)} %shard_map.46), channel_id=1, source_target_pairs={{0,4},{4,0},{8,12},{12,8},{1,5},{5,1},{9,13},{13,9},{2,6},{6,2},{1... | collective-permute-start | bytes 393224 | tf_op jit(solution)/shard_map/ppermute | solution.py:74
  28.8 5.9 %collective-permute-start.4 = (f32[64,512]{1,0:T(8,128)S(1)}, f32[64,512]{1,0:T(8,128)S(1)}, u32[]{:S(2)}, u32[]{:S(2)}) collective-permute-start(f32[64,512]{1,0:T(8,128)S(1)} %add.56), channel_id=1, source_target_pairs={{0,8},{4,12},{8,0},{12,4},{1,9},{5,13},{9,1},{13,5},{2,10},{6,14},... | collective-permute-start | bytes 393224 | tf_op jit(solution)/shard_map/ppermute | solution.py:74
  34.8 4.4 %collective-permute-start.5 = (f32[64]{0:T(128)S(1)}, f32[64]{0:T(128)S(1)}, u32[]{:S(2)}, u32[]{:S(2)}) collective-permute-start(f32[64]{0:T(128)S(1)} %get-tuple-element.5), channel_id=1, source_target_pairs={{0,2},{2,0},{1,3},{3,1},{4,6},{6,4},{5,7},{7,5},{8,10},{10,8},{9,1... | collective-permute-start | bytes 776 | tf_op jit(solution)/shard_map/ppermute | solution.py:74

commit v22 on v21

--- a/solution.py
+++ b/solution.py
@@ -6,9 +6,15 @@
 from jax.experimental.pallas import tpu as pltpu
 
 
-def hankel_kernel(x_ref, n_ref, o_ref, h_ref):
+def hankel_kernel(x_ref, n_hbm, o_ref, h_ref, n_ref, copies):
     width = h_ref.shape[1]
-    channels = n_ref.shape[1] // width
+    channels = n_hbm.shape[1] // width
+
+    def fetch(c):
+        return pltpu.make_async_copy(
+            n_hbm.at[:, pl.ds(c * width, width)], n_ref.at[c % 2], copies.at[c % 2]
+        )
+
     taps_blocks = width // 128
     out_blocks = o_ref.shape[1] // 128
     blocks = taps_blocks + out_blocks
@@ -32,22 +38,15 @@
                 h_ref[slot, p * 128 : (p + 1) * 128, a * 128 : (a + 1) * 128] = (
                     windows[a + p] * scale[a]
                 ).astype(jnp.bfloat16)
-        start = pl.multiple_of(c * width, 128)
-        return acc + jnp.dot(n_ref[:, pl.ds(start, width)], h_ref[slot], preferred_element_type=jnp.float32)
-
-    def two_channels(i, acc):
-        acc = one_channel(2 * i, 0, acc)
-        return one_channel(2 * i + 1, 1, acc)
+        fetch(c).wait()
+        if c + 1 < channels:
+            fetch(c + 1).start()
+        return acc + jnp.dot(n_ref[c % 2], h_ref[slot], preferred_element_type=jnp.float32)
 
     acc = jnp.zeros(o_ref.shape, jnp.float32)
-    if channels <= 16:
-        for c in range(channels):
-            acc = one_channel(c, c % 2, acc)
-    else:
-        pairs = channels // 2
-        acc = lax.fori_loop(0, pairs, two_channels, acc, unroll=2 if pairs % 2 == 0 else 1)
-        if channels % 2:
-            acc = one_channel(channels - 1, 0, acc)
+    fetch(0).start()
+    for c in range(channels):
+        acc = one_channel(c, c % 2, acc)
     o_ref[...] = acc
 
 
@@ -62,7 +61,12 @@
     return pl.pallas_call(
         hankel_kernel,
         out_shape=jax.ShapeDtypeStruct((rows, seg_len), jnp.float32),
-        scratch_shapes=[pltpu.VMEM((2, filter_taps, seg_len), jnp.bfloat16)],
+        in_specs=[pl.BlockSpec(memory_space=pltpu.VMEM), pl.BlockSpec(memory_space=pl.ANY)],
+        scratch_shapes=[
+            pltpu.VMEM((2, filter_taps, seg_len), jnp.bfloat16),
+            pltpu.VMEM((2, rows, filter_taps), jnp.bfloat16),
+            pltpu.SemaphoreType.DMA((2,)),
+        ],
     )(blocks, normed.reshape(rows, channels * filter_taps))
 
 

time: 40.2 us -> 48 us (1.19); the launches traced: 39.9 us -> 47.1 us
  Pallas kernels: 4.72 us -> 11.9 us
    pallas_call x1, Pallas kernels: 4.72 us -> 11.9 us  [correlate(): pl.pallas_call(hankel_kernel, out_shape=jax.ShapeDtypeStruct((rows, seg_l...]
  transfers between devices with their start and end apart: 6 -> 6, of which waited for: 5 -> 5; matrix products, arithmetic and copies ran while one was open for 15% -> 13% of each run, Pallas kernels for 0% -> 0%
where the time goes in v22:
time: 48 us; the launch traced here: 47.1 us
  starting transfers between devices  14.2 us (30%)
  Pallas kernels  11.9 us (25%)
  waiting for transfers between devices  11.6 us (24%)
  other arithmetic  5.37 us (11%)
  local copies, waits for them, and re-layouts  3.81 us (8%)
    pallas_call x1, Pallas kernels, correlate(): pl.pallas_call(hankel_kernel, out_shape=jax.ShapeDtypeStruct((rows, seg_l...  11.9 us
    ppermute x3, waiting for transfers between devices, ordered_sum(): part = part + lax.ppermute(part, axis, [(i, i ^ step) for i in range(size)])  8.35 us
    ppermute x3, starting transfers between devices, ordered_sum(): part = part + lax.ppermute(part, axis, [(i, i ^ step) for i in range(size)])  6.89 us
    ppermute x2, starting transfers between devices, gather_owned(): lax.ppermute(here, 'region', [(r, r ^ step) for r in range(regions)])  5.89 us
    another operation x1, local copies, waits for them, and re-layouts, correlate(): normed.reshape(rows, channels * filter_taps)  1.84 us
    ppermute x2, waiting for transfers between devices, gather_owned(): lax.ppermute(here, 'region', [(r, r ^ step) for r in range(regions)])  1.72 us
    reduce_sum x1, other arithmetic, per_device(): jnp.sum(widened_templates * widened_templates, axis=4, keepdims=True)  1.65 us
    ppermute x1, waiting for transfers between devices, gather_owned(): lax.ppermute(records[:, :, :filter_taps], 'seg', [(s + 1, s) for s in ran...  1.57 us
  transfers between devices with their start and end apart: 6, of which 5 were waited for; matrix products, arithmetic and copies ran while one was open for 13% of the time, Pallas kernels for 0%

profile of v22, /device:TPU:0, one launch (start us, length us, event | category | flops | bytes accessed | tf_op | source)
XLA Modules:
  0.0 47.1 jit_solution(959653195385163956)
XLA Ops:
  0.0 1.4 %collective-permute-start = (bf16[2,3,512]{2,0,1:T(2,128)(2,1)}, bf16[2,3,512]{2,0,1:T(2,128)(2,1)S(1)}, u32[]{:S(2)}, u32[]{:S(2)}) collective-permute-start(bf16[2,3,512]{2,0,1:T(2,128)(2,1)} %param.4), channel_id=1, source_target_pairs={{2,0},{3,1},{6,4},{7,5},{10,8},{11,9},{14,12},{15,13},{18,16},{19,... | collective-permute-start | bytes 18440 | tf_op jit(solution)/shard_map/ppermute | solution.py:93
  1.4 0.7 %convert_bitcast_fusion = f32[64,4,3]{0,1,2:T(4,128)S(1)} fusion(s32[1,64,4,3]{1,2,3,0:T(4,128)} %param.6), kind=kLoop, calls=%fused_computation.16 | loop fusion | flops 768 | bytes 6144 | tf_op jit(solution)/shard_map/mul | solution.py:144
  2.1 0.1 copy.9
  2.3 1.7 %fusion.3 = f32[64,4,3]{1,2,0:T(4,128)S(1)} fusion(bf16[1,64,4,3,512]{4,2,3,1,0:T(4,128)(2,1)} %param.5), kind=kLoop, calls=%fused_computation.6 | loop fusion | flops 1178880 | bytes 789504 | tf_op jit(solution)/shard_map/reduce_sum | solution.py:142
  4.0 0.5 %fusion.2 = bf16[1,64,4,3,512]{4,2,3,1,0:T(4,128)(2,1)S(1)} fusion(bf16[1,64,4,3,512]{4,2,3,1,0:T(4,128)(2,1)S(1)} %copy-done, f32[64,4,3]{1,2,0:T(4,128)S(1)} %add_sqrt_fusion, f32[64,4,3]{1,2,0:T(4,128)S(1)} %copy.9), kind=kLoop, calls=%fused_computation.5 | loop fusion | flops 1572864 | bytes 1579008 | tf_op jit(solution)/shard_map/convert_element_type | solution.py:144
  4.6 1.6 %collective-permute-done = bf16[2,3,512]{2,0,1:T(2,128)(2,1)S(1)} collective-permute-done((bf16[2,3,512]{2,0,1:T(2,128)(2,1)}, bf16[2,3,512]{2,0,1:T(2,128)(2,1)S(1)}, u32[]{:S(2)}, u32[]{:S(2)}) %collective-permute-start) | collective-permute-done | bytes 6176 | tf_op jit(solution)/shard_map/ppermute | solution.py:93
  6.3 2.8 %collective-permute-start.1 = (bf16[2,4,1024]{2,0,1:T(2,128)(2,1)S(1)}, bf16[2,4,1024]{2,0,1:T(2,128)(2,1)S(1)}, u32[]{:S(2)}, u32[]{:S(2)}) collective-permute-start(bf16[2,4,1024]{2,0,1:T(2,128)(2,1)S(1)} %pad_maximum_fusion.5), channel_id=1, source_target_pairs={{0,4},{4,0},{8,12},{12,8},{1,5},{5,1},{9,13},{13,9},{2,6},{6,2},{1... | collective-permute-start | bytes 49160 | tf_op jit(solution)/shard_map/ppermute | solution.py:106
  9.1 1.7 %collective-permute-done.1 = bf16[2,4,1024]{2,0,1:T(2,128)(2,1)S(1)} collective-permute-done((bf16[2,4,1024]{2,0,1:T(2,128)(2,1)S(1)}, bf16[2,4,1024]{2,0,1:T(2,128)(2,1)S(1)}, u32[]{:S(2)}, u32[]{:S(2)}) %collective-permute-start.1) | collective-permute-done | bytes 16416 | tf_op jit(solution)/shard_map/ppermute | solution.py:106
  10.8 3.1 %collective-permute-start.2 = (bf16[4,4,1024]{2,0,1:T(4,128)(2,1)S(1)}, bf16[4,4,1024]{2,0,1:T(4,128)(2,1)S(1)}, u32[]{:S(2)}, u32[]{:S(2)}) collective-permute-start(bf16[4,4,1024]{2,0,1:T(4,128)(2,1)S(1)} %pad_maximum_fusion.4), channel_id=1, source_target_pairs={{0,8},{4,12},{8,0},{12,4},{1,9},{5,13},{9,1},{13,5},{2,10},{6,14},... | collective-permute-start | bytes 98312 | tf_op jit(solution)/shard_map/ppermute | solution.py:106
  14.1 0.6 %copy.10 = bf16[1,64,4,3,512]{4,3,2,1,0:T(4,128)(2,1)S(1)} copy(bf16[1,64,4,3,512]{4,2,3,1,0:T(4,128)(2,1)S(1)} %fusion.2) | data formatting | bytes 1572864 | tf_op jit(solution)/shard_map/convert_element_type | solution.py:144
  14.6 1.8 %reshape_reshape.4.n_hbm = bf16[64,6144]{1,0:T(8,128)(2,1)} reshape(bf16[1,64,4,3,512]{4,3,2,1,0:T(4,128)(2,1)S(1)} %copy.10) | data formatting | bytes 1572864 | tf_op jit(solution)/shard_map/reshape;reshape | solution.py:70
  16.6 0.2 convert_reduce_fusion.1
  17.0 0.1 fusion
  17.2 0.7 %rev.6.x_ref = f32[96,128]{1,0:T(8,128)} reverse(f32[96,128]{1,0:T(8,128)S(1)} %mul.38), dimensions={1} | reverse | bytes 98304 | tf_op jit(solution)/shard_map/rev | solution.py:60
  17.9 11.9 %shard_map.46 = f32[64,512]{1,0:T(8,128)} custom-call(f32[96,128]{1,0:T(8,128)} %rev.6.x_ref, bf16[64,6144]{1,0:T(8,128)(2,1)} %reshape_reshape.4.n_hbm), custom_call_target="tpu_custom_call" | custom-call | tf_op jit(solution)/shard_map/pallas_call | solution.py:61
  29.8 1.6 %collective-permute-start.3 = (f32[64,512]{1,0:T(8,128)}, f32[64,512]{1,0:T(8,128)S(1)}, u32[]{:S(2)}, u32[]{:S(2)}) collective-permute-start(f32[64,512]{1,0:T(8,128)} %shard_map.46), channel_id=1, source_target_pairs={{0,4},{4,0},{8,12},{12,8},{1,5},{5,1},{9,13},{13,9},{2,6},{6,2},{1... | collective-permute-start | bytes 393224 | tf_op jit(solution)/shard_map/ppermute | solution.py:78
  31.4 3.6 %collective-permute-done.3 = f32[64,512]{1,0:T(8,128)S(1)} collective-permute-done((f32[64,512]{1,0:T(8,128)}, f32[64,512]{1,0:T(8,128)S(1)}, u32[]{:S(2)}, u32[]{:S(2)}) %collective-permute-start.3) | collective-permute-done | bytes 131104 | tf_op jit(solution)/shard_map/ppermute | solution.py:78
  35.1 0.9 %add.56 = f32[64,512]{1,0:T(8,128)S(1)} add(f32[64,512]{1,0:T(8,128)} %shard_map.46, f32[64,512]{1,0:T(8,128)S(1)} %collective-permute-done.3) | non-fusion elementwise | flops 32768 | bytes 393216 | tf_op jit(solution)/shard_map/add | solution.py:78
  36.0 2.4 %collective-permute-start.4 = (f32[64,512]{1,0:T(8,128)S(1)}, f32[64,512]{1,0:T(8,128)S(1)}, u32[]{:S(2)}, u32[]{:S(2)}) collective-permute-start(f32[64,512]{1,0:T(8,128)S(1)} %add.56), channel_id=1, source_target_pairs={{0,8},{4,12},{8,0},{12,4},{1,9},{5,13},{9,1},{13,5},{2,10},{6,14},... | collective-permute-start | bytes 393224 | tf_op jit(solution)/shard_map/ppermute | solution.py:78
  38.4 3.5 %collective-permute-done.4 = f32[64,512]{1,0:T(8,128)S(1)} collective-permute-done((f32[64,512]{1,0:T(8,128)S(1)}, f32[64,512]{1,0:T(8,128)S(1)}, u32[]{:S(2)}, u32[]{:S(2)}) %collective-permute-start.4) | collective-permute-done | bytes 131104 | tf_op jit(solution)/shard_map/ppermute | solution.py:78
  42.0 2.8 %collective-permute-start.5 = (f32[64]{0:T(128)S(1)}, f32[64]{0:T(128)S(1)}, u32[]{:S(2)}, u32[]{:S(2)}) collective-permute-start(f32[64]{0:T(128)S(1)} %get-tuple-element.5), channel_id=1, source_target_pairs={{0,2},{2,0},{1,3},{3,1},{4,6},{6,4},{5,7},{7,5},{8,10},{10,8},{9,1... | collective-permute-start | bytes 776 | tf_op jit(solution)/shard_map/ppermute | solution.py:78
  44.9 0.2 rev.7
  45.2 1.2 %collective-permute-done.5 = f32[64]{0:T(128)S(1)} collective-permute-done((f32[64]{0:T(128)S(1)}, f32[64]{0:T(128)S(1)}, u32[]{:S(2)}, u32[]{:S(2)}) %collective-permute-start.5) | collective-permute-done | bytes 288 | tf_op jit(solution)/shard_map/ppermute | solution.py:78
  46.4 0.7 %broadcast_divide_fusion = f32[1,64,512]{2,1,0:T(8,128)} fusion(f32[1,64,512]{2,1,0:T(8,128)S(1)} %reshape.115, f32[64]{0:T(128)S(1)} %add_sqrt_fusion.1), kind=kLoop, calls=%fused_computation.9 | loop fusion | flops 32768 | bytes 262400 | tf_op jit(solution)/shard_map/div | solution.py:149
  (27 shorter events, 1.1 us)
Async XLA Ops:
  0.0 4.0 %copy-start = (bf16[1,64,4,3,512]{4,2,3,1,0:T(4,128)(2,1)S(1)}, bf16[1,64,4,3,512]{4,2,3,1,0:T(4,128)(2,1)}, u32[]{:S(2)}) copy-start(bf16[1,64,4,3,512]{4,2,3,1,0:T(4,128)(2,1)} %param.5) | copy-start | bytes 2359300
  0.0 6.2 %collective-permute-start = (bf16[2,3,512]{2,0,1:T(2,128)(2,1)}, bf16[2,3,512]{2,0,1:T(2,128)(2,1)S(1)}, u32[]{:S(2)}, u32[]{:S(2)}) collective-permute-start(bf16[2,3,512]{2,0,1:T(2,128)(2,1)} %param.4), channel_id=1, source_target_pairs={{2,0},{3,1},{6,4},{7,5},{10,8},{11,9},{14,12},{15,13},{18,16},{19,... | collective-permute-start | bytes 18440 | tf_op jit(solution)/shard_map/ppermute | solution.py:93
  3.9 0.7 %copy-start.2 = (s32[2]{0:T(128)S(1)}, s32[2]{0:T(128)}, u32[]{:S(2)}) copy-start(s32[2]{0:T(128)} %param.7) | copy-start | bytes 28
  3.9 2.3 %copy-start.1 = (bf16[2,3,512]{2,0,1:T(2,128)(2,1)S(1)}, bf16[2,3,512]{2,0,1:T(2,128)(2,1)}, u32[]{:S(2)}) copy-start(bf16[2,3,512]{2,0,1:T(2,128)(2,1)} %param.4) | copy-start | bytes 18436
  6.3 4.5 %collective-permute-start.1 = (bf16[2,4,1024]{2,0,1:T(2,128)(2,1)S(1)}, bf16[2,4,1024]{2,0,1:T(2,128)(2,1)S(1)}, u32[]{:S(2)}, u32[]{:S(2)}) collective-permute-start(bf16[2,4,1024]{2,0,1:T(2,128)(2,1)S(1)} %pad_maximum_fusion.5), channel_id=1, source_target_pairs={{0,4},{4,0},{8,12},{12,8},{1,5},{5,1},{9,13},{13,9},{2,6},{6,2},{1... | collective-permute-start | bytes 49160 | tf_op jit(solution)/shard_map/ppermute | solution.py:106
  10.8 5.7 %collective-permute-start.2 = (bf16[4,4,1024]{2,0,1:T(4,128)(2,1)S(1)}, bf16[4,4,1024]{2,0,1:T(4,128)(2,1)S(1)}, u32[]{:S(2)}, u32[]{:S(2)}) collective-permute-start(bf16[4,4,1024]{2,0,1:T(4,128)(2,1)S(1)} %pad_maximum_fusion.4), channel_id=1, source_target_pairs={{0,8},{4,12},{8,0},{12,4},{1,9},{5,13},{9,1},{13,5},{2,10},{6,14},... | collective-permute-start | bytes 98312 | tf_op jit(solution)/shard_map/ppermute | solution.py:106
  29.8 5.2 %collective-permute-start.3 = (f32[64,512]{1,0:T(8,128)}, f32[64,512]{1,0:T(8,128)S(1)}, u32[]{:S(2)}, u32[]{:S(2)}) collective-permute-start(f32[64,512]{1,0:T(8,128)} %shard_map.46), channel_id=1, source_target_pairs={{0,4},{4,0},{8,12},{12,8},{1,5},{5,1},{9,13},{13,9},{2,6},{6,2},{1... | collective-permute-start | bytes 393224 | tf_op jit(solution)/shard_map/ppermute | solution.py:78
  36.0 5.9 %collective-permute-start.4 = (f32[64,512]{1,0:T(8,128)S(1)}, f32[64,512]{1,0:T(8,128)S(1)}, u32[]{:S(2)}, u32[]{:S(2)}) collective-permute-start(f32[64,512]{1,0:T(8,128)S(1)} %add.56), channel_id=1, source_target_pairs={{0,8},{4,12},{8,0},{12,4},{1,9},{5,13},{9,1},{13,5},{2,10},{6,14},... | collective-permute-start | bytes 393224 | tf_op jit(solution)/shard_map/ppermute | solution.py:78
  42.0 4.4 %collective-permute-start.5 = (f32[64]{0:T(128)S(1)}, f32[64]{0:T(128)S(1)}, u32[]{:S(2)}, u32[]{:S(2)}) collective-permute-start(f32[64]{0:T(128)S(1)} %get-tuple-element.5), channel_id=1, source_target_pairs={{0,2},{2,0},{1,3},{3,1},{4,6},{6,4},{5,7},{7,5},{8,10},{10,8},{9,1... | collective-permute-start | bytes 776 | tf_op jit(solution)/shard_map/ppermute | solution.py:78

commit v23 on v21

--- a/solution.py
+++ b/solution.py
@@ -16,9 +16,19 @@
     lane = lax.broadcasted_iota(jnp.int32, (128, 128), 1)
     low = lane >= row
 
+    components = x_ref.shape[1] // (blocks * 128)
+
     def one_channel(c, slot, acc):
+        station, component = divmod(c, components)
+        base = component * blocks * 128
         rolled = [
-            pltpu.roll(x_ref[pl.ds(c * blocks + m, 128, stride=0), :], 0, 1, stride=1, stride_axis=0)
+            pltpu.roll(
+                jnp.broadcast_to(x_ref[pl.ds(station, 1), pl.ds(base + m * 128, 128)], (128, 128)),
+                0,
+                1,
+                stride=1,
+                stride_axis=0,
+            )
             for m in range(blocks)
         ]
         windows = [jnp.where(low, rolled[m], rolled[m + 1]) for m in range(blocks - 1)]
@@ -35,20 +45,15 @@
         start = pl.multiple_of(c * width, 128)
         return acc + jnp.dot(n_ref[:, pl.ds(start, width)], h_ref[slot], preferred_element_type=jnp.float32)
 
-    def two_channels(i, acc):
-        acc = one_channel(2 * i, 0, acc)
-        return one_channel(2 * i + 1, 1, acc)
+    acc = jnp.zeros(o_ref.shape, jnp.float32)
+    for c in range(channels):
+        acc = one_channel(c, c % 2, acc)
+    o_ref[...] = acc
 
-    acc = jnp.zeros(o_ref.shape, jnp.float32)
-    if channels <= 16:
-        for c in range(channels):
-            acc = one_channel(c, c % 2, acc)
-    else:
-        pairs = channels // 2
-        acc = lax.fori_loop(0, pairs, two_channels, acc, unroll=2 if pairs % 2 == 0 else 1)
-        if channels % 2:
-            acc = one_channel(channels - 1, 0, acc)
-    o_ref[...] = acc
+
+def reverse_blocks(rows):
+    shape = rows.shape
+    return rows.reshape(shape[:-1] + (shape[-1] // 128, 128))[..., ::-1].reshape(shape)
 
 
 def unflip(stacked):
@@ -56,14 +61,13 @@
     return stacked.reshape(rows, seg_len // 128, 128)[..., ::-1].reshape(rows, seg_len)
 
 
-def correlate(normed, flat_owned, seg_len):
+def correlate(normed, owned, seg_len):
     rows, channels, filter_taps = normed.shape
-    blocks = flat_owned.reshape(channels * (flat_owned.shape[1] // 128), 128)[:, ::-1]
     return pl.pallas_call(
         hankel_kernel,
         out_shape=jax.ShapeDtypeStruct((rows, seg_len), jnp.float32),
         scratch_shapes=[pltpu.VMEM((2, filter_taps, seg_len), jnp.bfloat16)],
-    )(blocks, normed.reshape(rows, channels * filter_taps))
+    )(owned, normed.reshape(rows, channels * filter_taps))
 
 
 def ordered_sum(part, axis):
@@ -90,9 +94,8 @@
         records[:, :, :filter_taps], "seg", [(s + 1, s) for s in range(segs - 1)]
     )
     tag = jnp.broadcast_to(station_region.astype(jnp.bfloat16)[:, None, None], (local_count, 1, seg_len + filter_taps))
-    payload = jnp.concatenate(
-        [jnp.concatenate([records, ahead], axis=2), tag], axis=1
-    )
+    window = jnp.concatenate([reverse_blocks(records), reverse_blocks(ahead)], axis=2)
+    payload = jnp.concatenate([window, tag], axis=1)
     me = lax.axis_index("region")
     stations = regions * local_count
     if regions & (regions - 1) == 0:
@@ -131,7 +134,7 @@
     seg_len = records.shape[2]
     owned_rows, filled = gather_owned(records, station_region, capacity, filter_taps)
     owned_rows = owned_rows.astype(jnp.float32) * filled[:, None, None]
-    flat_owned = owned_rows.reshape(capacity * components, seg_len + filter_taps)
+    flat_owned = owned_rows.reshape(capacity, components * (seg_len + filter_taps))
     weight = channel_mask.astype(jnp.float32)
     widened_templates = templates.astype(jnp.float32)
     template_norm = jnp.sqrt(

time: 40.2 us -> 40.4 us (level)
  matrix products: 0.13 us -> 0.75 us
  local copies, waits for them, and re-layouts: 3.81 us -> 3.33 us
    dot_general x1, matrix products: 0.13 us -> 0.75 us  [gather_owned(): jnp.dot(placing.astype(jnp.bfloat16), rows.reshape(stations, -1), preferr...]
    rev x1 -> x2, local copies, waits for them, and re-layouts: 0.7 us -> 0.2 us  [reverse_blocks(): rows.reshape(shape[:-1] + (shape[-1] // 128, 128))[..., ::-1].reshape(shape)]
where the time goes in v23:
time: 40.4 us; the launch traced here: 40.1 us
  starting transfers between devices  14.2 us (35%)
  waiting for transfers between devices  11.6 us (29%)
  other arithmetic  5.36 us (13%)
  Pallas kernels  4.73 us (12%)
  local copies, waits for them, and re-layouts  3.33 us (8%)
  matrix products  0.75 us (2%)
    ppermute x3, waiting for transfers between devices, ordered_sum(): part = part + lax.ppermute(part, axis, [(i, i ^ step) for i in range(size)])  8.47 us
    ppermute x3, starting transfers between devices, ordered_sum(): part = part + lax.ppermute(part, axis, [(i, i ^ step) for i in range(size)])  6.88 us
    ppermute x2, starting transfers between devices, gather_owned(): lax.ppermute(here, 'region', [(r, r ^ step) for r in range(regions)])  5.89 us
    pallas_call x1, Pallas kernels, correlate(): pl.pallas_call(hankel_kernel, out_shape=jax.ShapeDtypeStruct((rows, seg_l...  4.73 us
    another operation x1, local copies, waits for them, and re-layouts, correlate(): normed.reshape(rows, channels * filter_taps)  1.84 us
    ppermute x2, waiting for transfers between devices, gather_owned(): lax.ppermute(here, 'region', [(r, r ^ step) for r in range(regions)])  1.72 us
    reduce_sum x1, other arithmetic, per_device(): jnp.sum(widened_templates * widened_templates, axis=4, keepdims=True)  1.65 us
    ppermute x1, starting transfers between devices, gather_owned(): lax.ppermute(records[:, :, :filter_taps], 'seg', [(s + 1, s) for s in ran...  1.41 us
  transfers between devices with their start and end apart: 6, of which 5 were waited for; matrix products, arithmetic and copies ran while one was open for 15% of the time, Pallas kernels for 0%

profile of v23, /device:TPU:0, one launch (start us, length us, event | category | flops | bytes accessed | tf_op | source)
XLA Modules:
  0.0 40.1 jit_solution(18148054120180967896)
XLA Ops:
  0.0 1.4 %collective-permute-start = (bf16[2,3,512]{2,0,1:T(2,128)(2,1)}, bf16[2,3,512]{2,0,1:T(2,128)(2,1)S(1)}, u32[]{:S(2)}, u32[]{:S(2)}) collective-permute-start(bf16[2,3,512]{2,0,1:T(2,128)(2,1)} %param.4), channel_id=1, source_target_pairs={{2,0},{3,1},{6,4},{7,5},{10,8},{11,9},{14,12},{15,13},{18,16},{19,... | collective-permute-start | bytes 18440 | tf_op jit(solution)/shard_map/ppermute | solution.py:93
  1.4 0.7 %convert_bitcast_fusion = f32[64,4,3]{0,1,2:T(4,128)S(1)} fusion(s32[1,64,4,3]{1,2,3,0:T(4,128)} %param.6), kind=kLoop, calls=%fused_computation.16 | loop fusion | flops 768 | bytes 6144 | tf_op jit(solution)/shard_map/mul | solution.py:143
  2.1 0.1 copy.29
  2.3 1.7 %fusion.4 = f32[64,4,3]{1,2,0:T(4,128)S(1)} fusion(bf16[1,64,4,3,512]{4,2,3,1,0:T(4,128)(2,1)} %param.5), kind=kLoop, calls=%fused_computation.7 | loop fusion | flops 1178880 | bytes 789504 | tf_op jit(solution)/shard_map/reduce_sum | solution.py:141
  4.0 0.5 %fusion.3 = bf16[1,64,4,3,512]{4,2,3,1,0:T(4,128)(2,1)S(1)} fusion(bf16[1,64,4,3,512]{4,2,3,1,0:T(4,128)(2,1)S(1)} %copy-done, f32[64,4,3]{1,2,0:T(4,128)S(1)} %add_sqrt_fusion, f32[64,4,3]{1,2,0:T(4,128)S(1)} %copy.29), kind=kLoop, calls=%fused_computation.6 | loop fusion | flops 1572864 | bytes 1579008 | tf_op jit(solution)/shard_map/convert_element_type | solution.py:143
  4.8 1.4 %collective-permute-done = bf16[2,3,512]{2,0,1:T(2,128)(2,1)S(1)} collective-permute-done((bf16[2,3,512]{2,0,1:T(2,128)(2,1)}, bf16[2,3,512]{2,0,1:T(2,128)(2,1)S(1)}, u32[]{:S(2)}, u32[]{:S(2)}) %collective-permute-start) | collective-permute-done | bytes 6176 | tf_op jit(solution)/shard_map/ppermute | solution.py:93
  6.4 2.8 %collective-permute-start.1 = (bf16[2,4,1024]{2,1,0:T(4,128)(2,1)S(1)}, bf16[2,4,1024]{2,1,0:T(4,128)(2,1)S(1)}, u32[]{:S(2)}, u32[]{:S(2)}) collective-permute-start(bf16[2,4,1024]{2,1,0:T(4,128)(2,1)S(1)} %pad_maximum_fusion.3), channel_id=1, source_target_pairs={{0,4},{4,0},{8,12},{12,8},{1,5},{5,1},{9,13},{13,9},{2,6},{6,2},{1... | collective-permute-start | bytes 49160 | tf_op jit(solution)/shard_map/ppermute | solution.py:105
  9.2 1.7 %collective-permute-done.1 = bf16[2,4,1024]{2,1,0:T(4,128)(2,1)S(1)} collective-permute-done((bf16[2,4,1024]{2,1,0:T(4,128)(2,1)S(1)}, bf16[2,4,1024]{2,1,0:T(4,128)(2,1)S(1)}, u32[]{:S(2)}, u32[]{:S(2)}) %collective-permute-start.1) | collective-permute-done | bytes 16416 | tf_op jit(solution)/shard_map/ppermute | solution.py:105
  11.0 3.1 %collective-permute-start.2 = (bf16[4,4,1024]{2,1,0:T(4,128)(2,1)S(1)}, bf16[4,4,1024]{2,1,0:T(4,128)(2,1)S(1)}, u32[]{:S(2)}, u32[]{:S(2)}) collective-permute-start(bf16[4,4,1024]{2,1,0:T(4,128)(2,1)S(1)} %pad_maximum_fusion.2), channel_id=1, source_target_pairs={{0,8},{4,12},{8,0},{12,4},{1,9},{5,13},{9,1},{13,5},{2,10},{6,14},... | collective-permute-start | bytes 98312 | tf_op jit(solution)/shard_map/ppermute | solution.py:105
  14.2 0.6 %copy.30 = bf16[1,64,4,3,512]{4,3,2,1,0:T(4,128)(2,1)S(1)} copy(bf16[1,64,4,3,512]{4,2,3,1,0:T(4,128)(2,1)S(1)} %fusion.3) | data formatting | bytes 1572864 | tf_op jit(solution)/shard_map/convert_element_type | solution.py:143
  14.8 1.8 %reshape_reshape.3.n_ref = bf16[64,6144]{1,0:T(8,128)(2,1)} reshape(bf16[1,64,4,3,512]{4,3,2,1,0:T(4,128)(2,1)S(1)} %copy.30) | data formatting | bytes 1572864 | tf_op jit(solution)/shard_map/reshape;reshape | solution.py:70
  16.7 0.1 convert_reduce_fusion
  16.9 0.2 convert_reduce_fusion.1
  17.2 0.8 %fusion.1.x_ref = f32[4,3072]{1,0:T(4,128)} fusion(bf16[8,3072]{1,0:T(8,128)(2,1)S(1)} %bitcast.12, f32[4]{0:T(128)S(1)} %convert_reduce_fusion.2, s32[8]{0:T(128)S(1)} %convert_reduce_fusion.1, pred[8]{0:T(512)(128)(4,1)S(1)} %broadcast_compare_fusion), kind=kOutput, calls=%fused_computation.2 | convolution fusion | flops 233536 | bytes 98360 | tf_op jit(solution)/shard_map/dot_general | solution.py:124
  17.9 4.7 %shard_map.46 = f32[64,512]{1,0:T(8,128)} custom-call(f32[4,3072]{1,0:T(4,128)} %fusion.1.x_ref, bf16[64,6144]{1,0:T(8,128)(2,1)} %reshape_reshape.3.n_ref), custom_call_target="tpu_custom_call" | custom-call | tf_op jit(solution)/shard_map/pallas_call | solution.py:66
  22.7 1.6 %collective-permute-start.3 = (f32[64,512]{1,0:T(8,128)}, f32[64,512]{1,0:T(8,128)S(1)}, u32[]{:S(2)}, u32[]{:S(2)}) collective-permute-start(f32[64,512]{1,0:T(8,128)} %shard_map.46), channel_id=1, source_target_pairs={{0,4},{4,0},{8,12},{12,8},{1,5},{5,1},{9,13},{13,9},{2,6},{6,2},{1... | collective-permute-start | bytes 393224 | tf_op jit(solution)/shard_map/ppermute | solution.py:78
  24.3 3.6 %collective-permute-done.3 = f32[64,512]{1,0:T(8,128)S(1)} collective-permute-done((f32[64,512]{1,0:T(8,128)}, f32[64,512]{1,0:T(8,128)S(1)}, u32[]{:S(2)}, u32[]{:S(2)}) %collective-permute-start.3) | collective-permute-done | bytes 131104 | tf_op jit(solution)/shard_map/ppermute | solution.py:78
  27.9 0.9 %add.56 = f32[64,512]{1,0:T(8,128)S(1)} add(f32[64,512]{1,0:T(8,128)} %shard_map.46, f32[64,512]{1,0:T(8,128)S(1)} %collective-permute-done.3) | non-fusion elementwise | flops 32768 | bytes 393216 | tf_op jit(solution)/shard_map/add | solution.py:78
  28.8 2.3 %collective-permute-start.4 = (f32[64,512]{1,0:T(8,128)S(1)}, f32[64,512]{1,0:T(8,128)S(1)}, u32[]{:S(2)}, u32[]{:S(2)}) collective-permute-start(f32[64,512]{1,0:T(8,128)S(1)} %add.56), channel_id=1, source_target_pairs={{0,8},{4,12},{8,0},{12,4},{1,9},{5,13},{9,1},{13,5},{2,10},{6,14},... | collective-permute-start | bytes 393224 | tf_op jit(solution)/shard_map/ppermute | solution.py:78
  31.1 3.6 %collective-permute-done.4 = f32[64,512]{1,0:T(8,128)S(1)} collective-permute-done((f32[64,512]{1,0:T(8,128)S(1)}, f32[64,512]{1,0:T(8,128)S(1)}, u32[]{:S(2)}, u32[]{:S(2)}) %collective-permute-start.4) | collective-permute-done | bytes 131104 | tf_op jit(solution)/shard_map/ppermute | solution.py:78
  34.8 3.0 %collective-permute-start.5 = (f32[64]{0:T(128)S(1)}, f32[64]{0:T(128)S(1)}, u32[]{:S(2)}, u32[]{:S(2)}) collective-permute-start(f32[64]{0:T(128)S(1)} %get-tuple-element.5), channel_id=1, source_target_pairs={{0,2},{2,0},{1,3},{3,1},{4,6},{6,4},{5,7},{7,5},{8,10},{10,8},{9,1... | collective-permute-start | bytes 776 | tf_op jit(solution)/shard_map/ppermute | solution.py:78
  37.9 0.2 rev.11
  38.1 1.2 %collective-permute-done.5 = f32[64]{0:T(128)S(1)} collective-permute-done((f32[64]{0:T(128)S(1)}, f32[64]{0:T(128)S(1)}, u32[]{:S(2)}, u32[]{:S(2)}) %collective-permute-start.5) | collective-permute-done | bytes 288 | tf_op jit(solution)/shard_map/ppermute | solution.py:78
  39.4 0.7 %broadcast_divide_fusion = f32[1,64,512]{2,1,0:T(8,128)} fusion(f32[1,64,512]{2,1,0:T(8,128)S(1)} %reshape.128, f32[64]{0:T(128)S(1)} %add_sqrt_fusion.1), kind=kLoop, calls=%fused_computation.10 | loop fusion | flops 32768 | bytes 262400 | tf_op jit(solution)/shard_map/div | solution.py:148
  (33 shorter events, 1.1 us)
Async XLA Ops:
  0.0 4.0 %copy-start = (bf16[1,64,4,3,512]{4,2,3,1,0:T(4,128)(2,1)S(1)}, bf16[1,64,4,3,512]{4,2,3,1,0:T(4,128)(2,1)}, u32[]{:S(2)}) copy-start(bf16[1,64,4,3,512]{4,2,3,1,0:T(4,128)(2,1)} %param.5) | copy-start | bytes 2359300
  0.0 6.2 %collective-permute-start = (bf16[2,3,512]{2,0,1:T(2,128)(2,1)}, bf16[2,3,512]{2,0,1:T(2,128)(2,1)S(1)}, u32[]{:S(2)}, u32[]{:S(2)}) collective-permute-start(bf16[2,3,512]{2,0,1:T(2,128)(2,1)} %param.4), channel_id=1, source_target_pairs={{2,0},{3,1},{6,4},{7,5},{10,8},{11,9},{14,12},{15,13},{18,16},{19,... | collective-permute-start | bytes 18440 | tf_op jit(solution)/shard_map/ppermute | solution.py:93
  3.9 0.7 %copy-start.1 = (bf16[2,3,512]{2,0,1:T(2,128)(2,1)S(1)}, bf16[2,3,512]{2,0,1:T(2,128)(2,1)}, u32[]{:S(2)}) copy-start(bf16[2,3,512]{2,0,1:T(2,128)(2,1)} %param.4) | copy-start | bytes 18436
  3.9 0.7 %copy-start.2 = (s32[2]{0:T(128)S(1)}, s32[2]{0:T(128)}, u32[]{:S(2)}) copy-start(s32[2]{0:T(128)} %param.7) | copy-start | bytes 28
  6.4 4.5 %collective-permute-start.1 = (bf16[2,4,1024]{2,1,0:T(4,128)(2,1)S(1)}, bf16[2,4,1024]{2,1,0:T(4,128)(2,1)S(1)}, u32[]{:S(2)}, u32[]{:S(2)}) collective-permute-start(bf16[2,4,1024]{2,1,0:T(4,128)(2,1)S(1)} %pad_maximum_fusion.3), channel_id=1, source_target_pairs={{0,4},{4,0},{8,12},{12,8},{1,5},{5,1},{9,13},{13,9},{2,6},{6,2},{1... | collective-permute-start | bytes 49160 | tf_op jit(solution)/shard_map/ppermute | solution.py:105
  11.0 5.7 %collective-permute-start.2 = (bf16[4,4,1024]{2,1,0:T(4,128)(2,1)S(1)}, bf16[4,4,1024]{2,1,0:T(4,128)(2,1)S(1)}, u32[]{:S(2)}, u32[]{:S(2)}) collective-permute-start(bf16[4,4,1024]{2,1,0:T(4,128)(2,1)S(1)} %pad_maximum_fusion.2), channel_id=1, source_target_pairs={{0,8},{4,12},{8,0},{12,4},{1,9},{5,13},{9,1},{13,5},{2,10},{6,14},... | collective-permute-start | bytes 98312 | tf_op jit(solution)/shard_map/ppermute | solution.py:105
  22.7 5.2 %collective-permute-start.3 = (f32[64,512]{1,0:T(8,128)}, f32[64,512]{1,0:T(8,128)S(1)}, u32[]{:S(2)}, u32[]{:S(2)}) collective-permute-start(f32[64,512]{1,0:T(8,128)} %shard_map.46), channel_id=1, source_target_pairs={{0,4},{4,0},{8,12},{12,8},{1,5},{5,1},{9,13},{13,9},{2,6},{6,2},{1... | collective-permute-start | bytes 393224 | tf_op jit(solution)/shard_map/ppermute | solution.py:78
  28.8 5.9 %collective-permute-start.4 = (f32[64,512]{1,0:T(8,128)S(1)}, f32[64,512]{1,0:T(8,128)S(1)}, u32[]{:S(2)}, u32[]{:S(2)}) collective-permute-start(f32[64,512]{1,0:T(8,128)S(1)} %add.56), channel_id=1, source_target_pairs={{0,8},{4,12},{8,0},{12,4},{1,9},{5,13},{9,1},{13,5},{2,10},{6,14},... | collective-permute-start | bytes 393224 | tf_op jit(solution)/shard_map/ppermute | solution.py:78
  34.8 4.5 %collective-permute-start.5 = (f32[64]{0:T(128)S(1)}, f32[64]{0:T(128)S(1)}, u32[]{:S(2)}, u32[]{:S(2)}) collective-permute-start(f32[64]{0:T(128)S(1)} %get-tuple-element.5), channel_id=1, source_target_pairs={{0,2},{2,0},{1,3},{3,1},{4,6},{6,4},{5,7},{7,5},{8,10},{10,8},{9,1... | collective-permute-start | bytes 776 | tf_op jit(solution)/shard_map/ppermute | solution.py:78

commit v24 on v21

--- a/solution.py
+++ b/solution.py
@@ -82,6 +82,27 @@
     return jnp.sum(jnp.take(jnp.stack(received), order, axis=0), axis=0)
 
 
+def sum_and_power(part):
+    regions = lax.axis_size("region")
+    segs = lax.axis_size("seg")
+    if regions & (regions - 1) or regions < 2 or segs != 2:
+        stacked = ordered_sum(part, "region")
+        return stacked, ordered_sum(jnp.sum(stacked * stacked, axis=1), "seg")
+    step = 1
+    while step < regions // 2:
+        part = part + lax.ppermute(part, "region", [(r, r ^ step) for r in range(regions)])
+        step *= 2
+    partner = lax.ppermute(part, "region", [(r, r ^ step) for r in range(regions)])
+    other = lax.ppermute(part, "seg", [(0, 1), (1, 0)])
+    other_partner = lax.ppermute(
+        part, ("region", "seg"), [(r * 2 + s, (r ^ step) * 2 + 1 - s) for r in range(regions) for s in range(2)]
+    )
+    stacked = part + partner
+    stacked_other = other + other_partner
+    power = jnp.sum(stacked * stacked, axis=1) + jnp.sum(stacked_other * stacked_other, axis=1)
+    return stacked, power
+
+
 def gather_owned(records, station_region, capacity, filter_taps):
     local_count, components, seg_len = records.shape
     regions = lax.axis_size("region")
@@ -140,8 +161,7 @@
     normed = (widened_templates * weight[..., None] / template_norm).astype(jnp.bfloat16)
     normed = normed.reshape(local_batches * kept, capacity * components, filter_taps)
     total_len = seg_len * lax.axis_size("seg")
-    stacked = ordered_sum(correlate(normed, flat_owned, seg_len), "region")
-    power_sum = ordered_sum(jnp.sum(stacked * stacked, axis=1), "seg")
+    stacked, power_sum = sum_and_power(correlate(normed, flat_owned, seg_len))
     detect = unflip(stacked) / jnp.sqrt(power_sum / total_len + 1e-06)[:, None]
     return detect.reshape(local_batches, kept, seg_len)
 

time: 40.2 us -> 42.5 us (1.057)
  waiting for transfers between devices: 11.6 us -> 14.6 us
  starting transfers between devices: 14.1 us -> 13.3 us
    ppermute x3 -> x4, waiting for transfers between devices: 8.34 us -> 11.3 us  [the longest x2 7.28 us: sum_and_power(): lax.ppermute(part, 'region', [(r, r ^ step) for r in range(regions)])]
    ppermute x3 -> x4, starting transfers between devices: 6.83 us -> 6.03 us  [the longest x2 3.99 us: sum_and_power(): lax.ppermute(part, 'region', [(r, r ^ step) for r in range(regions)])]
  transfers between devices with their start and end apart: 6 -> 7, of which waited for: 5 -> 5; matrix products, arithmetic and copies ran while one was open for 15% -> 14% of each run, Pallas kernels for 0% -> 0%
where the time goes in v24:
time: 42.5 us; the launch traced here: 42.2 us
  waiting for transfers between devices  14.6 us (34%)
  starting transfers between devices  13.3 us (31%)
  other arithmetic  5.49 us (13%)
  Pallas kernels  4.72 us (11%)
  local copies, waits for them, and re-layouts  3.81 us (9%)
    ppermute x2, waiting for transfers between devices, sum_and_power(): lax.ppermute(part, 'region', [(r, r ^ step) for r in range(regions)])  7.28 us
    ppermute x2, starting transfers between devices, gather_owned(): lax.ppermute(here, 'region', [(r, r ^ step) for r in range(regions)])  5.89 us
    pallas_call x1, Pallas kernels, correlate(): pl.pallas_call(hankel_kernel, out_shape=jax.ShapeDtypeStruct((rows, seg_l...  4.72 us
    ppermute x1, waiting for transfers between devices, sum_and_power(): lax.ppermute(part, ('region', 'seg'), [(r * 2 + s, (r ^ step) * 2 + 1 - s...  4.02 us
    ppermute x2, starting transfers between devices, sum_and_power(): lax.ppermute(part, 'region', [(r, r ^ step) for r in range(regions)])  3.99 us
    another operation x1, local copies, waits for them, and re-layouts, correlate(): normed.reshape(rows, channels * filter_taps)  1.84 us
    ppermute x2, waiting for transfers between devices, gather_owned(): lax.ppermute(here, 'region', [(r, r ^ step) for r in range(regions)])  1.72 us
    reduce_sum x1, other arithmetic, per_device(): jnp.sum(widened_templates * widened_templates, axis=4, keepdims=True)  1.65 us
  transfers between devices with their start and end apart: 7, of which 5 were waited for; matrix products, arithmetic and copies ran while one was open for 14% of the time, Pallas kernels for 0%

profile of v24, /device:TPU:0, one launch (start us, length us, event | category | flops | bytes accessed | tf_op | source)
XLA Modules:
  0.0 42.2 jit_solution(605678342173677041)
XLA Ops:
  0.0 1.4 %collective-permute-start = (bf16[2,3,512]{2,0,1:T(2,128)(2,1)}, bf16[2,3,512]{2,0,1:T(2,128)(2,1)S(1)}, u32[]{:S(2)}, u32[]{:S(2)}) collective-permute-start(bf16[2,3,512]{2,0,1:T(2,128)(2,1)} %param.4), channel_id=1, source_target_pairs={{2,0},{3,1},{6,4},{7,5},{10,8},{11,9},{14,12},{15,13},{18,16},{19,... | collective-permute-start | bytes 18440 | tf_op jit(solution)/shard_map/ppermute | solution.py:110
  1.4 0.7 %convert_bitcast_fusion = f32[64,4,3]{0,1,2:T(4,128)S(1)} fusion(s32[1,64,4,3]{1,2,3,0:T(4,128)} %param.6), kind=kLoop, calls=%fused_computation.17 | loop fusion | flops 768 | bytes 6144 | tf_op jit(solution)/shard_map/mul | solution.py:161
  2.3 1.7 %fusion.3 = f32[64,4,3]{1,2,0:T(4,128)S(1)} fusion(bf16[1,64,4,3,512]{4,2,3,1,0:T(4,128)(2,1)} %param.5), kind=kLoop, calls=%fused_computation.6 | loop fusion | flops 1178880 | bytes 789504 | tf_op jit(solution)/shard_map/reduce_sum | solution.py:159
  4.0 0.5 %fusion.2 = bf16[1,64,4,3,512]{4,2,3,1,0:T(4,128)(2,1)S(1)} fusion(bf16[1,64,4,3,512]{4,2,3,1,0:T(4,128)(2,1)S(1)} %copy-done, f32[64,4,3]{1,2,0:T(4,128)S(1)} %add_sqrt_fusion, f32[64,4,3]{1,2,0:T(4,128)S(1)} %copy.9), kind=kLoop, calls=%fused_computation.5 | loop fusion | flops 1572864 | bytes 1579008 | tf_op jit(solution)/shard_map/convert_element_type | solution.py:161
  4.6 1.6 %collective-permute-done = bf16[2,3,512]{2,0,1:T(2,128)(2,1)S(1)} collective-permute-done((bf16[2,3,512]{2,0,1:T(2,128)(2,1)}, bf16[2,3,512]{2,0,1:T(2,128)(2,1)S(1)}, u32[]{:S(2)}, u32[]{:S(2)}) %collective-permute-start) | collective-permute-done | bytes 6176 | tf_op jit(solution)/shard_map/ppermute | solution.py:110
  6.3 2.8 %collective-permute-start.1 = (bf16[2,4,1024]{2,0,1:T(2,128)(2,1)S(1)}, bf16[2,4,1024]{2,0,1:T(2,128)(2,1)S(1)}, u32[]{:S(2)}, u32[]{:S(2)}) collective-permute-start(bf16[2,4,1024]{2,0,1:T(2,128)(2,1)S(1)} %pad_maximum_fusion.5), channel_id=1, source_target_pairs={{0,4},{4,0},{8,12},{12,8},{1,5},{5,1},{9,13},{13,9},{2,6},{6,2},{1... | collective-permute-start | bytes 49160 | tf_op jit(solution)/shard_map/ppermute | solution.py:123
  9.1 1.7 %collective-permute-done.1 = bf16[2,4,1024]{2,0,1:T(2,128)(2,1)S(1)} collective-permute-done((bf16[2,4,1024]{2,0,1:T(2,128)(2,1)S(1)}, bf16[2,4,1024]{2,0,1:T(2,128)(2,1)S(1)}, u32[]{:S(2)}, u32[]{:S(2)}) %collective-permute-start.1) | collective-permute-done | bytes 16416 | tf_op jit(solution)/shard_map/ppermute | solution.py:123
  10.8 3.1 %collective-permute-start.2 = (bf16[4,4,1024]{2,0,1:T(4,128)(2,1)S(1)}, bf16[4,4,1024]{2,0,1:T(4,128)(2,1)S(1)}, u32[]{:S(2)}, u32[]{:S(2)}) collective-permute-start(bf16[4,4,1024]{2,0,1:T(4,128)(2,1)S(1)} %pad_maximum_fusion.4), channel_id=1, source_target_pairs={{0,8},{4,12},{8,0},{12,4},{1,9},{5,13},{9,1},{13,5},{2,10},{6,14},... | collective-permute-start | bytes 98312 | tf_op jit(solution)/shard_map/ppermute | solution.py:123
  14.1 0.6 %copy.10 = bf16[1,64,4,3,512]{4,3,2,1,0:T(4,128)(2,1)S(1)} copy(bf16[1,64,4,3,512]{4,2,3,1,0:T(4,128)(2,1)S(1)} %fusion.2) | data formatting | bytes 1572864 | tf_op jit(solution)/shard_map/convert_element_type | solution.py:161
  14.6 1.8 %reshape_reshape.4.n_ref = bf16[64,6144]{1,0:T(8,128)(2,1)} reshape(bf16[1,64,4,3,512]{4,3,2,1,0:T(4,128)(2,1)S(1)} %copy.10) | data formatting | bytes 1572864 | tf_op jit(solution)/shard_map/reshape;reshape | solution.py:66
  16.6 0.2 convert_reduce_fusion.1
  17.0 0.1 fusion
  17.2 0.7 %rev.6.x_ref = f32[96,128]{1,0:T(8,128)} reverse(f32[96,128]{1,0:T(8,128)S(1)} %mul.41), dimensions={1} | reverse | bytes 98304 | tf_op jit(solution)/shard_map/rev | solution.py:61
  17.9 4.7 %shard_map.46 = f32[64,512]{1,0:T(8,128)} custom-call(f32[96,128]{1,0:T(8,128)} %rev.6.x_ref, bf16[64,6144]{1,0:T(8,128)(2,1)} %reshape_reshape.4.n_ref), custom_call_target="tpu_custom_call" | custom-call | tf_op jit(solution)/shard_map/pallas_call | solution.py:62
  22.7 1.6 %collective-permute-start.3 = (f32[64,512]{1,0:T(8,128)}, f32[64,512]{1,0:T(8,128)S(1)}, u32[]{:S(2)}, u32[]{:S(2)}) collective-permute-start(f32[64,512]{1,0:T(8,128)} %shard_map.46), channel_id=1, source_target_pairs={{0,4},{4,0},{8,12},{12,8},{1,5},{5,1},{9,13},{13,9},{2,6},{6,2},{1... | collective-permute-start | bytes 393224 | tf_op jit(solution)/shard_map/ppermute | solution.py:93
  24.2 3.6 %collective-permute-done.3 = f32[64,512]{1,0:T(8,128)S(1)} collective-permute-done((f32[64,512]{1,0:T(8,128)}, f32[64,512]{1,0:T(8,128)S(1)}, u32[]{:S(2)}, u32[]{:S(2)}) %collective-permute-start.3) | collective-permute-done | bytes 131104 | tf_op jit(solution)/shard_map/ppermute | solution.py:93
  27.8 0.9 %add.67 = f32[64,512]{1,0:T(8,128)S(1)} add(f32[64,512]{1,0:T(8,128)} %shard_map.46, f32[64,512]{1,0:T(8,128)S(1)} %collective-permute-done.3) | non-fusion elementwise | flops 32768 | bytes 393216 | tf_op jit(solution)/shard_map/add | solution.py:93
  28.8 2.4 %collective-permute-start.4 = (f32[64,512]{1,0:T(8,128)S(1)}, f32[64,512]{1,0:T(8,128)S(1)}, u32[]{:S(2)}, u32[]{:S(2)}) collective-permute-start(f32[64,512]{1,0:T(8,128)S(1)} %add.67), channel_id=1, source_target_pairs={{0,8},{4,12},{8,0},{12,4},{1,9},{5,13},{9,1},{13,5},{2,10},{6,14},... | collective-permute-start | bytes 393224 | tf_op jit(solution)/shard_map/ppermute | solution.py:95
  31.2 1.4 %collective-permute-start.6 = (f32[64,512]{1,0:T(8,128)S(1)}, f32[64,512]{1,0:T(8,128)S(1)}, u32[]{:S(2)}, u32[]{:S(2)}) collective-permute-start(f32[64,512]{1,0:T(8,128)S(1)} %add.67), channel_id=1, source_target_pairs={{0,10},{2,8},{4,14},{6,12},{8,2},{10,0},{12,6},{14,4},{1,11},{3,9}... | collective-permute-start | bytes 393224 | tf_op jit(solution)/shard_map/ppermute | solution.py:97
  32.6 0.6 %collective-permute-start.5 = (f32[64,512]{1,0:T(8,128)S(1)}, f32[64,512]{1,0:T(8,128)S(1)}, u32[]{:S(2)}, u32[]{:S(2)}) collective-permute-start(f32[64,512]{1,0:T(8,128)S(1)} %add.67), channel_id=1, source_target_pairs={{0,2},{2,0},{1,3},{3,1},{4,6},{6,4},{5,7},{7,5},{8,10},{10,8},{9,1... | collective-permute-start | bytes 393224 | tf_op jit(solution)/shard_map/ppermute | solution.py:96
  33.2 3.7 %collective-permute-done.4 = f32[64,512]{1,0:T(8,128)S(1)} collective-permute-done((f32[64,512]{1,0:T(8,128)S(1)}, f32[64,512]{1,0:T(8,128)S(1)}, u32[]{:S(2)}, u32[]{:S(2)}) %collective-permute-start.4) | collective-permute-done | bytes 131104 | tf_op jit(solution)/shard_map/ppermute | solution.py:95
  37.1 0.2 rev.7
  37.3 4.0 %collective-permute-done.6 = f32[64,512]{1,0:T(8,128)S(1)} collective-permute-done((f32[64,512]{1,0:T(8,128)S(1)}, f32[64,512]{1,0:T(8,128)S(1)}, u32[]{:S(2)}, u32[]{:S(2)}) %collective-permute-start.6) | collective-permute-done | bytes 131104 | tf_op jit(solution)/shard_map/ppermute | solution.py:97
  41.5 0.8 %broadcast_divide_fusion = f32[1,64,512]{2,1,0:T(8,128)} fusion(f32[1,64,512]{2,1,0:T(8,128)S(1)} %reshape.124, f32[64]{0:T(128)S(1)} %add_sqrt_fusion.1), kind=kLoop, calls=%fused_computation.10 | loop fusion | flops 32768 | bytes 262400 | tf_op jit(solution)/shard_map/div | solution.py:165
  (30 shorter events, 1.3 us)
Async XLA Ops:
  0.0 4.0 %copy-start = (bf16[1,64,4,3,512]{4,2,3,1,0:T(4,128)(2,1)S(1)}, bf16[1,64,4,3,512]{4,2,3,1,0:T(4,128)(2,1)}, u32[]{:S(2)}) copy-start(bf16[1,64,4,3,512]{4,2,3,1,0:T(4,128)(2,1)} %param.5) | copy-start | bytes 2359300
  0.0 6.2 %collective-permute-start = (bf16[2,3,512]{2,0,1:T(2,128)(2,1)}, bf16[2,3,512]{2,0,1:T(2,128)(2,1)S(1)}, u32[]{:S(2)}, u32[]{:S(2)}) collective-permute-start(bf16[2,3,512]{2,0,1:T(2,128)(2,1)} %param.4), channel_id=1, source_target_pairs={{2,0},{3,1},{6,4},{7,5},{10,8},{11,9},{14,12},{15,13},{18,16},{19,... | collective-permute-start | bytes 18440 | tf_op jit(solution)/shard_map/ppermute | solution.py:110
  3.9 0.7 %copy-start.2 = (s32[2]{0:T(128)S(1)}, s32[2]{0:T(128)}, u32[]{:S(2)}) copy-start(s32[2]{0:T(128)} %param.7) | copy-start | bytes 28
  3.9 2.3 %copy-start.1 = (bf16[2,3,512]{2,0,1:T(2,128)(2,1)S(1)}, bf16[2,3,512]{2,0,1:T(2,128)(2,1)}, u32[]{:S(2)}) copy-start(bf16[2,3,512]{2,0,1:T(2,128)(2,1)} %param.4) | copy-start | bytes 18436
  6.3 4.5 %collective-permute-start.1 = (bf16[2,4,1024]{2,0,1:T(2,128)(2,1)S(1)}, bf16[2,4,1024]{2,0,1:T(2,128)(2,1)S(1)}, u32[]{:S(2)}, u32[]{:S(2)}) collective-permute-start(bf16[2,4,1024]{2,0,1:T(2,128)(2,1)S(1)} %pad_maximum_fusion.5), channel_id=1, source_target_pairs={{0,4},{4,0},{8,12},{12,8},{1,5},{5,1},{9,13},{13,9},{2,6},{6,2},{1... | collective-permute-start | bytes 49160 | tf_op jit(solution)/shard_map/ppermute | solution.py:123
  10.8 5.7 %collective-permute-start.2 = (bf16[4,4,1024]{2,0,1:T(4,128)(2,1)S(1)}, bf16[4,4,1024]{2,0,1:T(4,128)(2,1)S(1)}, u32[]{:S(2)}, u32[]{:S(2)}) collective-permute-start(bf16[4,4,1024]{2,0,1:T(4,128)(2,1)S(1)} %pad_maximum_fusion.4), channel_id=1, source_target_pairs={{0,8},{4,12},{8,0},{12,4},{1,9},{5,13},{9,1},{13,5},{2,10},{6,14},... | collective-permute-start | bytes 98312 | tf_op jit(solution)/shard_map/ppermute | solution.py:123
  22.7 5.2 %collective-permute-start.3 = (f32[64,512]{1,0:T(8,128)}, f32[64,512]{1,0:T(8,128)S(1)}, u32[]{:S(2)}, u32[]{:S(2)}) collective-permute-start(f32[64,512]{1,0:T(8,128)} %shard_map.46), channel_id=1, source_target_pairs={{0,4},{4,0},{8,12},{12,8},{1,5},{5,1},{9,13},{13,9},{2,6},{6,2},{1... | collective-permute-start | bytes 393224 | tf_op jit(solution)/shard_map/ppermute | solution.py:93
  28.8 8.1 %collective-permute-start.4 = (f32[64,512]{1,0:T(8,128)S(1)}, f32[64,512]{1,0:T(8,128)S(1)}, u32[]{:S(2)}, u32[]{:S(2)}) collective-permute-start(f32[64,512]{1,0:T(8,128)S(1)} %add.67), channel_id=1, source_target_pairs={{0,8},{4,12},{8,0},{12,4},{1,9},{5,13},{9,1},{13,5},{2,10},{6,14},... | collective-permute-start | bytes 393224 | tf_op jit(solution)/shard_map/ppermute | solution.py:95
  31.2 10.2 %collective-permute-start.6 = (f32[64,512]{1,0:T(8,128)S(1)}, f32[64,512]{1,0:T(8,128)S(1)}, u32[]{:S(2)}, u32[]{:S(2)}) collective-permute-start(f32[64,512]{1,0:T(8,128)S(1)} %add.67), channel_id=1, source_target_pairs={{0,10},{2,8},{4,14},{6,12},{8,2},{10,0},{12,6},{14,4},{1,11},{3,9}... | collective-permute-start | bytes 393224 | tf_op jit(solution)/shard_map/ppermute | solution.py:97
  32.6 8.8 %collective-permute-start.5 = (f32[64,512]{1,0:T(8,128)S(1)}, f32[64,512]{1,0:T(8,128)S(1)}, u32[]{:S(2)}, u32[]{:S(2)}) collective-permute-start(f32[64,512]{1,0:T(8,128)S(1)} %add.67), channel_id=1, source_target_pairs={{0,2},{2,0},{1,3},{3,1},{4,6},{6,4},{5,7},{7,5},{8,10},{10,8},{9,1... | collective-permute-start | bytes 393224 | tf_op jit(solution)/shard_map/ppermute | solution.py:96

commit v25 on v21

--- a/solution.py
+++ b/solution.py
@@ -48,12 +48,17 @@
         acc = lax.fori_loop(0, pairs, two_channels, acc, unroll=2 if pairs % 2 == 0 else 1)
         if channels % 2:
             acc = one_channel(channels - 1, 0, acc)
-    o_ref[...] = acc
-
-
-def unflip(stacked):
-    rows, seg_len = stacked.shape
-    return stacked.reshape(rows, seg_len // 128, 128)[..., ::-1].reshape(rows, seg_len)
+    exchange = (row + lane == 127).astype(jnp.bfloat16)
+    high = acc.astype(jnp.bfloat16)
+    rest = acc - high.astype(jnp.float32)
+    middle = rest.astype(jnp.bfloat16)
+    low_part = (rest - middle.astype(jnp.float32)).astype(jnp.bfloat16)
+    for a in range(out_blocks):
+        cols = slice(a * 128, (a + 1) * 128)
+        flipped = jnp.dot(high[:, cols], exchange, preferred_element_type=jnp.float32)
+        flipped = flipped + jnp.dot(middle[:, cols], exchange, preferred_element_type=jnp.float32)
+        flipped = flipped + jnp.dot(low_part[:, cols], exchange, preferred_element_type=jnp.float32)
+        o_ref[:, cols] = flipped
 
 
 def correlate(normed, flat_owned, seg_len):
@@ -142,7 +147,7 @@
     total_len = seg_len * lax.axis_size("seg")
     stacked = ordered_sum(correlate(normed, flat_owned, seg_len), "region")
     power_sum = ordered_sum(jnp.sum(stacked * stacked, axis=1), "seg")
-    detect = unflip(stacked) / jnp.sqrt(power_sum / total_len + 1e-06)[:, None]
+    detect = stacked / jnp.sqrt(power_sum / total_len + 1e-06)[:, None]
     return detect.reshape(local_batches, kept, seg_len)
 
 

time: 40.2 us -> 40.4 us (level)
    div x1 -> x0, other arithmetic: 0.75 us -> none  [per_device(): detect = unflip(stacked) / jnp.sqrt(power_sum / total_len + 1e-06)[:, None]]
    reshape x0 -> x1, other arithmetic: none -> 0.75 us  [per_device(): return detect.reshape(local_batches, kept, seg_len)]
  transfers between devices with their start and end apart: 6 -> 6, of which waited for: 5 -> 5; matrix products, arithmetic and copies ran while one was open for 15% -> 14% of each run, Pallas kernels for 0% -> 0%
where the time goes in v25:
time: 40.4 us; the launch traced here: 40.1 us
  starting transfers between devices  14.1 us (35%)
  waiting for transfers between devices  11.9 us (29%)
  other arithmetic  5.37 us (13%)
  Pallas kernels  4.85 us (12%)
  local copies, waits for them, and re-layouts  3.53 us (9%)
    ppermute x3, waiting for transfers between devices, ordered_sum(): part = part + lax.ppermute(part, axis, [(i, i ^ step) for i in range(size)])  8.64 us
    ppermute x3, starting transfers between devices, ordered_sum(): part = part + lax.ppermute(part, axis, [(i, i ^ step) for i in range(size)])  6.83 us
    ppermute x2, starting transfers between devices, gather_owned(): lax.ppermute(here, 'region', [(r, r ^ step) for r in range(regions)])  5.89 us
    pallas_call x1, Pallas kernels, correlate(): pl.pallas_call(hankel_kernel, out_shape=jax.ShapeDtypeStruct((rows, seg_l...  4.85 us
    another operation x1, local copies, waits for them, and re-layouts, correlate(): normed.reshape(rows, channels * filter_taps)  1.84 us
    ppermute x2, waiting for transfers between devices, gather_owned(): lax.ppermute(here, 'region', [(r, r ^ step) for r in range(regions)])  1.72 us
    reduce_sum x1, other arithmetic, per_device(): jnp.sum(widened_templates * widened_templates, axis=4, keepdims=True)  1.65 us
    ppermute x1, waiting for transfers between devices, gather_owned(): lax.ppermute(records[:, :, :filter_taps], 'seg', [(s + 1, s) for s in ran...  1.57 us
  transfers between devices with their start and end apart: 6, of which 5 were waited for; matrix products, arithmetic and copies ran while one was open for 14% of the time, Pallas kernels for 0%

profile of v25, /device:TPU:0, one launch (start us, length us, event | category | flops | bytes accessed | tf_op | source)
XLA Modules:
  0.0 40.1 jit_solution(15616465680890083553)
XLA Ops:
  0.0 1.4 %collective-permute-start = (bf16[2,3,512]{2,0,1:T(2,128)(2,1)}, bf16[2,3,512]{2,0,1:T(2,128)(2,1)S(1)}, u32[]{:S(2)}, u32[]{:S(2)}) collective-permute-start(bf16[2,3,512]{2,0,1:T(2,128)(2,1)} %param.4), channel_id=1, source_target_pairs={{2,0},{3,1},{6,4},{7,5},{10,8},{11,9},{14,12},{15,13},{18,16},{19,... | collective-permute-start | bytes 18440 | tf_op jit(solution)/shard_map/ppermute | solution.py:94
  1.4 0.7 %convert_bitcast_fusion = f32[64,4,3]{0,1,2:T(4,128)S(1)} fusion(s32[1,64,4,3]{1,2,3,0:T(4,128)} %param.6), kind=kLoop, calls=%fused_computation.16 | loop fusion | flops 768 | bytes 6144 | tf_op jit(solution)/shard_map/mul | solution.py:145
  2.1 0.1 copy.9
  2.3 1.7 %fusion.3 = f32[64,4,3]{1,2,0:T(4,128)S(1)} fusion(bf16[1,64,4,3,512]{4,2,3,1,0:T(4,128)(2,1)} %param.5), kind=kLoop, calls=%fused_computation.6 | loop fusion | flops 1178880 | bytes 789504 | tf_op jit(solution)/shard_map/reduce_sum | solution.py:143
  4.0 0.5 %fusion.2 = bf16[1,64,4,3,512]{4,2,3,1,0:T(4,128)(2,1)S(1)} fusion(bf16[1,64,4,3,512]{4,2,3,1,0:T(4,128)(2,1)S(1)} %copy-done, f32[64,4,3]{1,2,0:T(4,128)S(1)} %add_sqrt_fusion, f32[64,4,3]{1,2,0:T(4,128)S(1)} %copy.9), kind=kLoop, calls=%fused_computation.5 | loop fusion | flops 1572864 | bytes 1579008 | tf_op jit(solution)/shard_map/convert_element_type | solution.py:145
  4.6 1.6 %collective-permute-done = bf16[2,3,512]{2,0,1:T(2,128)(2,1)S(1)} collective-permute-done((bf16[2,3,512]{2,0,1:T(2,128)(2,1)}, bf16[2,3,512]{2,0,1:T(2,128)(2,1)S(1)}, u32[]{:S(2)}, u32[]{:S(2)}) %collective-permute-start) | collective-permute-done | bytes 6176 | tf_op jit(solution)/shard_map/ppermute | solution.py:94
  6.3 2.8 %collective-permute-start.1 = (bf16[2,4,1024]{2,0,1:T(2,128)(2,1)S(1)}, bf16[2,4,1024]{2,0,1:T(2,128)(2,1)S(1)}, u32[]{:S(2)}, u32[]{:S(2)}) collective-permute-start(bf16[2,4,1024]{2,0,1:T(2,128)(2,1)S(1)} %pad_maximum_fusion.5), channel_id=1, source_target_pairs={{0,4},{4,0},{8,12},{12,8},{1,5},{5,1},{9,13},{13,9},{2,6},{6,2},{1... | collective-permute-start | bytes 49160 | tf_op jit(solution)/shard_map/ppermute | solution.py:107
  9.1 1.7 %collective-permute-done.1 = bf16[2,4,1024]{2,0,1:T(2,128)(2,1)S(1)} collective-permute-done((bf16[2,4,1024]{2,0,1:T(2,128)(2,1)S(1)}, bf16[2,4,1024]{2,0,1:T(2,128)(2,1)S(1)}, u32[]{:S(2)}, u32[]{:S(2)}) %collective-permute-start.1) | collective-permute-done | bytes 16416 | tf_op jit(solution)/shard_map/ppermute | solution.py:107
  10.8 3.1 %collective-permute-start.2 = (bf16[4,4,1024]{2,0,1:T(4,128)(2,1)S(1)}, bf16[4,4,1024]{2,0,1:T(4,128)(2,1)S(1)}, u32[]{:S(2)}, u32[]{:S(2)}) collective-permute-start(bf16[4,4,1024]{2,0,1:T(4,128)(2,1)S(1)} %pad_maximum_fusion.4), channel_id=1, source_target_pairs={{0,8},{4,12},{8,0},{12,4},{1,9},{5,13},{9,1},{13,5},{2,10},{6,14},... | collective-permute-start | bytes 98312 | tf_op jit(solution)/shard_map/ppermute | solution.py:107
  14.1 0.6 %copy.10 = bf16[1,64,4,3,512]{4,3,2,1,0:T(4,128)(2,1)S(1)} copy(bf16[1,64,4,3,512]{4,2,3,1,0:T(4,128)(2,1)S(1)} %fusion.2) | data formatting | bytes 1572864 | tf_op jit(solution)/shard_map/convert_element_type | solution.py:145
  14.6 1.8 %reshape_reshape.4.n_ref = bf16[64,6144]{1,0:T(8,128)(2,1)} reshape(bf16[1,64,4,3,512]{4,3,2,1,0:T(4,128)(2,1)S(1)} %copy.10) | data formatting | bytes 1572864 | tf_op jit(solution)/shard_map/reshape;reshape | solution.py:71
  16.5 0.1 convert_reduce_fusion
  16.6 0.2 convert_reduce_fusion.1
  17.0 0.1 fusion
  17.2 0.7 %rev.3.x_ref = f32[96,128]{1,0:T(8,128)} reverse(f32[96,128]{1,0:T(8,128)S(1)} %mul.38), dimensions={1} | reverse | bytes 98304 | tf_op jit(solution)/shard_map/rev | solution.py:66
  17.9 4.8 %shard_map.46 = f32[64,512]{1,0:T(8,128)} custom-call(f32[96,128]{1,0:T(8,128)} %rev.3.x_ref, bf16[64,6144]{1,0:T(8,128)(2,1)} %reshape_reshape.4.n_ref), custom_call_target="tpu_custom_call" | custom-call | tf_op jit(solution)/shard_map/pallas_call | solution.py:67
  22.8 1.6 %collective-permute-start.3 = (f32[64,512]{1,0:T(8,128)}, f32[64,512]{1,0:T(8,128)S(1)}, u32[]{:S(2)}, u32[]{:S(2)}) collective-permute-start(f32[64,512]{1,0:T(8,128)} %shard_map.46), channel_id=1, source_target_pairs={{0,4},{4,0},{8,12},{12,8},{1,5},{5,1},{9,13},{13,9},{2,6},{6,2},{1... | collective-permute-start | bytes 393224 | tf_op jit(solution)/shard_map/ppermute | solution.py:79
  24.4 3.6 %collective-permute-done.3 = f32[64,512]{1,0:T(8,128)S(1)} collective-permute-done((f32[64,512]{1,0:T(8,128)}, f32[64,512]{1,0:T(8,128)S(1)}, u32[]{:S(2)}, u32[]{:S(2)}) %collective-permute-start.3) | collective-permute-done | bytes 131104 | tf_op jit(solution)/shard_map/ppermute | solution.py:79
  28.0 0.9 %add.56 = f32[64,512]{1,0:T(8,128)S(1)} add(f32[64,512]{1,0:T(8,128)} %shard_map.46, f32[64,512]{1,0:T(8,128)S(1)} %collective-permute-done.3) | non-fusion elementwise | flops 32768 | bytes 393216 | tf_op jit(solution)/shard_map/add | solution.py:79
  28.9 2.4 %collective-permute-start.4 = (f32[64,512]{1,0:T(8,128)S(1)}, f32[64,512]{1,0:T(8,128)S(1)}, u32[]{:S(2)}, u32[]{:S(2)}) collective-permute-start(f32[64,512]{1,0:T(8,128)S(1)} %add.56), channel_id=1, source_target_pairs={{0,8},{4,12},{8,0},{12,4},{1,9},{5,13},{9,1},{13,5},{2,10},{6,14},... | collective-permute-start | bytes 393224 | tf_op jit(solution)/shard_map/ppermute | solution.py:79
  31.3 3.5 %collective-permute-done.4 = f32[64,512]{1,0:T(8,128)S(1)} collective-permute-done((f32[64,512]{1,0:T(8,128)S(1)}, f32[64,512]{1,0:T(8,128)S(1)}, u32[]{:S(2)}, u32[]{:S(2)}) %collective-permute-start.4) | collective-permute-done | bytes 131104 | tf_op jit(solution)/shard_map/ppermute | solution.py:79
  34.9 2.8 %collective-permute-start.5 = (f32[64]{0:T(128)S(1)}, f32[64]{0:T(128)S(1)}, u32[]{:S(2)}, u32[]{:S(2)}) collective-permute-start(f32[64]{0:T(128)S(1)} %get-tuple-element.5), channel_id=1, source_target_pairs={{0,2},{2,0},{1,3},{3,1},{4,6},{6,4},{5,7},{7,5},{8,10},{10,8},{9,1... | collective-permute-start | bytes 776 | tf_op jit(solution)/shard_map/ppermute | solution.py:79
  37.8 1.5 %collective-permute-done.5 = f32[64]{0:T(128)S(1)} collective-permute-done((f32[64]{0:T(128)S(1)}, f32[64]{0:T(128)S(1)}, u32[]{:S(2)}, u32[]{:S(2)}) %collective-permute-start.5) | collective-permute-done | bytes 288 | tf_op jit(solution)/shard_map/ppermute | solution.py:79
  39.3 0.7 %divide_bitcast_fusion = f32[1,64,512]{2,1,0:T(8,128)} fusion(f32[64,512]{1,0:T(8,128)S(1)} %get-tuple-element.6, f32[64]{0:T(128)S(1)} %add_sqrt_fusion.1), kind=kLoop, calls=%fused_computation.7 | loop fusion | flops 32768 | bytes 262400 | tf_op jit(solution)/shard_map/reshape | solution.py:151
  (24 shorter events, 0.8 us)
Async XLA Ops:
  0.0 4.0 %copy-start = (bf16[1,64,4,3,512]{4,2,3,1,0:T(4,128)(2,1)S(1)}, bf16[1,64,4,3,512]{4,2,3,1,0:T(4,128)(2,1)}, u32[]{:S(2)}) copy-start(bf16[1,64,4,3,512]{4,2,3,1,0:T(4,128)(2,1)} %param.5) | copy-start | bytes 2359300
  0.0 6.2 %collective-permute-start = (bf16[2,3,512]{2,0,1:T(2,128)(2,1)}, bf16[2,3,512]{2,0,1:T(2,128)(2,1)S(1)}, u32[]{:S(2)}, u32[]{:S(2)}) collective-permute-start(bf16[2,3,512]{2,0,1:T(2,128)(2,1)} %param.4), channel_id=1, source_target_pairs={{2,0},{3,1},{6,4},{7,5},{10,8},{11,9},{14,12},{15,13},{18,16},{19,... | collective-permute-start | bytes 18440 | tf_op jit(solution)/shard_map/ppermute | solution.py:94
  3.9 0.7 %copy-start.2 = (s32[2]{0:T(128)S(1)}, s32[2]{0:T(128)}, u32[]{:S(2)}) copy-start(s32[2]{0:T(128)} %param.7) | copy-start | bytes 28
  3.9 2.3 %copy-start.1 = (bf16[2,3,512]{2,0,1:T(2,128)(2,1)S(1)}, bf16[2,3,512]{2,0,1:T(2,128)(2,1)}, u32[]{:S(2)}) copy-start(bf16[2,3,512]{2,0,1:T(2,128)(2,1)} %param.4) | copy-start | bytes 18436
  6.3 4.5 %collective-permute-start.1 = (bf16[2,4,1024]{2,0,1:T(2,128)(2,1)S(1)}, bf16[2,4,1024]{2,0,1:T(2,128)(2,1)S(1)}, u32[]{:S(2)}, u32[]{:S(2)}) collective-permute-start(bf16[2,4,1024]{2,0,1:T(2,128)(2,1)S(1)} %pad_maximum_fusion.5), channel_id=1, source_target_pairs={{0,4},{4,0},{8,12},{12,8},{1,5},{5,1},{9,13},{13,9},{2,6},{6,2},{1... | collective-permute-start | bytes 49160 | tf_op jit(solution)/shard_map/ppermute | solution.py:107
  10.8 5.7 %collective-permute-start.2 = (bf16[4,4,1024]{2,0,1:T(4,128)(2,1)S(1)}, bf16[4,4,1024]{2,0,1:T(4,128)(2,1)S(1)}, u32[]{:S(2)}, u32[]{:S(2)}) collective-permute-start(bf16[4,4,1024]{2,0,1:T(4,128)(2,1)S(1)} %pad_maximum_fusion.4), channel_id=1, source_target_pairs={{0,8},{4,12},{8,0},{12,4},{1,9},{5,13},{9,1},{13,5},{2,10},{6,14},... | collective-permute-start | bytes 98312 | tf_op jit(solution)/shard_map/ppermute | solution.py:107
  22.8 5.2 %collective-permute-start.3 = (f32[64,512]{1,0:T(8,128)}, f32[64,512]{1,0:T(8,128)S(1)}, u32[]{:S(2)}, u32[]{:S(2)}) collective-permute-start(f32[64,512]{1,0:T(8,128)} %shard_map.46), channel_id=1, source_target_pairs={{0,4},{4,0},{8,12},{12,8},{1,5},{5,1},{9,13},{13,9},{2,6},{6,2},{1... | collective-permute-start | bytes 393224 | tf_op jit(solution)/shard_map/ppermute | solution.py:79
  28.9 5.9 %collective-permute-start.4 = (f32[64,512]{1,0:T(8,128)S(1)}, f32[64,512]{1,0:T(8,128)S(1)}, u32[]{:S(2)}, u32[]{:S(2)}) collective-permute-start(f32[64,512]{1,0:T(8,128)S(1)} %add.56), channel_id=1, source_target_pairs={{0,8},{4,12},{8,0},{12,4},{1,9},{5,13},{9,1},{13,5},{2,10},{6,14},... | collective-permute-start | bytes 393224 | tf_op jit(solution)/shard_map/ppermute | solution.py:79
  34.9 4.4 %collective-permute-start.5 = (f32[64]{0:T(128)S(1)}, f32[64]{0:T(128)S(1)}, u32[]{:S(2)}, u32[]{:S(2)}) collective-permute-start(f32[64]{0:T(128)S(1)} %get-tuple-element.5), channel_id=1, source_target_pairs={{0,2},{2,0},{1,3},{3,1},{4,6},{6,4},{5,7},{7,5},{8,10},{10,8},{9,1... | collective-permute-start | bytes 776 | tf_op jit(solution)/shard_map/ppermute | solution.py:79

commit v26 on v21

--- a/solution.py
+++ b/solution.py
@@ -142,7 +142,8 @@
     total_len = seg_len * lax.axis_size("seg")
     stacked = ordered_sum(correlate(normed, flat_owned, seg_len), "region")
     power_sum = ordered_sum(jnp.sum(stacked * stacked, axis=1), "seg")
-    detect = unflip(stacked) / jnp.sqrt(power_sum / total_len + 1e-06)[:, None]
+    ordered = lax.optimization_barrier(unflip(stacked))
+    detect = ordered / jnp.sqrt(power_sum / total_len + 1e-06)[:, None]
     return detect.reshape(local_batches, kept, seg_len)
 
 

time: 40.2 us -> 40.3 us (level)
    div x1 -> x0, other arithmetic: 0.75 us -> none  [per_device(): detect = unflip(stacked) / jnp.sqrt(power_sum / total_len + 1e-06)[:, None]]
    reshape x0 -> x1, other arithmetic: none -> 0.75 us  [per_device(): return detect.reshape(local_batches, kept, seg_len)]
where the time goes in v26:
time: 40.3 us; the launch traced here: 40 us
  starting transfers between devices  14.1 us (35%)
  waiting for transfers between devices  11.7 us (29%)
  other arithmetic  5.37 us (13%)
  Pallas kernels  4.72 us (12%)
  local copies, waits for them, and re-layouts  3.76 us (9%)
    ppermute x3, waiting for transfers between devices, ordered_sum(): part = part + lax.ppermute(part, axis, [(i, i ^ step) for i in range(size)])  8.44 us
    ppermute x3, starting transfers between devices, ordered_sum(): part = part + lax.ppermute(part, axis, [(i, i ^ step) for i in range(size)])  6.84 us
    ppermute x2, starting transfers between devices, gather_owned(): lax.ppermute(here, 'region', [(r, r ^ step) for r in range(regions)])  5.89 us
    pallas_call x1, Pallas kernels, correlate(): pl.pallas_call(hankel_kernel, out_shape=jax.ShapeDtypeStruct((rows, seg_l...  4.72 us
    another operation x1, local copies, waits for them, and re-layouts, correlate(): normed.reshape(rows, channels * filter_taps)  1.84 us
    ppermute x2, waiting for transfers between devices, gather_owned(): lax.ppermute(here, 'region', [(r, r ^ step) for r in range(regions)])  1.72 us
    reduce_sum x1, other arithmetic, per_device(): jnp.sum(widened_templates * widened_templates, axis=4, keepdims=True)  1.65 us
    ppermute x1, waiting for transfers between devices, gather_owned(): lax.ppermute(records[:, :, :filter_taps], 'seg', [(s + 1, s) for s in ran...  1.57 us
  transfers between devices with their start and end apart: 6, of which 5 were waited for; matrix products, arithmetic and copies ran while one was open for 15% of the time, Pallas kernels for 0%

profile of v26, /device:TPU:0, one launch (start us, length us, event | category | flops | bytes accessed | tf_op | source)
XLA Modules:
  0.0 40.0 jit_solution(4904376271452745444)
XLA Ops:
  0.0 1.4 %collective-permute-start = (bf16[2,3,512]{2,0,1:T(2,128)(2,1)}, bf16[2,3,512]{2,0,1:T(2,128)(2,1)S(1)}, u32[]{:S(2)}, u32[]{:S(2)}) collective-permute-start(bf16[2,3,512]{2,0,1:T(2,128)(2,1)} %param.4), channel_id=1, source_target_pairs={{2,0},{3,1},{6,4},{7,5},{10,8},{11,9},{14,12},{15,13},{18,16},{19,... | collective-permute-start | bytes 18440 | tf_op jit(solution)/shard_map/ppermute | solution.py:89
  1.4 0.7 %convert_bitcast_fusion = f32[64,4,3]{0,1,2:T(4,128)S(1)} fusion(s32[1,64,4,3]{1,2,3,0:T(4,128)} %param.6), kind=kLoop, calls=%fused_computation.17 | loop fusion | flops 768 | bytes 6144 | tf_op jit(solution)/shard_map/mul | solution.py:140
  2.1 0.1 copy.9
  2.3 1.7 %fusion.3 = f32[64,4,3]{1,2,0:T(4,128)S(1)} fusion(bf16[1,64,4,3,512]{4,2,3,1,0:T(4,128)(2,1)} %param.5), kind=kLoop, calls=%fused_computation.6 | loop fusion | flops 1178880 | bytes 789504 | tf_op jit(solution)/shard_map/reduce_sum | solution.py:138
  4.0 0.5 %fusion.2 = bf16[1,64,4,3,512]{4,2,3,1,0:T(4,128)(2,1)S(1)} fusion(bf16[1,64,4,3,512]{4,2,3,1,0:T(4,128)(2,1)S(1)} %copy-done, f32[64,4,3]{1,2,0:T(4,128)S(1)} %add_sqrt_fusion, f32[64,4,3]{1,2,0:T(4,128)S(1)} %copy.9), kind=kLoop, calls=%fused_computation.5 | loop fusion | flops 1572864 | bytes 1579008 | tf_op jit(solution)/shard_map/convert_element_type | solution.py:140
  4.6 1.6 %collective-permute-done = bf16[2,3,512]{2,0,1:T(2,128)(2,1)S(1)} collective-permute-done((bf16[2,3,512]{2,0,1:T(2,128)(2,1)}, bf16[2,3,512]{2,0,1:T(2,128)(2,1)S(1)}, u32[]{:S(2)}, u32[]{:S(2)}) %collective-permute-start) | collective-permute-done | bytes 6176 | tf_op jit(solution)/shard_map/ppermute | solution.py:89
  6.3 2.8 %collective-permute-start.1 = (bf16[2,4,1024]{2,0,1:T(2,128)(2,1)S(1)}, bf16[2,4,1024]{2,0,1:T(2,128)(2,1)S(1)}, u32[]{:S(2)}, u32[]{:S(2)}) collective-permute-start(bf16[2,4,1024]{2,0,1:T(2,128)(2,1)S(1)} %pad_maximum_fusion.5), channel_id=1, source_target_pairs={{0,4},{4,0},{8,12},{12,8},{1,5},{5,1},{9,13},{13,9},{2,6},{6,2},{1... | collective-permute-start | bytes 49160 | tf_op jit(solution)/shard_map/ppermute | solution.py:102
  9.1 1.7 %collective-permute-done.1 = bf16[2,4,1024]{2,0,1:T(2,128)(2,1)S(1)} collective-permute-done((bf16[2,4,1024]{2,0,1:T(2,128)(2,1)S(1)}, bf16[2,4,1024]{2,0,1:T(2,128)(2,1)S(1)}, u32[]{:S(2)}, u32[]{:S(2)}) %collective-permute-start.1) | collective-permute-done | bytes 16416 | tf_op jit(solution)/shard_map/ppermute | solution.py:102
  10.8 3.1 %collective-permute-start.2 = (bf16[4,4,1024]{2,0,1:T(4,128)(2,1)S(1)}, bf16[4,4,1024]{2,0,1:T(4,128)(2,1)S(1)}, u32[]{:S(2)}, u32[]{:S(2)}) collective-permute-start(bf16[4,4,1024]{2,0,1:T(4,128)(2,1)S(1)} %pad_maximum_fusion.4), channel_id=1, source_target_pairs={{0,8},{4,12},{8,0},{12,4},{1,9},{5,13},{9,1},{13,5},{2,10},{6,14},... | collective-permute-start | bytes 98312 | tf_op jit(solution)/shard_map/ppermute | solution.py:102
  14.1 0.6 %copy.10 = bf16[1,64,4,3,512]{4,3,2,1,0:T(4,128)(2,1)S(1)} copy(bf16[1,64,4,3,512]{4,2,3,1,0:T(4,128)(2,1)S(1)} %fusion.2) | data formatting | bytes 1572864 | tf_op jit(solution)/shard_map/convert_element_type | solution.py:140
  14.6 1.8 %reshape_reshape.4.n_ref = bf16[64,6144]{1,0:T(8,128)(2,1)} reshape(bf16[1,64,4,3,512]{4,3,2,1,0:T(4,128)(2,1)S(1)} %copy.10) | data formatting | bytes 1572864 | tf_op jit(solution)/shard_map/reshape;reshape | solution.py:66
  16.6 0.2 convert_reduce_fusion.1
  17.0 0.1 fusion
  17.2 0.7 %rev.6.x_ref = f32[96,128]{1,0:T(8,128)} reverse(f32[96,128]{1,0:T(8,128)S(1)} %mul.38), dimensions={1} | reverse | bytes 98304 | tf_op jit(solution)/shard_map/rev | solution.py:61
  17.9 4.7 %shard_map.46 = f32[64,512]{1,0:T(8,128)} custom-call(f32[96,128]{1,0:T(8,128)} %rev.6.x_ref, bf16[64,6144]{1,0:T(8,128)(2,1)} %reshape_reshape.4.n_ref), custom_call_target="tpu_custom_call" | custom-call | tf_op jit(solution)/shard_map/pallas_call | solution.py:62
  22.7 1.6 %collective-permute-start.3 = (f32[64,512]{1,0:T(8,128)}, f32[64,512]{1,0:T(8,128)S(1)}, u32[]{:S(2)}, u32[]{:S(2)}) collective-permute-start(f32[64,512]{1,0:T(8,128)} %shard_map.46), channel_id=1, source_target_pairs={{0,4},{4,0},{8,12},{12,8},{1,5},{5,1},{9,13},{13,9},{2,6},{6,2},{1... | collective-permute-start | bytes 393224 | tf_op jit(solution)/shard_map/ppermute | solution.py:74
  24.2 3.6 %collective-permute-done.3 = f32[64,512]{1,0:T(8,128)S(1)} collective-permute-done((f32[64,512]{1,0:T(8,128)}, f32[64,512]{1,0:T(8,128)S(1)}, u32[]{:S(2)}, u32[]{:S(2)}) %collective-permute-start.3) | collective-permute-done | bytes 131104 | tf_op jit(solution)/shard_map/ppermute | solution.py:74
  27.8 0.9 %add.56 = f32[64,512]{1,0:T(8,128)S(1)} add(f32[64,512]{1,0:T(8,128)} %shard_map.46, f32[64,512]{1,0:T(8,128)S(1)} %collective-permute-done.3) | non-fusion elementwise | flops 32768 | bytes 393216 | tf_op jit(solution)/shard_map/add | solution.py:74
  28.8 2.4 %collective-permute-start.4 = (f32[64,512]{1,0:T(8,128)S(1)}, f32[64,512]{1,0:T(8,128)S(1)}, u32[]{:S(2)}, u32[]{:S(2)}) collective-permute-start(f32[64,512]{1,0:T(8,128)S(1)} %add.56), channel_id=1, source_target_pairs={{0,8},{4,12},{8,0},{12,4},{1,9},{5,13},{9,1},{13,5},{2,10},{6,14},... | collective-permute-start | bytes 393224 | tf_op jit(solution)/shard_map/ppermute | solution.py:74
  31.2 3.5 %collective-permute-done.4 = f32[64,512]{1,0:T(8,128)S(1)} collective-permute-done((f32[64,512]{1,0:T(8,128)S(1)}, f32[64,512]{1,0:T(8,128)S(1)}, u32[]{:S(2)}, u32[]{:S(2)}) %collective-permute-start.4) | collective-permute-done | bytes 131104 | tf_op jit(solution)/shard_map/ppermute | solution.py:74
  34.9 2.8 %collective-permute-start.5 = (f32[64]{0:T(128)S(1)}, f32[64]{0:T(128)S(1)}, u32[]{:S(2)}, u32[]{:S(2)}) collective-permute-start(f32[64]{0:T(128)S(1)} %get-tuple-element.5), channel_id=1, source_target_pairs={{0,2},{2,0},{1,3},{3,1},{4,6},{6,4},{5,7},{7,5},{8,10},{10,8},{9,1... | collective-permute-start | bytes 776 | tf_op jit(solution)/shard_map/ppermute | solution.py:74
  37.7 0.2 rev.7
  37.9 1.3 %collective-permute-done.5 = f32[64]{0:T(128)S(1)} collective-permute-done((f32[64]{0:T(128)S(1)}, f32[64]{0:T(128)S(1)}, u32[]{:S(2)}, u32[]{:S(2)}) %collective-permute-start.5) | collective-permute-done | bytes 288 | tf_op jit(solution)/shard_map/ppermute | solution.py:74
  39.3 0.7 %divide_bitcast_fusion = f32[1,64,512]{2,1,0:T(8,128)} fusion(f32[64,512]{1,0:T(8,128)S(1)} %bitcast.10, f32[64]{0:T(128)S(1)} %add_sqrt_fusion.1), kind=kLoop, calls=%fused_computation.8 | loop fusion | flops 32768 | bytes 262400 | tf_op jit(solution)/shard_map/reshape | solution.py:147
  (27 shorter events, 1.0 us)
Async XLA Ops:
  0.0 4.0 %copy-start = (bf16[1,64,4,3,512]{4,2,3,1,0:T(4,128)(2,1)S(1)}, bf16[1,64,4,3,512]{4,2,3,1,0:T(4,128)(2,1)}, u32[]{:S(2)}) copy-start(bf16[1,64,4,3,512]{4,2,3,1,0:T(4,128)(2,1)} %param.5) | copy-start | bytes 2359300
  0.0 6.2 %collective-permute-start = (bf16[2,3,512]{2,0,1:T(2,128)(2,1)}, bf16[2,3,512]{2,0,1:T(2,128)(2,1)S(1)}, u32[]{:S(2)}, u32[]{:S(2)}) collective-permute-start(bf16[2,3,512]{2,0,1:T(2,128)(2,1)} %param.4), channel_id=1, source_target_pairs={{2,0},{3,1},{6,4},{7,5},{10,8},{11,9},{14,12},{15,13},{18,16},{19,... | collective-permute-start | bytes 18440 | tf_op jit(solution)/shard_map/ppermute | solution.py:89
  3.9 0.7 %copy-start.2 = (s32[2]{0:T(128)S(1)}, s32[2]{0:T(128)}, u32[]{:S(2)}) copy-start(s32[2]{0:T(128)} %param.7) | copy-start | bytes 28
  3.9 2.3 %copy-start.1 = (bf16[2,3,512]{2,0,1:T(2,128)(2,1)S(1)}, bf16[2,3,512]{2,0,1:T(2,128)(2,1)}, u32[]{:S(2)}) copy-start(bf16[2,3,512]{2,0,1:T(2,128)(2,1)} %param.4) | copy-start | bytes 18436
  6.3 4.5 %collective-permute-start.1 = (bf16[2,4,1024]{2,0,1:T(2,128)(2,1)S(1)}, bf16[2,4,1024]{2,0,1:T(2,128)(2,1)S(1)}, u32[]{:S(2)}, u32[]{:S(2)}) collective-permute-start(bf16[2,4,1024]{2,0,1:T(2,128)(2,1)S(1)} %pad_maximum_fusion.5), channel_id=1, source_target_pairs={{0,4},{4,0},{8,12},{12,8},{1,5},{5,1},{9,13},{13,9},{2,6},{6,2},{1... | collective-permute-start | bytes 49160 | tf_op jit(solution)/shard_map/ppermute | solution.py:102
  10.8 5.7 %collective-permute-start.2 = (bf16[4,4,1024]{2,0,1:T(4,128)(2,1)S(1)}, bf16[4,4,1024]{2,0,1:T(4,128)(2,1)S(1)}, u32[]{:S(2)}, u32[]{:S(2)}) collective-permute-start(bf16[4,4,1024]{2,0,1:T(4,128)(2,1)S(1)} %pad_maximum_fusion.4), channel_id=1, source_target_pairs={{0,8},{4,12},{8,0},{12,4},{1,9},{5,13},{9,1},{13,5},{2,10},{6,14},... | collective-permute-start | bytes 98312 | tf_op jit(solution)/shard_map/ppermute | solution.py:102
  22.7 5.2 %collective-permute-start.3 = (f32[64,512]{1,0:T(8,128)}, f32[64,512]{1,0:T(8,128)S(1)}, u32[]{:S(2)}, u32[]{:S(2)}) collective-permute-start(f32[64,512]{1,0:T(8,128)} %shard_map.46), channel_id=1, source_target_pairs={{0,4},{4,0},{8,12},{12,8},{1,5},{5,1},{9,13},{13,9},{2,6},{6,2},{1... | collective-permute-start | bytes 393224 | tf_op jit(solution)/shard_map/ppermute | solution.py:74
  28.8 5.9 %collective-permute-start.4 = (f32[64,512]{1,0:T(8,128)S(1)}, f32[64,512]{1,0:T(8,128)S(1)}, u32[]{:S(2)}, u32[]{:S(2)}) collective-permute-start(f32[64,512]{1,0:T(8,128)S(1)} %add.56), channel_id=1, source_target_pairs={{0,8},{4,12},{8,0},{12,4},{1,9},{5,13},{9,1},{13,5},{2,10},{6,14},... | collective-permute-start | bytes 393224 | tf_op jit(solution)/shard_map/ppermute | solution.py:74
  34.9 4.4 %collective-permute-start.5 = (f32[64]{0:T(128)S(1)}, f32[64]{0:T(128)S(1)}, u32[]{:S(2)}, u32[]{:S(2)}) collective-permute-start(f32[64]{0:T(128)S(1)} %get-tuple-element.5), channel_id=1, source_target_pairs={{0,2},{2,0},{1,3},{3,1},{4,6},{6,4},{5,7},{7,5},{8,10},{10,8},{9,1... | collective-permute-start | bytes 776 | tf_op jit(solution)/shard_map/ppermute | solution.py:74

commit v27 on v21

--- a/solution.py
+++ b/solution.py
@@ -17,21 +17,29 @@
     low = lane >= row
 
     def one_channel(c, slot, acc):
-        rolled = [
-            pltpu.roll(x_ref[pl.ds(c * blocks + m, 128, stride=0), :], 0, 1, stride=1, stride_axis=0)
-            for m in range(blocks)
-        ]
-        windows = [jnp.where(low, rolled[m], rolled[m + 1]) for m in range(blocks - 1)]
-        squares = [jnp.sum(w * w, axis=0, keepdims=True) for w in windows]
+        def window(m):
+            rolled = [
+                pltpu.roll(x_ref[pl.ds(c * blocks + k, 128, stride=0), :], 0, 1, stride=1, stride_axis=0)
+                for k in (m, m + 1)
+            ]
+            return jnp.where(low, rolled[0], rolled[1])
+
+        squares = []
+        for m in range(blocks - 1):
+            w = window(m)
+            squares.append(jnp.sum(w * w, axis=0, keepdims=True))
         scale = [
             1.0 / jnp.sqrt(jnp.maximum(sum(squares[a + p] for p in range(taps_blocks)), 1.0))
             for a in range(out_blocks)
         ]
-        for p in range(taps_blocks):
-            for a in range(out_blocks):
-                h_ref[slot, p * 128 : (p + 1) * 128, a * 128 : (a + 1) * 128] = (
-                    windows[a + p] * scale[a]
-                ).astype(jnp.bfloat16)
+        for m in range(blocks - 1):
+            w = window(m)
+            for p in range(taps_blocks):
+                a = m - p
+                if 0 <= a < out_blocks:
+                    h_ref[slot, p * 128 : (p + 1) * 128, a * 128 : (a + 1) * 128] = (w * scale[a]).astype(
+                        jnp.bfloat16
+                    )
         start = pl.multiple_of(c * width, 128)
         return acc + jnp.dot(n_ref[:, pl.ds(start, width)], h_ref[slot], preferred_element_type=jnp.float32)
 

time: 40.2 us -> 42.3 us (1.052)
  Pallas kernels: 4.72 us -> 6.77 us
    pallas_call x1, Pallas kernels: 4.72 us -> 6.77 us  [correlate(): pl.pallas_call(hankel_kernel, out_shape=jax.ShapeDtypeStruct((rows, seg_l...]
  transfers between devices with their start and end apart: 6 -> 6, of which waited for: 5 -> 5; matrix products, arithmetic and copies ran while one was open for 15% -> 14% of each run, Pallas kernels for 0% -> 0%
where the time goes in v27:
time: 42.3 us; the launch traced here: 42 us
  starting transfers between devices  14.1 us (33%)
  waiting for transfers between devices  11.6 us (27%)
  Pallas kernels  6.77 us (16%)
  other arithmetic  5.37 us (13%)
  local copies, waits for them, and re-layouts  3.81 us (9%)
    ppermute x3, waiting for transfers between devices, ordered_sum(): part = part + lax.ppermute(part, axis, [(i, i ^ step) for i in range(size)])  8.35 us
    ppermute x3, starting transfers between devices, ordered_sum(): part = part + lax.ppermute(part, axis, [(i, i ^ step) for i in range(size)])  6.82 us
    pallas_call x1, Pallas kernels, correlate(): pl.pallas_call(hankel_kernel, out_shape=jax.ShapeDtypeStruct((rows, seg_l...  6.77 us
    ppermute x2, starting transfers between devices, gather_owned(): lax.ppermute(here, 'region', [(r, r ^ step) for r in range(regions)])  5.89 us
    another operation x1, local copies, waits for them, and re-layouts, correlate(): normed.reshape(rows, channels * filter_taps)  1.84 us
    ppermute x2, waiting for transfers between devices, gather_owned(): lax.ppermute(here, 'region', [(r, r ^ step) for r in range(regions)])  1.72 us
    reduce_sum x1, other arithmetic, per_device(): jnp.sum(widened_templates * widened_templates, axis=4, keepdims=True)  1.65 us
    ppermute x1, waiting for transfers between devices, gather_owned(): lax.ppermute(records[:, :, :filter_taps], 'seg', [(s + 1, s) for s in ran...  1.57 us
  transfers between devices with their start and end apart: 6, of which 5 were waited for; matrix products, arithmetic and copies ran while one was open for 14% of the time, Pallas kernels for 0%

profile of v27, /device:TPU:0, one launch (start us, length us, event | category | flops | bytes accessed | tf_op | source)
XLA Modules:
  0.0 42.0 jit_solution(16098287264567486756)
XLA Ops:
  0.0 1.4 %collective-permute-start = (bf16[2,3,512]{2,0,1:T(2,128)(2,1)}, bf16[2,3,512]{2,0,1:T(2,128)(2,1)S(1)}, u32[]{:S(2)}, u32[]{:S(2)}) collective-permute-start(bf16[2,3,512]{2,0,1:T(2,128)(2,1)} %param.4), channel_id=1, source_target_pairs={{2,0},{3,1},{6,4},{7,5},{10,8},{11,9},{14,12},{15,13},{18,16},{19,... | collective-permute-start | bytes 18440 | tf_op jit(solution)/shard_map/ppermute | solution.py:97
  1.4 0.7 %convert_bitcast_fusion = f32[64,4,3]{0,1,2:T(4,128)S(1)} fusion(s32[1,64,4,3]{1,2,3,0:T(4,128)} %param.6), kind=kLoop, calls=%fused_computation.16 | loop fusion | flops 768 | bytes 6144 | tf_op jit(solution)/shard_map/mul | solution.py:148
  2.1 0.1 copy.9
  2.3 1.7 %fusion.3 = f32[64,4,3]{1,2,0:T(4,128)S(1)} fusion(bf16[1,64,4,3,512]{4,2,3,1,0:T(4,128)(2,1)} %param.5), kind=kLoop, calls=%fused_computation.6 | loop fusion | flops 1178880 | bytes 789504 | tf_op jit(solution)/shard_map/reduce_sum | solution.py:146
  4.0 0.5 %fusion.2 = bf16[1,64,4,3,512]{4,2,3,1,0:T(4,128)(2,1)S(1)} fusion(bf16[1,64,4,3,512]{4,2,3,1,0:T(4,128)(2,1)S(1)} %copy-done, f32[64,4,3]{1,2,0:T(4,128)S(1)} %add_sqrt_fusion, f32[64,4,3]{1,2,0:T(4,128)S(1)} %copy.9), kind=kLoop, calls=%fused_computation.5 | loop fusion | flops 1572864 | bytes 1579008 | tf_op jit(solution)/shard_map/convert_element_type | solution.py:148
  4.6 1.6 %collective-permute-done = bf16[2,3,512]{2,0,1:T(2,128)(2,1)S(1)} collective-permute-done((bf16[2,3,512]{2,0,1:T(2,128)(2,1)}, bf16[2,3,512]{2,0,1:T(2,128)(2,1)S(1)}, u32[]{:S(2)}, u32[]{:S(2)}) %collective-permute-start) | collective-permute-done | bytes 6176 | tf_op jit(solution)/shard_map/ppermute | solution.py:97
  6.3 2.8 %collective-permute-start.1 = (bf16[2,4,1024]{2,0,1:T(2,128)(2,1)S(1)}, bf16[2,4,1024]{2,0,1:T(2,128)(2,1)S(1)}, u32[]{:S(2)}, u32[]{:S(2)}) collective-permute-start(bf16[2,4,1024]{2,0,1:T(2,128)(2,1)S(1)} %pad_maximum_fusion.5), channel_id=1, source_target_pairs={{0,4},{4,0},{8,12},{12,8},{1,5},{5,1},{9,13},{13,9},{2,6},{6,2},{1... | collective-permute-start | bytes 49160 | tf_op jit(solution)/shard_map/ppermute | solution.py:110
  9.1 1.7 %collective-permute-done.1 = bf16[2,4,1024]{2,0,1:T(2,128)(2,1)S(1)} collective-permute-done((bf16[2,4,1024]{2,0,1:T(2,128)(2,1)S(1)}, bf16[2,4,1024]{2,0,1:T(2,128)(2,1)S(1)}, u32[]{:S(2)}, u32[]{:S(2)}) %collective-permute-start.1) | collective-permute-done | bytes 16416 | tf_op jit(solution)/shard_map/ppermute | solution.py:110
  10.8 3.1 %collective-permute-start.2 = (bf16[4,4,1024]{2,0,1:T(4,128)(2,1)S(1)}, bf16[4,4,1024]{2,0,1:T(4,128)(2,1)S(1)}, u32[]{:S(2)}, u32[]{:S(2)}) collective-permute-start(bf16[4,4,1024]{2,0,1:T(4,128)(2,1)S(1)} %pad_maximum_fusion.4), channel_id=1, source_target_pairs={{0,8},{4,12},{8,0},{12,4},{1,9},{5,13},{9,1},{13,5},{2,10},{6,14},... | collective-permute-start | bytes 98312 | tf_op jit(solution)/shard_map/ppermute | solution.py:110
  14.1 0.6 %copy.10 = bf16[1,64,4,3,512]{4,3,2,1,0:T(4,128)(2,1)S(1)} copy(bf16[1,64,4,3,512]{4,2,3,1,0:T(4,128)(2,1)S(1)} %fusion.2) | data formatting | bytes 1572864 | tf_op jit(solution)/shard_map/convert_element_type | solution.py:148
  14.6 1.8 %reshape_reshape.4.n_ref = bf16[64,6144]{1,0:T(8,128)(2,1)} reshape(bf16[1,64,4,3,512]{4,3,2,1,0:T(4,128)(2,1)S(1)} %copy.10) | data formatting | bytes 1572864 | tf_op jit(solution)/shard_map/reshape;reshape | solution.py:74
  16.6 0.2 convert_reduce_fusion.1
  17.0 0.1 fusion
  17.2 0.7 %rev.6.x_ref = f32[96,128]{1,0:T(8,128)} reverse(f32[96,128]{1,0:T(8,128)S(1)} %mul.38), dimensions={1} | reverse | bytes 98304 | tf_op jit(solution)/shard_map/rev | solution.py:69
  17.9 6.8 %shard_map.46 = f32[64,512]{1,0:T(8,128)} custom-call(f32[96,128]{1,0:T(8,128)} %rev.6.x_ref, bf16[64,6144]{1,0:T(8,128)(2,1)} %reshape_reshape.4.n_ref), custom_call_target="tpu_custom_call" | custom-call | tf_op jit(solution)/shard_map/pallas_call | solution.py:70
  24.7 1.6 %collective-permute-start.3 = (f32[64,512]{1,0:T(8,128)}, f32[64,512]{1,0:T(8,128)S(1)}, u32[]{:S(2)}, u32[]{:S(2)}) collective-permute-start(f32[64,512]{1,0:T(8,128)} %shard_map.46), channel_id=1, source_target_pairs={{0,4},{4,0},{8,12},{12,8},{1,5},{5,1},{9,13},{13,9},{2,6},{6,2},{1... | collective-permute-start | bytes 393224 | tf_op jit(solution)/shard_map/ppermute | solution.py:82
  26.3 3.6 %collective-permute-done.3 = f32[64,512]{1,0:T(8,128)S(1)} collective-permute-done((f32[64,512]{1,0:T(8,128)}, f32[64,512]{1,0:T(8,128)S(1)}, u32[]{:S(2)}, u32[]{:S(2)}) %collective-permute-start.3) | collective-permute-done | bytes 131104 | tf_op jit(solution)/shard_map/ppermute | solution.py:82
  29.9 0.9 %add.56 = f32[64,512]{1,0:T(8,128)S(1)} add(f32[64,512]{1,0:T(8,128)} %shard_map.46, f32[64,512]{1,0:T(8,128)S(1)} %collective-permute-done.3) | non-fusion elementwise | flops 32768 | bytes 393216 | tf_op jit(solution)/shard_map/add | solution.py:82
  30.8 2.4 %collective-permute-start.4 = (f32[64,512]{1,0:T(8,128)S(1)}, f32[64,512]{1,0:T(8,128)S(1)}, u32[]{:S(2)}, u32[]{:S(2)}) collective-permute-start(f32[64,512]{1,0:T(8,128)S(1)} %add.56), channel_id=1, source_target_pairs={{0,8},{4,12},{8,0},{12,4},{1,9},{5,13},{9,1},{13,5},{2,10},{6,14},... | collective-permute-start | bytes 393224 | tf_op jit(solution)/shard_map/ppermute | solution.py:82
  33.2 3.5 %collective-permute-done.4 = f32[64,512]{1,0:T(8,128)S(1)} collective-permute-done((f32[64,512]{1,0:T(8,128)S(1)}, f32[64,512]{1,0:T(8,128)S(1)}, u32[]{:S(2)}, u32[]{:S(2)}) %collective-permute-start.4) | collective-permute-done | bytes 131104 | tf_op jit(solution)/shard_map/ppermute | solution.py:82
  36.9 2.8 %collective-permute-start.5 = (f32[64]{0:T(128)S(1)}, f32[64]{0:T(128)S(1)}, u32[]{:S(2)}, u32[]{:S(2)}) collective-permute-start(f32[64]{0:T(128)S(1)} %get-tuple-element.5), channel_id=1, source_target_pairs={{0,2},{2,0},{1,3},{3,1},{4,6},{6,4},{5,7},{7,5},{8,10},{10,8},{9,1... | collective-permute-start | bytes 776 | tf_op jit(solution)/shard_map/ppermute | solution.py:82
  39.8 0.2 rev.7
  40.0 1.2 %collective-permute-done.5 = f32[64]{0:T(128)S(1)} collective-permute-done((f32[64]{0:T(128)S(1)}, f32[64]{0:T(128)S(1)}, u32[]{:S(2)}, u32[]{:S(2)}) %collective-permute-start.5) | collective-permute-done | bytes 288 | tf_op jit(solution)/shard_map/ppermute | solution.py:82
  41.2 0.7 %broadcast_divide_fusion = f32[1,64,512]{2,1,0:T(8,128)} fusion(f32[1,64,512]{2,1,0:T(8,128)S(1)} %reshape.115, f32[64]{0:T(128)S(1)} %add_sqrt_fusion.1), kind=kLoop, calls=%fused_computation.9 | loop fusion | flops 32768 | bytes 262400 | tf_op jit(solution)/shard_map/div | solution.py:153
  (27 shorter events, 1.1 us)
Async XLA Ops:
  0.0 4.0 %copy-start = (bf16[1,64,4,3,512]{4,2,3,1,0:T(4,128)(2,1)S(1)}, bf16[1,64,4,3,512]{4,2,3,1,0:T(4,128)(2,1)}, u32[]{:S(2)}) copy-start(bf16[1,64,4,3,512]{4,2,3,1,0:T(4,128)(2,1)} %param.5) | copy-start | bytes 2359300
  0.0 6.2 %collective-permute-start = (bf16[2,3,512]{2,0,1:T(2,128)(2,1)}, bf16[2,3,512]{2,0,1:T(2,128)(2,1)S(1)}, u32[]{:S(2)}, u32[]{:S(2)}) collective-permute-start(bf16[2,3,512]{2,0,1:T(2,128)(2,1)} %param.4), channel_id=1, source_target_pairs={{2,0},{3,1},{6,4},{7,5},{10,8},{11,9},{14,12},{15,13},{18,16},{19,... | collective-permute-start | bytes 18440 | tf_op jit(solution)/shard_map/ppermute | solution.py:97
  3.9 0.7 %copy-start.2 = (s32[2]{0:T(128)S(1)}, s32[2]{0:T(128)}, u32[]{:S(2)}) copy-start(s32[2]{0:T(128)} %param.7) | copy-start | bytes 28
  3.9 2.3 %copy-start.1 = (bf16[2,3,512]{2,0,1:T(2,128)(2,1)S(1)}, bf16[2,3,512]{2,0,1:T(2,128)(2,1)}, u32[]{:S(2)}) copy-start(bf16[2,3,512]{2,0,1:T(2,128)(2,1)} %param.4) | copy-start | bytes 18436
  6.3 4.5 %collective-permute-start.1 = (bf16[2,4,1024]{2,0,1:T(2,128)(2,1)S(1)}, bf16[2,4,1024]{2,0,1:T(2,128)(2,1)S(1)}, u32[]{:S(2)}, u32[]{:S(2)}) collective-permute-start(bf16[2,4,1024]{2,0,1:T(2,128)(2,1)S(1)} %pad_maximum_fusion.5), channel_id=1, source_target_pairs={{0,4},{4,0},{8,12},{12,8},{1,5},{5,1},{9,13},{13,9},{2,6},{6,2},{1... | collective-permute-start | bytes 49160 | tf_op jit(solution)/shard_map/ppermute | solution.py:110
  10.8 5.7 %collective-permute-start.2 = (bf16[4,4,1024]{2,0,1:T(4,128)(2,1)S(1)}, bf16[4,4,1024]{2,0,1:T(4,128)(2,1)S(1)}, u32[]{:S(2)}, u32[]{:S(2)}) collective-permute-start(bf16[4,4,1024]{2,0,1:T(4,128)(2,1)S(1)} %pad_maximum_fusion.4), channel_id=1, source_target_pairs={{0,8},{4,12},{8,0},{12,4},{1,9},{5,13},{9,1},{13,5},{2,10},{6,14},... | collective-permute-start | bytes 98312 | tf_op jit(solution)/shard_map/ppermute | solution.py:110
  24.7 5.2 %collective-permute-start.3 = (f32[64,512]{1,0:T(8,128)}, f32[64,512]{1,0:T(8,128)S(1)}, u32[]{:S(2)}, u32[]{:S(2)}) collective-permute-start(f32[64,512]{1,0:T(8,128)} %shard_map.46), channel_id=1, source_target_pairs={{0,4},{4,0},{8,12},{12,8},{1,5},{5,1},{9,13},{13,9},{2,6},{6,2},{1... | collective-permute-start | bytes 393224 | tf_op jit(solution)/shard_map/ppermute | solution.py:82
  30.8 5.9 %collective-permute-start.4 = (f32[64,512]{1,0:T(8,128)S(1)}, f32[64,512]{1,0:T(8,128)S(1)}, u32[]{:S(2)}, u32[]{:S(2)}) collective-permute-start(f32[64,512]{1,0:T(8,128)S(1)} %add.56), channel_id=1, source_target_pairs={{0,8},{4,12},{8,0},{12,4},{1,9},{5,13},{9,1},{13,5},{2,10},{6,14},... | collective-permute-start | bytes 393224 | tf_op jit(solution)/shard_map/ppermute | solution.py:82
  36.9 4.4 %collective-permute-start.5 = (f32[64]{0:T(128)S(1)}, f32[64]{0:T(128)S(1)}, u32[]{:S(2)}, u32[]{:S(2)}) collective-permute-start(f32[64]{0:T(128)S(1)} %get-tuple-element.5), channel_id=1, source_target_pairs={{0,2},{2,0},{1,3},{3,1},{4,6},{6,4},{5,7},{7,5},{8,10},{10,8},{9,1... | collective-permute-start | bytes 776 | tf_op jit(solution)/shard_map/ppermute | solution.py:82

commit v28 on v21

--- a/solution.py
+++ b/solution.py
@@ -40,7 +40,7 @@
         return one_channel(2 * i + 1, 1, acc)
 
     acc = jnp.zeros(o_ref.shape, jnp.float32)
-    if channels <= 16:
+    if channels <= 2:
         for c in range(channels):
             acc = one_channel(c, c % 2, acc)
     else:

time: 40.2 us -> 40.9 us (1.017)
  Pallas kernels: 4.72 us -> 5.36 us
    pallas_call x1, Pallas kernels: 4.72 us -> 5.36 us  [correlate(): pl.pallas_call(hankel_kernel, out_shape=jax.ShapeDtypeStruct((rows, seg_l...]
where the time goes in v28:
time: 40.9 us; the launch traced here: 40.6 us
  starting transfers between devices  14.1 us (34%)
  waiting for transfers between devices  11.6 us (28%)
  other arithmetic  5.37 us (13%)
  Pallas kernels  5.36 us (13%)
  local copies, waits for them, and re-layouts  3.81 us (9%)
    ppermute x3, waiting for transfers between devices, ordered_sum(): part = part + lax.ppermute(part, axis, [(i, i ^ step) for i in range(size)])  8.34 us
    ppermute x3, starting transfers between devices, ordered_sum(): part = part + lax.ppermute(part, axis, [(i, i ^ step) for i in range(size)])  6.84 us
    ppermute x2, starting transfers between devices, gather_owned(): lax.ppermute(here, 'region', [(r, r ^ step) for r in range(regions)])  5.89 us
    pallas_call x1, Pallas kernels, correlate(): pl.pallas_call(hankel_kernel, out_shape=jax.ShapeDtypeStruct((rows, seg_l...  5.36 us
    another operation x1, local copies, waits for them, and re-layouts, correlate(): normed.reshape(rows, channels * filter_taps)  1.84 us
    ppermute x2, waiting for transfers between devices, gather_owned(): lax.ppermute(here, 'region', [(r, r ^ step) for r in range(regions)])  1.72 us
    reduce_sum x1, other arithmetic, per_device(): jnp.sum(widened_templates * widened_templates, axis=4, keepdims=True)  1.65 us
    ppermute x1, waiting for transfers between devices, gather_owned(): lax.ppermute(records[:, :, :filter_taps], 'seg', [(s + 1, s) for s in ran...  1.57 us
  transfers between devices with their start and end apart: 6, of which 5 were waited for; matrix products, arithmetic and copies ran while one was open for 15% of the time, Pallas kernels for 0%

profile of v28, /device:TPU:0, one launch (start us, length us, event | category | flops | bytes accessed | tf_op | source)
XLA Modules:
  0.0 40.6 jit_solution(8159459063084747760)
XLA Ops:
  0.0 1.4 %collective-permute-start = (bf16[2,3,512]{2,0,1:T(2,128)(2,1)}, bf16[2,3,512]{2,0,1:T(2,128)(2,1)S(1)}, u32[]{:S(2)}, u32[]{:S(2)}) collective-permute-start(bf16[2,3,512]{2,0,1:T(2,128)(2,1)} %param.4), channel_id=1, source_target_pairs={{2,0},{3,1},{6,4},{7,5},{10,8},{11,9},{14,12},{15,13},{18,16},{19,... | collective-permute-start | bytes 18440 | tf_op jit(solution)/shard_map/ppermute | solution.py:89
  1.4 0.7 %convert_bitcast_fusion = f32[64,4,3]{0,1,2:T(4,128)S(1)} fusion(s32[1,64,4,3]{1,2,3,0:T(4,128)} %param.6), kind=kLoop, calls=%fused_computation.16 | loop fusion | flops 768 | bytes 6144 | tf_op jit(solution)/shard_map/mul | solution.py:140
  2.1 0.1 copy.9
  2.3 1.7 %fusion.3 = f32[64,4,3]{1,2,0:T(4,128)S(1)} fusion(bf16[1,64,4,3,512]{4,2,3,1,0:T(4,128)(2,1)} %param.5), kind=kLoop, calls=%fused_computation.6 | loop fusion | flops 1178880 | bytes 789504 | tf_op jit(solution)/shard_map/reduce_sum | solution.py:138
  4.0 0.5 %fusion.2 = bf16[1,64,4,3,512]{4,2,3,1,0:T(4,128)(2,1)S(1)} fusion(bf16[1,64,4,3,512]{4,2,3,1,0:T(4,128)(2,1)S(1)} %copy-done, f32[64,4,3]{1,2,0:T(4,128)S(1)} %add_sqrt_fusion, f32[64,4,3]{1,2,0:T(4,128)S(1)} %copy.9), kind=kLoop, calls=%fused_computation.5 | loop fusion | flops 1572864 | bytes 1579008 | tf_op jit(solution)/shard_map/convert_element_type | solution.py:140
  4.6 1.6 %collective-permute-done = bf16[2,3,512]{2,0,1:T(2,128)(2,1)S(1)} collective-permute-done((bf16[2,3,512]{2,0,1:T(2,128)(2,1)}, bf16[2,3,512]{2,0,1:T(2,128)(2,1)S(1)}, u32[]{:S(2)}, u32[]{:S(2)}) %collective-permute-start) | collective-permute-done | bytes 6176 | tf_op jit(solution)/shard_map/ppermute | solution.py:89
  6.3 2.8 %collective-permute-start.1 = (bf16[2,4,1024]{2,0,1:T(2,128)(2,1)S(1)}, bf16[2,4,1024]{2,0,1:T(2,128)(2,1)S(1)}, u32[]{:S(2)}, u32[]{:S(2)}) collective-permute-start(bf16[2,4,1024]{2,0,1:T(2,128)(2,1)S(1)} %pad_maximum_fusion.5), channel_id=1, source_target_pairs={{0,4},{4,0},{8,12},{12,8},{1,5},{5,1},{9,13},{13,9},{2,6},{6,2},{1... | collective-permute-start | bytes 49160 | tf_op jit(solution)/shard_map/ppermute | solution.py:102
  9.1 1.7 %collective-permute-done.1 = bf16[2,4,1024]{2,0,1:T(2,128)(2,1)S(1)} collective-permute-done((bf16[2,4,1024]{2,0,1:T(2,128)(2,1)S(1)}, bf16[2,4,1024]{2,0,1:T(2,128)(2,1)S(1)}, u32[]{:S(2)}, u32[]{:S(2)}) %collective-permute-start.1) | collective-permute-done | bytes 16416 | tf_op jit(solution)/shard_map/ppermute | solution.py:102
  10.8 3.1 %collective-permute-start.2 = (bf16[4,4,1024]{2,0,1:T(4,128)(2,1)S(1)}, bf16[4,4,1024]{2,0,1:T(4,128)(2,1)S(1)}, u32[]{:S(2)}, u32[]{:S(2)}) collective-permute-start(bf16[4,4,1024]{2,0,1:T(4,128)(2,1)S(1)} %pad_maximum_fusion.4), channel_id=1, source_target_pairs={{0,8},{4,12},{8,0},{12,4},{1,9},{5,13},{9,1},{13,5},{2,10},{6,14},... | collective-permute-start | bytes 98312 | tf_op jit(solution)/shard_map/ppermute | solution.py:102
  14.1 0.6 %copy.10 = bf16[1,64,4,3,512]{4,3,2,1,0:T(4,128)(2,1)S(1)} copy(bf16[1,64,4,3,512]{4,2,3,1,0:T(4,128)(2,1)S(1)} %fusion.2) | data formatting | bytes 1572864 | tf_op jit(solution)/shard_map/convert_element_type | solution.py:140
  14.6 1.8 %reshape_reshape.4.n_ref = bf16[64,6144]{1,0:T(8,128)(2,1)} reshape(bf16[1,64,4,3,512]{4,3,2,1,0:T(4,128)(2,1)S(1)} %copy.10) | data formatting | bytes 1572864 | tf_op jit(solution)/shard_map/reshape;reshape | solution.py:66
  16.6 0.2 convert_reduce_fusion.1
  17.0 0.1 fusion
  17.2 0.7 %rev.6.x_ref = f32[96,128]{1,0:T(8,128)} reverse(f32[96,128]{1,0:T(8,128)S(1)} %mul.38), dimensions={1} | reverse | bytes 98304 | tf_op jit(solution)/shard_map/rev | solution.py:61
  17.9 5.4 %shard_map.46 = f32[64,512]{1,0:T(8,128)} custom-call(f32[96,128]{1,0:T(8,128)} %rev.6.x_ref, bf16[64,6144]{1,0:T(8,128)(2,1)} %reshape_reshape.4.n_ref), custom_call_target="tpu_custom_call" | custom-call | tf_op jit(solution)/shard_map/pallas_call | solution.py:62
  23.3 1.6 %collective-permute-start.3 = (f32[64,512]{1,0:T(8,128)}, f32[64,512]{1,0:T(8,128)S(1)}, u32[]{:S(2)}, u32[]{:S(2)}) collective-permute-start(f32[64,512]{1,0:T(8,128)} %shard_map.46), channel_id=1, source_target_pairs={{0,4},{4,0},{8,12},{12,8},{1,5},{5,1},{9,13},{13,9},{2,6},{6,2},{1... | collective-permute-start | bytes 393224 | tf_op jit(solution)/shard_map/ppermute | solution.py:74
  24.9 3.6 %collective-permute-done.3 = f32[64,512]{1,0:T(8,128)S(1)} collective-permute-done((f32[64,512]{1,0:T(8,128)}, f32[64,512]{1,0:T(8,128)S(1)}, u32[]{:S(2)}, u32[]{:S(2)}) %collective-permute-start.3) | collective-permute-done | bytes 131104 | tf_op jit(solution)/shard_map/ppermute | solution.py:74
  28.5 0.9 %add.56 = f32[64,512]{1,0:T(8,128)S(1)} add(f32[64,512]{1,0:T(8,128)} %shard_map.46, f32[64,512]{1,0:T(8,128)S(1)} %collective-permute-done.3) | non-fusion elementwise | flops 32768 | bytes 393216 | tf_op jit(solution)/shard_map/add | solution.py:74
  29.4 2.4 %collective-permute-start.4 = (f32[64,512]{1,0:T(8,128)S(1)}, f32[64,512]{1,0:T(8,128)S(1)}, u32[]{:S(2)}, u32[]{:S(2)}) collective-permute-start(f32[64,512]{1,0:T(8,128)S(1)} %add.56), channel_id=1, source_target_pairs={{0,8},{4,12},{8,0},{12,4},{1,9},{5,13},{9,1},{13,5},{2,10},{6,14},... | collective-permute-start | bytes 393224 | tf_op jit(solution)/shard_map/ppermute | solution.py:74
  31.8 3.5 %collective-permute-done.4 = f32[64,512]{1,0:T(8,128)S(1)} collective-permute-done((f32[64,512]{1,0:T(8,128)S(1)}, f32[64,512]{1,0:T(8,128)S(1)}, u32[]{:S(2)}, u32[]{:S(2)}) %collective-permute-start.4) | collective-permute-done | bytes 131104 | tf_op jit(solution)/shard_map/ppermute | solution.py:74
  35.5 2.8 %collective-permute-start.5 = (f32[64]{0:T(128)S(1)}, f32[64]{0:T(128)S(1)}, u32[]{:S(2)}, u32[]{:S(2)}) collective-permute-start(f32[64]{0:T(128)S(1)} %get-tuple-element.5), channel_id=1, source_target_pairs={{0,2},{2,0},{1,3},{3,1},{4,6},{6,4},{5,7},{7,5},{8,10},{10,8},{9,1... | collective-permute-start | bytes 776 | tf_op jit(solution)/shard_map/ppermute | solution.py:74
  38.4 0.2 rev.7
  38.6 1.2 %collective-permute-done.5 = f32[64]{0:T(128)S(1)} collective-permute-done((f32[64]{0:T(128)S(1)}, f32[64]{0:T(128)S(1)}, u32[]{:S(2)}, u32[]{:S(2)}) %collective-permute-start.5) | collective-permute-done | bytes 288 | tf_op jit(solution)/shard_map/ppermute | solution.py:74
  39.8 0.7 %broadcast_divide_fusion = f32[1,64,512]{2,1,0:T(8,128)} fusion(f32[1,64,512]{2,1,0:T(8,128)S(1)} %reshape.115, f32[64]{0:T(128)S(1)} %add_sqrt_fusion.1), kind=kLoop, calls=%fused_computation.9 | loop fusion | flops 32768 | bytes 262400 | tf_op jit(solution)/shard_map/div | solution.py:145
  (27 shorter events, 1.1 us)
Async XLA Ops:
  0.0 4.0 %copy-start = (bf16[1,64,4,3,512]{4,2,3,1,0:T(4,128)(2,1)S(1)}, bf16[1,64,4,3,512]{4,2,3,1,0:T(4,128)(2,1)}, u32[]{:S(2)}) copy-start(bf16[1,64,4,3,512]{4,2,3,1,0:T(4,128)(2,1)} %param.5) | copy-start | bytes 2359300
  0.0 6.2 %collective-permute-start = (bf16[2,3,512]{2,0,1:T(2,128)(2,1)}, bf16[2,3,512]{2,0,1:T(2,128)(2,1)S(1)}, u32[]{:S(2)}, u32[]{:S(2)}) collective-permute-start(bf16[2,3,512]{2,0,1:T(2,128)(2,1)} %param.4), channel_id=1, source_target_pairs={{2,0},{3,1},{6,4},{7,5},{10,8},{11,9},{14,12},{15,13},{18,16},{19,... | collective-permute-start | bytes 18440 | tf_op jit(solution)/shard_map/ppermute | solution.py:89
  3.9 0.7 %copy-start.2 = (s32[2]{0:T(128)S(1)}, s32[2]{0:T(128)}, u32[]{:S(2)}) copy-start(s32[2]{0:T(128)} %param.7) | copy-start | bytes 28
  3.9 2.3 %copy-start.1 = (bf16[2,3,512]{2,0,1:T(2,128)(2,1)S(1)}, bf16[2,3,512]{2,0,1:T(2,128)(2,1)}, u32[]{:S(2)}) copy-start(bf16[2,3,512]{2,0,1:T(2,128)(2,1)} %param.4) | copy-start | bytes 18436
  6.3 4.5 %collective-permute-start.1 = (bf16[2,4,1024]{2,0,1:T(2,128)(2,1)S(1)}, bf16[2,4,1024]{2,0,1:T(2,128)(2,1)S(1)}, u32[]{:S(2)}, u32[]{:S(2)}) collective-permute-start(bf16[2,4,1024]{2,0,1:T(2,128)(2,1)S(1)} %pad_maximum_fusion.5), channel_id=1, source_target_pairs={{0,4},{4,0},{8,12},{12,8},{1,5},{5,1},{9,13},{13,9},{2,6},{6,2},{1... | collective-permute-start | bytes 49160 | tf_op jit(solution)/shard_map/ppermute | solution.py:102
  10.8 5.7 %collective-permute-start.2 = (bf16[4,4,1024]{2,0,1:T(4,128)(2,1)S(1)}, bf16[4,4,1024]{2,0,1:T(4,128)(2,1)S(1)}, u32[]{:S(2)}, u32[]{:S(2)}) collective-permute-start(bf16[4,4,1024]{2,0,1:T(4,128)(2,1)S(1)} %pad_maximum_fusion.4), channel_id=1, source_target_pairs={{0,8},{4,12},{8,0},{12,4},{1,9},{5,13},{9,1},{13,5},{2,10},{6,14},... | collective-permute-start | bytes 98312 | tf_op jit(solution)/shard_map/ppermute | solution.py:102
  23.3 5.2 %collective-permute-start.3 = (f32[64,512]{1,0:T(8,128)}, f32[64,512]{1,0:T(8,128)S(1)}, u32[]{:S(2)}, u32[]{:S(2)}) collective-permute-start(f32[64,512]{1,0:T(8,128)} %shard_map.46), channel_id=1, source_target_pairs={{0,4},{4,0},{8,12},{12,8},{1,5},{5,1},{9,13},{13,9},{2,6},{6,2},{1... | collective-permute-start | bytes 393224 | tf_op jit(solution)/shard_map/ppermute | solution.py:74
  29.4 5.9 %collective-permute-start.4 = (f32[64,512]{1,0:T(8,128)S(1)}, f32[64,512]{1,0:T(8,128)S(1)}, u32[]{:S(2)}, u32[]{:S(2)}) collective-permute-start(f32[64,512]{1,0:T(8,128)S(1)} %add.56), channel_id=1, source_target_pairs={{0,8},{4,12},{8,0},{12,4},{1,9},{5,13},{9,1},{13,5},{2,10},{6,14},... | collective-permute-start | bytes 393224 | tf_op jit(solution)/shard_map/ppermute | solution.py:74
  35.5 4.4 %collective-permute-start.5 = (f32[64]{0:T(128)S(1)}, f32[64]{0:T(128)S(1)}, u32[]{:S(2)}, u32[]{:S(2)}) collective-permute-start(f32[64]{0:T(128)S(1)} %get-tuple-element.5), channel_id=1, source_target_pairs={{0,2},{2,0},{1,3},{3,1},{4,6},{6,4},{5,7},{7,5},{8,10},{10,8},{9,1... | collective-permute-start | bytes 776 | tf_op jit(solution)/shard_map/ppermute | solution.py:74

commit v29 on v21

--- a/solution.py
+++ b/solution.py
@@ -42,7 +42,7 @@
     acc = jnp.zeros(o_ref.shape, jnp.float32)
     if channels <= 16:
         for c in range(channels):
-            acc = one_channel(c, c % 2, acc)
+            acc = one_channel(c, c % 3, acc)
     else:
         pairs = channels // 2
         acc = lax.fori_loop(0, pairs, two_channels, acc, unroll=2 if pairs % 2 == 0 else 1)
@@ -62,7 +62,7 @@
     return pl.pallas_call(
         hankel_kernel,
         out_shape=jax.ShapeDtypeStruct((rows, seg_len), jnp.float32),
-        scratch_shapes=[pltpu.VMEM((2, filter_taps, seg_len), jnp.bfloat16)],
+        scratch_shapes=[pltpu.VMEM((3, filter_taps, seg_len), jnp.bfloat16)],
     )(blocks, normed.reshape(rows, channels * filter_taps))
 
 

time: 40.2 us -> 40.3 us (level)
  no operation moved by 1% of the time
where the time goes in v29:
time: 40.3 us; the launch traced here: 40 us
  starting transfers between devices  14.1 us (35%)
  waiting for transfers between devices  11.6 us (29%)
  other arithmetic  5.37 us (13%)
  Pallas kernels  4.76 us (12%)
  local copies, waits for them, and re-layouts  3.81 us (9%)
    ppermute x3, waiting for transfers between devices, ordered_sum(): part = part + lax.ppermute(part, axis, [(i, i ^ step) for i in range(size)])  8.34 us
    ppermute x3, starting transfers between devices, ordered_sum(): part = part + lax.ppermute(part, axis, [(i, i ^ step) for i in range(size)])  6.83 us
    ppermute x2, starting transfers between devices, gather_owned(): lax.ppermute(here, 'region', [(r, r ^ step) for r in range(regions)])  5.89 us
    pallas_call x1, Pallas kernels, correlate(): pl.pallas_call(hankel_kernel, out_shape=jax.ShapeDtypeStruct((rows, seg_l...  4.76 us
    another operation x1, local copies, waits for them, and re-layouts, correlate(): normed.reshape(rows, channels * filter_taps)  1.84 us
    ppermute x2, waiting for transfers between devices, gather_owned(): lax.ppermute(here, 'region', [(r, r ^ step) for r in range(regions)])  1.72 us
    reduce_sum x1, other arithmetic, per_device(): jnp.sum(widened_templates * widened_templates, axis=4, keepdims=True)  1.65 us
    ppermute x1, waiting for transfers between devices, gather_owned(): lax.ppermute(records[:, :, :filter_taps], 'seg', [(s + 1, s) for s in ran...  1.57 us
  transfers between devices with their start and end apart: 6, of which 5 were waited for; matrix products, arithmetic and copies ran while one was open for 15% of the time, Pallas kernels for 0%

profile of v29, /device:TPU:0, one launch (start us, length us, event | category | flops | bytes accessed | tf_op | source)
XLA Modules:
  0.0 40.0 jit_solution(4245302472009838760)
XLA Ops:
  0.0 1.4 %collective-permute-start = (bf16[2,3,512]{2,0,1:T(2,128)(2,1)}, bf16[2,3,512]{2,0,1:T(2,128)(2,1)S(1)}, u32[]{:S(2)}, u32[]{:S(2)}) collective-permute-start(bf16[2,3,512]{2,0,1:T(2,128)(2,1)} %param.4), channel_id=1, source_target_pairs={{2,0},{3,1},{6,4},{7,5},{10,8},{11,9},{14,12},{15,13},{18,16},{19,... | collective-permute-start | bytes 18440 | tf_op jit(solution)/shard_map/ppermute | solution.py:89
  1.4 0.7 %convert_bitcast_fusion = f32[64,4,3]{0,1,2:T(4,128)S(1)} fusion(s32[1,64,4,3]{1,2,3,0:T(4,128)} %param.6), kind=kLoop, calls=%fused_computation.16 | loop fusion | flops 768 | bytes 6144 | tf_op jit(solution)/shard_map/mul | solution.py:140
  2.1 0.1 copy.9
  2.3 1.7 %fusion.3 = f32[64,4,3]{1,2,0:T(4,128)S(1)} fusion(bf16[1,64,4,3,512]{4,2,3,1,0:T(4,128)(2,1)} %param.5), kind=kLoop, calls=%fused_computation.6 | loop fusion | flops 1178880 | bytes 789504 | tf_op jit(solution)/shard_map/reduce_sum | solution.py:138
  4.0 0.5 %fusion.2 = bf16[1,64,4,3,512]{4,2,3,1,0:T(4,128)(2,1)S(1)} fusion(bf16[1,64,4,3,512]{4,2,3,1,0:T(4,128)(2,1)S(1)} %copy-done, f32[64,4,3]{1,2,0:T(4,128)S(1)} %add_sqrt_fusion, f32[64,4,3]{1,2,0:T(4,128)S(1)} %copy.9), kind=kLoop, calls=%fused_computation.5 | loop fusion | flops 1572864 | bytes 1579008 | tf_op jit(solution)/shard_map/convert_element_type | solution.py:140
  4.6 1.6 %collective-permute-done = bf16[2,3,512]{2,0,1:T(2,128)(2,1)S(1)} collective-permute-done((bf16[2,3,512]{2,0,1:T(2,128)(2,1)}, bf16[2,3,512]{2,0,1:T(2,128)(2,1)S(1)}, u32[]{:S(2)}, u32[]{:S(2)}) %collective-permute-start) | collective-permute-done | bytes 6176 | tf_op jit(solution)/shard_map/ppermute | solution.py:89
  6.3 2.8 %collective-permute-start.1 = (bf16[2,4,1024]{2,0,1:T(2,128)(2,1)S(1)}, bf16[2,4,1024]{2,0,1:T(2,128)(2,1)S(1)}, u32[]{:S(2)}, u32[]{:S(2)}) collective-permute-start(bf16[2,4,1024]{2,0,1:T(2,128)(2,1)S(1)} %pad_maximum_fusion.5), channel_id=1, source_target_pairs={{0,4},{4,0},{8,12},{12,8},{1,5},{5,1},{9,13},{13,9},{2,6},{6,2},{1... | collective-permute-start | bytes 49160 | tf_op jit(solution)/shard_map/ppermute | solution.py:102
  9.1 1.7 %collective-permute-done.1 = bf16[2,4,1024]{2,0,1:T(2,128)(2,1)S(1)} collective-permute-done((bf16[2,4,1024]{2,0,1:T(2,128)(2,1)S(1)}, bf16[2,4,1024]{2,0,1:T(2,128)(2,1)S(1)}, u32[]{:S(2)}, u32[]{:S(2)}) %collective-permute-start.1) | collective-permute-done | bytes 16416 | tf_op jit(solution)/shard_map/ppermute | solution.py:102
  10.8 3.1 %collective-permute-start.2 = (bf16[4,4,1024]{2,0,1:T(4,128)(2,1)S(1)}, bf16[4,4,1024]{2,0,1:T(4,128)(2,1)S(1)}, u32[]{:S(2)}, u32[]{:S(2)}) collective-permute-start(bf16[4,4,1024]{2,0,1:T(4,128)(2,1)S(1)} %pad_maximum_fusion.4), channel_id=1, source_target_pairs={{0,8},{4,12},{8,0},{12,4},{1,9},{5,13},{9,1},{13,5},{2,10},{6,14},... | collective-permute-start | bytes 98312 | tf_op jit(solution)/shard_map/ppermute | solution.py:102
  14.1 0.6 %copy.10 = bf16[1,64,4,3,512]{4,3,2,1,0:T(4,128)(2,1)S(1)} copy(bf16[1,64,4,3,512]{4,2,3,1,0:T(4,128)(2,1)S(1)} %fusion.2) | data formatting | bytes 1572864 | tf_op jit(solution)/shard_map/convert_element_type | solution.py:140
  14.6 1.8 %reshape_reshape.4.n_ref = bf16[64,6144]{1,0:T(8,128)(2,1)} reshape(bf16[1,64,4,3,512]{4,3,2,1,0:T(4,128)(2,1)S(1)} %copy.10) | data formatting | bytes 1572864 | tf_op jit(solution)/shard_map/reshape;reshape | solution.py:66
  16.6 0.2 convert_reduce_fusion.1
  17.0 0.1 fusion
  17.2 0.7 %rev.6.x_ref = f32[96,128]{1,0:T(8,128)} reverse(f32[96,128]{1,0:T(8,128)S(1)} %mul.38), dimensions={1} | reverse | bytes 98304 | tf_op jit(solution)/shard_map/rev | solution.py:61
  17.9 4.8 %shard_map.46 = f32[64,512]{1,0:T(8,128)} custom-call(f32[96,128]{1,0:T(8,128)} %rev.6.x_ref, bf16[64,6144]{1,0:T(8,128)(2,1)} %reshape_reshape.4.n_ref), custom_call_target="tpu_custom_call" | custom-call | tf_op jit(solution)/shard_map/pallas_call | solution.py:62
  22.7 1.6 %collective-permute-start.3 = (f32[64,512]{1,0:T(8,128)}, f32[64,512]{1,0:T(8,128)S(1)}, u32[]{:S(2)}, u32[]{:S(2)}) collective-permute-start(f32[64,512]{1,0:T(8,128)} %shard_map.46), channel_id=1, source_target_pairs={{0,4},{4,0},{8,12},{12,8},{1,5},{5,1},{9,13},{13,9},{2,6},{6,2},{1... | collective-permute-start | bytes 393224 | tf_op jit(solution)/shard_map/ppermute | solution.py:74
  24.3 3.6 %collective-permute-done.3 = f32[64,512]{1,0:T(8,128)S(1)} collective-permute-done((f32[64,512]{1,0:T(8,128)}, f32[64,512]{1,0:T(8,128)S(1)}, u32[]{:S(2)}, u32[]{:S(2)}) %collective-permute-start.3) | collective-permute-done | bytes 131104 | tf_op jit(solution)/shard_map/ppermute | solution.py:74
  27.9 0.9 %add.56 = f32[64,512]{1,0:T(8,128)S(1)} add(f32[64,512]{1,0:T(8,128)} %shard_map.46, f32[64,512]{1,0:T(8,128)S(1)} %collective-permute-done.3) | non-fusion elementwise | flops 32768 | bytes 393216 | tf_op jit(solution)/shard_map/add | solution.py:74
  28.8 2.4 %collective-permute-start.4 = (f32[64,512]{1,0:T(8,128)S(1)}, f32[64,512]{1,0:T(8,128)S(1)}, u32[]{:S(2)}, u32[]{:S(2)}) collective-permute-start(f32[64,512]{1,0:T(8,128)S(1)} %add.56), channel_id=1, source_target_pairs={{0,8},{4,12},{8,0},{12,4},{1,9},{5,13},{9,1},{13,5},{2,10},{6,14},... | collective-permute-start | bytes 393224 | tf_op jit(solution)/shard_map/ppermute | solution.py:74
  31.2 3.5 %collective-permute-done.4 = f32[64,512]{1,0:T(8,128)S(1)} collective-permute-done((f32[64,512]{1,0:T(8,128)S(1)}, f32[64,512]{1,0:T(8,128)S(1)}, u32[]{:S(2)}, u32[]{:S(2)}) %collective-permute-start.4) | collective-permute-done | bytes 131104 | tf_op jit(solution)/shard_map/ppermute | solution.py:74
  34.9 2.8 %collective-permute-start.5 = (f32[64]{0:T(128)S(1)}, f32[64]{0:T(128)S(1)}, u32[]{:S(2)}, u32[]{:S(2)}) collective-permute-start(f32[64]{0:T(128)S(1)} %get-tuple-element.5), channel_id=1, source_target_pairs={{0,2},{2,0},{1,3},{3,1},{4,6},{6,4},{5,7},{7,5},{8,10},{10,8},{9,1... | collective-permute-start | bytes 776 | tf_op jit(solution)/shard_map/ppermute | solution.py:74
  37.8 0.2 rev.7
  38.0 1.2 %collective-permute-done.5 = f32[64]{0:T(128)S(1)} collective-permute-done((f32[64]{0:T(128)S(1)}, f32[64]{0:T(128)S(1)}, u32[]{:S(2)}, u32[]{:S(2)}) %collective-permute-start.5) | collective-permute-done | bytes 288 | tf_op jit(solution)/shard_map/ppermute | solution.py:74
  39.2 0.7 %broadcast_divide_fusion = f32[1,64,512]{2,1,0:T(8,128)} fusion(f32[1,64,512]{2,1,0:T(8,128)S(1)} %reshape.115, f32[64]{0:T(128)S(1)} %add_sqrt_fusion.1), kind=kLoop, calls=%fused_computation.9 | loop fusion | flops 32768 | bytes 262400 | tf_op jit(solution)/shard_map/div | solution.py:145
  (27 shorter events, 1.1 us)
Async XLA Ops:
  0.0 4.0 %copy-start = (bf16[1,64,4,3,512]{4,2,3,1,0:T(4,128)(2,1)S(1)}, bf16[1,64,4,3,512]{4,2,3,1,0:T(4,128)(2,1)}, u32[]{:S(2)}) copy-start(bf16[1,64,4,3,512]{4,2,3,1,0:T(4,128)(2,1)} %param.5) | copy-start | bytes 2359300
  0.0 6.2 %collective-permute-start = (bf16[2,3,512]{2,0,1:T(2,128)(2,1)}, bf16[2,3,512]{2,0,1:T(2,128)(2,1)S(1)}, u32[]{:S(2)}, u32[]{:S(2)}) collective-permute-start(bf16[2,3,512]{2,0,1:T(2,128)(2,1)} %param.4), channel_id=1, source_target_pairs={{2,0},{3,1},{6,4},{7,5},{10,8},{11,9},{14,12},{15,13},{18,16},{19,... | collective-permute-start | bytes 18440 | tf_op jit(solution)/shard_map/ppermute | solution.py:89
  3.9 0.7 %copy-start.2 = (s32[2]{0:T(128)S(1)}, s32[2]{0:T(128)}, u32[]{:S(2)}) copy-start(s32[2]{0:T(128)} %param.7) | copy-start | bytes 28
  3.9 2.3 %copy-start.1 = (bf16[2,3,512]{2,0,1:T(2,128)(2,1)S(1)}, bf16[2,3,512]{2,0,1:T(2,128)(2,1)}, u32[]{:S(2)}) copy-start(bf16[2,3,512]{2,0,1:T(2,128)(2,1)} %param.4) | copy-start | bytes 18436
  6.3 4.5 %collective-permute-start.1 = (bf16[2,4,1024]{2,0,1:T(2,128)(2,1)S(1)}, bf16[2,4,1024]{2,0,1:T(2,128)(2,1)S(1)}, u32[]{:S(2)}, u32[]{:S(2)}) collective-permute-start(bf16[2,4,1024]{2,0,1:T(2,128)(2,1)S(1)} %pad_maximum_fusion.5), channel_id=1, source_target_pairs={{0,4},{4,0},{8,12},{12,8},{1,5},{5,1},{9,13},{13,9},{2,6},{6,2},{1... | collective-permute-start | bytes 49160 | tf_op jit(solution)/shard_map/ppermute | solution.py:102
  10.8 5.7 %collective-permute-start.2 = (bf16[4,4,1024]{2,0,1:T(4,128)(2,1)S(1)}, bf16[4,4,1024]{2,0,1:T(4,128)(2,1)S(1)}, u32[]{:S(2)}, u32[]{:S(2)}) collective-permute-start(bf16[4,4,1024]{2,0,1:T(4,128)(2,1)S(1)} %pad_maximum_fusion.4), channel_id=1, source_target_pairs={{0,8},{4,12},{8,0},{12,4},{1,9},{5,13},{9,1},{13,5},{2,10},{6,14},... | collective-permute-start | bytes 98312 | tf_op jit(solution)/shard_map/ppermute | solution.py:102
  22.7 5.2 %collective-permute-start.3 = (f32[64,512]{1,0:T(8,128)}, f32[64,512]{1,0:T(8,128)S(1)}, u32[]{:S(2)}, u32[]{:S(2)}) collective-permute-start(f32[64,512]{1,0:T(8,128)} %shard_map.46), channel_id=1, source_target_pairs={{0,4},{4,0},{8,12},{12,8},{1,5},{5,1},{9,13},{13,9},{2,6},{6,2},{1... | collective-permute-start | bytes 393224 | tf_op jit(solution)/shard_map/ppermute | solution.py:74
  28.8 5.9 %collective-permute-start.4 = (f32[64,512]{1,0:T(8,128)S(1)}, f32[64,512]{1,0:T(8,128)S(1)}, u32[]{:S(2)}, u32[]{:S(2)}) collective-permute-start(f32[64,512]{1,0:T(8,128)S(1)} %add.56), channel_id=1, source_target_pairs={{0,8},{4,12},{8,0},{12,4},{1,9},{5,13},{9,1},{13,5},{2,10},{6,14},... | collective-permute-start | bytes 393224 | tf_op jit(solution)/shard_map/ppermute | solution.py:74
  34.9 4.4 %collective-permute-start.5 = (f32[64]{0:T(128)S(1)}, f32[64]{0:T(128)S(1)}, u32[]{:S(2)}, u32[]{:S(2)}) collective-permute-start(f32[64]{0:T(128)S(1)} %get-tuple-element.5), channel_id=1, source_target_pairs={{0,2},{2,0},{1,3},{3,1},{4,6},{6,4},{5,7},{7,5},{8,10},{10,8},{9,1... | collective-permute-start | bytes 776 | tf_op jit(solution)/shard_map/ppermute | solution.py:74

commit v30 on v21

--- a/solution.py
+++ b/solution.py
@@ -118,11 +118,10 @@
     ranks = jnp.sum(earlier.astype(jnp.int32), axis=1)
     slot_index = jnp.arange(capacity, dtype=jnp.int32)
     placing = (region_of[None, :] == me) & (ranks[None, :] == slot_index[:, None])
-    owned_rows = jnp.dot(
-        placing.astype(jnp.bfloat16), rows.reshape(stations, -1), preferred_element_type=jnp.float32
-    ).astype(jnp.bfloat16)
+    filled = jnp.sum(placing.astype(jnp.float32), axis=1)
+    weights = (placing.astype(jnp.float32) * filled[:, None]).astype(jnp.bfloat16)
+    owned_rows = jnp.dot(weights, rows.reshape(stations, -1), preferred_element_type=jnp.float32)
     owned_rows = owned_rows.reshape(capacity, components, seg_len + filter_taps)
-    filled = jnp.sum(placing.astype(jnp.float32), axis=1)
     return owned_rows, filled
 
 
@@ -130,7 +129,6 @@
     local_batches, kept, capacity, components, filter_taps = templates.shape
     seg_len = records.shape[2]
     owned_rows, filled = gather_owned(records, station_region, capacity, filter_taps)
-    owned_rows = owned_rows.astype(jnp.float32) * filled[:, None, None]
     flat_owned = owned_rows.reshape(capacity * components, seg_len + filter_taps)
     weight = channel_mask.astype(jnp.float32)
     widened_templates = templates.astype(jnp.float32)

time: 40.2 us -> 40.2 us (level)
  no operation moved by 1% of the time
where the time goes in v30:
time: 40.2 us; the launch traced here: 39.9 us
  starting transfers between devices  14.1 us (35%)
  waiting for transfers between devices  11.6 us (29%)
  other arithmetic  5.36 us (13%)
  Pallas kernels  4.73 us (12%)
  local copies, waits for them, and re-layouts  3.7 us (9%)
    ppermute x3, waiting for transfers between devices, ordered_sum(): part = part + lax.ppermute(part, axis, [(i, i ^ step) for i in range(size)])  8.36 us
    ppermute x3, starting transfers between devices, ordered_sum(): part = part + lax.ppermute(part, axis, [(i, i ^ step) for i in range(size)])  6.81 us
    ppermute x2, starting transfers between devices, gather_owned(): lax.ppermute(here, 'region', [(r, r ^ step) for r in range(regions)])  5.89 us
    pallas_call x1, Pallas kernels, correlate(): pl.pallas_call(hankel_kernel, out_shape=jax.ShapeDtypeStruct((rows, seg_l...  4.73 us
    another operation x1, local copies, waits for them, and re-layouts, correlate(): normed.reshape(rows, channels * filter_taps)  1.84 us
    ppermute x2, waiting for transfers between devices, gather_owned(): lax.ppermute(here, 'region', [(r, r ^ step) for r in range(regions)])  1.72 us
    reduce_sum x1, other arithmetic, per_device(): jnp.sum(widened_templates * widened_templates, axis=4, keepdims=True)  1.65 us
    ppermute x1, waiting for transfers between devices, gather_owned(): lax.ppermute(records[:, :, :filter_taps], 'seg', [(s + 1, s) for s in ran...  1.57 us
  transfers between devices with their start and end apart: 6, of which 5 were waited for; matrix products, arithmetic and copies ran while one was open for 15% of the time, Pallas kernels for 0%

profile of v30, /device:TPU:0, one launch (start us, length us, event | category | flops | bytes accessed | tf_op | source)
XLA Modules:
  0.0 39.9 jit_solution(16677622167323474413)
XLA Ops:
  0.0 1.4 %collective-permute-start = (bf16[2,3,512]{2,0,1:T(2,128)(2,1)}, bf16[2,3,512]{2,0,1:T(2,128)(2,1)S(1)}, u32[]{:S(2)}, u32[]{:S(2)}) collective-permute-start(bf16[2,3,512]{2,0,1:T(2,128)(2,1)} %param.4), channel_id=1, source_target_pairs={{2,0},{3,1},{6,4},{7,5},{10,8},{11,9},{14,12},{15,13},{18,16},{19,... | collective-permute-start | bytes 18440 | tf_op jit(solution)/shard_map/ppermute | solution.py:89
  1.4 0.7 %convert_bitcast_fusion = f32[64,4,3]{0,1,2:T(4,128)S(1)} fusion(s32[1,64,4,3]{1,2,3,0:T(4,128)} %param.6), kind=kLoop, calls=%fused_computation.14 | loop fusion | flops 768 | bytes 6144 | tf_op jit(solution)/shard_map/mul | solution.py:138
  2.1 0.1 copy.9
  2.3 1.7 %fusion.2 = f32[64,4,3]{1,2,0:T(4,128)S(1)} fusion(bf16[1,64,4,3,512]{4,2,3,1,0:T(4,128)(2,1)} %param.5), kind=kLoop, calls=%fused_computation.4 | loop fusion | flops 1178880 | bytes 789504 | tf_op jit(solution)/shard_map/reduce_sum | solution.py:136
  4.0 0.5 %fusion.1 = bf16[1,64,4,3,512]{4,2,3,1,0:T(4,128)(2,1)S(1)} fusion(bf16[1,64,4,3,512]{4,2,3,1,0:T(4,128)(2,1)S(1)} %copy-done, f32[64,4,3]{1,2,0:T(4,128)S(1)} %add_sqrt_fusion, f32[64,4,3]{1,2,0:T(4,128)S(1)} %copy.9), kind=kLoop, calls=%fused_computation.3 | loop fusion | flops 1572864 | bytes 1579008 | tf_op jit(solution)/shard_map/convert_element_type | solution.py:138
  4.6 1.6 %collective-permute-done = bf16[2,3,512]{2,0,1:T(2,128)(2,1)S(1)} collective-permute-done((bf16[2,3,512]{2,0,1:T(2,128)(2,1)}, bf16[2,3,512]{2,0,1:T(2,128)(2,1)S(1)}, u32[]{:S(2)}, u32[]{:S(2)}) %collective-permute-start) | collective-permute-done | bytes 6176 | tf_op jit(solution)/shard_map/ppermute | solution.py:89
  6.3 2.8 %collective-permute-start.1 = (bf16[2,4,1024]{2,0,1:T(2,128)(2,1)S(1)}, bf16[2,4,1024]{2,0,1:T(2,128)(2,1)S(1)}, u32[]{:S(2)}, u32[]{:S(2)}) collective-permute-start(bf16[2,4,1024]{2,0,1:T(2,128)(2,1)S(1)} %pad_maximum_fusion.5), channel_id=1, source_target_pairs={{0,4},{4,0},{8,12},{12,8},{1,5},{5,1},{9,13},{13,9},{2,6},{6,2},{1... | collective-permute-start | bytes 49160 | tf_op jit(solution)/shard_map/ppermute | solution.py:102
  9.1 1.7 %collective-permute-done.1 = bf16[2,4,1024]{2,0,1:T(2,128)(2,1)S(1)} collective-permute-done((bf16[2,4,1024]{2,0,1:T(2,128)(2,1)S(1)}, bf16[2,4,1024]{2,0,1:T(2,128)(2,1)S(1)}, u32[]{:S(2)}, u32[]{:S(2)}) %collective-permute-start.1) | collective-permute-done | bytes 16416 | tf_op jit(solution)/shard_map/ppermute | solution.py:102
  10.8 3.1 %collective-permute-start.2 = (bf16[4,4,1024]{2,0,1:T(4,128)(2,1)S(1)}, bf16[4,4,1024]{2,0,1:T(4,128)(2,1)S(1)}, u32[]{:S(2)}, u32[]{:S(2)}) collective-permute-start(bf16[4,4,1024]{2,0,1:T(4,128)(2,1)S(1)} %pad_maximum_fusion.4), channel_id=1, source_target_pairs={{0,8},{4,12},{8,0},{12,4},{1,9},{5,13},{9,1},{13,5},{2,10},{6,14},... | collective-permute-start | bytes 98312 | tf_op jit(solution)/shard_map/ppermute | solution.py:102
  14.1 0.6 %copy.10 = bf16[1,64,4,3,512]{4,3,2,1,0:T(4,128)(2,1)S(1)} copy(bf16[1,64,4,3,512]{4,2,3,1,0:T(4,128)(2,1)S(1)} %fusion.1) | data formatting | bytes 1572864 | tf_op jit(solution)/shard_map/convert_element_type | solution.py:138
  14.6 1.8 %reshape_reshape.3.n_ref = bf16[64,6144]{1,0:T(8,128)(2,1)} reshape(bf16[1,64,4,3,512]{4,3,2,1,0:T(4,128)(2,1)S(1)} %copy.10) | data formatting | bytes 1572864 | tf_op jit(solution)/shard_map/reshape;reshape | solution.py:66
  16.6 0.2 convert_reduce_fusion.1
  17.0 0.2 fusion.4
  17.2 0.7 %rev.6.x_ref = f32[96,128]{1,0:T(8,128)} reverse(f32[96,128]{1,0:T(8,128)S(1)} %reshape_reshape_reshape.3), dimensions={1} | reverse | bytes 98304 | tf_op jit(solution)/shard_map/rev | solution.py:61
  17.9 4.7 %shard_map.46 = f32[64,512]{1,0:T(8,128)} custom-call(f32[96,128]{1,0:T(8,128)} %rev.6.x_ref, bf16[64,6144]{1,0:T(8,128)(2,1)} %reshape_reshape.3.n_ref), custom_call_target="tpu_custom_call" | custom-call | tf_op jit(solution)/shard_map/pallas_call | solution.py:62
  22.6 1.6 %collective-permute-start.3 = (f32[64,512]{1,0:T(8,128)}, f32[64,512]{1,0:T(8,128)S(1)}, u32[]{:S(2)}, u32[]{:S(2)}) collective-permute-start(f32[64,512]{1,0:T(8,128)} %shard_map.46), channel_id=1, source_target_pairs={{0,4},{4,0},{8,12},{12,8},{1,5},{5,1},{9,13},{13,9},{2,6},{6,2},{1... | collective-permute-start | bytes 393224 | tf_op jit(solution)/shard_map/ppermute | solution.py:74
  24.2 3.6 %collective-permute-done.3 = f32[64,512]{1,0:T(8,128)S(1)} collective-permute-done((f32[64,512]{1,0:T(8,128)}, f32[64,512]{1,0:T(8,128)S(1)}, u32[]{:S(2)}, u32[]{:S(2)}) %collective-permute-start.3) | collective-permute-done | bytes 131104 | tf_op jit(solution)/shard_map/ppermute | solution.py:74
  27.8 0.9 %add.56 = f32[64,512]{1,0:T(8,128)S(1)} add(f32[64,512]{1,0:T(8,128)} %shard_map.46, f32[64,512]{1,0:T(8,128)S(1)} %collective-permute-done.3) | non-fusion elementwise | flops 32768 | bytes 393216 | tf_op jit(solution)/shard_map/add | solution.py:74
  28.7 2.4 %collective-permute-start.4 = (f32[64,512]{1,0:T(8,128)S(1)}, f32[64,512]{1,0:T(8,128)S(1)}, u32[]{:S(2)}, u32[]{:S(2)}) collective-permute-start(f32[64,512]{1,0:T(8,128)S(1)} %add.56), channel_id=1, source_target_pairs={{0,8},{4,12},{8,0},{12,4},{1,9},{5,13},{9,1},{13,5},{2,10},{6,14},... | collective-permute-start | bytes 393224 | tf_op jit(solution)/shard_map/ppermute | solution.py:74
  31.1 3.5 %collective-permute-done.4 = f32[64,512]{1,0:T(8,128)S(1)} collective-permute-done((f32[64,512]{1,0:T(8,128)S(1)}, f32[64,512]{1,0:T(8,128)S(1)}, u32[]{:S(2)}, u32[]{:S(2)}) %collective-permute-start.4) | collective-permute-done | bytes 131104 | tf_op jit(solution)/shard_map/ppermute | solution.py:74
  34.8 2.8 %collective-permute-start.5 = (f32[64]{0:T(128)S(1)}, f32[64]{0:T(128)S(1)}, u32[]{:S(2)}, u32[]{:S(2)}) collective-permute-start(f32[64]{0:T(128)S(1)} %get-tuple-element.5), channel_id=1, source_target_pairs={{0,2},{2,0},{1,3},{3,1},{4,6},{6,4},{5,7},{7,5},{8,10},{10,8},{9,1... | collective-permute-start | bytes 776 | tf_op jit(solution)/shard_map/ppermute | solution.py:74
  37.6 0.2 rev.7
  37.9 1.2 %collective-permute-done.5 = f32[64]{0:T(128)S(1)} collective-permute-done((f32[64]{0:T(128)S(1)}, f32[64]{0:T(128)S(1)}, u32[]{:S(2)}, u32[]{:S(2)}) %collective-permute-start.5) | collective-permute-done | bytes 288 | tf_op jit(solution)/shard_map/ppermute | solution.py:74
  39.1 0.7 %broadcast_divide_fusion = f32[1,64,512]{2,1,0:T(8,128)} fusion(f32[1,64,512]{2,1,0:T(8,128)S(1)} %reshape.110, f32[64]{0:T(128)S(1)} %add_sqrt_fusion.1), kind=kLoop, calls=%fused_computation.7 | loop fusion | flops 32768 | bytes 262400 | tf_op jit(solution)/shard_map/div | solution.py:143
  (24 shorter events, 0.9 us)
Async XLA Ops:
  0.0 4.0 %copy-start = (bf16[1,64,4,3,512]{4,2,3,1,0:T(4,128)(2,1)S(1)}, bf16[1,64,4,3,512]{4,2,3,1,0:T(4,128)(2,1)}, u32[]{:S(2)}) copy-start(bf16[1,64,4,3,512]{4,2,3,1,0:T(4,128)(2,1)} %param.5) | copy-start | bytes 2359300
  0.0 6.2 %collective-permute-start = (bf16[2,3,512]{2,0,1:T(2,128)(2,1)}, bf16[2,3,512]{2,0,1:T(2,128)(2,1)S(1)}, u32[]{:S(2)}, u32[]{:S(2)}) collective-permute-start(bf16[2,3,512]{2,0,1:T(2,128)(2,1)} %param.4), channel_id=1, source_target_pairs={{2,0},{3,1},{6,4},{7,5},{10,8},{11,9},{14,12},{15,13},{18,16},{19,... | collective-permute-start | bytes 18440 | tf_op jit(solution)/shard_map/ppermute | solution.py:89
  3.9 0.7 %copy-start.2 = (s32[2]{0:T(128)S(1)}, s32[2]{0:T(128)}, u32[]{:S(2)}) copy-start(s32[2]{0:T(128)} %param.7) | copy-start | bytes 28
  3.9 2.3 %copy-start.1 = (bf16[2,3,512]{2,0,1:T(2,128)(2,1)S(1)}, bf16[2,3,512]{2,0,1:T(2,128)(2,1)}, u32[]{:S(2)}) copy-start(bf16[2,3,512]{2,0,1:T(2,128)(2,1)} %param.4) | copy-start | bytes 18436
  6.3 4.5 %collective-permute-start.1 = (bf16[2,4,1024]{2,0,1:T(2,128)(2,1)S(1)}, bf16[2,4,1024]{2,0,1:T(2,128)(2,1)S(1)}, u32[]{:S(2)}, u32[]{:S(2)}) collective-permute-start(bf16[2,4,1024]{2,0,1:T(2,128)(2,1)S(1)} %pad_maximum_fusion.5), channel_id=1, source_target_pairs={{0,4},{4,0},{8,12},{12,8},{1,5},{5,1},{9,13},{13,9},{2,6},{6,2},{1... | collective-permute-start | bytes 49160 | tf_op jit(solution)/shard_map/ppermute | solution.py:102
  10.8 5.7 %collective-permute-start.2 = (bf16[4,4,1024]{2,0,1:T(4,128)(2,1)S(1)}, bf16[4,4,1024]{2,0,1:T(4,128)(2,1)S(1)}, u32[]{:S(2)}, u32[]{:S(2)}) collective-permute-start(bf16[4,4,1024]{2,0,1:T(4,128)(2,1)S(1)} %pad_maximum_fusion.4), channel_id=1, source_target_pairs={{0,8},{4,12},{8,0},{12,4},{1,9},{5,13},{9,1},{13,5},{2,10},{6,14},... | collective-permute-start | bytes 98312 | tf_op jit(solution)/shard_map/ppermute | solution.py:102
  22.6 5.2 %collective-permute-start.3 = (f32[64,512]{1,0:T(8,128)}, f32[64,512]{1,0:T(8,128)S(1)}, u32[]{:S(2)}, u32[]{:S(2)}) collective-permute-start(f32[64,512]{1,0:T(8,128)} %shard_map.46), channel_id=1, source_target_pairs={{0,4},{4,0},{8,12},{12,8},{1,5},{5,1},{9,13},{13,9},{2,6},{6,2},{1... | collective-permute-start | bytes 393224 | tf_op jit(solution)/shard_map/ppermute | solution.py:74
  28.7 5.9 %collective-permute-start.4 = (f32[64,512]{1,0:T(8,128)S(1)}, f32[64,512]{1,0:T(8,128)S(1)}, u32[]{:S(2)}, u32[]{:S(2)}) collective-permute-start(f32[64,512]{1,0:T(8,128)S(1)} %add.56), channel_id=1, source_target_pairs={{0,8},{4,12},{8,0},{12,4},{1,9},{5,13},{9,1},{13,5},{2,10},{6,14},... | collective-permute-start | bytes 393224 | tf_op jit(solution)/shard_map/ppermute | solution.py:74
  34.8 4.4 %collective-permute-start.5 = (f32[64]{0:T(128)S(1)}, f32[64]{0:T(128)S(1)}, u32[]{:S(2)}, u32[]{:S(2)}) collective-permute-start(f32[64]{0:T(128)S(1)} %get-tuple-element.5), channel_id=1, source_target_pairs={{0,2},{2,0},{1,3},{3,1},{4,6},{6,4},{5,7},{7,5},{8,10},{10,8},{9,1... | collective-permute-start | bytes 776 | tf_op jit(solution)/shard_map/ppermute | solution.py:74
